TPU v7x, 32 devices: a whole 2x2x4 slice. The times are simulated.
32 devices in a mesh: expert: 4 (over y, x), dp: 8 (over z, core).
Axes of the slice: x: 2, y: 2, z: 4, core: 2. Of those that a mesh axis runs over, the one named last changes fastest.
Arguments:
- routes: int32 [4096, 2], P(('expert', 'dp')), may hold values from 0 to 1, as said below
- expert_inputs: bfloat16 [8, 4, 512, 2048], P('dp', 'expert'), may hold values from -6 to 6
- hidden_grad: bfloat16 [8, 4, 512, 2048], P('dp', 'expert'), may hold values from -6 to 6
- weight: float32 [2048, 8192], P('dp', 'expert'), may hold values from -0.125 to 0.125
- moment_one: float32 [2048, 8192], P('dp', 'expert'), may hold values from -6 to 6
- moment_two: float32 [2048, 8192], P('dp', 'expert'), may hold values from 0.5 to 4
Outputs:
- token_grad: bfloat16 [4096, 2048], P(('expert', 'dp'))
- new_weight: float32 [2048, 8192], P('dp', 'expert')
- new_first: float32 [2048, 8192], P('dp', 'expert')
- new_second: float32 [2048, 8192], P('dp', 'expert')
Inputs may be any that keep to these rules, and one draw needn't show every extreme that they name: `routes`: each token names 2 different experts; the tokens of one device name one expert at most 128 times, and in every device's tokens some expert is named exactly 128 times.
All inputs are finite; a program needn't handle non-finite values.
Results may differ from a plain program's by a relative error of at most 0.0045.
The roundings to bfloat16 on the way count: a program that leaves them out, or rounds other values in their place, can miss the bound.
Values may be sent and summed in bfloat16 or wider, within the bound.
No kernel may reach another device: no remote copies, remote signals or barrier semaphores. Data moves between devices by JAX's collectives and lax.ppermute only.
A program may use at most 128 MiB of HBM per device.

v0:
```python
import jax
import jax.numpy as jnp
from jax import lax
from jax.sharding import PartitionSpec as P

beta_one = 0.9
beta_two = 0.95
learn_rate = 0.003
decay = 0.1
epsilon = 1e-08
loss_scale = 64.0
bias_one = 1.0 - (0.9**50) ** 2
bias_two = 1.0 - (0.95**50) ** 2


def adamw(weight, moment_one, moment_two, grad):
    new_first = beta_one * moment_one + (1.0 - beta_one) * grad
    new_second = beta_two * moment_two + (1.0 - beta_two) * grad * grad
    update = new_first / bias_one / (jnp.sqrt(new_second / bias_two) + epsilon)
    new_weight = weight - learn_rate * (update + decay * weight)
    return (new_weight, new_first, new_second)


def shards(routes, expert_inputs, hidden_grad, weight, moment_one, moment_two):
    n_expert = lax.axis_size("expert")
    experts = n_expert // 2
    slot_rows = expert_inputs.shape[2]
    capacity = slot_rows // n_expert
    width = expert_inputs.shape[3]
    tok_count = routes.shape[0]
    top_count = routes.shape[1]
    flat_routes = routes.reshape(-1)
    onehot = (flat_routes[:, None] == jnp.arange(experts, dtype=jnp.int32)[None, :]).astype(
        jnp.int32
    )
    running = jnp.cumsum(onehot, axis=0)
    slots = jnp.sum((running - 1) * onehot, axis=1).reshape(tok_count, top_count)
    counts = jnp.sum(onehot, axis=0)
    all_counts = lax.all_gather(counts[None, :], "expert", axis=0, tiled=True)
    my_expert = lax.axis_index("expert") // 2
    chosen = jnp.arange(experts, dtype=jnp.int32)[None, :] == my_expert
    my_counts = jnp.sum(jnp.where(chosen, all_counts, 0), axis=1)
    valid = (jnp.arange(capacity, dtype=jnp.int32)[None, :] < my_counts[:, None]).reshape(-1)
    inputs_flat = expert_inputs.reshape(slot_rows, width)
    grad_flat = hidden_grad.reshape(slot_rows, -1)
    masked = jnp.where(valid[:, None], grad_flat, jnp.zeros_like(grad_flat))
    wbf = weight.astype(jnp.bfloat16)
    partial_rows = lax.dot_general(
        masked,
        lax.all_gather(wbf, "dp", axis=0, tiled=True),
        (((1,), (1,)), ((), ())),
        preferred_element_type=jnp.float32,
    )
    sent = partial_rows.reshape(n_expert, capacity, width)
    received = lax.all_to_all(sent, "expert", split_axis=0, concat_axis=0, tiled=True)
    paired = jnp.sum(received.reshape(experts, 2, capacity, width), axis=1).astype(jnp.bfloat16)
    picked = paired[routes, slots]
    token_grad = jnp.sum(picked.astype(jnp.float32), axis=1).astype(jnp.bfloat16)
    owned = lax.psum_scatter(
        lax.dot_general(
            inputs_flat, masked, (((0,), (0,)), ((), ())), preferred_element_type=jnp.float32
        ).astype(jnp.bfloat16),
        "dp",
        scatter_dimension=0,
        tiled=True,
    ).astype(jnp.float32)
    new_weight, new_first, new_second = adamw(weight, moment_one, moment_two, owned / loss_scale)
    return (token_grad, new_weight, new_first, new_second)


def solution(mesh):
    in_specs = (
        P(("expert", "dp"), None),
        P("dp", "expert", None, None),
        P("dp", "expert", None, None),
        P("dp", "expert"),
        P("dp", "expert"),
        P("dp", "expert"),
    )
    out_specs = (P(("expert", "dp"), None), P("dp", "expert"), P("dp", "expert"), P("dp", "expert"))
    return jax.shard_map(shards, mesh=mesh, in_specs=in_specs, out_specs=out_specs, check_vma=False)
```

profile of v0, /device:TPU:0, one launch (start us, length us, event | category | flops | bytes accessed | tf_op | source)
XLA Modules:
  0.0 221.4 jit_solution(1023216353679421165)
XLA Ops:
  7.2 2.9 %convert_element_type.25 = bf16[256,2048]{1,0:T(8,128)(2,1)} convert(f32[256,2048]{1,0:T(8,128)} %param.9) | non-fusion elementwise | flops 524288 | bytes 3145728 | tf_op jit(solution)/shard_map/convert_element_type | solution.py:47
  10.2 0.1 copy.31
  10.3 0.1 eq.42
  10.4 0.1 eq.38
  10.6 0.6 reduce-window.6
  11.2 0.2 slice_reduce_fusion
  11.4 0.2 reduce-window.9
  11.6 0.6 dynamic-slice
  12.9 0.1 fusion.14
  13.1 0.2 dynamic-update-slice
  13.3 8.8 %all-reduce = s32[8]{0:T(128)S(1)} all-reduce(s32[8]{0:T(128)S(1)} %dynamic-update-slice), channel_id=2, replica_groups=mesh['expert'=4,'dp'=8] {'expert'}, use_global_device_ids=true, to_apply=%add | all-reduce | flops 8 | bytes 64
  22.1 0.1 reshape.114
  22.2 0.1 select_reduce_fusion
  22.4 8.8 %convert_bitcast_fusion = bf16[2048,2048]{0,1:T(8,128)(2,1)} fusion(bf16[1,1,512,2048]{3,2,1,0:T(8,128)(2,1)S(1)} %copy-done, bf16[1,1,512,2048]{3,2,1,0:T(8,128)(2,1)} %param.8, pred[512]{0:T(512)(128)(4,1)S(1)} %get-tuple-element.21), kind=kOutput, calls=%fused_computation.3 | convolution fusion | flops 4300210176 | bytes 12583424 | tf_op jit(solution)/shard_map/dot_general | solution.py:60
  31.2 63.8 %all-gather.3.cloned.1.call-done = bf16[2048,2048]{1,0:T(8,128)(2,1)} async-done(((bf16[256,2048]{1,0:T(8,128)(2,1)}), bf16[2048,2048]{1,0:T(8,128)(2,1)}) %all-gather.3.cloned.1.call-update) | async-done | bytes 8388624 | tf_op jit(solution)/shard_map/all_gather | solution.py:50
  95.0 10.5 %fusion = f32[4,128,2048]{2,1,0:T(8,128)} fusion(bf16[2048,2048]{1,0:T(8,128)(2,1)} %all-gather.3.cloned.1.call-done, bf16[4,128,2048]{2,1,0:T(8,128)(2,1)} %bitcast.39, pred[4,128]{1,0:T(4,128)(4,1)S(1)} %get-tuple-element.22), kind=kOutput, calls=%fused_computation.1 | convolution fusion | flops 4296015872 | bytes 14680576 | tf_op jit(solution)/shard_map/dot_general | solution.py:48
  105.6 5.1 %all-to-all-start = ((f32[4,128,2048]{2,1,0:T(8,128)}), f32[4,128,2048]{2,1,0:T(8,128)}, u32[]{:S(2)}, u32[]{:S(2)}) async-start(f32[4,128,2048]{2,1,0:T(8,128)} %fusion), calls=%async_computation | async-start | bytes 8388608 | tf_op jit(solution)/shard_map/all_to_all | solution.py:55
  110.7 2.9 %copy.40 = f32[256,2048]{0,1:T(8,128)} copy(f32[256,2048]{1,0:T(8,128)} %param.9) | data formatting | bytes 4194304 | tf_op args[3]
  113.6 0.1 reshape.106
  113.8 0.1 copy.36
  113.9 0.1 reshape.108
  114.1 2.9 %copy.37 = f32[256,2048]{0,1:T(8,128)} copy(f32[256,2048]{1,0:T(8,128)} %param.10) | data formatting | bytes 4194304 | tf_op args[4]
  117.0 2.9 %copy.38 = f32[256,2048]{0,1:T(8,128)} copy(f32[256,2048]{1,0:T(8,128)} %param.11) | data formatting | bytes 4194304 | tf_op args[5]
  119.9 65.6 %reduce-scatter.2.cloned.1.call-done = bf16[256,2048]{0,1:T(8,128)(2,1)} async-done(((bf16[2048,2048]{0,1:T(8,128)(2,1)}), bf16[256,2048]{0,1:T(8,128)(2,1)}) %reduce-scatter.2.cloned.1.call-update) | async-done | bytes 1048592 | tf_op jit(solution)/shard_map/reduce_scatter | solution.py:59
  185.5 7.0 %multiply_subtract_fusion = (f32[256,2048]{0,1:T(8,128)}, f32[256,2048]{0,1:T(8,128)}, f32[256,2048]{0,1:T(8,128)}) fusion(f32[256,2048]{0,1:T(8,128)} %copy.40, bf16[256,2048]{0,1:T(8,128)(2,1)} %reduce-scatter.2.cloned.1.call-done, f32[256,2048]{0,1:T(8,128)} %copy.37, f32[256,2048]{0,1:T(8,128)} %copy.38), kind=kLoop, calls=%fused_computation.13 | loop fusion | flops 8912896 | bytes 13631488 | tf_op jit(solution)/shard_map/sub | solution.py:20
  192.5 2.9 %copy.41 = f32[256,2048]{1,0:T(8,128)} copy(f32[256,2048]{0,1:T(8,128)} %get-tuple-element.18) | data formatting | bytes 4194304
  195.4 2.9 %copy.42 = f32[256,2048]{1,0:T(8,128)} copy(f32[256,2048]{0,1:T(8,128)} %get-tuple-element.19) | data formatting | bytes 4194304
  198.2 2.9 %copy.43 = f32[256,2048]{1,0:T(8,128)} copy(f32[256,2048]{0,1:T(8,128)} %get-tuple-element.20) | data formatting | bytes 4194304
  201.1 2.7 %bitcast_reduce_fusion = bf16[2,128,2048]{2,1,0:T(8,128)(2,1)S(1)} fusion(f32[4,128,2048]{2,1,0:T(8,128)} %all-to-all-done), kind=kLoop, calls=%fused_computation.4 | loop fusion | flops 524288 | bytes 5242880 | tf_op jit(solution)/shard_map/reduce_sum | solution.py:56
  203.9 5.3 %gather_fusion = bf16[256,2048]{1,0:T(8,128)(2,1)} fusion(bf16[2,128,2048]{2,1,0:T(8,128)(2,1)S(1)} %bitcast_reduce_fusion, s32[256]{0:T(256)S(1)} %reshape.108), kind=kCustom, calls=%fused_computation | custom fusion | bytes 2099200 | tf_op jit(solution)/shard_map/gather | solution.py:57
  209.2 1.7 reshape.111
  210.9 3.6 %reduce_sum.52 = bf16[128,2048]{1,0:T(8,128)(2,1)} reduce(bf16[128,2,2048]{2,1,0:T(2,128)(2,1)S(1)} %reshape.111, bf16[]{:T(256)} %constant.46.clone.1), dimensions={1}, to_apply=%region_6.7 | reduce | flops 262144 | bytes 1572866 | tf_op jit(solution)/shard_map/reduce_sum | solution.py:58
  (18 shorter events, 0.4 us)
Async XLA Ops:
  7.2 15.2 %copy-start = (bf16[1,1,512,2048]{3,2,1,0:T(8,128)(2,1)S(1)}, bf16[1,1,512,2048]{3,2,1,0:T(8,128)(2,1)}, u32[]{:S(2)}) copy-start(bf16[1,1,512,2048]{3,2,1,0:T(8,128)(2,1)} %param.7) | copy-start | bytes 6291460
  7.2 4.4 %copy-start.2 = (u32[32]{0:T(128)S(1)}, u32[32]{0:T(128)}, u32[]{:S(2)}) copy-start(u32[32]{0:T(128)} %constant.77) | copy-start | bytes 388
  7.2 3.0 %copy-start.1 = (s32[128,2]{0,1:T(2,128)S(1)}, s32[128,2]{0,1:T(2,128)}, u32[]{:S(2)}) copy-start(s32[128,2]{0,1:T(2,128)} %param.6) | copy-start | bytes 3076
  7.2 87.8 %all-gather.3.cloned.1.call-start = ((), (), s32[]{:S(2)}) async-start(), calls=%async_computation.2 | async-start | bytes 9437184 | tf_op jit(solution)/shard_map/all_gather | solution.py:50
  10.1 175.4 %reduce-scatter.2.cloned.1.call-start = ((), (), s32[]{:S(2)}) async-start(), calls=%async_computation.3 | async-start | bytes 9437184 | tf_op jit(solution)/shard_map/reduce_scatter | solution.py:59
  105.6 95.5 %all-to-all-start = ((f32[4,128,2048]{2,1,0:T(8,128)}), f32[4,128,2048]{2,1,0:T(8,128)}, u32[]{:S(2)}, u32[]{:S(2)}) async-start(f32[4,128,2048]{2,1,0:T(8,128)} %fusion), calls=%async_computation | async-start | bytes 8388608 | tf_op jit(solution)/shard_map/all_to_all | solution.py:55
Sparse Core Ops, SparseCore 0:
  10.2 84.7 all-gather.2
  97.3 88.1 reduce-scatter.1
where the time goes:
time: 222 us; the launch traced here: 221 us
  waiting for transfers between devices  129 us (58%)
  local copies, waits for them, and re-layouts  26.4 us (12%)
  matrix products  19.4 us (9%)
  other arithmetic  17.4 us (8%)
  between operations  14.8 us (7%)
  blocking collectives  8.82 us (4%)
  starting transfers between devices  5.2 us (2%)
    reduce_scatter x1, waiting for transfers between devices, shards(): lax.psum_scatter(lax.dot_general(inputs_flat, masked, (((0,), (0,)), ((),...  65.6 us
    all_gather x1, waiting for transfers between devices, shards(): lax.all_gather(wbf, 'dp', axis=0, tiled=True)  63.8 us
    unnamed x16, local copies, waits for them, and re-layouts  18.3 us
    dot_general x1, matrix products, shards(): lax.dot_general(masked, lax.all_gather(wbf, 'dp', axis=0, tiled=True), ((...  10.5 us
    unnamed x1, blocking collectives  8.82 us
    dot_general x1, matrix products, shards(): lax.dot_general(inputs_flat, masked, (((0,), (0,)), ((), ())), preferred_...  8.81 us
    gather x2, local copies, waits for them, and re-layouts, shards(): picked = paired[routes, slots]  7.06 us
    sub x1, other arithmetic, adamw(): new_weight = weight - learn_rate * (update + decay * weight)  6.97 us
  transfers between devices with their start and end apart: 3, of which 2 were waited for; matrix products, arithmetic and copies ran while one was open for 21% of the time, Pallas kernels for 0%

commit v1 on v0

--- a/solution.py
+++ b/solution.py
@@ -21,14 +21,64 @@
     return (new_weight, new_first, new_second)
 
 
+def gather_counts(counts, n_expert, me_e):
+    got = [counts]
+    for k in range(1, n_expert):
+        got.append(lax.ppermute(counts, "expert", [(i, (i + k) % n_expert) for i in range(n_expert)]))
+    stacked = jnp.stack(got)
+    src = (me_e - jnp.arange(n_expert, dtype=jnp.int32)) % n_expert
+    return stacked[src]
+
+
+def gather_rows_relative(block, n, me):
+    left = [None] * n
+    right = [None] * n
+    cur_r = block
+    cur_l = block
+    for t in range(1, n):
+        cur_r = lax.ppermute(cur_r, "dp", [(p, p + 1) for p in range(t - 1, n - 1)])
+        right[t] = cur_r
+        cur_l = lax.ppermute(cur_l, "dp", [(p, p - 1) for p in range(1, n - t + 1)])
+        left[t] = cur_l
+    parts = [block]
+    for r in range(1, n):
+        parts.append(jnp.where(me + r < n, left[r], right[n - r]))
+    return jnp.concatenate(parts, axis=0)
+
+
+def reduce_scatter_rows(full, n, me, rows):
+    def own_block(q):
+        q = jnp.clip(q, 0, n - 1)
+        return lax.dynamic_slice_in_dim(full, q * rows, rows, axis=0)
+
+    recv_r = None
+    recv_l = None
+    for t in range(1, n):
+        pay_r = own_block(me + n - t)
+        pay_l = own_block(me - n + t)
+        if recv_r is not None:
+            pay_r = pay_r + recv_r.astype(jnp.float32)
+            pay_l = pay_l + recv_l.astype(jnp.float32)
+        recv_r = lax.ppermute(pay_r.astype(jnp.bfloat16), "dp", [(p, p + 1) for p in range(0, t)])
+        recv_l = lax.ppermute(pay_l.astype(jnp.bfloat16), "dp", [(p, p - 1) for p in range(n - t, n)])
+    total = own_block(me)
+    if recv_r is not None:
+        total = total + recv_r.astype(jnp.float32) + recv_l.astype(jnp.float32)
+    return total
+
+
 def shards(routes, expert_inputs, hidden_grad, weight, moment_one, moment_two):
     n_expert = lax.axis_size("expert")
+    n_dp = lax.axis_size("dp")
     experts = n_expert // 2
     slot_rows = expert_inputs.shape[2]
     capacity = slot_rows // n_expert
     width = expert_inputs.shape[3]
+    rows = weight.shape[0]
     tok_count = routes.shape[0]
     top_count = routes.shape[1]
+    me_e = lax.axis_index("expert")
+    me_p = lax.axis_index("dp")
     flat_routes = routes.reshape(-1)
     onehot = (flat_routes[:, None] == jnp.arange(experts, dtype=jnp.int32)[None, :]).astype(
         jnp.int32
@@ -36,8 +86,8 @@
     running = jnp.cumsum(onehot, axis=0)
     slots = jnp.sum((running - 1) * onehot, axis=1).reshape(tok_count, top_count)
     counts = jnp.sum(onehot, axis=0)
-    all_counts = lax.all_gather(counts[None, :], "expert", axis=0, tiled=True)
-    my_expert = lax.axis_index("expert") // 2
+    all_counts = gather_counts(counts, n_expert, me_e)
+    my_expert = me_e // 2
     chosen = jnp.arange(experts, dtype=jnp.int32)[None, :] == my_expert
     my_counts = jnp.sum(jnp.where(chosen, all_counts, 0), axis=1)
     valid = (jnp.arange(capacity, dtype=jnp.int32)[None, :] < my_counts[:, None]).reshape(-1)
@@ -45,25 +95,20 @@
     grad_flat = hidden_grad.reshape(slot_rows, -1)
     masked = jnp.where(valid[:, None], grad_flat, jnp.zeros_like(grad_flat))
     wbf = weight.astype(jnp.bfloat16)
+    w_rel = gather_rows_relative(wbf, n_dp, me_p)
     partial_rows = lax.dot_general(
-        masked,
-        lax.all_gather(wbf, "dp", axis=0, tiled=True),
-        (((1,), (1,)), ((), ())),
-        preferred_element_type=jnp.float32,
+        masked, w_rel, (((1,), (1,)), ((), ())), preferred_element_type=jnp.float32
     )
     sent = partial_rows.reshape(n_expert, capacity, width)
     received = lax.all_to_all(sent, "expert", split_axis=0, concat_axis=0, tiled=True)
     paired = jnp.sum(received.reshape(experts, 2, capacity, width), axis=1).astype(jnp.bfloat16)
     picked = paired[routes, slots]
-    token_grad = jnp.sum(picked.astype(jnp.float32), axis=1).astype(jnp.bfloat16)
-    owned = lax.psum_scatter(
-        lax.dot_general(
-            inputs_flat, masked, (((0,), (0,)), ((), ())), preferred_element_type=jnp.float32
-        ).astype(jnp.bfloat16),
-        "dp",
-        scatter_dimension=0,
-        tiled=True,
-    ).astype(jnp.float32)
+    token_rel = jnp.sum(picked.astype(jnp.float32), axis=1).astype(jnp.bfloat16)
+    token_grad = jnp.roll(token_rel, me_p * rows, axis=1)
+    full = lax.dot_general(
+        inputs_flat, masked, (((0,), (0,)), ((), ())), preferred_element_type=jnp.float32
+    )
+    owned = reduce_scatter_rows(full, n_dp, me_p, rows)
     new_weight, new_first, new_second = adamw(weight, moment_one, moment_two, owned / loss_scale)
     return (token_grad, new_weight, new_first, new_second)
 

time: 222 us -> 276 us (1.24)
  the two profiles are of different devices: /device:TPU:0 before, /device:TPU:24 now
where the time goes in v1:
time: 276 us; the launch traced here: 275 us
  waiting for transfers between devices  96.8 us (35%)
  starting transfers between devices  69 us (25%)
  other arithmetic  63.1 us (23%)
  local copies, waits for them, and re-layouts  28.9 us (10%)
  matrix products  15.9 us (6%)
    ppermute x7, waiting for transfers between devices, gather_rows_relative(): cur_r = lax.ppermute(cur_r, 'dp', [(p, p + 1) for p in range(t - 1, n - 1)])  42.9 us
    ppermute x7, waiting for transfers between devices, reduce_scatter_rows(): lax.ppermute(pay_l.astype(jnp.bfloat16), 'dp', [(p, p - 1) for p in range...  27.3 us
    unnamed x23, local copies, waits for them, and re-layouts  21.3 us
    ppermute x7, starting transfers between devices, reduce_scatter_rows(): lax.ppermute(pay_l.astype(jnp.bfloat16), 'dp', [(p, p - 1) for p in range...  21.3 us
    unnamed x8, other arithmetic  19.1 us
    ppermute x7, starting transfers between devices, gather_rows_relative(): cur_r = lax.ppermute(cur_r, 'dp', [(p, p + 1) for p in range(t - 1, n - 1)])  15.2 us
    all_to_all x1, waiting for transfers between devices, shards(): lax.all_to_all(sent, 'expert', split_axis=0, concat_axis=0, tiled=True)  14.6 us
    convert_element_type x6, other arithmetic, reduce_scatter_rows(): pay_r.astype(jnp.bfloat16)  14.6 us
  transfers between devices with their start and end apart: 32, of which 14 were waited for; matrix products, arithmetic and copies ran while one was open for 30% of the time, Pallas kernels for 0%

profile of v1, /device:TPU:24, one launch (start us, length us, event | category | flops | bytes accessed | tf_op | source)
XLA Modules:
  0.0 274.8 jit_solution(6330281441516302806)
XLA Ops:
  0.7 3.4 %constant_dynamic-update-slice_fusion = (bf16[2048,2048]{1,0:T(8,128)(2,1)}, bf16[256,2048]{1,0:T(8,128)(2,1)}) fusion(f32[256,2048]{1,0:T(8,128)} %param.9), kind=kLoop, calls=%fused_computation.57 | loop fusion | flops 524287 | bytes 4194304
  5.9 3.4 %collective-permute-start.4 = (bf16[256,2048]{1,0:T(8,128)(2,1)}, bf16[256,2048]{1,0:T(8,128)(2,1)}, u32[]{:S(2)}, u32[]{:S(2)}) collective-permute-start(bf16[256,2048]{1,0:T(8,128)(2,1)} %get-tuple-element.22), channel_id=1, source_target_pairs={{0,1},{1,2},{2,3},{3,4},{4,5},{5,6},{6,7},{8,9},{9,10},{10,11},{11... | collective-permute-start | bytes 3145736 | tf_op jit(solution)/shard_map/ppermute | solution.py:39
  19.2 6.3 %fusion.15 = f32[2048,2048]{1,0:T(8,128)S(1)} fusion(bf16[1,1,512,2048]{3,2,1,0:T(8,128)(2,1)S(1)} %copy-done, bf16[1,1,512,2048]{3,2,1,0:T(8,128)(2,1)} %param.8, pred[512]{0:T(512)(128)(4,1)S(1)} %get-tuple-element.27), kind=kOutput, calls=%fused_computation.31 | convolution fusion | flops 4296015872 | bytes 20972032 | tf_op jit(solution)/shard_map/dot_general | solution.py:108
  25.5 5.7 %copy-done.2 = f32[2048,2048]{1,0:T(8,128)} copy-done((f32[2048,2048]{1,0:T(8,128)}, f32[2048,2048]{1,0:T(8,128)S(1)}, u32[]{:S(2)}) %copy-start.2) | copy-done | bytes 16777240
  34.1 4.6 %collective-permute-start.11 = (bf16[256,2048]{1,0:T(8,128)(2,1)}, bf16[256,2048]{1,0:T(8,128)(2,1)}, u32[]{:S(2)}, u32[]{:S(2)}) collective-permute-start(bf16[256,2048]{1,0:T(8,128)(2,1)} %collective-permute-done.3), channel_id=1, source_target_pairs={{1,0},{2,1},{3,2},{4,3},{5,4},{6,5},{9,8},{10,9},{11,10},{12,11},{... | collective-permute-start | bytes 3145736 | tf_op jit(solution)/shard_map/ppermute | solution.py:41
  41.4 7.3 %collective-permute-done.5 = bf16[256,2048]{1,0:T(8,128)(2,1)} collective-permute-done((bf16[256,2048]{1,0:T(8,128)(2,1)}, bf16[256,2048]{1,0:T(8,128)(2,1)}, u32[]{:S(2)}, u32[]{:S(2)}) %collective-permute-start.5) | collective-permute-done | bytes 1048608 | tf_op jit(solution)/shard_map/ppermute | solution.py:39
  54.8 10.2 %collective-permute-done.6 = bf16[256,2048]{1,0:T(8,128)(2,1)} collective-permute-done((bf16[256,2048]{1,0:T(8,128)(2,1)}, bf16[256,2048]{1,0:T(8,128)(2,1)}, u32[]{:S(2)}, u32[]{:S(2)}) %collective-permute-start.6) | collective-permute-done | bytes 1048608 | tf_op jit(solution)/shard_map/ppermute | solution.py:39
  72.2 9.3 %collective-permute-done.7 = bf16[256,2048]{1,0:T(8,128)(2,1)} collective-permute-done((bf16[256,2048]{1,0:T(8,128)(2,1)}, bf16[256,2048]{1,0:T(8,128)(2,1)}, u32[]{:S(2)}, u32[]{:S(2)}) %collective-permute-start.7) | collective-permute-done | bytes 1048608 | tf_op jit(solution)/shard_map/ppermute | solution.py:39
  90.2 7.7 %collective-permute-done.8 = bf16[256,2048]{1,0:T(8,128)(2,1)} collective-permute-done((bf16[256,2048]{1,0:T(8,128)(2,1)}, bf16[256,2048]{1,0:T(8,128)(2,1)}, u32[]{:S(2)}, u32[]{:S(2)}) %collective-permute-start.8) | collective-permute-done | bytes 1048608 | tf_op jit(solution)/shard_map/ppermute | solution.py:39
  101.5 3.1 %fusion.12 = bf16[256,2048]{0,1:T(8,128)(2,1)} fusion(bf16[256,2048]{0,1:T(8,128)(2,1)} %collective-permute-done.21, f32[2048,2048]{1,0:T(8,128)} %copy-done.2, s32[]{:T(128)S(6)} %select_n.183), kind=kLoop, calls=%fused_computation.26 | loop fusion | flops 1572864 | bytes 4194308 | tf_op jit(solution)/shard_map/convert_element_type | solution.py:62
  105.9 8.4 %collective-permute-done.9 = bf16[256,2048]{1,0:T(8,128)(2,1)} collective-permute-done((bf16[256,2048]{1,0:T(8,128)(2,1)}, bf16[256,2048]{1,0:T(8,128)(2,1)}, u32[]{:S(2)}, u32[]{:S(2)}) %collective-permute-start.9) | collective-permute-done | bytes 1048608 | tf_op jit(solution)/shard_map/ppermute | solution.py:39
  117.3 8.1 %collective-permute-done.22 = bf16[256,2048]{0,1:T(8,128)(2,1)S(1)} collective-permute-done((bf16[256,2048]{0,1:T(8,128)(2,1)}, bf16[256,2048]{0,1:T(8,128)(2,1)S(1)}, u32[]{:S(2)}, u32[]{:S(2)}) %collective-permute-start.22) | collective-permute-done | bytes 1048608 | tf_op jit(solution)/shard_map/ppermute | solution.py:62
  125.5 3.8 %fusion.13 = (bf16[256,2048]{0,1:T(8,128)(2,1)}, bf16[256,2048]{0,1:T(8,128)(2,1)S(1)}) fusion(bf16[256,2048]{0,1:T(8,128)(2,1)S(1)} %collective-permute-done.22, f32[2048,2048]{1,0:T(8,128)} %copy-done.2, s32[]{:T(128)S(6)} %select_n.182, bf16[256,2048]{0,1:T(8,128)(2,1)S(1)} %collective-permute-done.24, s32[]{:T(128)S(6)} %select_n.194), kind=kLoop, calls=%fused_computation.28 | loop fusion | flops 3145728 | bytes 8388616 | tf_op jit(solution)/shard_map/convert_element_type | solution.py:62
  139.1 4.3 %collective-permute-done.25 = bf16[256,2048]{0,1:T(8,128)(2,1)S(1)} collective-permute-done((bf16[256,2048]{0,1:T(8,128)(2,1)S(1)}, bf16[256,2048]{0,1:T(8,128)(2,1)S(1)}, u32[]{:S(2)}, u32[]{:S(2)}) %collective-permute-start.25) | collective-permute-done | bytes 1048608 | tf_op jit(solution)/shard_map/ppermute | solution.py:63
  145.3 3.8 %collective-permute-start.26 = (bf16[256,2048]{0,1:T(8,128)(2,1)S(1)}, bf16[256,2048]{0,1:T(8,128)(2,1)S(1)}, u32[]{:S(2)}, u32[]{:S(2)}) collective-permute-start(bf16[256,2048]{0,1:T(8,128)(2,1)S(1)} %fusion.3), channel_id=1, source_target_pairs={{5,4},{6,5},{7,6},{13,12},{14,13},{15,14},{21,20},{22,21},{23,22},... | collective-permute-start | bytes 3145736 | tf_op jit(solution)/shard_map/ppermute | solution.py:63
  154.3 7.1 %collective-permute-done.26 = bf16[256,2048]{0,1:T(8,128)(2,1)S(1)} collective-permute-done((bf16[256,2048]{0,1:T(8,128)(2,1)S(1)}, bf16[256,2048]{0,1:T(8,128)(2,1)S(1)}, u32[]{:S(2)}, u32[]{:S(2)}) %collective-permute-start.26) | collective-permute-done | bytes 1048608 | tf_op jit(solution)/shard_map/ppermute | solution.py:63
  163.2 3.8 %collective-permute-start.27 = (bf16[256,2048]{0,1:T(8,128)(2,1)S(1)}, bf16[256,2048]{0,1:T(8,128)(2,1)S(1)}, u32[]{:S(2)}, u32[]{:S(2)}) collective-permute-start(bf16[256,2048]{0,1:T(8,128)(2,1)S(1)} %fusion.4), channel_id=1, source_target_pairs={{4,3},{5,4},{6,5},{7,6},{12,11},{13,12},{14,13},{15,14},{20,19},{2... | collective-permute-start | bytes 3145736 | tf_op jit(solution)/shard_map/ppermute | solution.py:63
  172.4 7.0 %collective-permute-done.27 = bf16[256,2048]{0,1:T(8,128)(2,1)S(1)} collective-permute-done((bf16[256,2048]{0,1:T(8,128)(2,1)S(1)}, bf16[256,2048]{0,1:T(8,128)(2,1)S(1)}, u32[]{:S(2)}, u32[]{:S(2)}) %collective-permute-start.27) | collective-permute-done | bytes 1048608 | tf_op jit(solution)/shard_map/ppermute | solution.py:63
  181.2 3.8 %collective-permute-start.28 = (bf16[256,2048]{0,1:T(8,128)(2,1)S(1)}, bf16[256,2048]{0,1:T(8,128)(2,1)S(1)}, u32[]{:S(2)}, u32[]{:S(2)}) collective-permute-start(bf16[256,2048]{0,1:T(8,128)(2,1)S(1)} %fusion.5), channel_id=1, source_target_pairs={{3,2},{4,3},{5,4},{6,5},{7,6},{11,10},{12,11},{13,12},{14,13},{15,... | collective-permute-start | bytes 3145736 | tf_op jit(solution)/shard_map/ppermute | solution.py:63
  185.0 9.6 %fusion = f32[4,128,2048]{2,1,0:T(8,128)} fusion(bf16[2048,2048]{1,0:T(8,128)(2,1)} %select_dynamic-update-slice_fusion, bf16[4,128,2048]{2,1,0:T(8,128)(2,1)S(1)} %bitcast.108, pred[4,128]{1,0:T(4,128)(4,1)S(1)} %get-tuple-element.28), kind=kOutput, calls=%fused_computation.2 | convolution fusion | flops 4296015872 | bytes 14680576 | tf_op jit(solution)/shard_map/dot_general | solution.py:99
  194.6 4.9 %all-to-all-start = ((f32[4,128,2048]{2,1,0:T(8,128)}), f32[4,128,2048]{2,1,0:T(8,128)}, u32[]{:S(2)}, u32[]{:S(2)}) async-start(f32[4,128,2048]{2,1,0:T(8,128)} %fusion), calls=%async_computation | async-start | bytes 8388608 | tf_op jit(solution)/shard_map/all_to_all | solution.py:103
  203.4 3.4 %collective-permute-start.23 = (bf16[256,2048]{0,1:T(8,128)(2,1)}, bf16[256,2048]{0,1:T(8,128)(2,1)}, u32[]{:S(2)}, u32[]{:S(2)}) collective-permute-start(bf16[256,2048]{0,1:T(8,128)(2,1)} %get-tuple-element.23), channel_id=1, source_target_pairs={{0,1},{1,2},{2,3},{3,4},{4,5},{5,6},{6,7},{8,9},{9,10},{10,11},{11... | collective-permute-start | bytes 3145736 | tf_op jit(solution)/shard_map/ppermute | solution.py:62
  206.8 8.9 %collective-permute-done.29 = bf16[256,2048]{0,1:T(8,128)(2,1)} collective-permute-done((bf16[256,2048]{0,1:T(8,128)(2,1)S(1)}, bf16[256,2048]{0,1:T(8,128)(2,1)}, u32[]{:S(2)}, u32[]{:S(2)}) %collective-permute-start.29) | collective-permute-done | bytes 1048608 | tf_op jit(solution)/shard_map/ppermute | solution.py:63
  215.7 3.1 %fusion.7 = bf16[256,2048]{0,1:T(8,128)(2,1)} fusion(bf16[256,2048]{0,1:T(8,128)(2,1)} %collective-permute-done.29, f32[2048,2048]{1,0:T(8,128)} %copy-done.2, s32[]{:T(128)S(6)} %select_n.189), kind=kLoop, calls=%fused_computation.16 | loop fusion | flops 1572864 | bytes 4194308 | tf_op jit(solution)/shard_map/convert_element_type | solution.py:63
  218.8 4.4 %collective-permute-start.30 = (bf16[256,2048]{0,1:T(8,128)(2,1)}, bf16[256,2048]{0,1:T(8,128)(2,1)}, u32[]{:S(2)}, u32[]{:S(2)}) collective-permute-start(bf16[256,2048]{0,1:T(8,128)(2,1)} %fusion.7), channel_id=1, source_target_pairs={{1,0},{2,1},{3,2},{4,3},{5,4},{6,5},{7,6},{9,8},{10,9},{11,10},{12... | collective-permute-start | bytes 3145736 | tf_op jit(solution)/shard_map/ppermute | solution.py:63
  225.6 2.9 %copy.37 = f32[256,2048]{0,1:T(8,128)} copy(f32[256,2048]{1,0:T(8,128)} %param.10) | data formatting | bytes 4194304 | tf_op args[4]
  231.3 14.6 %all-to-all-done = f32[4,128,2048]{2,1,0:T(8,128)} async-done(((f32[4,128,2048]{2,1,0:T(8,128)}), f32[4,128,2048]{2,1,0:T(8,128)}, u32[]{:S(2)}, u32[]{:S(2)}) %all-to-all-start) | async-done | bytes 4194336 | tf_op jit(solution)/shard_map/all_to_all | solution.py:103
  248.7 4.3 %gather_fusion.1 = bf16[256,2048]{1,0:T(8,128)(2,1)S(1)} fusion(bf16[2,128,2048]{2,1,0:T(8,128)(2,1)S(1)} %bitcast_reduce_fusion, s32[256]{0:T(256)S(1)} %reshape.165), kind=kCustom, calls=%fused_computation.1 | custom fusion | bytes 2099200 | tf_op jit(solution)/shard_map/gather | solution.py:105
  254.6 3.8 %reduce_sum.52 = bf16[128,2048]{1,0:T(8,128)(2,1)S(1)} reduce(bf16[128,2,2048]{2,1,0:T(2,128)(2,1)} %reshape.168, bf16[]{:T(256)} %constant.112.clone.1), dimensions={1}, to_apply=%region_6.7 | reduce | flops 262144 | bytes 1572866 | tf_op jit(solution)/shard_map/reduce_sum | solution.py:106
  259.4 7.5 %multiply_subtract_fusion = (f32[256,2048]{0,1:T(8,128)}, f32[256,2048]{0,1:T(8,128)}, f32[256,2048]{0,1:T(8,128)}) fusion(f32[256,2048]{0,1:T(8,128)S(1)} %copy-done.3, bf16[256,2048]{0,1:T(8,128)(2,1)} %collective-permute-done.30, bf16[256,2048]{0,1:T(8,128)(2,1)} %collective-permute-done.23, f32[2048,2048]{1,0:T(8,128)} %copy-done.2, s32[]{:T(128)S(6)} %select_n.181, ...), kind=kLoop, calls=%fused_computation.34 | loop fusion | flops 10485760 | bytes 16777220 | tf_op jit(solution)/shard_map/sub | solution.py:20
  266.9 3.0 %copy.41 = f32[256,2048]{1,0:T(8,128)} copy(f32[256,2048]{0,1:T(8,128)} %get-tuple-element.18) | data formatting | bytes 4194304
  271.7 3.0 %copy.43 = f32[256,2048]{1,0:T(8,128)} copy(f32[256,2048]{0,1:T(8,128)} %get-tuple-element.20) | data formatting | bytes 4194304
  (103 shorter events, 89.1 us)
Async XLA Ops:
  4.0 30.1 %collective-permute-start.3 = (bf16[256,2048]{1,0:T(8,128)(2,1)}, bf16[256,2048]{1,0:T(8,128)(2,1)}, u32[]{:S(2)}, u32[]{:S(2)}) collective-permute-start(bf16[256,2048]{1,0:T(8,128)(2,1)} %get-tuple-element.22), channel_id=1, source_target_pairs={{1,0},{2,1},{3,2},{4,3},{5,4},{6,5},{7,6},{9,8},{10,9},{11,10},{12... | collective-permute-start | bytes 3145736 | tf_op jit(solution)/shard_map/ppermute | solution.py:41
  5.9 26.3 %collective-permute-start.4 = (bf16[256,2048]{1,0:T(8,128)(2,1)}, bf16[256,2048]{1,0:T(8,128)(2,1)}, u32[]{:S(2)}, u32[]{:S(2)}) collective-permute-start(bf16[256,2048]{1,0:T(8,128)(2,1)} %get-tuple-element.22), channel_id=1, source_target_pairs={{0,1},{1,2},{2,3},{3,4},{4,5},{5,6},{6,7},{8,9},{9,10},{10,11},{11... | collective-permute-start | bytes 3145736 | tf_op jit(solution)/shard_map/ppermute | solution.py:39
  10.9 3.8 %collective-permute-start.2 = (s32[2]{0:T(128)S(1)}, s32[2]{0:T(128)S(1)}, u32[]{:S(2)}, u32[]{:S(2)}) collective-permute-start(s32[2]{0:T(128)S(1)} %get-tuple-element.17), channel_id=1, source_target_pairs={{0,24},{8,0},{16,8},{24,16},{1,25},{9,1},{17,9},{25,17},{2,26},{10... | collective-permute-start | bytes 32 | tf_op jit(solution)/shard_map/ppermute | solution.py:27
  13.4 3.5 %collective-permute-start.1 = (s32[2]{0:T(128)S(1)}, s32[2]{0:T(128)S(1)}, u32[]{:S(2)}, u32[]{:S(2)}) collective-permute-start(s32[2]{0:T(128)S(1)} %get-tuple-element.17), channel_id=1, source_target_pairs={{0,16},{8,24},{16,0},{24,8},{1,17},{9,25},{17,1},{25,9},{2,18},{10... | collective-permute-start | bytes 32 | tf_op jit(solution)/shard_map/ppermute | solution.py:27
  13.9 4.4 %collective-permute-start = (s32[2]{0:T(128)S(1)}, s32[2]{0:T(128)S(1)}, u32[]{:S(2)}, u32[]{:S(2)}) collective-permute-start(s32[2]{0:T(128)S(1)} %get-tuple-element.17), channel_id=1, source_target_pairs={{0,8},{8,16},{16,24},{24,0},{1,9},{9,17},{17,25},{25,1},{2,10},{10... | collective-permute-start | bytes 32 | tf_op jit(solution)/shard_map/ppermute | solution.py:27
  31.4 7.3 %collective-permute-start.17 = (bf16[256,2048]{0,1:T(8,128)(2,1)S(1)}, bf16[256,2048]{0,1:T(8,128)(2,1)S(1)}, u32[]{:S(2)}, u32[]{:S(2)}) collective-permute-start(bf16[256,2048]{0,1:T(8,128)(2,1)S(1)} %get-tuple-element.25), channel_id=1, source_target_pairs={{0,1},{8,9},{16,17},{24,25}} | collective-permute-start | bytes 3145736 | tf_op jit(solution)/shard_map/ppermute | solution.py:62
  32.2 16.4 %collective-permute-start.5 = (bf16[256,2048]{1,0:T(8,128)(2,1)}, bf16[256,2048]{1,0:T(8,128)(2,1)}, u32[]{:S(2)}, u32[]{:S(2)}) collective-permute-start(bf16[256,2048]{1,0:T(8,128)(2,1)} %collective-permute-done.4), channel_id=1, source_target_pairs={{1,2},{2,3},{3,4},{4,5},{5,6},{6,7},{9,10},{10,11},{11,12},{12,13}... | collective-permute-start | bytes 3145736 | tf_op jit(solution)/shard_map/ppermute | solution.py:39
  34.1 16.4 %collective-permute-start.11 = (bf16[256,2048]{1,0:T(8,128)(2,1)}, bf16[256,2048]{1,0:T(8,128)(2,1)}, u32[]{:S(2)}, u32[]{:S(2)}) collective-permute-start(bf16[256,2048]{1,0:T(8,128)(2,1)} %collective-permute-done.3), channel_id=1, source_target_pairs={{1,0},{2,1},{3,2},{4,3},{5,4},{6,5},{9,8},{10,9},{11,10},{12,11},{... | collective-permute-start | bytes 3145736 | tf_op jit(solution)/shard_map/ppermute | solution.py:41
  40.6 11.6 %collective-permute-start.18 = (bf16[256,2048]{0,1:T(8,128)(2,1)S(1)}, bf16[256,2048]{0,1:T(8,128)(2,1)S(1)}, u32[]{:S(2)}, u32[]{:S(2)}) collective-permute-start(bf16[256,2048]{0,1:T(8,128)(2,1)S(1)} %fusion.8), channel_id=1, source_target_pairs={{0,1},{1,2},{8,9},{9,10},{16,17},{17,18},{24,25},{25,26}} | collective-permute-start | bytes 3145736 | tf_op jit(solution)/shard_map/ppermute | solution.py:62
  48.6 16.4 %collective-permute-start.6 = (bf16[256,2048]{1,0:T(8,128)(2,1)}, bf16[256,2048]{1,0:T(8,128)(2,1)}, u32[]{:S(2)}, u32[]{:S(2)}) collective-permute-start(bf16[256,2048]{1,0:T(8,128)(2,1)} %collective-permute-done.5), channel_id=1, source_target_pairs={{2,3},{3,4},{4,5},{5,6},{6,7},{10,11},{11,12},{12,13},{13,14},{14,... | collective-permute-start | bytes 3145736 | tf_op jit(solution)/shard_map/ppermute | solution.py:39
  50.6 16.4 %collective-permute-start.12 = (bf16[256,2048]{1,0:T(8,128)(2,1)}, bf16[256,2048]{1,0:T(8,128)(2,1)}, u32[]{:S(2)}, u32[]{:S(2)}) collective-permute-start(bf16[256,2048]{1,0:T(8,128)(2,1)} %collective-permute-done.11), channel_id=1, source_target_pairs={{1,0},{2,1},{3,2},{4,3},{5,4},{9,8},{10,9},{11,10},{12,11},{13,12}... | collective-permute-start | bytes 3145736 | tf_op jit(solution)/shard_map/ppermute | solution.py:41
  54.1 14.6 %collective-permute-start.19 = (bf16[256,2048]{0,1:T(8,128)(2,1)S(1)}, bf16[256,2048]{0,1:T(8,128)(2,1)S(1)}, u32[]{:S(2)}, u32[]{:S(2)}) collective-permute-start(bf16[256,2048]{0,1:T(8,128)(2,1)S(1)} %fusion.9), channel_id=1, source_target_pairs={{0,1},{1,2},{2,3},{8,9},{9,10},{10,11},{16,17},{17,18},{18,19},{24... | collective-permute-start | bytes 3145736 | tf_op jit(solution)/shard_map/ppermute | solution.py:62
  65.1 16.4 %collective-permute-start.7 = (bf16[256,2048]{1,0:T(8,128)(2,1)}, bf16[256,2048]{1,0:T(8,128)(2,1)}, u32[]{:S(2)}, u32[]{:S(2)}) collective-permute-start(bf16[256,2048]{1,0:T(8,128)(2,1)} %collective-permute-done.6), channel_id=1, source_target_pairs={{3,4},{4,5},{5,6},{6,7},{11,12},{12,13},{13,14},{14,15},{19,20},{2... | collective-permute-start | bytes 3145736 | tf_op jit(solution)/shard_map/ppermute | solution.py:39
  67.0 16.4 %collective-permute-start.13 = (bf16[256,2048]{1,0:T(8,128)(2,1)}, bf16[256,2048]{1,0:T(8,128)(2,1)}, u32[]{:S(2)}, u32[]{:S(2)}) collective-permute-start(bf16[256,2048]{1,0:T(8,128)(2,1)} %collective-permute-done.12), channel_id=1, source_target_pairs={{1,0},{2,1},{3,2},{4,3},{9,8},{10,9},{11,10},{12,11},{17,16},{18,1... | collective-permute-start | bytes 3145736 | tf_op jit(solution)/shard_map/ppermute | solution.py:41
  70.5 14.6 %collective-permute-start.20 = (bf16[256,2048]{0,1:T(8,128)(2,1)S(1)}, bf16[256,2048]{0,1:T(8,128)(2,1)}, u32[]{:S(2)}, u32[]{:S(2)}) collective-permute-start(bf16[256,2048]{0,1:T(8,128)(2,1)S(1)} %fusion.10), channel_id=1, source_target_pairs={{0,1},{1,2},{2,3},{3,4},{8,9},{9,10},{10,11},{11,12},{16,17},{17,1... | collective-permute-start | bytes 3145736 | tf_op jit(solution)/shard_map/ppermute | solution.py:62
  81.5 16.4 %collective-permute-start.8 = (bf16[256,2048]{1,0:T(8,128)(2,1)}, bf16[256,2048]{1,0:T(8,128)(2,1)}, u32[]{:S(2)}, u32[]{:S(2)}) collective-permute-start(bf16[256,2048]{1,0:T(8,128)(2,1)} %collective-permute-done.7), channel_id=1, source_target_pairs={{4,5},{5,6},{6,7},{12,13},{13,14},{14,15},{20,21},{21,22},{22,23},... | collective-permute-start | bytes 3145736 | tf_op jit(solution)/shard_map/ppermute | solution.py:39
  83.4 16.4 %collective-permute-start.14 = (bf16[256,2048]{1,0:T(8,128)(2,1)}, bf16[256,2048]{1,0:T(8,128)(2,1)}, u32[]{:S(2)}, u32[]{:S(2)}) collective-permute-start(bf16[256,2048]{1,0:T(8,128)(2,1)} %collective-permute-done.13), channel_id=1, source_target_pairs={{1,0},{2,1},{3,2},{9,8},{10,9},{11,10},{17,16},{18,17},{19,18},{25... | collective-permute-start | bytes 3145736 | tf_op jit(solution)/shard_map/ppermute | solution.py:41
  87.2 14.3 %collective-permute-start.21 = (bf16[256,2048]{0,1:T(8,128)(2,1)S(1)}, bf16[256,2048]{0,1:T(8,128)(2,1)}, u32[]{:S(2)}, u32[]{:S(2)}) collective-permute-start(bf16[256,2048]{0,1:T(8,128)(2,1)S(1)} %fusion.11), channel_id=1, source_target_pairs={{0,1},{1,2},{2,3},{3,4},{4,5},{8,9},{9,10},{10,11},{11,12},{12,13}... | collective-permute-start | bytes 3145736 | tf_op jit(solution)/shard_map/ppermute | solution.py:62
  88.9 28.4 %collective-permute-start.24 = (bf16[256,2048]{0,1:T(8,128)(2,1)S(1)}, bf16[256,2048]{0,1:T(8,128)(2,1)S(1)}, u32[]{:S(2)}, u32[]{:S(2)}) collective-permute-start(bf16[256,2048]{0,1:T(8,128)(2,1)S(1)} %get-tuple-element.26), channel_id=1, source_target_pairs={{7,6},{15,14},{23,22},{31,30}} | collective-permute-start | bytes 3145736 | tf_op jit(solution)/shard_map/ppermute | solution.py:63
  97.9 16.4 %collective-permute-start.9 = (bf16[256,2048]{1,0:T(8,128)(2,1)}, bf16[256,2048]{1,0:T(8,128)(2,1)}, u32[]{:S(2)}, u32[]{:S(2)}) collective-permute-start(bf16[256,2048]{1,0:T(8,128)(2,1)} %collective-permute-done.8), channel_id=1, source_target_pairs={{5,6},{6,7},{13,14},{14,15},{21,22},{22,23},{29,30},{30,31}} | collective-permute-start | bytes 3145736 | tf_op jit(solution)/shard_map/ppermute | solution.py:39
  99.8 16.8 %collective-permute-start.15 = (bf16[256,2048]{1,0:T(8,128)(2,1)}, bf16[256,2048]{1,0:T(8,128)(2,1)}, u32[]{:S(2)}, u32[]{:S(2)}) collective-permute-start(bf16[256,2048]{1,0:T(8,128)(2,1)} %collective-permute-done.14), channel_id=1, source_target_pairs={{1,0},{2,1},{9,8},{10,9},{17,16},{18,17},{25,24},{26,25}} | collective-permute-start | bytes 3145736 | tf_op jit(solution)/shard_map/ppermute | solution.py:41
  104.6 20.8 %collective-permute-start.22 = (bf16[256,2048]{0,1:T(8,128)(2,1)}, bf16[256,2048]{0,1:T(8,128)(2,1)S(1)}, u32[]{:S(2)}, u32[]{:S(2)}) collective-permute-start(bf16[256,2048]{0,1:T(8,128)(2,1)} %fusion.12), channel_id=1, source_target_pairs={{0,1},{1,2},{2,3},{3,4},{4,5},{5,6},{8,9},{9,10},{10,11},{11,12},{... | collective-permute-start | bytes 3145736 | tf_op jit(solution)/shard_map/ppermute | solution.py:62
  114.3 17.0 %collective-permute-start.10 = (bf16[256,2048]{1,0:T(8,128)(2,1)}, bf16[256,2048]{1,0:T(8,128)(2,1)}, u32[]{:S(2)}, u32[]{:S(2)}) collective-permute-start(bf16[256,2048]{1,0:T(8,128)(2,1)} %collective-permute-done.9), channel_id=1, source_target_pairs={{6,7},{14,15},{22,23},{30,31}} | collective-permute-start | bytes 3145736 | tf_op jit(solution)/shard_map/ppermute | solution.py:39
  116.6 53.1 %collective-permute-start.16 = (bf16[256,2048]{1,0:T(8,128)(2,1)}, bf16[256,2048]{1,0:T(8,128)(2,1)S(1)}, u32[]{:S(2)}, u32[]{:S(2)}) collective-permute-start(bf16[256,2048]{1,0:T(8,128)(2,1)} %collective-permute-done.15), channel_id=1, source_target_pairs={{1,0},{9,8},{17,16},{25,24}} | collective-permute-start | bytes 3145736 | tf_op jit(solution)/shard_map/ppermute | solution.py:41
  129.2 14.2 %collective-permute-start.25 = (bf16[256,2048]{0,1:T(8,128)(2,1)S(1)}, bf16[256,2048]{0,1:T(8,128)(2,1)S(1)}, u32[]{:S(2)}, u32[]{:S(2)}) collective-permute-start(bf16[256,2048]{0,1:T(8,128)(2,1)S(1)} %get-tuple-element.24), channel_id=1, source_target_pairs={{6,5},{7,6},{14,13},{15,14},{22,21},{23,22},{30,29},{31,30}} | collective-permute-start | bytes 3145736 | tf_op jit(solution)/shard_map/ppermute | solution.py:63
  145.3 16.1 %collective-permute-start.26 = (bf16[256,2048]{0,1:T(8,128)(2,1)S(1)}, bf16[256,2048]{0,1:T(8,128)(2,1)S(1)}, u32[]{:S(2)}, u32[]{:S(2)}) collective-permute-start(bf16[256,2048]{0,1:T(8,128)(2,1)S(1)} %fusion.3), channel_id=1, source_target_pairs={{5,4},{6,5},{7,6},{13,12},{14,13},{15,14},{21,20},{22,21},{23,22},... | collective-permute-start | bytes 3145736 | tf_op jit(solution)/shard_map/ppermute | solution.py:63
  163.2 16.1 %collective-permute-start.27 = (bf16[256,2048]{0,1:T(8,128)(2,1)S(1)}, bf16[256,2048]{0,1:T(8,128)(2,1)S(1)}, u32[]{:S(2)}, u32[]{:S(2)}) collective-permute-start(bf16[256,2048]{0,1:T(8,128)(2,1)S(1)} %fusion.4), channel_id=1, source_target_pairs={{4,3},{5,4},{6,5},{7,6},{12,11},{13,12},{14,13},{15,14},{20,19},{2... | collective-permute-start | bytes 3145736 | tf_op jit(solution)/shard_map/ppermute | solution.py:63
  181.2 18.3 %collective-permute-start.28 = (bf16[256,2048]{0,1:T(8,128)(2,1)S(1)}, bf16[256,2048]{0,1:T(8,128)(2,1)S(1)}, u32[]{:S(2)}, u32[]{:S(2)}) collective-permute-start(bf16[256,2048]{0,1:T(8,128)(2,1)S(1)} %fusion.5), channel_id=1, source_target_pairs={{3,2},{4,3},{5,4},{6,5},{7,6},{11,10},{12,11},{13,12},{14,13},{15,... | collective-permute-start | bytes 3145736 | tf_op jit(solution)/shard_map/ppermute | solution.py:63
  194.6 51.4 %all-to-all-start = ((f32[4,128,2048]{2,1,0:T(8,128)}), f32[4,128,2048]{2,1,0:T(8,128)}, u32[]{:S(2)}, u32[]{:S(2)}) async-start(f32[4,128,2048]{2,1,0:T(8,128)} %fusion), calls=%async_computation | async-start | bytes 8388608 | tf_op jit(solution)/shard_map/all_to_all | solution.py:103
  201.3 14.3 %collective-permute-start.29 = (bf16[256,2048]{0,1:T(8,128)(2,1)S(1)}, bf16[256,2048]{0,1:T(8,128)(2,1)}, u32[]{:S(2)}, u32[]{:S(2)}) collective-permute-start(bf16[256,2048]{0,1:T(8,128)(2,1)S(1)} %fusion.6), channel_id=1, source_target_pairs={{2,1},{3,2},{4,3},{5,4},{6,5},{7,6},{10,9},{11,10},{12,11},{13,12}... | collective-permute-start | bytes 3145736 | tf_op jit(solution)/shard_map/ppermute | solution.py:63
  203.4 56.0 %collective-permute-start.23 = (bf16[256,2048]{0,1:T(8,128)(2,1)}, bf16[256,2048]{0,1:T(8,128)(2,1)}, u32[]{:S(2)}, u32[]{:S(2)}) collective-permute-start(bf16[256,2048]{0,1:T(8,128)(2,1)} %get-tuple-element.23), channel_id=1, source_target_pairs={{0,1},{1,2},{2,3},{3,4},{4,5},{5,6},{6,7},{8,9},{9,10},{10,11},{11... | collective-permute-start | bytes 3145736 | tf_op jit(solution)/shard_map/ppermute | solution.py:62
  218.8 40.6 %collective-permute-start.30 = (bf16[256,2048]{0,1:T(8,128)(2,1)}, bf16[256,2048]{0,1:T(8,128)(2,1)}, u32[]{:S(2)}, u32[]{:S(2)}) collective-permute-start(bf16[256,2048]{0,1:T(8,128)(2,1)} %fusion.7), channel_id=1, source_target_pairs={{1,0},{2,1},{3,2},{4,3},{5,4},{6,5},{7,6},{9,8},{10,9},{11,10},{12... | collective-permute-start | bytes 3145736 | tf_op jit(solution)/shard_map/ppermute | solution.py:63
  (8 other events, 77.9 us)

commit v2 on v0

v2 whole, which is shorter than its diff:
```python
import jax
import jax.numpy as jnp
from jax import lax
from jax.sharding import Mesh
from jax.sharding import PartitionSpec as P

beta_one = 0.9
beta_two = 0.95
learn_rate = 0.003
decay = 0.1
epsilon = 1e-08
loss_scale = 64.0
bias_one = 1.0 - (0.9**50) ** 2
bias_two = 1.0 - (0.95**50) ** 2
CORES = 2
DP = ("z", "core")


def adamw(weight, moment_one, moment_two, grad):
    new_first = beta_one * moment_one + (1.0 - beta_one) * grad
    new_second = beta_two * moment_two + (1.0 - beta_two) * grad * grad
    update = new_first / bias_one / (jnp.sqrt(new_second / bias_two) + epsilon)
    new_weight = weight - learn_rate * (update + decay * weight)
    return (new_weight, new_first, new_second)


SWAP = [(0, 1), (1, 0)]


def shards(routes, expert_inputs, hidden_grad, weight, moment_one, moment_two):
    n_expert = lax.axis_size("expert")
    n_z = lax.axis_size("z")
    experts = n_expert // 2
    slot_rows = expert_inputs.shape[2]
    capacity = slot_rows // n_expert
    width = expert_inputs.shape[3]
    rows = weight.shape[0]
    tok_count = routes.shape[0]
    top_count = routes.shape[1]
    me_c = lax.axis_index("core")
    flat_routes = routes.reshape(-1)
    onehot = (flat_routes[:, None] == jnp.arange(experts, dtype=jnp.int32)[None, :]).astype(
        jnp.int32
    )
    running = jnp.cumsum(onehot, axis=0)
    slots = jnp.sum((running - 1) * onehot, axis=1).reshape(tok_count, top_count)
    counts = jnp.sum(onehot, axis=0)
    all_counts = lax.all_gather(counts[None, :], "expert", axis=0, tiled=True)
    my_expert = lax.axis_index("expert") // 2
    chosen = jnp.arange(experts, dtype=jnp.int32)[None, :] == my_expert
    my_counts = jnp.sum(jnp.where(chosen, all_counts, 0), axis=1)
    valid = (jnp.arange(capacity, dtype=jnp.int32)[None, :] < my_counts[:, None]).reshape(-1)
    inputs_flat = expert_inputs.reshape(slot_rows, width)
    grad_flat = hidden_grad.reshape(slot_rows, -1)
    masked = jnp.where(valid[:, None], grad_flat, jnp.zeros_like(grad_flat))

    wbf = weight.astype(jnp.bfloat16)
    w_mine = lax.all_gather(wbf, "z", axis=0, tiled=True)
    w_other = lax.ppermute(w_mine, "core", SWAP)
    w_rel = jnp.concatenate([w_mine, w_other], axis=0)
    partial_rows = lax.dot_general(
        masked, w_rel, (((1,), (1,)), ((), ())), preferred_element_type=jnp.float32
    )
    sent = partial_rows.reshape(n_expert, capacity, width)
    received = lax.all_to_all(sent, "expert", split_axis=0, concat_axis=0, tiled=True)
    paired = jnp.sum(received.reshape(experts, 2, capacity, width), axis=1).astype(jnp.bfloat16)
    picked = paired[routes, slots]
    token_rel = jnp.sum(picked.astype(jnp.float32), axis=1).astype(jnp.bfloat16)
    split = token_rel.reshape(tok_count, CORES, n_z, rows)
    split = jnp.where(me_c == 0, split, split[:, ::-1])
    token_grad = jnp.transpose(split, (0, 2, 1, 3)).reshape(tok_count, width)

    by_class = inputs_flat.reshape(slot_rows, n_z, CORES, rows)
    in_mine = lax.dynamic_index_in_dim(by_class, me_c, axis=2, keepdims=False)
    in_other = lax.dynamic_index_in_dim(by_class, 1 - me_c, axis=2, keepdims=False)
    dims = (((0,), (0,)), ((), ()))
    g_other = lax.dot_general(
        in_other.reshape(slot_rows, n_z * rows), masked, dims, preferred_element_type=jnp.float32
    )
    g_recv = lax.ppermute(g_other.astype(jnp.bfloat16), "core", SWAP)
    g_mine = lax.dot_general(
        in_mine.reshape(slot_rows, n_z * rows), masked, dims, preferred_element_type=jnp.float32
    )
    chip = (g_mine + g_recv.astype(jnp.float32)).astype(jnp.bfloat16)
    owned = lax.psum_scatter(chip, "z", scatter_dimension=0, tiled=True).astype(jnp.float32)
    new_weight, new_first, new_second = adamw(weight, moment_one, moment_two, owned / loss_scale)
    return (token_grad, new_weight, new_first, new_second)


def solution(mesh):
    n_expert, n_dp = mesh.devices.shape
    split_mesh = Mesh(mesh.devices.reshape(n_expert, n_dp // CORES, CORES), ("expert",) + DP)
    in_specs = (
        P(("expert",) + DP, None),
        P(DP, "expert", None, None),
        P(DP, "expert", None, None),
        P(DP, "expert"),
        P(DP, "expert"),
        P(DP, "expert"),
    )
    out_specs = (P(("expert",) + DP, None), P(DP, "expert"), P(DP, "expert"), P(DP, "expert"))
    return jax.shard_map(
        shards, mesh=split_mesh, in_specs=in_specs, out_specs=out_specs, check_vma=False
    )
```

time: 222 us -> 294 us (1.32)
  the two profiles are of different devices: /device:TPU:0 before, /device:TPU:24 now
where the time goes in v2:
time: 294 us; the launch traced here: 289 us
  waiting for transfers between devices  218 us (74%)
  matrix products  16.2 us (6%)
  between operations  14.9 us (5%)
  local copies, waits for them, and re-layouts  14.1 us (5%)
  other arithmetic  13.7 us (5%)
  blocking collectives  7.37 us (3%)
  starting transfers between devices  5.38 us (2%)
    all_gather x1, waiting for transfers between devices, shards(): w_mine = lax.all_gather(wbf, 'z', axis=0, tiled=True)  79.4 us
    reduce_scatter x1, waiting for transfers between devices, shards(): lax.psum_scatter(chip, 'z', scatter_dimension=0, tiled=True)  76.1 us
    all_to_all x1, waiting for transfers between devices, shards(): lax.all_to_all(sent, 'expert', split_axis=0, concat_axis=0, tiled=True)  47.5 us
    dot_general x1, matrix products, shards(): lax.dot_general(masked, w_rel, (((1,), (1,)), ((), ())), preferred_elemen...  9.41 us
    unnamed x12, local copies, waits for them, and re-layouts  7.5 us
    unnamed x1, blocking collectives  7.37 us
    ppermute x1, waiting for transfers between devices, shards(): w_other = lax.ppermute(w_mine, 'core', SWAP)  7.31 us
    ppermute x1, waiting for transfers between devices, shards(): g_recv = lax.ppermute(g_other.astype(jnp.bfloat16), 'core', SWAP)  7.15 us
  transfers between devices with their start and end apart: 5, of which 5 were waited for; matrix products, arithmetic and copies ran while one was open for 0% of the time, Pallas kernels for 0%

profile of v2, /device:TPU:24, one launch (start us, length us, event | category | flops | bytes accessed | tf_op | source)
XLA Modules:
  0.0 289.2 jit_solution(15638671455127075837)
XLA Ops:
  7.2 0.8 copy.38
  8.0 0.1 eq.46
  8.2 0.1 eq.42
  8.3 0.6 reduce-window.6
  9.0 0.2 slice_reduce_fusion
  9.2 0.2 reduce-window.9
  9.4 1.2 dynamic-slice
  11.3 0.1 fusion.16
  11.5 0.2 dynamic-update-slice
  11.7 7.4 %all-reduce = s32[8]{0:T(128)S(1)} all-reduce(s32[8]{0:T(128)S(1)} %dynamic-update-slice), channel_id=2, replica_groups=mesh['expert'=4,'z'=4,'core'=2] {'expert'}, use_global_device_ids=true, to_apply=%add | all-reduce | flops 8 | bytes 64
  19.2 0.1 select_reduce_fusion
  19.3 2.9 copy.46
  22.2 0.2 constant_dynamic-slice_fusion
  22.5 1.3 copy-done.2
  23.8 2.4 convolution_convert_fusion
  26.3 7.1 %collective-permute-done.1 = bf16[1024,2048]{1,0:T(8,128)(2,1)S(1)} collective-permute-done((bf16[1024,2048]{1,0:T(8,128)(2,1)S(1)}, bf16[1024,2048]{1,0:T(8,128)(2,1)S(1)}, u32[]{:S(2)}, u32[]{:S(2)}) %collective-permute-start.1) | collective-permute-done | bytes 4194336 | tf_op jit(solution)/shard_map/ppermute | solution.py:80
  33.5 4.4 %add_convert_fusion = bf16[1024,2048]{1,0:T(8,128)(2,1)} fusion(bf16[1024,2048]{1,0:T(8,128)(2,1)S(1)} %collective-permute-done.1, bf16[512,1024]{0,1:T(8,128)(2,1)S(1)} %bitcast.49, bf16[1,1,512,2048]{3,2,1,0:T(8,128)(2,1)S(1)} %copy-done.2, pred[512]{0:T(512)(128)(4,1)S(1)} %get-tuple-element.24), kind=kOutput, calls=%fused_computation.5 | convolution fusion | flops 2154823680 | bytes 11534848 | tf_op jit(solution)/shard_map/dot_general | solution.py:81
  37.9 76.1 %reduce-scatter.2.cloned.1.call-done = bf16[256,2048]{1,0:T(8,128)(2,1)} async-done(((bf16[1024,2048]{1,0:T(8,128)(2,1)}), bf16[256,2048]{1,0:T(8,128)(2,1)}) %reduce-scatter.2.cloned.1.call-update) | async-done | bytes 1048592 | tf_op jit(solution)/shard_map/reduce_scatter | solution.py:85
  114.0 6.8 %multiply_subtract_fusion = (f32[256,2048]{1,0:T(8,128)}, f32[256,2048]{1,0:T(8,128)}, f32[256,2048]{1,0:T(8,128)}, bf16[256,2048]{1,0:T(8,128)(2,1)}) fusion(f32[256,2048]{1,0:T(8,128)S(1)} %copy-done, bf16[256,2048]{1,0:T(8,128)(2,1)} %reduce-scatter.2.cloned.1.call-done, f32[256,2048]{1,0:T(8,128)} %param.10, f32[256,2048]{1,0:T(8,128)} %param.11), kind=kLoop, calls=%fused_computation.17 | loop fusion | flops 9437184 | bytes 14680064 | tf_op jit(solution)/shard_map/sub | solution.py:23
  120.9 79.4 %all-gather.3.cloned.1.call-done = bf16[1024,2048]{1,0:T(8,128)(2,1)} async-done(((bf16[256,2048]{1,0:T(8,128)(2,1)}), bf16[1024,2048]{1,0:T(8,128)(2,1)}) %all-gather.3.cloned.1.call-update) | async-done | bytes 4194320 | tf_op jit(solution)/shard_map/all_gather | solution.py:58
  200.4 7.3 %collective-permute-done = bf16[1024,2048]{1,0:T(8,128)(2,1)S(1)} collective-permute-done((bf16[1024,2048]{1,0:T(8,128)(2,1)}, bf16[1024,2048]{1,0:T(8,128)(2,1)S(1)}, u32[]{:S(2)}, u32[]{:S(2)}) %collective-permute-start) | collective-permute-done | bytes 4194336 | tf_op jit(solution)/shard_map/ppermute | solution.py:59
  207.7 9.4 %fusion = f32[4,128,2048]{2,1,0:T(8,128)} fusion(bf16[1024,2048]{1,0:T(8,128)(2,1)S(1)} %collective-permute-done, bf16[1024,2048]{1,0:T(8,128)(2,1)} %all-gather.3.cloned.1.call-done, bf16[4,128,2048]{2,1,0:T(8,128)(2,1)} %bitcast.52, pred[4,128]{1,0:T(4,128)(4,1)S(1)} %get-tuple-element.25), kind=kOutput, calls=%fused_computation.2 | convolution fusion | flops 4312793088 | bytes 14680576 | tf_op jit(solution)/shard_map/dot_general | solution.py:61
  217.1 5.2 %all-to-all-start = ((f32[4,128,2048]{2,1,0:T(8,128)}), f32[4,128,2048]{2,1,0:T(8,128)}, u32[]{:S(2)}, u32[]{:S(2)}) async-start(f32[4,128,2048]{2,1,0:T(8,128)} %fusion), calls=%async_computation | async-start | bytes 8388608 | tf_op jit(solution)/shard_map/all_to_all | solution.py:65
  222.3 0.1 reshape.125
  222.6 0.1 reshape.130
  222.8 47.5 %all-to-all-done = f32[4,128,2048]{2,1,0:T(8,128)} async-done(((f32[4,128,2048]{2,1,0:T(8,128)}), f32[4,128,2048]{2,1,0:T(8,128)}, u32[]{:S(2)}, u32[]{:S(2)}) %all-to-all-start) | async-done | bytes 4194336 | tf_op jit(solution)/shard_map/all_to_all | solution.py:65
  270.3 2.7 bitcast_reduce_fusion
  273.0 4.3 %gather_fusion = bf16[256,2048]{1,0:T(8,128)(2,1)S(1)} fusion(bf16[2,128,2048]{2,1,0:T(8,128)(2,1)S(1)} %bitcast_reduce_fusion, s32[256]{0:T(256)S(1)} %reshape.130), kind=kCustom, calls=%fused_computation | custom fusion | bytes 2099200 | tf_op jit(solution)/shard_map/gather | solution.py:67
  277.3 0.7 reshape.133
  278.1 2.8 reduce_sum.52
  280.9 0.3 copy.44
  281.4 1.0 copy.47
  (22 shorter events, 0.8 us)
Async XLA Ops:
  7.2 106.9 %reduce-scatter.2.cloned.1.call-start = ((), (), s32[]{:S(2)}) async-start(), calls=%async_computation.3 | async-start | bytes 5242880 | tf_op jit(solution)/shard_map/reduce_scatter | solution.py:85
  22.2 1.6 copy-start.2
  26.2 7.2 %collective-permute-start.1 = (bf16[1024,2048]{1,0:T(8,128)(2,1)S(1)}, bf16[1024,2048]{1,0:T(8,128)(2,1)S(1)}, u32[]{:S(2)}, u32[]{:S(2)}) collective-permute-start(bf16[1024,2048]{1,0:T(8,128)(2,1)S(1)} %convolution_convert_fusion), channel_id=1, source_target_pairs={{0,1},{1,0},{2,3},{3,2},{4,5},{5,4},{6,7},{7,6},{8,9},{9,8},{10,11... | collective-permute-start | bytes 12582920 | tf_op jit(solution)/shard_map/ppermute | solution.py:80
  37.8 76.2 %copy-start = (f32[256,2048]{1,0:T(8,128)S(1)}, f32[256,2048]{1,0:T(8,128)}, u32[]{:S(2)}) copy-start(f32[256,2048]{1,0:T(8,128)} %param.9) | copy-start | bytes 6291460
  37.8 162.5 %all-gather.3.cloned.1.call-start = ((), (), s32[]{:S(2)}) async-start(), calls=%async_computation.2 | async-start | bytes 5242880 | tf_op jit(solution)/shard_map/all_gather | solution.py:58
  200.3 7.4 %collective-permute-start = (bf16[1024,2048]{1,0:T(8,128)(2,1)}, bf16[1024,2048]{1,0:T(8,128)(2,1)S(1)}, u32[]{:S(2)}, u32[]{:S(2)}) collective-permute-start(bf16[1024,2048]{1,0:T(8,128)(2,1)} %all-gather.3.cloned.1.call-done), channel_id=1, source_target_pairs={{0,1},{1,0},{2,3},{3,2},{4,5},{5,4},{6,7},{7,6},{8,9},{9,8},{10,11... | collective-permute-start | bytes 12582920 | tf_op jit(solution)/shard_map/ppermute | solution.py:59
  217.1 5.4 %copy-start.1 = (s32[128,2]{0,1:T(2,128)S(1)}, s32[128,2]{0,1:T(2,128)}, u32[]{:S(2)}) copy-start(s32[128,2]{0,1:T(2,128)} %param.6) | copy-start | bytes 3076
  217.1 53.2 %all-to-all-start = ((f32[4,128,2048]{2,1,0:T(8,128)}), f32[4,128,2048]{2,1,0:T(8,128)}, u32[]{:S(2)}, u32[]{:S(2)}) async-start(f32[4,128,2048]{2,1,0:T(8,128)} %fusion), calls=%async_computation | async-start | bytes 8388608 | tf_op jit(solution)/shard_map/all_to_all | solution.py:65
Sparse Core Ops, SparseCore 0:
  38.0 76.0 reduce-scatter.1
  121.0 79.2 all-gather.2

commit v3 on v2

--- a/solution.py
+++ b/solution.py
@@ -27,6 +27,22 @@
 SWAP = [(0, 1), (1, 0)]
 
 
+def gather_relative(block, axis, n, me):
+    left = [None] * n
+    right = [None] * n
+    cur_r = block
+    cur_l = block
+    for t in range(1, n):
+        cur_r = lax.ppermute(cur_r, axis, [(p, p + 1) for p in range(t - 1, n - 1)])
+        right[t] = cur_r
+        cur_l = lax.ppermute(cur_l, axis, [(p, p - 1) for p in range(1, n - t + 1)])
+        left[t] = cur_l
+    parts = [block]
+    for r in range(1, n):
+        parts.append(jnp.where(me + r < n, left[r], right[n - r]))
+    return jnp.concatenate(parts, axis=0)
+
+
 def shards(routes, expert_inputs, hidden_grad, weight, moment_one, moment_two):
     n_expert = lax.axis_size("expert")
     n_z = lax.axis_size("z")
@@ -38,6 +54,7 @@
     tok_count = routes.shape[0]
     top_count = routes.shape[1]
     me_c = lax.axis_index("core")
+    me_z = lax.axis_index("z")
     flat_routes = routes.reshape(-1)
     onehot = (flat_routes[:, None] == jnp.arange(experts, dtype=jnp.int32)[None, :]).astype(
         jnp.int32
@@ -55,18 +72,18 @@
     masked = jnp.where(valid[:, None], grad_flat, jnp.zeros_like(grad_flat))
 
     wbf = weight.astype(jnp.bfloat16)
-    w_mine = lax.all_gather(wbf, "z", axis=0, tiled=True)
+    w_mine = gather_relative(wbf, "z", n_z, me_z)
     w_other = lax.ppermute(w_mine, "core", SWAP)
-    w_rel = jnp.concatenate([w_mine, w_other], axis=0)
-    partial_rows = lax.dot_general(
-        masked, w_rel, (((1,), (1,)), ((), ())), preferred_element_type=jnp.float32
-    )
+    cols = (((1,), (1,)), ((), ()))
+    out_mine = lax.dot_general(masked, w_mine, cols, preferred_element_type=jnp.float32)
+    out_other = lax.dot_general(masked, w_other, cols, preferred_element_type=jnp.float32)
+    partial_rows = jnp.concatenate([out_mine, out_other], axis=1)
     sent = partial_rows.reshape(n_expert, capacity, width)
     received = lax.all_to_all(sent, "expert", split_axis=0, concat_axis=0, tiled=True)
     paired = jnp.sum(received.reshape(experts, 2, capacity, width), axis=1).astype(jnp.bfloat16)
     picked = paired[routes, slots]
     token_rel = jnp.sum(picked.astype(jnp.float32), axis=1).astype(jnp.bfloat16)
-    split = token_rel.reshape(tok_count, CORES, n_z, rows)
+    split = jnp.roll(token_rel.reshape(tok_count, CORES, n_z, rows), me_z, axis=2)
     split = jnp.where(me_c == 0, split, split[:, ::-1])
     token_grad = jnp.transpose(split, (0, 2, 1, 3)).reshape(tok_count, width)
 

time: 294 us -> 291 us (0.990)
  waiting for transfers between devices: 218 us -> 201 us
  starting transfers between devices: 5.38 us -> 16.2 us
  other arithmetic: 13.7 us -> 19.5 us
  matrix products: 16.2 us -> 11.5 us
    all_gather x1 -> x0, waiting for transfers between devices: 79.4 us -> none  [shards(): w_mine = lax.all_gather(wbf, 'z', axis=0, tiled=True)]
    ppermute x0 -> x6, waiting for transfers between devices: none -> 66.4 us  [the longest x3 66.4 us: gather_relative(): cur_r = lax.ppermute(cur_r, axis, [(p, p + 1) for p in range(t - 1, n - 1)])]
    ppermute x0 -> x6, starting transfers between devices: none -> 11 us  [the longest x3 7.18 us: gather_relative(): cur_l = lax.ppermute(cur_l, axis, [(p, p - 1) for p in range(1, n - t + 1)])]
    dot_general x1 -> x2, matrix products: 9.41 us -> 4.76 us  [the longest x1 2.39 us: shards(): lax.dot_general(masked, w_mine, cols, preferred_element_type=jnp.float32)]
    ppermute x1, waiting for transfers between devices: 7.31 us -> 3.92 us  [shards(): w_other = lax.ppermute(w_mine, 'core', SWAP)]
    concatenate x0 -> x3, other arithmetic: none -> 3.34 us  [the longest x1 2.47 us: shards(): partial_rows = jnp.concatenate([out_mine, out_other], axis=1)]
    unnamed x12 -> x14, local copies, waits for them, and re-layouts: 7.5 us -> 8.34 us
  transfers between devices with their start and end apart: 5 -> 10, of which waited for: 5 -> 7; matrix products, arithmetic and copies ran while one was open for 0% -> 2% of each run, Pallas kernels for 0% -> 0%
where the time goes in v3:
time: 291 us; the launch traced here: 286 us
  waiting for transfers between devices  201 us (69%)
  other arithmetic  19.5 us (7%)
  starting transfers between devices  16.2 us (6%)
  between operations  15 us (5%)
  local copies, waits for them, and re-layouts  14.9 us (5%)
  matrix products  11.5 us (4%)
  blocking collectives  7.37 us (3%)
    reduce_scatter x1, waiting for transfers between devices, shards(): lax.psum_scatter(chip, 'z', scatter_dimension=0, tiled=True)  76.2 us
    ppermute x3, waiting for transfers between devices, gather_relative(): cur_r = lax.ppermute(cur_r, axis, [(p, p + 1) for p in range(t - 1, n - 1)])  66.4 us
    all_to_all x1, waiting for transfers between devices, shards(): lax.all_to_all(sent, 'expert', split_axis=0, concat_axis=0, tiled=True)  47.5 us
    unnamed x14, local copies, waits for them, and re-layouts  8.34 us
    unnamed x1, blocking collectives  7.37 us
    ppermute x3, starting transfers between devices, gather_relative(): cur_l = lax.ppermute(cur_l, axis, [(p, p - 1) for p in range(1, n - t + 1)])  7.18 us
    ppermute x1, waiting for transfers between devices, shards(): g_recv = lax.ppermute(g_other.astype(jnp.bfloat16), 'core', SWAP)  7.15 us
    sub x1, other arithmetic, adamw(): new_weight = weight - learn_rate * (update + decay * weight)  6.44 us
  transfers between devices with their start and end apart: 10, of which 7 were waited for; matrix products, arithmetic and copies ran while one was open for 2% of the time, Pallas kernels for 0%

profile of v3, /device:TPU:24, one launch (start us, length us, event | category | flops | bytes accessed | tf_op | source)
XLA Modules:
  0.0 285.7 jit_solution(14756585561970324566)
XLA Ops:
  7.2 0.8 copy.38
  9.4 1.2 dynamic-slice
  11.7 7.4 %all-reduce = s32[8]{0:T(128)S(1)} all-reduce(s32[8]{0:T(128)S(1)} %dynamic-update-slice), channel_id=2, replica_groups=mesh['expert'=4,'z'=4,'core'=2] {'expert'}, use_global_device_ids=true, to_apply=%add | all-reduce | flops 8 | bytes 64
  19.3 2.9 %copy.46 = bf16[1,1,512,2048]{2,3,1,0:T(8,128)(2,1)S(1)} copy(bf16[1,1,512,2048]{3,2,1,0:T(8,128)(2,1)} %param.7) | data formatting | bytes 4194304 | tf_op args[1]
  22.5 1.3 copy-done.2
  23.8 2.4 convolution_convert_fusion
  26.3 7.1 %collective-permute-done.7 = bf16[1024,2048]{1,0:T(8,128)(2,1)S(1)} collective-permute-done((bf16[1024,2048]{1,0:T(8,128)(2,1)S(1)}, bf16[1024,2048]{1,0:T(8,128)(2,1)S(1)}, u32[]{:S(2)}, u32[]{:S(2)}) %collective-permute-start.7) | collective-permute-done | bytes 4194336 | tf_op jit(solution)/shard_map/ppermute | solution.py:97
  33.5 4.4 %add_convert_fusion = bf16[1024,2048]{1,0:T(8,128)(2,1)} fusion(bf16[1024,2048]{1,0:T(8,128)(2,1)S(1)} %collective-permute-done.7, bf16[512,1024]{0,1:T(8,128)(2,1)S(1)} %bitcast.52, bf16[1,1,512,2048]{3,2,1,0:T(8,128)(2,1)S(1)} %copy-done.2, pred[512]{0:T(512)(128)(4,1)S(1)} %fusion.14), kind=kOutput, calls=%fused_computation.1 | convolution fusion | flops 2154823680 | bytes 11534848 | tf_op jit(solution)/shard_map/dot_general | solution.py:98
  37.8 76.2 %reduce-scatter.2.cloned.1.call-done = bf16[256,2048]{1,0:T(8,128)(2,1)} async-done(((bf16[1024,2048]{1,0:T(8,128)(2,1)}), bf16[256,2048]{1,0:T(8,128)(2,1)}) %reduce-scatter.2.cloned.1.call-update) | async-done | bytes 1048592 | tf_op jit(solution)/shard_map/reduce_scatter | solution.py:102
  114.0 6.4 %multiply_subtract_fusion = (f32[256,2048]{1,0:T(8,128)}, f32[256,2048]{1,0:T(8,128)}, f32[256,2048]{1,0:T(8,128)}, bf16[256,2048]{1,0:T(8,128)(2,1)S(1)}) fusion(f32[256,2048]{1,0:T(8,128)S(1)} %copy-done, bf16[256,2048]{1,0:T(8,128)(2,1)} %reduce-scatter.2.cloned.1.call-done, f32[256,2048]{1,0:T(8,128)} %param.10, f32[256,2048]{1,0:T(8,128)} %param.11), kind=kLoop, calls=%fused_computation.16 | loop fusion | flops 9437184 | bytes 14680064 | tf_op jit(solution)/shard_map/sub | solution.py:23
  120.5 1.3 collective-permute-start.1
  121.8 4.6 %collective-permute-start = (bf16[256,2048]{1,0:T(8,128)(2,1)S(1)}, bf16[256,2048]{1,0:T(8,128)(2,1)S(1)}, u32[]{:S(2)}, u32[]{:S(2)}) collective-permute-start(bf16[256,2048]{1,0:T(8,128)(2,1)S(1)} %get-tuple-element.21), channel_id=1, source_target_pairs={{2,0},{4,2},{6,4},{3,1},{5,3},{7,5},{10,8},{12,10},{14,12},{11,9},... | collective-permute-start | bytes 3145736 | tf_op jit(solution)/shard_map/ppermute | solution.py:38
  126.4 21.1 %collective-permute-done.1 = bf16[256,2048]{1,0:T(8,128)(2,1)S(1)} collective-permute-done((bf16[256,2048]{1,0:T(8,128)(2,1)S(1)}, bf16[256,2048]{1,0:T(8,128)(2,1)S(1)}, u32[]{:S(2)}, u32[]{:S(2)}) %collective-permute-start.1) | collective-permute-done | bytes 1048608 | tf_op jit(solution)/shard_map/ppermute | solution.py:36
  147.5 1.3 collective-permute-start.2
  148.8 1.7 collective-permute-start.4
  150.4 23.3 %collective-permute-done.2 = bf16[256,2048]{1,0:T(8,128)(2,1)} collective-permute-done((bf16[256,2048]{1,0:T(8,128)(2,1)S(1)}, bf16[256,2048]{1,0:T(8,128)(2,1)}, u32[]{:S(2)}, u32[]{:S(2)}) %collective-permute-start.2) | collective-permute-done | bytes 1048608 | tf_op jit(solution)/shard_map/ppermute | solution.py:36
  173.7 1.3 collective-permute-start.3
  175.1 0.9 collective-permute-start.5
  176.0 1.3 broadcast_select_fusion.2
  177.3 22.0 %collective-permute-done.3 = bf16[256,2048]{1,0:T(8,128)(2,1)} collective-permute-done((bf16[256,2048]{1,0:T(8,128)(2,1)}, bf16[256,2048]{1,0:T(8,128)(2,1)}, u32[]{:S(2)}, u32[]{:S(2)}) %collective-permute-start.3) | collective-permute-done | bytes 1048608 | tf_op jit(solution)/shard_map/ppermute | solution.py:36
  199.3 1.3 broadcast_select_fusion.3
  201.5 0.8 copy-done.3
  202.4 2.4 fusion.9
  204.8 3.9 %collective-permute-done.6 = bf16[1024,2048]{1,0:T(8,128)(2,1)S(1)} collective-permute-done((bf16[1024,2048]{1,0:T(8,128)(2,1)S(1)}, bf16[1024,2048]{1,0:T(8,128)(2,1)S(1)}, u32[]{:S(2)}, u32[]{:S(2)}) %collective-permute-start.6) | collective-permute-done | bytes 4194336 | tf_op jit(solution)/shard_map/ppermute | solution.py:76
  208.7 2.4 fusion.8
  211.1 2.5 pad_maximum_fusion.1
  213.5 5.0 %all-to-all-start = ((f32[4,128,2048]{2,1,0:T(8,128)}), f32[4,128,2048]{2,1,0:T(8,128)}, u32[]{:S(2)}, u32[]{:S(2)}) async-start(f32[4,128,2048]{2,1,0:T(8,128)} %bitcast.48), calls=%async_computation | async-start | bytes 8388608 | tf_op jit(solution)/shard_map/all_to_all | solution.py:82
  219.1 47.5 %all-to-all-done = f32[4,128,2048]{2,1,0:T(8,128)} async-done(((f32[4,128,2048]{2,1,0:T(8,128)}), f32[4,128,2048]{2,1,0:T(8,128)}, u32[]{:S(2)}, u32[]{:S(2)}) %all-to-all-start) | async-done | bytes 4194336 | tf_op jit(solution)/shard_map/all_to_all | solution.py:82
  266.5 2.7 bitcast_reduce_fusion
  269.3 4.3 %gather_fusion = bf16[256,2048]{1,0:T(8,128)(2,1)S(1)} fusion(bf16[2,128,2048]{2,1,0:T(8,128)(2,1)S(1)} %bitcast_reduce_fusion, s32[256]{0:T(256)S(1)} %reshape.126), kind=kCustom, calls=%fused_computation | custom fusion | bytes 2099200 | tf_op jit(solution)/shard_map/gather | solution.py:84
  274.3 2.8 reduce_sum.52
  277.8 1.0 copy.47
  (40 shorter events, 5.0 us)
Async XLA Ops:
  7.2 106.9 %reduce-scatter.2.cloned.1.call-start = ((), (), s32[]{:S(2)}) async-start(), calls=%async_computation.2 | async-start | bytes 5242880 | tf_op jit(solution)/shard_map/reduce_scatter | solution.py:102
  22.2 1.6 copy-start.2
  26.2 7.2 %collective-permute-start.7 = (bf16[1024,2048]{1,0:T(8,128)(2,1)S(1)}, bf16[1024,2048]{1,0:T(8,128)(2,1)S(1)}, u32[]{:S(2)}, u32[]{:S(2)}) collective-permute-start(bf16[1024,2048]{1,0:T(8,128)(2,1)S(1)} %convolution_convert_fusion), channel_id=1, source_target_pairs={{0,1},{1,0},{2,3},{3,2},{4,5},{5,4},{6,7},{7,6},{8,9},{9,8},{10,11... | collective-permute-start | bytes 12582920 | tf_op jit(solution)/shard_map/ppermute | solution.py:97
  37.8 76.2 %copy-start = (f32[256,2048]{1,0:T(8,128)S(1)}, f32[256,2048]{1,0:T(8,128)}, u32[]{:S(2)}) copy-start(f32[256,2048]{1,0:T(8,128)} %param.9) | copy-start | bytes 6291460
  120.5 27.0 %collective-permute-start.1 = (bf16[256,2048]{1,0:T(8,128)(2,1)S(1)}, bf16[256,2048]{1,0:T(8,128)(2,1)S(1)}, u32[]{:S(2)}, u32[]{:S(2)}) collective-permute-start(bf16[256,2048]{1,0:T(8,128)(2,1)S(1)} %get-tuple-element.21), channel_id=1, source_target_pairs={{0,2},{2,4},{4,6},{1,3},{3,5},{5,7},{8,10},{10,12},{12,14},{9,11},... | collective-permute-start | bytes 3145736 | tf_op jit(solution)/shard_map/ppermute | solution.py:36
  121.8 27.0 %collective-permute-start = (bf16[256,2048]{1,0:T(8,128)(2,1)S(1)}, bf16[256,2048]{1,0:T(8,128)(2,1)S(1)}, u32[]{:S(2)}, u32[]{:S(2)}) collective-permute-start(bf16[256,2048]{1,0:T(8,128)(2,1)S(1)} %get-tuple-element.21), channel_id=1, source_target_pairs={{2,0},{4,2},{6,4},{3,1},{5,3},{7,5},{10,8},{12,10},{14,12},{11,9},... | collective-permute-start | bytes 3145736 | tf_op jit(solution)/shard_map/ppermute | solution.py:38
  147.5 26.3 %collective-permute-start.2 = (bf16[256,2048]{1,0:T(8,128)(2,1)S(1)}, bf16[256,2048]{1,0:T(8,128)(2,1)}, u32[]{:S(2)}, u32[]{:S(2)}) collective-permute-start(bf16[256,2048]{1,0:T(8,128)(2,1)S(1)} %collective-permute-done.1), channel_id=1, source_target_pairs={{2,4},{4,6},{3,5},{5,7},{10,12},{12,14},{11,13},{13,15},{18,20},{2... | collective-permute-start | bytes 3145736 | tf_op jit(solution)/shard_map/ppermute | solution.py:36
  148.8 26.3 %collective-permute-start.4 = (bf16[256,2048]{1,0:T(8,128)(2,1)S(1)}, bf16[256,2048]{1,0:T(8,128)(2,1)}, u32[]{:S(2)}, u32[]{:S(2)}) collective-permute-start(bf16[256,2048]{1,0:T(8,128)(2,1)S(1)} %collective-permute-done), channel_id=1, source_target_pairs={{2,0},{4,2},{3,1},{5,3},{10,8},{12,10},{11,9},{13,11},{18,16},{20,... | collective-permute-start | bytes 3145736 | tf_op jit(solution)/shard_map/ppermute | solution.py:38
  173.7 25.6 %collective-permute-start.3 = (bf16[256,2048]{1,0:T(8,128)(2,1)}, bf16[256,2048]{1,0:T(8,128)(2,1)}, u32[]{:S(2)}, u32[]{:S(2)}) collective-permute-start(bf16[256,2048]{1,0:T(8,128)(2,1)} %collective-permute-done.2), channel_id=1, source_target_pairs={{4,6},{5,7},{12,14},{13,15},{20,22},{21,23},{28,30},{29,31}} | collective-permute-start | bytes 3145736 | tf_op jit(solution)/shard_map/ppermute | solution.py:36
  175.1 25.6 %collective-permute-start.5 = (bf16[256,2048]{1,0:T(8,128)(2,1)}, bf16[256,2048]{1,0:T(8,128)(2,1)S(1)}, u32[]{:S(2)}, u32[]{:S(2)}) collective-permute-start(bf16[256,2048]{1,0:T(8,128)(2,1)} %collective-permute-done.4), channel_id=1, source_target_pairs={{2,0},{3,1},{10,8},{11,9},{18,16},{19,17},{26,24},{27,25}} | collective-permute-start | bytes 3145736 | tf_op jit(solution)/shard_map/ppermute | solution.py:38
  200.8 1.6 copy-start.3
  201.5 7.2 %collective-permute-start.6 = (bf16[1024,2048]{1,0:T(8,128)(2,1)S(1)}, bf16[1024,2048]{1,0:T(8,128)(2,1)S(1)}, u32[]{:S(2)}, u32[]{:S(2)}) collective-permute-start(bf16[1024,2048]{1,0:T(8,128)(2,1)S(1)} %pad_maximum_fusion), channel_id=1, source_target_pairs={{0,1},{1,0},{2,3},{3,2},{4,5},{5,4},{6,7},{7,6},{8,9},{9,8},{10,11... | collective-permute-start | bytes 12582920 | tf_op jit(solution)/shard_map/ppermute | solution.py:76
  213.5 5.2 %copy-start.1 = (s32[128,2]{0,1:T(2,128)S(1)}, s32[128,2]{0,1:T(2,128)}, u32[]{:S(2)}) copy-start(s32[128,2]{0,1:T(2,128)} %param.6) | copy-start | bytes 3076
  213.5 53.0 %all-to-all-start = ((f32[4,128,2048]{2,1,0:T(8,128)}), f32[4,128,2048]{2,1,0:T(8,128)}, u32[]{:S(2)}, u32[]{:S(2)}) async-start(f32[4,128,2048]{2,1,0:T(8,128)} %bitcast.48), calls=%async_computation | async-start | bytes 8388608 | tf_op jit(solution)/shard_map/all_to_all | solution.py:82
Sparse Core Ops, SparseCore 0:
  38.0 76.0 reduce-scatter.1

commit v4 on v3

--- a/solution.py
+++ b/solution.py
@@ -99,7 +99,9 @@
         in_mine.reshape(slot_rows, n_z * rows), masked, dims, preferred_element_type=jnp.float32
     )
     chip = (g_mine + g_recv.astype(jnp.float32)).astype(jnp.bfloat16)
-    owned = lax.psum_scatter(chip, "z", scatter_dimension=0, tiled=True).astype(jnp.float32)
+    owned = lax.psum_scatter(chip, "z", scatter_dimension=0, tiled=True)
+    token_grad, owned = lax.optimization_barrier((token_grad, owned))
+    owned = owned.astype(jnp.float32)
     new_weight, new_first, new_second = adamw(weight, moment_one, moment_two, owned / loss_scale)
     return (token_grad, new_weight, new_first, new_second)
 

time: 291 us -> 216 us (0.74)
  waiting for transfers between devices: 201 us -> 116 us
  matrix products: 11.5 us -> 20 us
  other arithmetic: 19.5 us -> 23 us
    reduce_scatter x1, waiting for transfers between devices: 76.2 us -> 21.7 us  [shards(): owned = lax.psum_scatter(chip, 'z', scatter_dimension=0, tiled=True)]
    ppermute x3, waiting for transfers between devices: 66.4 us -> 27.1 us  [gather_relative(): cur_r = lax.ppermute(cur_r, axis, [(p, p + 1) for p in range(t - 1, n - 1)])]
    ppermute x3, waiting for transfers between devices: 0.01 us -> 20.8 us  [gather_relative(): cur_l = lax.ppermute(cur_l, axis, [(p, p - 1) for p in range(1, n - t + 1)])]
    ppermute x1, waiting for transfers between devices: 7.15 us -> 0.01 us  [shards(): g_recv = lax.ppermute(g_other.astype(jnp.bfloat16), 'core', SWAP)]
    ppermute x1, waiting for transfers between devices: 3.92 us -> 0.01 us  [shards(): w_other = lax.ppermute(w_mine, 'core', SWAP)]
    unnamed x14 -> x26, local copies, waits for them, and re-layouts: 8.34 us -> 6.98 us
  transfers between devices with their start and end apart: 10 -> 10, of which waited for: 7 -> 6; matrix products, arithmetic and copies ran while one was open for 2% -> 22% of each run, Pallas kernels for 0% -> 0%
where the time goes in v4:
time: 216 us; the launch traced here: 212 us
  waiting for transfers between devices  116 us (54%)
  other arithmetic  23 us (11%)
  matrix products  20 us (9%)
  starting transfers between devices  16 us (7%)
  between operations  15.1 us (7%)
  local copies, waits for them, and re-layouts  14.6 us (7%)
  blocking collectives  7.37 us (3%)
    all_to_all x1, waiting for transfers between devices, shards(): lax.all_to_all(sent, 'expert', split_axis=0, concat_axis=0, tiled=True)  46.5 us
    ppermute x3, waiting for transfers between devices, gather_relative(): cur_r = lax.ppermute(cur_r, axis, [(p, p + 1) for p in range(t - 1, n - 1)])  27.1 us
    reduce_scatter x1, waiting for transfers between devices, shards(): owned = lax.psum_scatter(chip, 'z', scatter_dimension=0, tiled=True)  21.7 us
    ppermute x3, waiting for transfers between devices, gather_relative(): cur_l = lax.ppermute(cur_l, axis, [(p, p - 1) for p in range(1, n - t + 1)])  20.8 us
    unnamed x1, blocking collectives  7.37 us
    unnamed x26, local copies, waits for them, and re-layouts  6.98 us
    ppermute x3, starting transfers between devices, gather_relative(): cur_l = lax.ppermute(cur_l, axis, [(p, p - 1) for p in range(1, n - t + 1)])  6.96 us
    dot_general x1, matrix products, shards(): lax.dot_general(in_mine.reshape(slot_rows, n_z * rows), masked, dims, pre...  6.61 us
  transfers between devices with their start and end apart: 10, of which 6 were waited for; matrix products, arithmetic and copies ran while one was open for 22% of the time, Pallas kernels for 0%

profile of v4, /device:TPU:24, one launch (start us, length us, event | category | flops | bytes accessed | tf_op | source)
XLA Modules:
  0.0 212.1 jit_solution(8606197516854300406)
XLA Ops:
  7.2 1.7 convert_element_type.28
  9.0 1.3 collective-permute-start.1
  13.4 7.4 %all-reduce = s32[8]{0:T(128)S(1)} all-reduce(s32[8]{0:T(128)S(1)} %dynamic-update-slice), channel_id=2, replica_groups=mesh['expert'=4,'z'=4,'core'=2] {'expert'}, use_global_device_ids=true, to_apply=%add | all-reduce | flops 8 | bytes 64
  21.1 2.9 %copy.46 = bf16[1,1,512,2048]{2,3,1,0:T(8,128)(2,1)S(1)} copy(bf16[1,1,512,2048]{3,2,1,0:T(8,128)(2,1)} %param.7) | data formatting | bytes 4194304 | tf_op args[1]
  24.0 1.2 constant_dynamic-slice_fusion.1
  25.2 0.8 copy-done.6
  25.9 4.4 %convolution_convert_fusion = bf16[1024,2048]{1,0:T(8,128)(2,1)} fusion(bf16[512,1024]{0,1:T(8,128)(2,1)S(1)} %bitcast.53, bf16[1,1,512,2048]{3,2,1,0:T(8,128)(2,1)S(1)} %copy-done.6, pred[512]{0:T(512)(128)(4,1)S(1)} %fusion.14), kind=kOutput, calls=%fused_computation.5 | convolution fusion | flops 2150629376 | bytes 7340544 | tf_op jit(solution)/shard_map/dot_general | solution.py:94
  30.3 4.6 %collective-permute-start = (bf16[256,2048]{1,0:T(8,128)(2,1)S(1)}, bf16[256,2048]{1,0:T(8,128)(2,1)S(1)}, u32[]{:S(2)}, u32[]{:S(2)}) collective-permute-start(bf16[256,2048]{1,0:T(8,128)(2,1)S(1)} %convert_element_type.28), channel_id=1, source_target_pairs={{2,0},{4,2},{6,4},{3,1},{5,3},{7,5},{10,8},{12,10},{14,12},{11,9},... | collective-permute-start | bytes 3145736 | tf_op jit(solution)/shard_map/ppermute | solution.py:38
  34.9 0.9 collective-permute-done.1
  35.9 1.3 collective-permute-start.2
  37.2 20.8 %collective-permute-done = bf16[256,2048]{1,0:T(8,128)(2,1)S(1)} collective-permute-done((bf16[256,2048]{1,0:T(8,128)(2,1)S(1)}, bf16[256,2048]{1,0:T(8,128)(2,1)S(1)}, u32[]{:S(2)}, u32[]{:S(2)}) %collective-permute-start) | collective-permute-done | bytes 1048608 | tf_op jit(solution)/shard_map/ppermute | solution.py:38
  57.9 1.6 collective-permute-start.4
  59.6 2.8 %collective-permute-done.2 = bf16[256,2048]{1,0:T(8,128)(2,1)S(1)} collective-permute-done((bf16[256,2048]{1,0:T(8,128)(2,1)}, bf16[256,2048]{1,0:T(8,128)(2,1)S(1)}, u32[]{:S(2)}, u32[]{:S(2)}) %collective-permute-start.2) | collective-permute-done | bytes 1048608 | tf_op jit(solution)/shard_map/ppermute | solution.py:36
  62.3 1.3 collective-permute-start.3
  63.7 0.7 collective-permute-start.5
  64.5 23.4 %collective-permute-done.3 = bf16[256,2048]{1,0:T(8,128)(2,1)} collective-permute-done((bf16[256,2048]{1,0:T(8,128)(2,1)S(1)}, bf16[256,2048]{1,0:T(8,128)(2,1)}, u32[]{:S(2)}, u32[]{:S(2)}) %collective-permute-start.3) | collective-permute-done | bytes 1048608 | tf_op jit(solution)/shard_map/ppermute | solution.py:36
  87.9 1.4 broadcast_select_fusion.3
  89.3 1.4 broadcast_select_fusion.1
  90.7 2.4 %pad_maximum_fusion = bf16[1024,2048]{1,0:T(8,128)(2,1)} fusion(bf16[256,2048]{1,0:T(8,128)(2,1)S(1)} %broadcast_select_fusion.1, bf16[256,2048]{1,0:T(8,128)(2,1)S(1)} %broadcast_select_fusion.2, bf16[256,2048]{1,0:T(8,128)(2,1)S(1)} %broadcast_select_fusion.3, bf16[256,2048]{1,0:T(8,128)(2,1)S(1)} %convert_element_type.28), kind=kLoop, calls=%fused_computation.2 | loop fusion | flops 16777216 | bytes 8388608 | tf_op jit(solution)/shard_map/concatenate | solution.py:43
  93.3 1.1 copy-done.7
  94.5 6.6 %add_convert_fusion = bf16[1024,2048]{1,0:T(8,128)(2,1)} fusion(bf16[1024,2048]{1,0:T(8,128)(2,1)} %collective-permute-done.7, bf16[512,1024]{0,1:T(8,128)(2,1)S(1)} %bitcast.52, bf16[1,1,512,2048]{3,2,1,0:T(8,128)(2,1)S(1)} %copy-done.7, pred[512]{0:T(512)(128)(4,1)S(1)} %fusion.14), kind=kOutput, calls=%fused_computation.1 | convolution fusion | flops 2154823680 | bytes 11534848 | tf_op jit(solution)/shard_map/dot_general | solution.py:98
  101.1 4.4 %fusion.9 = f32[512,1024]{1,0:T(8,128)S(1)} fusion(bf16[1,1,512,2048]{3,2,1,0:T(8,128)(2,1)} %param.8, pred[512]{0:T(512)(128)(4,1)S(1)} %fusion.14, bf16[256,2048]{1,0:T(8,128)(2,1)} %copy-done.1, bf16[256,2048]{1,0:T(8,128)(2,1)S(1)} %broadcast_select_fusion.2, bf16[256,2048]{1,0:T(8,128)(2,1)S(1)} %broadcast_select_fusion.3, ...), kind=kOutput, calls=%fused_computation.24 | convolution fusion | flops 2165309440 | bytes 8389120 | tf_op jit(solution)/shard_map/dot_general | solution.py:78
  105.5 4.6 %fusion.8 = f32[512,1024]{1,0:T(8,128)S(1)} fusion(bf16[1024,2048]{1,0:T(8,128)(2,1)} %collective-permute-done.6, bf16[1,1,512,2048]{3,2,1,0:T(8,128)(2,1)S(1)} %copy-done.8, pred[512]{0:T(512)(128)(4,1)S(1)} %fusion.14), kind=kOutput, calls=%fused_computation.23 | convolution fusion | flops 2148532224 | bytes 8389120 | tf_op jit(solution)/shard_map/dot_general | solution.py:79
  110.2 2.5 %pad_maximum_fusion.1 = f32[512,2048]{1,0:T(8,128)} fusion(f32[512,1024]{1,0:T(8,128)S(1)} %fusion.8, f32[512,1024]{1,0:T(8,128)S(1)} %fusion.9), kind=kLoop, calls=%fused_computation.3 | loop fusion | flops 1048576 | bytes 8388608 | tf_op jit(solution)/shard_map/concatenate | solution.py:80
  112.6 5.1 %all-to-all-start = ((f32[4,128,2048]{2,1,0:T(8,128)}), f32[4,128,2048]{2,1,0:T(8,128)}, u32[]{:S(2)}, u32[]{:S(2)}) async-start(f32[4,128,2048]{2,1,0:T(8,128)} %bitcast.48), calls=%async_computation | async-start | bytes 8388608 | tf_op jit(solution)/shard_map/all_to_all | solution.py:82
  118.3 46.5 %all-to-all-done = f32[4,128,2048]{2,1,0:T(8,128)} async-done(((f32[4,128,2048]{2,1,0:T(8,128)}), f32[4,128,2048]{2,1,0:T(8,128)}, u32[]{:S(2)}, u32[]{:S(2)}) %all-to-all-start) | async-done | bytes 4194336 | tf_op jit(solution)/shard_map/all_to_all | solution.py:82
  164.8 2.7 %bitcast_reduce_fusion = bf16[2,128,2048]{2,1,0:T(8,128)(2,1)S(1)} fusion(f32[4,128,2048]{2,1,0:T(8,128)} %all-to-all-done), kind=kLoop, calls=%fused_computation.4 | loop fusion | flops 524288 | bytes 5242880 | tf_op jit(solution)/shard_map/reduce_sum | solution.py:83
  167.6 4.3 %gather_fusion = bf16[256,2048]{1,0:T(8,128)(2,1)S(1)} fusion(bf16[2,128,2048]{2,1,0:T(8,128)(2,1)S(1)} %bitcast_reduce_fusion, s32[256]{0:T(256)S(1)} %reshape.126), kind=kCustom, calls=%fused_computation | custom fusion | bytes 2099200 | tf_op jit(solution)/shard_map/gather | solution.py:84
  172.6 2.8 %reduce_sum.52 = bf16[128,2048]{1,0:T(8,128)(2,1)S(1)} reduce(bf16[128,2,2048]{2,1,0:T(2,128)(2,1)S(1)} %reshape.129, bf16[]{:T(256)} %constant.80.clone.1), dimensions={1}, to_apply=%region_6.7 | reduce | flops 262144 | bytes 1572866 | tf_op jit(solution)/shard_map/reduce_sum | solution.py:85
  176.1 21.7 %reduce-scatter.2.cloned.1.call-done = bf16[256,2048]{1,0:T(8,128)(2,1)} async-done(((bf16[1024,2048]{1,0:T(8,128)(2,1)}), bf16[256,2048]{1,0:T(8,128)(2,1)}) %reduce-scatter.2.cloned.1.call-update) | async-done | bytes 1048592 | tf_op jit(solution)/shard_map/reduce_scatter | solution.py:102
  197.9 1.0 copy.47
  198.9 6.4 %multiply_subtract_fusion = (f32[256,2048]{1,0:T(8,128)}, f32[256,2048]{1,0:T(8,128)}, f32[256,2048]{1,0:T(8,128)}) fusion(f32[256,2048]{1,0:T(8,128)S(1)} %copy-done, bf16[256,2048]{1,0:T(8,128)(2,1)} %reduce-scatter.2.cloned.1.call-done, f32[256,2048]{1,0:T(8,128)} %param.10, f32[256,2048]{1,0:T(8,128)} %param.11), kind=kLoop, calls=%fused_computation.16 | loop fusion | flops 8912896 | bytes 13631488 | tf_op jit(solution)/shard_map/sub | solution.py:23
  (53 shorter events, 5.0 us)
Async XLA Ops:
  7.2 4.8 %copy-start.9 = (u32[32]{0:T(128)S(1)}, u32[32]{0:T(128)}, u32[]{:S(2)}) copy-start(u32[32]{0:T(128)} %constant.114) | copy-start | bytes 388
  7.2 3.1 %copy-start.5 = (s32[128,2]{0,1:T(2,128)S(1)}, s32[128,2]{0,1:T(2,128)}, u32[]{:S(2)}) copy-start(s32[128,2]{0,1:T(2,128)} %param.6) | copy-start | bytes 3076
  7.2 190.7 %reduce-scatter.2.cloned.1.call-start = ((), (), s32[]{:S(2)}) async-start(), calls=%async_computation.2 | async-start | bytes 5242880 | tf_op jit(solution)/shard_map/reduce_scatter | solution.py:102
  9.0 26.9 %collective-permute-start.1 = (bf16[256,2048]{1,0:T(8,128)(2,1)S(1)}, bf16[256,2048]{1,0:T(8,128)(2,1)}, u32[]{:S(2)}, u32[]{:S(2)}) collective-permute-start(bf16[256,2048]{1,0:T(8,128)(2,1)S(1)} %convert_element_type.28), channel_id=1, source_target_pairs={{0,2},{2,4},{4,6},{1,3},{3,5},{5,7},{8,10},{10,12},{12,14},{9,11},... | collective-permute-start | bytes 3145736 | tf_op jit(solution)/shard_map/ppermute | solution.py:36
  24.0 2.0 copy-start.6
  30.3 63.0 %collective-permute-start.7 = (bf16[1024,2048]{1,0:T(8,128)(2,1)}, bf16[1024,2048]{1,0:T(8,128)(2,1)}, u32[]{:S(2)}, u32[]{:S(2)}) collective-permute-start(bf16[1024,2048]{1,0:T(8,128)(2,1)} %convolution_convert_fusion), channel_id=1, source_target_pairs={{0,1},{1,0},{2,3},{3,2},{4,5},{5,4},{6,7},{7,6},{8,9},{9,8},{10,11... | collective-permute-start | bytes 12582920 | tf_op jit(solution)/shard_map/ppermute | solution.py:97
  30.3 27.6 %collective-permute-start = (bf16[256,2048]{1,0:T(8,128)(2,1)S(1)}, bf16[256,2048]{1,0:T(8,128)(2,1)S(1)}, u32[]{:S(2)}, u32[]{:S(2)}) collective-permute-start(bf16[256,2048]{1,0:T(8,128)(2,1)S(1)} %convert_element_type.28), channel_id=1, source_target_pairs={{2,0},{4,2},{6,4},{3,1},{5,3},{7,5},{10,8},{12,10},{14,12},{11,9},... | collective-permute-start | bytes 3145736 | tf_op jit(solution)/shard_map/ppermute | solution.py:38
  35.9 26.5 %collective-permute-start.2 = (bf16[256,2048]{1,0:T(8,128)(2,1)}, bf16[256,2048]{1,0:T(8,128)(2,1)S(1)}, u32[]{:S(2)}, u32[]{:S(2)}) collective-permute-start(bf16[256,2048]{1,0:T(8,128)(2,1)} %collective-permute-done.1), channel_id=1, source_target_pairs={{2,4},{4,6},{3,5},{5,7},{10,12},{12,14},{11,13},{13,15},{18,20},{2... | collective-permute-start | bytes 3145736 | tf_op jit(solution)/shard_map/ppermute | solution.py:36
  57.9 5.7 %copy-start.3 = (bf16[256,2048]{1,0:T(8,128)(2,1)}, bf16[256,2048]{1,0:T(8,128)(2,1)S(1)}, u32[]{:S(2)}) copy-start(bf16[256,2048]{1,0:T(8,128)(2,1)S(1)} %collective-permute-done) | copy-start | bytes 3145732
  57.9 5.7 %collective-permute-start.4 = (bf16[256,2048]{1,0:T(8,128)(2,1)S(1)}, bf16[256,2048]{1,0:T(8,128)(2,1)}, u32[]{:S(2)}, u32[]{:S(2)}) collective-permute-start(bf16[256,2048]{1,0:T(8,128)(2,1)S(1)} %collective-permute-done), channel_id=1, source_target_pairs={{2,0},{4,2},{3,1},{5,3},{10,8},{12,10},{11,9},{13,11},{18,16},{20,... | collective-permute-start | bytes 3145736 | tf_op jit(solution)/shard_map/ppermute | solution.py:38
  62.3 25.6 %collective-permute-start.3 = (bf16[256,2048]{1,0:T(8,128)(2,1)S(1)}, bf16[256,2048]{1,0:T(8,128)(2,1)}, u32[]{:S(2)}, u32[]{:S(2)}) collective-permute-start(bf16[256,2048]{1,0:T(8,128)(2,1)S(1)} %collective-permute-done.2), channel_id=1, source_target_pairs={{4,6},{5,7},{12,14},{13,15},{20,22},{21,23},{28,30},{29,31}} | collective-permute-start | bytes 3145736 | tf_op jit(solution)/shard_map/ppermute | solution.py:36
  63.7 25.6 %collective-permute-start.5 = (bf16[256,2048]{1,0:T(8,128)(2,1)}, bf16[256,2048]{1,0:T(8,128)(2,1)S(1)}, u32[]{:S(2)}, u32[]{:S(2)}) collective-permute-start(bf16[256,2048]{1,0:T(8,128)(2,1)} %collective-permute-done.4), channel_id=1, source_target_pairs={{2,0},{3,1},{10,8},{11,9},{18,16},{19,17},{26,24},{27,25}} | collective-permute-start | bytes 3145736 | tf_op jit(solution)/shard_map/ppermute | solution.py:38
  64.4 23.5 %copy-start.4 = (bf16[256,2048]{1,0:T(8,128)(2,1)S(1)}, bf16[256,2048]{1,0:T(8,128)(2,1)}, u32[]{:S(2)}) copy-start(bf16[256,2048]{1,0:T(8,128)(2,1)} %copy-done.3) | copy-start | bytes 3145732
  90.7 2.7 %copy-start.1 = (bf16[256,2048]{1,0:T(8,128)(2,1)}, bf16[256,2048]{1,0:T(8,128)(2,1)S(1)}, u32[]{:S(2)}) copy-start(bf16[256,2048]{1,0:T(8,128)(2,1)S(1)} %broadcast_select_fusion.1) | copy-start | bytes 3145732
  90.7 2.7 %copy-start.2 = (bf16[512,4,1,256]{0,3,2,1:T(8,128)(2,1)S(1)}, bf16[512,4,1,256]{0,3,2,1:T(8,128)(2,1)}, u32[]{:S(2)}) copy-start(bf16[512,4,1,256]{0,3,2,1:T(8,128)(2,1)} %get-tuple-element.25) | copy-start | bytes 3145732
  90.7 3.8 %copy-start.7 = (bf16[1,1,512,2048]{3,2,1,0:T(8,128)(2,1)S(1)}, bf16[1,1,512,2048]{3,2,1,0:T(8,128)(2,1)}, u32[]{:S(2)}) copy-start(bf16[1,1,512,2048]{3,2,1,0:T(8,128)(2,1)} %param.8) | copy-start | bytes 6291460
  93.3 12.2 %collective-permute-start.6 = (bf16[1024,2048]{1,0:T(8,128)(2,1)}, bf16[1024,2048]{1,0:T(8,128)(2,1)}, u32[]{:S(2)}, u32[]{:S(2)}) collective-permute-start(bf16[1024,2048]{1,0:T(8,128)(2,1)} %pad_maximum_fusion), channel_id=1, source_target_pairs={{0,1},{1,0},{2,3},{3,2},{4,5},{5,4},{6,7},{7,6},{8,9},{9,8},{10,11... | collective-permute-start | bytes 12582920 | tf_op jit(solution)/shard_map/ppermute | solution.py:76
  101.1 4.4 %copy-start.8 = (bf16[1,1,512,2048]{3,2,1,0:T(8,128)(2,1)S(1)}, bf16[1,1,512,2048]{3,2,1,0:T(8,128)(2,1)}, u32[]{:S(2)}) copy-start(bf16[1,1,512,2048]{3,2,1,0:T(8,128)(2,1)} %param.8) | copy-start | bytes 6291460
  112.6 52.2 %all-to-all-start = ((f32[4,128,2048]{2,1,0:T(8,128)}), f32[4,128,2048]{2,1,0:T(8,128)}, u32[]{:S(2)}, u32[]{:S(2)}) async-start(f32[4,128,2048]{2,1,0:T(8,128)} %bitcast.48), calls=%async_computation | async-start | bytes 8388608 | tf_op jit(solution)/shard_map/all_to_all | solution.py:82
  175.7 23.1 %copy-start = (f32[256,2048]{1,0:T(8,128)S(1)}, f32[256,2048]{1,0:T(8,128)}, u32[]{:S(2)}) copy-start(f32[256,2048]{1,0:T(8,128)} %param.9) | copy-start | bytes 6291460
Sparse Core Ops, SparseCore 0:
  101.2 96.5 reduce-scatter.1

commit v5 on v4

--- a/solution.py
+++ b/solution.py
@@ -27,12 +27,19 @@
 SWAP = [(0, 1), (1, 0)]
 
 
-def gather_relative(block, axis, n, me):
+def flood_first(block, axis, n):
+    right = lax.ppermute(block, axis, [(p, p + 1) for p in range(0, n - 1)])
+    left = lax.ppermute(block, axis, [(p, p - 1) for p in range(1, n)])
+    return right, left
+
+
+def gather_relative(block, first, axis, n, me):
     left = [None] * n
     right = [None] * n
-    cur_r = block
-    cur_l = block
-    for t in range(1, n):
+    cur_r, cur_l = first
+    right[1] = cur_r
+    left[1] = cur_l
+    for t in range(2, n):
         cur_r = lax.ppermute(cur_r, axis, [(p, p + 1) for p in range(t - 1, n - 1)])
         right[t] = cur_r
         cur_l = lax.ppermute(cur_l, axis, [(p, p - 1) for p in range(1, n - t + 1)])
@@ -55,6 +62,11 @@
     top_count = routes.shape[1]
     me_c = lax.axis_index("core")
     me_z = lax.axis_index("z")
+    wbf = weight.astype(jnp.bfloat16)
+    first = flood_first(wbf, "z", n_z)
+    first, routes, expert_inputs, hidden_grad = lax.optimization_barrier(
+        (first, routes, expert_inputs, hidden_grad)
+    )
     flat_routes = routes.reshape(-1)
     onehot = (flat_routes[:, None] == jnp.arange(experts, dtype=jnp.int32)[None, :]).astype(
         jnp.int32
@@ -71,15 +83,19 @@
     grad_flat = hidden_grad.reshape(slot_rows, -1)
     masked = jnp.where(valid[:, None], grad_flat, jnp.zeros_like(grad_flat))
 
-    wbf = weight.astype(jnp.bfloat16)
-    w_mine = gather_relative(wbf, "z", n_z, me_z)
+    w_mine = gather_relative(wbf, first, "z", n_z, me_z)
     w_other = lax.ppermute(w_mine, "core", SWAP)
     cols = (((1,), (1,)), ((), ()))
+    half = width // CORES
     out_mine = lax.dot_general(masked, w_mine, cols, preferred_element_type=jnp.float32)
+    recv_mine = lax.all_to_all(
+        out_mine.reshape(n_expert, capacity, half), "expert", split_axis=0, concat_axis=0, tiled=True
+    )
     out_other = lax.dot_general(masked, w_other, cols, preferred_element_type=jnp.float32)
-    partial_rows = jnp.concatenate([out_mine, out_other], axis=1)
-    sent = partial_rows.reshape(n_expert, capacity, width)
-    received = lax.all_to_all(sent, "expert", split_axis=0, concat_axis=0, tiled=True)
+    recv_other = lax.all_to_all(
+        out_other.reshape(n_expert, capacity, half), "expert", split_axis=0, concat_axis=0, tiled=True
+    )
+    received = jnp.concatenate([recv_mine, recv_other], axis=2)
     paired = jnp.sum(received.reshape(experts, 2, capacity, width), axis=1).astype(jnp.bfloat16)
     picked = paired[routes, slots]
     token_rel = jnp.sum(picked.astype(jnp.float32), axis=1).astype(jnp.bfloat16)

time: 216 us -> 233 us (1.079); the launches traced: 212 us -> 233 us
  waiting for transfers between devices: 116 us -> 134 us
  starting transfers between devices: 16 us -> 20 us
    ppermute x3 -> x2, waiting for transfers between devices: 27.1 us -> 69.7 us  [gather_relative(): cur_r = lax.ppermute(cur_r, axis, [(p, p + 1) for p in range(t - 1, n - 1)])]
    reduce_scatter x1, waiting for transfers between devices: 21.7 us -> 0.02 us  [shards(): owned = lax.psum_scatter(chip, 'z', scatter_dimension=0, tiled=True)]
    ppermute x3 -> x2, waiting for transfers between devices: 20.8 us -> 0.01 us  [gather_relative(): cur_l = lax.ppermute(cur_l, axis, [(p, p - 1) for p in range(1, n - t + 1)])]
    ppermute x0 -> x2, waiting for transfers between devices: none -> 20.8 us  [the longest x1 19.7 us: flood_first(): right = lax.ppermute(block, axis, [(p, p + 1) for p in range(0, n - 1)])]
    ppermute x0 -> x2, starting transfers between devices: none -> 5.91 us  [the longest x1 4.61 us: flood_first(): left = lax.ppermute(block, axis, [(p, p - 1) for p in range(1, n)])]
    unnamed x26 -> x20, local copies, waits for them, and re-layouts: 6.98 us -> 2.94 us
    ppermute x3 -> x2, starting transfers between devices: 6.96 us -> 3.27 us  [gather_relative(): cur_l = lax.ppermute(cur_l, axis, [(p, p - 1) for p in range(1, n - t + 1)])]
    all_to_all x1 -> x2, starting transfers between devices: 5.12 us -> 8.24 us  [the longest x1 4.63 us: shards(): lax.all_to_all(out_other.reshape(n_expert, capacity, half), 'expert', spl...]
  transfers between devices with their start and end apart: 10 -> 11, of which waited for: 6 -> 6; matrix products, arithmetic and copies ran while one was open for 22% -> 15% of each run, Pallas kernels for 0% -> 0%
where the time goes in v5:
time: 233 us
  waiting for transfers between devices  134 us (58%)
  matrix products  21.8 us (9%)
  other arithmetic  21 us (9%)
  starting transfers between devices  20 us (9%)
  between operations  15 us (6%)
  local copies, waits for them, and re-layouts  13.5 us (6%)
  blocking collectives  7.37 us (3%)
    ppermute x2, waiting for transfers between devices, gather_relative(): cur_r = lax.ppermute(cur_r, axis, [(p, p + 1) for p in range(t - 1, n - 1)])  69.7 us
    all_to_all x1, waiting for transfers between devices, shards(): lax.all_to_all(out_other.reshape(n_expert, capacity, half), 'expert', spl...  24.4 us
    ppermute x1, waiting for transfers between devices, flood_first(): right = lax.ppermute(block, axis, [(p, p + 1) for p in range(0, n - 1)])  19.7 us
    all_to_all x1, waiting for transfers between devices, shards(): lax.all_to_all(out_mine.reshape(n_expert, capacity, half), 'expert', spli...  19.1 us
    unnamed x1, blocking collectives  7.37 us
    dot_general x1, matrix products, shards(): lax.dot_general(in_mine.reshape(slot_rows, n_z * rows), masked, dims, pre...  7.18 us
    dot_general x1, matrix products, shards(): lax.dot_general(masked, w_other, cols, preferred_element_type=jnp.float32)  6.52 us
    sub x1, other arithmetic, adamw(): new_weight = weight - learn_rate * (update + decay * weight)  6.42 us
  transfers between devices with their start and end apart: 11, of which 6 were waited for; matrix products, arithmetic and copies ran while one was open for 15% of the time, Pallas kernels for 0%

profile of v5, /device:TPU:24, one launch (start us, length us, event | category | flops | bytes accessed | tf_op | source)
XLA Modules:
  0.0 232.8 jit_solution(2685019355197223457)
XLA Ops:
  7.2 1.7 convert_element_type.27
  9.0 1.3 collective-permute-start
  10.3 4.6 %collective-permute-start.1 = (bf16[256,2048]{1,0:T(8,128)(2,1)S(1)}, bf16[256,2048]{1,0:T(8,128)(2,1)S(1)}, u32[]{:S(2)}, u32[]{:S(2)}) collective-permute-start(bf16[256,2048]{1,0:T(8,128)(2,1)S(1)} %convert_element_type.27), channel_id=1, source_target_pairs={{2,0},{4,2},{6,4},{3,1},{5,3},{7,5},{10,8},{12,10},{14,12},{11,9},... | collective-permute-start | bytes 3145736 | tf_op jit(solution)/shard_map/ppermute | solution.py:32
  16.2 19.7 %collective-permute-done = bf16[256,2048]{1,0:T(8,128)(2,1)} collective-permute-done((bf16[256,2048]{1,0:T(8,128)(2,1)S(1)}, bf16[256,2048]{1,0:T(8,128)(2,1)}, u32[]{:S(2)}, u32[]{:S(2)}) %collective-permute-start) | collective-permute-done | bytes 1048608 | tf_op jit(solution)/shard_map/ppermute | solution.py:31
  35.9 1.1 collective-permute-done.1
  38.8 7.4 %all-reduce = s32[8]{0:T(128)S(1)} all-reduce(s32[8]{0:T(128)S(1)} %dynamic-update-slice), channel_id=2, replica_groups=mesh['expert'=4,'z'=4,'core'=2] {'expert'}, use_global_device_ids=true, to_apply=%add | all-reduce | flops 8 | bytes 64
  46.5 2.9 %copy.46 = bf16[1,1,512,2048]{2,3,1,0:T(8,128)(2,1)S(1)} copy(bf16[1,1,512,2048]{3,2,1,0:T(8,128)(2,1)} %param.7) | data formatting | bytes 4194304 | tf_op jit(solution)/shard_map/optimization_barrier | solution.py:67
  49.4 1.2 constant_dynamic-slice_fusion.1
  50.6 0.8 copy-done.5
  51.3 4.3 %convolution_convert_fusion = bf16[1024,2048]{1,0:T(8,128)(2,1)} fusion(bf16[512,1024]{0,1:T(8,128)(2,1)S(1)} %bitcast.53, bf16[1,1,512,2048]{3,2,1,0:T(8,128)(2,1)S(1)} %copy-done.5, pred[512]{0:T(512)(128)(4,1)S(1)} %get-tuple-element.37), kind=kOutput, calls=%fused_computation.9 | convolution fusion | flops 2150629376 | bytes 7340544 | tf_op jit(solution)/shard_map/dot_general | solution.py:110
  55.7 1.6 collective-permute-start.4
  57.3 1.3 collective-permute-start.2
  58.6 1.6 collective-permute-start.5
  60.3 27.0 %collective-permute-done.2 = bf16[256,2048]{1,0:T(8,128)(2,1)} collective-permute-done((bf16[256,2048]{1,0:T(8,128)(2,1)}, bf16[256,2048]{1,0:T(8,128)(2,1)}, u32[]{:S(2)}, u32[]{:S(2)}) %collective-permute-start.2) | collective-permute-done | bytes 1048608 | tf_op jit(solution)/shard_map/ppermute | solution.py:43
  87.2 1.3 collective-permute-start.3
  88.5 7.2 %add_convert_fusion = bf16[1024,2048]{1,0:T(8,128)(2,1)} fusion(bf16[1024,2048]{1,0:T(8,128)(2,1)} %collective-permute-done.7, bf16[512,1024]{0,1:T(8,128)(2,1)S(1)} %bitcast.52, bf16[1,1,512,2048]{3,2,1,0:T(8,128)(2,1)} %param.8, pred[512]{0:T(512)(128)(4,1)S(1)} %get-tuple-element.37), kind=kOutput, calls=%fused_computation.1 | convolution fusion | flops 2154823680 | bytes 11534848 | tf_op jit(solution)/shard_map/dot_general | solution.py:114
  95.7 1.4 broadcast_select_fusion.5
  97.1 1.4 broadcast_select_fusion.4
  98.5 42.8 %collective-permute-done.3 = bf16[256,2048]{1,0:T(8,128)(2,1)} collective-permute-done((bf16[256,2048]{1,0:T(8,128)(2,1)}, bf16[256,2048]{1,0:T(8,128)(2,1)}, u32[]{:S(2)}, u32[]{:S(2)}) %collective-permute-start.3) | collective-permute-done | bytes 1048608 | tf_op jit(solution)/shard_map/ppermute | solution.py:43
  141.2 1.3 broadcast_select_fusion.6
  142.6 2.3 pad_maximum_fusion
  145.0 3.8 %fusion.2 = f32[4,128,1024]{2,1,0:T(8,128)} fusion(bf16[4,128,2048]{2,1,0:T(8,128)(2,1)S(1)} %bitcast.56, pred[4,128]{1,0:T(4,128)(4,1)S(1)} %get-tuple-element.38, bf16[256,2048]{1,0:T(8,128)(2,1)S(1)} %broadcast_select_fusion.4, bf16[256,2048]{1,0:T(8,128)(2,1)S(1)} %broadcast_select_fusion.5, bf16[256,2048]{1,0:T(8,128)(2,1)S(1)} %broadcast_select_fusion.6, ...), kind=kOutput, calls=%fused_computation.7 | convolution fusion | flops 2165309440 | bytes 8389120 | tf_op jit(solution)/shard_map/dot_general | solution.py:90
  148.8 3.6 %all-to-all-start = ((f32[4,128,1024]{2,1,0:T(8,128)}), f32[4,128,1024]{2,1,0:T(8,128)S(1)}, u32[]{:S(2)}, u32[]{:S(2)}) async-start(f32[4,128,1024]{2,1,0:T(8,128)} %fusion.2), calls=%async_computation | async-start | bytes 4194304 | tf_op jit(solution)/shard_map/all_to_all | solution.py:91
  152.4 6.5 %fusion = f32[4,128,1024]{2,1,0:T(8,128)} fusion(bf16[1024,2048]{1,0:T(8,128)(2,1)} %collective-permute-done.6, bf16[4,128,2048]{2,1,0:T(8,128)(2,1)} %bitcast.55, pred[4,128]{1,0:T(4,128)(4,1)S(1)} %get-tuple-element.38), kind=kOutput, calls=%fused_computation.5 | convolution fusion | flops 2148532224 | bytes 8389120 | tf_op jit(solution)/shard_map/dot_general | solution.py:94
  158.9 19.1 %all-to-all-done = f32[4,128,1024]{2,1,0:T(8,128)S(1)} async-done(((f32[4,128,1024]{2,1,0:T(8,128)}), f32[4,128,1024]{2,1,0:T(8,128)S(1)}, u32[]{:S(2)}, u32[]{:S(2)}) %all-to-all-start) | async-done | bytes 2097184 | tf_op jit(solution)/shard_map/all_to_all | solution.py:91
  178.0 4.6 %all-to-all-start.1 = ((f32[4,128,1024]{2,1,0:T(8,128)}), f32[4,128,1024]{2,1,0:T(8,128)}, u32[]{:S(2)}, u32[]{:S(2)}) async-start(f32[4,128,1024]{2,1,0:T(8,128)} %fusion), calls=%async_computation.1 | async-start | bytes 4194304 | tf_op jit(solution)/shard_map/all_to_all | solution.py:95
  183.2 24.4 %all-to-all-done.1 = f32[4,128,1024]{2,1,0:T(8,128)} async-done(((f32[4,128,1024]{2,1,0:T(8,128)}), f32[4,128,1024]{2,1,0:T(8,128)}, u32[]{:S(2)}, u32[]{:S(2)}) %all-to-all-start.1) | async-done | bytes 2097184 | tf_op jit(solution)/shard_map/all_to_all | solution.py:95
  207.6 2.2 bitcast_reduce_fusion
  209.7 4.3 %gather_fusion = bf16[256,2048]{1,0:T(8,128)(2,1)S(1)} fusion(bf16[2,128,2048]{2,1,0:T(8,128)(2,1)S(1)} %bitcast_reduce_fusion, s32[256]{0:T(256)S(1)} %reshape.138), kind=kCustom, calls=%fused_computation | custom fusion | bytes 2099200 | tf_op jit(solution)/shard_map/gather | solution.py:100
  214.8 2.8 %reduce_sum.52 = bf16[128,2048]{1,0:T(8,128)(2,1)S(1)} reduce(bf16[128,2,2048]{2,1,0:T(2,128)(2,1)S(1)} %reshape.141, bf16[]{:T(256)} %constant.80.clone.1), dimensions={1}, to_apply=%region_6.7 | reduce | flops 262144 | bytes 1572866 | tf_op jit(solution)/shard_map/reduce_sum | solution.py:101
  218.3 1.0 copy.47
  219.5 6.4 %multiply_subtract_fusion = (f32[256,2048]{1,0:T(8,128)}, f32[256,2048]{1,0:T(8,128)}, f32[256,2048]{1,0:T(8,128)}) fusion(f32[256,2048]{1,0:T(8,128)S(1)} %copy-done, bf16[256,2048]{1,0:T(8,128)(2,1)} %reduce-scatter.2.cloned.1.call-done, f32[256,2048]{1,0:T(8,128)} %param.10, f32[256,2048]{1,0:T(8,128)} %param.11), kind=kLoop, calls=%fused_computation.19 | loop fusion | flops 8912896 | bytes 13631488 | tf_op jit(solution)/shard_map/sub | solution.py:23
  (50 shorter events, 5.0 us)
Async XLA Ops:
  7.2 7.7 %copy-start.7 = (u32[32]{0:T(128)S(1)}, u32[32]{0:T(128)}, u32[]{:S(2)}) copy-start(u32[32]{0:T(128)} %constant.114) | copy-start | bytes 388
  7.2 29.8 %copy-start.4 = (s32[128,2]{0,1:T(2,128)S(1)}, s32[128,2]{0,1:T(2,128)}, u32[]{:S(2)}) copy-start(s32[128,2]{0,1:T(2,128)} %param.6) | copy-start | bytes 3076
  7.2 211.1 %reduce-scatter.2.cloned.1.call-start = ((), (), s32[]{:S(2)}) async-start(), calls=%async_computation.3 | async-start | bytes 5242880 | tf_op jit(solution)/shard_map/reduce_scatter | solution.py:118
  9.0 26.9 %collective-permute-start = (bf16[256,2048]{1,0:T(8,128)(2,1)S(1)}, bf16[256,2048]{1,0:T(8,128)(2,1)}, u32[]{:S(2)}, u32[]{:S(2)}) collective-permute-start(bf16[256,2048]{1,0:T(8,128)(2,1)S(1)} %convert_element_type.27), channel_id=1, source_target_pairs={{0,2},{2,4},{4,6},{1,3},{3,5},{5,7},{8,10},{10,12},{12,14},{9,11},... | collective-permute-start | bytes 3145736 | tf_op jit(solution)/shard_map/ppermute | solution.py:31
  10.3 26.7 %collective-permute-start.1 = (bf16[256,2048]{1,0:T(8,128)(2,1)S(1)}, bf16[256,2048]{1,0:T(8,128)(2,1)S(1)}, u32[]{:S(2)}, u32[]{:S(2)}) collective-permute-start(bf16[256,2048]{1,0:T(8,128)(2,1)S(1)} %convert_element_type.27), channel_id=1, source_target_pairs={{2,0},{4,2},{6,4},{3,1},{5,3},{7,5},{10,8},{12,10},{14,12},{11,9},... | collective-permute-start | bytes 3145736 | tf_op jit(solution)/shard_map/ppermute | solution.py:32
  36.9 9.5 %copy-start.2 = (bf16[256,2048]{1,0:T(8,128)(2,1)}, bf16[256,2048]{1,0:T(8,128)(2,1)S(1)}, u32[]{:S(2)}) copy-start(bf16[256,2048]{1,0:T(8,128)(2,1)S(1)} %collective-permute-done.1) | copy-start | bytes 3145732
  49.3 2.0 copy-start.5
  51.3 4.4 %copy-start.3 = (bf16[256,2048]{1,0:T(8,128)(2,1)S(1)}, bf16[256,2048]{1,0:T(8,128)(2,1)}, u32[]{:S(2)}) copy-start(bf16[256,2048]{1,0:T(8,128)(2,1)} %copy-done.2) | copy-start | bytes 3145732
  51.3 37.2 %copy-start.1 = (bf16[512,4,1,256]{0,3,2,1:T(8,128)(2,1)S(1)}, bf16[512,4,1,256]{0,3,2,1:T(8,128)(2,1)}, u32[]{:S(2)}) copy-start(bf16[512,4,1,256]{0,3,2,1:T(8,128)(2,1)} %get-tuple-element.35) | copy-start | bytes 3145732
  55.7 32.9 %collective-permute-start.7 = (bf16[1024,2048]{1,0:T(8,128)(2,1)}, bf16[1024,2048]{1,0:T(8,128)(2,1)}, u32[]{:S(2)}, u32[]{:S(2)}) collective-permute-start(bf16[1024,2048]{1,0:T(8,128)(2,1)} %convolution_convert_fusion), channel_id=1, source_target_pairs={{0,1},{1,0},{2,3},{3,2},{4,5},{5,4},{6,7},{7,6},{8,9},{9,8},{10,11... | collective-permute-start | bytes 12582920 | tf_op jit(solution)/shard_map/ppermute | solution.py:113
  55.7 2.9 %collective-permute-start.4 = (bf16[256,2048]{1,0:T(8,128)(2,1)S(1)}, bf16[256,2048]{1,0:T(8,128)(2,1)}, u32[]{:S(2)}, u32[]{:S(2)}) collective-permute-start(bf16[256,2048]{1,0:T(8,128)(2,1)S(1)} %copy-done.3), channel_id=1, source_target_pairs={{2,0},{4,2},{3,1},{5,3},{10,8},{12,10},{11,9},{13,11},{18,16},{20,... | collective-permute-start | bytes 3145736 | tf_op jit(solution)/shard_map/ppermute | solution.py:45
  57.3 29.9 %collective-permute-start.2 = (bf16[256,2048]{1,0:T(8,128)(2,1)}, bf16[256,2048]{1,0:T(8,128)(2,1)}, u32[]{:S(2)}, u32[]{:S(2)}) collective-permute-start(bf16[256,2048]{1,0:T(8,128)(2,1)} %collective-permute-done), channel_id=1, source_target_pairs={{2,4},{4,6},{3,5},{5,7},{10,12},{12,14},{11,13},{13,15},{18,20},{2... | collective-permute-start | bytes 3145736 | tf_op jit(solution)/shard_map/ppermute | solution.py:43
  58.6 38.5 %collective-permute-start.5 = (bf16[256,2048]{1,0:T(8,128)(2,1)}, bf16[256,2048]{1,0:T(8,128)(2,1)}, u32[]{:S(2)}, u32[]{:S(2)}) collective-permute-start(bf16[256,2048]{1,0:T(8,128)(2,1)} %collective-permute-done.4), channel_id=1, source_target_pairs={{2,0},{3,1},{10,8},{11,9},{18,16},{19,17},{26,24},{27,25}} | collective-permute-start | bytes 3145736 | tf_op jit(solution)/shard_map/ppermute | solution.py:45
  87.2 54.0 %collective-permute-start.3 = (bf16[256,2048]{1,0:T(8,128)(2,1)}, bf16[256,2048]{1,0:T(8,128)(2,1)}, u32[]{:S(2)}, u32[]{:S(2)}) collective-permute-start(bf16[256,2048]{1,0:T(8,128)(2,1)} %collective-permute-done.2), channel_id=1, source_target_pairs={{4,6},{5,7},{12,14},{13,15},{20,22},{21,23},{28,30},{29,31}} | collective-permute-start | bytes 3145736 | tf_op jit(solution)/shard_map/ppermute | solution.py:43
  142.6 2.4 %copy-start.6 = (bf16[1,1,512,2048]{3,2,1,0:T(8,128)(2,1)S(1)}, bf16[1,1,512,2048]{3,2,1,0:T(8,128)(2,1)}, u32[]{:S(2)}) copy-start(bf16[1,1,512,2048]{3,2,1,0:T(8,128)(2,1)} %param.8) | copy-start | bytes 6291460
  144.9 7.5 %collective-permute-start.6 = (bf16[1024,2048]{1,0:T(8,128)(2,1)}, bf16[1024,2048]{1,0:T(8,128)(2,1)}, u32[]{:S(2)}, u32[]{:S(2)}) collective-permute-start(bf16[1024,2048]{1,0:T(8,128)(2,1)} %pad_maximum_fusion), channel_id=1, source_target_pairs={{0,1},{1,0},{2,3},{3,2},{4,5},{5,4},{6,7},{7,6},{8,9},{9,8},{10,11... | collective-permute-start | bytes 12582920 | tf_op jit(solution)/shard_map/ppermute | solution.py:87
  148.8 29.3 %all-to-all-start = ((f32[4,128,1024]{2,1,0:T(8,128)}), f32[4,128,1024]{2,1,0:T(8,128)S(1)}, u32[]{:S(2)}, u32[]{:S(2)}) async-start(f32[4,128,1024]{2,1,0:T(8,128)} %fusion.2), calls=%async_computation | async-start | bytes 4194304 | tf_op jit(solution)/shard_map/all_to_all | solution.py:91
  178.0 29.5 %all-to-all-start.1 = ((f32[4,128,1024]{2,1,0:T(8,128)}), f32[4,128,1024]{2,1,0:T(8,128)}, u32[]{:S(2)}, u32[]{:S(2)}) async-start(f32[4,128,1024]{2,1,0:T(8,128)} %fusion), calls=%async_computation.1 | async-start | bytes 4194304 | tf_op jit(solution)/shard_map/all_to_all | solution.py:95
  217.9 1.6 copy-start
Sparse Core Ops, SparseCore 0:
  95.9 87.0 reduce-scatter.1

commit v6 on v2

--- a/solution.py
+++ b/solution.py
@@ -27,6 +27,16 @@
 SWAP = [(0, 1), (1, 0)]
 
 
+def ring_order(n_z):
+    count = CORES * n_z
+    pos_of = [z if c == 0 else count - 1 - z for z in range(n_z) for c in range(CORES)]
+    at_pos = [0] * count
+    for p, j in enumerate(pos_of):
+        at_pos[j] = p
+    pairs = [(at_pos[j], at_pos[(j + 1) % count]) for j in range(count)]
+    return pos_of, pairs
+
+
 def shards(routes, expert_inputs, hidden_grad, weight, moment_one, moment_two):
     n_expert = lax.axis_size("expert")
     n_z = lax.axis_size("z")
@@ -38,6 +48,7 @@
     tok_count = routes.shape[0]
     top_count = routes.shape[1]
     me_c = lax.axis_index("core")
+    me_z = lax.axis_index("z")
     flat_routes = routes.reshape(-1)
     onehot = (flat_routes[:, None] == jnp.arange(experts, dtype=jnp.int32)[None, :]).astype(
         jnp.int32
@@ -54,21 +65,36 @@
     grad_flat = hidden_grad.reshape(slot_rows, -1)
     masked = jnp.where(valid[:, None], grad_flat, jnp.zeros_like(grad_flat))
 
+    pos_of, pairs = ring_order(n_z)
+    count = CORES * n_z
+    me_pos = jnp.asarray(pos_of, jnp.int32)[me_z * CORES + me_c]
     wbf = weight.astype(jnp.bfloat16)
-    w_mine = lax.all_gather(wbf, "z", axis=0, tiled=True)
-    w_other = lax.ppermute(w_mine, "core", SWAP)
-    w_rel = jnp.concatenate([w_mine, w_other], axis=0)
-    partial_rows = lax.dot_general(
-        masked, w_rel, (((1,), (1,)), ((), ())), preferred_element_type=jnp.float32
-    )
-    sent = partial_rows.reshape(n_expert, capacity, width)
-    received = lax.all_to_all(sent, "expert", split_axis=0, concat_axis=0, tiled=True)
+    cols = (((1,), (1,)), ((), ()))
+    cur = wbf
+    held = [wbf]
+    recv = []
+    for t in range(1, count):
+        cur = lax.ppermute(cur, DP, pairs)
+        held.append(cur)
+        if t % 2 == 1:
+            w_pair = jnp.concatenate(held[t - 1 : t + 1], axis=0)
+            out = lax.dot_general(masked, w_pair, cols, preferred_element_type=jnp.float32)
+            recv.append(
+                lax.all_to_all(
+                    out.reshape(n_expert, capacity, 2 * rows),
+                    "expert",
+                    split_axis=0,
+                    concat_axis=0,
+                    tiled=True,
+                )
+            )
+    received = jnp.concatenate(recv, axis=2)
     paired = jnp.sum(received.reshape(experts, 2, capacity, width), axis=1).astype(jnp.bfloat16)
     picked = paired[routes, slots]
-    token_rel = jnp.sum(picked.astype(jnp.float32), axis=1).astype(jnp.bfloat16)
-    split = token_rel.reshape(tok_count, CORES, n_z, rows)
-    split = jnp.where(me_c == 0, split, split[:, ::-1])
-    token_grad = jnp.transpose(split, (0, 2, 1, 3)).reshape(tok_count, width)
+    token_step = jnp.sum(picked.astype(jnp.float32), axis=1).astype(jnp.bfloat16)
+    step_of = (me_pos - jnp.asarray(pos_of, jnp.int32)) % count
+    token_grad = jnp.take(token_step.reshape(tok_count, count, rows), step_of, axis=1)
+    token_grad = token_grad.reshape(tok_count, width)
 
     by_class = inputs_flat.reshape(slot_rows, n_z, CORES, rows)
     in_mine = lax.dynamic_index_in_dim(by_class, me_c, axis=2, keepdims=False)
@@ -82,7 +108,9 @@
         in_mine.reshape(slot_rows, n_z * rows), masked, dims, preferred_element_type=jnp.float32
     )
     chip = (g_mine + g_recv.astype(jnp.float32)).astype(jnp.bfloat16)
-    owned = lax.psum_scatter(chip, "z", scatter_dimension=0, tiled=True).astype(jnp.float32)
+    owned = lax.psum_scatter(chip, "z", scatter_dimension=0, tiled=True)
+    token_grad, owned = lax.optimization_barrier((token_grad, owned))
+    owned = owned.astype(jnp.float32)
     new_weight, new_first, new_second = adamw(weight, moment_one, moment_two, owned / loss_scale)
     return (token_grad, new_weight, new_first, new_second)
 

time: 294 us -> 269 us (0.915)
  waiting for transfers between devices: 218 us -> 165 us
  starting transfers between devices: 5.38 us -> 16.9 us
  matrix products: 16.2 us -> 24.3 us
  local copies, waits for them, and re-layouts: 14.1 us -> 20.6 us
    ppermute x1 -> x7, waiting for transfers between devices: 7.31 us -> 130 us  [shards(): cur = lax.ppermute(cur, DP, pairs)]
    all_gather x1 -> x0, waiting for transfers between devices: 79.4 us -> none  [shards(): w_mine = lax.all_gather(wbf, 'z', axis=0, tiled=True)]
    reduce_scatter x1, waiting for transfers between devices: 76.1 us -> 0.02 us  [shards(): owned = lax.psum_scatter(chip, 'z', scatter_dimension=0, tiled=True)]
    all_to_all x1 -> x4, waiting for transfers between devices: 47.5 us -> 35.6 us  [shards(): lax.all_to_all(out.reshape(n_expert, capacity, 2 * rows), 'expert', split...]
    all_to_all x1 -> x4, starting transfers between devices: 5.17 us -> 16.3 us  [shards(): lax.all_to_all(out.reshape(n_expert, capacity, 2 * rows), 'expert', split...]
    dot_general x1 -> x4, matrix products: 9.41 us -> 17.5 us  [shards(): lax.dot_general(masked, w_pair, cols, preferred_element_type=jnp.float32)]
    ppermute x1, waiting for transfers between devices: 7.15 us -> 0.01 us  [shards(): g_recv = lax.ppermute(g_other.astype(jnp.bfloat16), 'core', SWAP)]
    unnamed x12 -> x23, local copies, waits for them, and re-layouts: 7.5 us -> 8.52 us
  transfers between devices with their start and end apart: 5 -> 13, of which waited for: 5 -> 9; matrix products, arithmetic and copies ran while one was open for 0% -> 16% of each run, Pallas kernels for 0% -> 0%
where the time goes in v6:
time: 269 us; the launch traced here: 266 us
  waiting for transfers between devices  165 us (61%)
  matrix products  24.3 us (9%)
  local copies, waits for them, and re-layouts  20.6 us (8%)
  starting transfers between devices  16.9 us (6%)
  other arithmetic  16.2 us (6%)
  between operations  15 us (6%)
  blocking collectives  7.37 us (3%)
    ppermute x7, waiting for transfers between devices, shards(): cur = lax.ppermute(cur, DP, pairs)  130 us
    all_to_all x4, waiting for transfers between devices, shards(): lax.all_to_all(out.reshape(n_expert, capacity, 2 * rows), 'expert', split...  35.6 us
    dot_general x4, matrix products, shards(): lax.dot_general(masked, w_pair, cols, preferred_element_type=jnp.float32)  17.5 us
    all_to_all x4, starting transfers between devices, shards(): lax.all_to_all(out.reshape(n_expert, capacity, 2 * rows), 'expert', split...  16.3 us
    unnamed x23, local copies, waits for them, and re-layouts  8.52 us
    unnamed x1, blocking collectives  7.37 us
    gather x2, local copies, waits for them, and re-layouts, shards(): picked = paired[routes, slots]  7.04 us
    sub x1, other arithmetic, adamw(): new_weight = weight - learn_rate * (update + decay * weight)  6.42 us
  transfers between devices with their start and end apart: 13, of which 9 were waited for; matrix products, arithmetic and copies ran while one was open for 16% of the time, Pallas kernels for 0%

profile of v6, /device:TPU:24, one launch (start us, length us, event | category | flops | bytes accessed | tf_op | source)
XLA Modules:
  0.0 265.7 jit_solution(5535322125244121582)
XLA Ops:
  9.5 1.2 dynamic-slice
  11.7 7.4 %all-reduce = s32[8]{0:T(128)S(1)} all-reduce(s32[8]{0:T(128)S(1)} %dynamic-update-slice), channel_id=2, replica_groups=mesh['expert'=4,'z'=4,'core'=2] {'expert'}, use_global_device_ids=true, to_apply=%add | all-reduce | flops 8 | bytes 64
  19.3 2.9 %copy.51 = bf16[1,1,512,2048]{2,3,1,0:T(8,128)(2,1)S(1)} copy(bf16[1,1,512,2048]{3,2,1,0:T(8,128)(2,1)} %param.9) | data formatting | bytes 4194304 | tf_op args[1]
  22.4 1.4 copy-done.5
  23.8 2.4 convolution_convert_fusion
  27.0 14.4 %collective-permute-done = bf16[256,2048]{1,0:T(8,128)(2,1)} collective-permute-done((bf16[256,2048]{1,0:T(8,128)(2,1)S(1)}, bf16[256,2048]{1,0:T(8,128)(2,1)}, u32[]{:S(2)}, u32[]{:S(2)}) %collective-permute-start) | collective-permute-done | bytes 1048608 | tf_op jit(solution)/shard_map/ppermute | solution.py:77
  41.4 4.4 %add_convert_fusion = bf16[1024,2048]{1,0:T(8,128)(2,1)} fusion(bf16[1024,2048]{1,0:T(8,128)(2,1)S(1)} %collective-permute-done.7, bf16[512,1024]{0,1:T(8,128)(2,1)S(1)} %bitcast.59, bf16[1,1,512,2048]{3,2,1,0:T(8,128)(2,1)S(1)} %copy-done.5, pred[512]{0:T(512)(128)(4,1)S(1)} %get-tuple-element.29), kind=kOutput, calls=%fused_computation.2 | convolution fusion | flops 2154823680 | bytes 11534848 | tf_op jit(solution)/shard_map/dot_general | solution.py:107
  45.8 19.2 %collective-permute-done.1 = bf16[256,2048]{1,0:T(8,128)(2,1)} collective-permute-done((bf16[256,2048]{1,0:T(8,128)(2,1)}, bf16[256,2048]{1,0:T(8,128)(2,1)}, u32[]{:S(2)}, u32[]{:S(2)}) %collective-permute-start.1) | collective-permute-done | bytes 1048608 | tf_op jit(solution)/shard_map/ppermute | solution.py:77
  65.0 59.9 %collective-permute-done.2 = bf16[256,2048]{1,0:T(8,128)(2,1)S(1)} collective-permute-done((bf16[256,2048]{1,0:T(8,128)(2,1)}, bf16[256,2048]{1,0:T(8,128)(2,1)S(1)}, u32[]{:S(2)}, u32[]{:S(2)}) %collective-permute-start.2) | collective-permute-done | bytes 1048608 | tf_op jit(solution)/shard_map/ppermute | solution.py:77
  125.0 21.3 %collective-permute-done.3 = bf16[256,2048]{1,0:T(8,128)(2,1)S(1)} collective-permute-done((bf16[256,2048]{1,0:T(8,128)(2,1)S(1)}, bf16[256,2048]{1,0:T(8,128)(2,1)S(1)}, u32[]{:S(2)}, u32[]{:S(2)}) %collective-permute-start.3) | collective-permute-done | bytes 1048608 | tf_op jit(solution)/shard_map/ppermute | solution.py:77
  147.3 14.9 %collective-permute-done.4 = bf16[256,2048]{1,0:T(8,128)(2,1)} collective-permute-done((bf16[256,2048]{1,0:T(8,128)(2,1)S(1)}, bf16[256,2048]{1,0:T(8,128)(2,1)}, u32[]{:S(2)}, u32[]{:S(2)}) %collective-permute-start.4) | collective-permute-done | bytes 1048608 | tf_op jit(solution)/shard_map/ppermute | solution.py:77
  162.2 4.1 %fusion.3 = f32[4,128,512]{2,1,0:T(8,128)} fusion(bf16[256,2048]{1,0:T(8,128)(2,1)} %collective-permute-done, bf16[256,2048]{1,0:T(8,128)(2,1)S(1)} %convert_element_type.28, bf16[4,128,2048]{2,1,0:T(8,128)(2,1)} %bitcast.62, pred[4,128]{1,0:T(4,128)(4,1)S(1)} %get-tuple-element.30), kind=kOutput, calls=%fused_computation.13 | convolution fusion | flops 1078984704 | bytes 5243392 | tf_op jit(solution)/shard_map/dot_general | solution.py:81
  166.3 4.1 %all-to-all-start = ((f32[4,128,512]{2,1,0:T(8,128)}), f32[4,128,512]{2,1,0:T(8,128)S(1)}, u32[]{:S(2)}, u32[]{:S(2)}) async-start(f32[4,128,512]{2,1,0:T(8,128)} %fusion.3), calls=%async_computation | async-start | bytes 2097152 | tf_op jit(solution)/shard_map/all_to_all | solution.py:83
  170.4 4.5 %fusion.6 = f32[4,128,512]{2,1,0:T(8,128)} fusion(bf16[256,2048]{1,0:T(8,128)(2,1)} %copy-done.7, bf16[256,2048]{1,0:T(8,128)(2,1)} %collective-permute-done.1, bf16[4,128,2048]{2,1,0:T(8,128)(2,1)} %bitcast.63, pred[4,128]{1,0:T(4,128)(4,1)S(1)} %get-tuple-element.30), kind=kOutput, calls=%fused_computation.17 | convolution fusion | flops 1078984704 | bytes 5243392 | tf_op jit(solution)/shard_map/dot_general | solution.py:81
  174.9 7.2 %all-to-all-done = f32[4,128,512]{2,1,0:T(8,128)S(1)} async-done(((f32[4,128,512]{2,1,0:T(8,128)}), f32[4,128,512]{2,1,0:T(8,128)S(1)}, u32[]{:S(2)}, u32[]{:S(2)}) %all-to-all-start) | async-done | bytes 1048608 | tf_op jit(solution)/shard_map/all_to_all | solution.py:83
  182.1 4.2 %all-to-all-start.1 = ((f32[4,128,512]{2,1,0:T(8,128)}), f32[4,128,512]{2,1,0:T(8,128)}, u32[]{:S(2)}, u32[]{:S(2)}) async-start(f32[4,128,512]{2,1,0:T(8,128)} %fusion.6), calls=%async_computation.1 | async-start | bytes 2097152 | tf_op jit(solution)/shard_map/all_to_all | solution.py:83
  186.4 4.4 %fusion.9 = f32[4,128,512]{2,1,0:T(8,128)} fusion(bf16[256,2048]{1,0:T(8,128)(2,1)} %collective-permute-done.4, bf16[256,2048]{1,0:T(8,128)(2,1)} %copy-done.6, bf16[4,128,2048]{2,1,0:T(8,128)(2,1)} %bitcast.64, pred[4,128]{1,0:T(4,128)(4,1)S(1)} %get-tuple-element.30), kind=kOutput, calls=%fused_computation.21 | convolution fusion | flops 1078984704 | bytes 5243392 | tf_op jit(solution)/shard_map/dot_general | solution.py:81
  190.8 8.7 %all-to-all-done.1 = f32[4,128,512]{2,1,0:T(8,128)} async-done(((f32[4,128,512]{2,1,0:T(8,128)}), f32[4,128,512]{2,1,0:T(8,128)}, u32[]{:S(2)}, u32[]{:S(2)}) %all-to-all-start.1) | async-done | bytes 1048608 | tf_op jit(solution)/shard_map/all_to_all | solution.py:83
  199.5 3.5 %all-to-all-start.2 = ((f32[4,128,512]{2,1,0:T(8,128)}), f32[4,128,512]{2,1,0:T(8,128)S(1)}, u32[]{:S(2)}, u32[]{:S(2)}) async-start(f32[4,128,512]{2,1,0:T(8,128)} %fusion.9), calls=%async_computation.2 | async-start | bytes 2097152 | tf_op jit(solution)/shard_map/all_to_all | solution.py:83
  203.0 4.4 %fusion.12 = f32[4,128,512]{2,1,0:T(8,128)} fusion(bf16[256,2048]{1,0:T(8,128)(2,1)} %collective-permute-done.6, bf16[256,2048]{1,0:T(8,128)(2,1)} %collective-permute-done.5, bf16[4,128,2048]{2,1,0:T(8,128)(2,1)} %bitcast.65, pred[4,128]{1,0:T(4,128)(4,1)S(1)} %get-tuple-element.30), kind=kOutput, calls=%fused_computation.25 | convolution fusion | flops 1078984704 | bytes 5243392 | tf_op jit(solution)/shard_map/dot_general | solution.py:81
  207.5 8.6 %all-to-all-done.2 = f32[4,128,512]{2,1,0:T(8,128)S(1)} async-done(((f32[4,128,512]{2,1,0:T(8,128)}), f32[4,128,512]{2,1,0:T(8,128)S(1)}, u32[]{:S(2)}, u32[]{:S(2)}) %all-to-all-start.2) | async-done | bytes 1048608 | tf_op jit(solution)/shard_map/all_to_all | solution.py:83
  216.1 4.4 %all-to-all-start.3 = ((f32[4,128,512]{2,1,0:T(8,128)}), f32[4,128,512]{2,1,0:T(8,128)}, u32[]{:S(2)}, u32[]{:S(2)}) async-start(f32[4,128,512]{2,1,0:T(8,128)} %fusion.12), calls=%async_computation.3 | async-start | bytes 2097152 | tf_op jit(solution)/shard_map/all_to_all | solution.py:83
  222.4 11.1 %all-to-all-done.3 = f32[4,128,512]{2,1,0:T(8,128)} async-done(((f32[4,128,512]{2,1,0:T(8,128)}), f32[4,128,512]{2,1,0:T(8,128)}, u32[]{:S(2)}, u32[]{:S(2)}) %all-to-all-start.3) | async-done | bytes 1048608 | tf_op jit(solution)/shard_map/all_to_all | solution.py:83
  233.5 2.7 %bitcast_reduce_fusion = bf16[2,128,2048]{2,1,0:T(8,128)(2,1)S(1)} fusion(f32[4,128,512]{2,1,0:T(8,128)} %all-to-all-done.3, f32[4,128,512]{2,1,0:T(8,128)} %copy-done.2, f32[4,128,512]{2,1,0:T(8,128)} %all-to-all-done.1, f32[4,128,512]{2,1,0:T(8,128)} %copy-done.1), kind=kLoop, calls=%fused_computation.4 | loop fusion | flops 3670016 | bytes 5242880 | tf_op jit(solution)/shard_map/reduce_sum | solution.py:92
  236.2 5.3 %gather_fusion = bf16[256,2048]{1,0:T(8,128)(2,1)} fusion(bf16[2,128,2048]{2,1,0:T(8,128)(2,1)S(1)} %bitcast_reduce_fusion, s32[256]{0:T(256)S(1)} %reshape.158), kind=kCustom, calls=%fused_computation | custom fusion | bytes 2099200 | tf_op jit(solution)/shard_map/gather | solution.py:93
  241.5 1.7 reshape.161
  243.2 3.6 %reduce_sum.52 = bf16[128,2048]{1,0:T(8,128)(2,1)} reduce(bf16[128,2,2048]{2,1,0:T(2,128)(2,1)S(1)} %reshape.161, bf16[]{:T(256)} %constant.89.clone.1), dimensions={1}, to_apply=%region_6.7 | reduce | flops 262144 | bytes 1572866 | tf_op jit(solution)/shard_map/reduce_sum | solution.py:94
  246.9 1.3 copy.48
  249.0 1.0 copy.50
  250.0 1.4 bitcast_select_fusion
  251.4 1.0 copy.52
  252.4 6.4 %multiply_subtract_fusion = (f32[256,2048]{1,0:T(8,128)}, f32[256,2048]{1,0:T(8,128)}, f32[256,2048]{1,0:T(8,128)}) fusion(f32[256,2048]{1,0:T(8,128)S(1)} %copy-done, bf16[256,2048]{1,0:T(8,128)(2,1)} %reduce-scatter.2.cloned.1.call-done, f32[256,2048]{1,0:T(8,128)} %param.12, f32[256,2048]{1,0:T(8,128)} %param.13), kind=kLoop, calls=%fused_computation.31 | loop fusion | flops 8912896 | bytes 13631488 | tf_op jit(solution)/shard_map/sub | solution.py:23
  (60 shorter events, 7.4 us)
Async XLA Ops:
  7.2 244.2 %reduce-scatter.2.cloned.1.call-start = ((), (), s32[]{:S(2)}) async-start(), calls=%async_computation.5 | async-start | bytes 5242880 | tf_op jit(solution)/shard_map/reduce_scatter | solution.py:111
  22.2 1.6 copy-start.5
  23.8 2.5 copy-start
  26.2 15.2 %collective-permute-start.7 = (bf16[1024,2048]{1,0:T(8,128)(2,1)S(1)}, bf16[1024,2048]{1,0:T(8,128)(2,1)S(1)}, u32[]{:S(2)}, u32[]{:S(2)}) collective-permute-start(bf16[1024,2048]{1,0:T(8,128)(2,1)S(1)} %convolution_convert_fusion), channel_id=1, source_target_pairs={{0,1},{1,0},{2,3},{3,2},{4,5},{5,4},{6,7},{7,6},{8,9},{9,8},{10,11... | collective-permute-start | bytes 12582920 | tf_op jit(solution)/shard_map/ppermute | solution.py:106
  26.5 14.9 %collective-permute-start = (bf16[256,2048]{1,0:T(8,128)(2,1)S(1)}, bf16[256,2048]{1,0:T(8,128)(2,1)}, u32[]{:S(2)}, u32[]{:S(2)}) collective-permute-start(bf16[256,2048]{1,0:T(8,128)(2,1)S(1)} %convert_element_type.28), channel_id=1, source_target_pairs={{0,2},{2,4},{4,6},{6,7},{7,5},{5,3},{3,1},{1,0},{8,10},{10,12},{12... | collective-permute-start | bytes 3145736 | tf_op jit(solution)/shard_map/ppermute | solution.py:77
  41.4 23.6 %collective-permute-start.1 = (bf16[256,2048]{1,0:T(8,128)(2,1)}, bf16[256,2048]{1,0:T(8,128)(2,1)}, u32[]{:S(2)}, u32[]{:S(2)}) collective-permute-start(bf16[256,2048]{1,0:T(8,128)(2,1)} %collective-permute-done), channel_id=1, source_target_pairs={{0,2},{2,4},{4,6},{6,7},{7,5},{5,3},{3,1},{1,0},{8,10},{10,12},{12... | collective-permute-start | bytes 3145736 | tf_op jit(solution)/shard_map/ppermute | solution.py:77
  65.0 59.9 %collective-permute-start.2 = (bf16[256,2048]{1,0:T(8,128)(2,1)}, bf16[256,2048]{1,0:T(8,128)(2,1)S(1)}, u32[]{:S(2)}, u32[]{:S(2)}) collective-permute-start(bf16[256,2048]{1,0:T(8,128)(2,1)} %collective-permute-done.1), channel_id=1, source_target_pairs={{0,2},{2,4},{4,6},{6,7},{7,5},{5,3},{3,1},{1,0},{8,10},{10,12},{12... | collective-permute-start | bytes 3145736 | tf_op jit(solution)/shard_map/ppermute | solution.py:77
  125.0 37.2 %copy-start.7 = (bf16[256,2048]{1,0:T(8,128)(2,1)}, bf16[256,2048]{1,0:T(8,128)(2,1)S(1)}, u32[]{:S(2)}) copy-start(bf16[256,2048]{1,0:T(8,128)(2,1)S(1)} %collective-permute-done.2) | copy-start | bytes 3145732
  125.0 21.3 %collective-permute-start.3 = (bf16[256,2048]{1,0:T(8,128)(2,1)S(1)}, bf16[256,2048]{1,0:T(8,128)(2,1)S(1)}, u32[]{:S(2)}, u32[]{:S(2)}) collective-permute-start(bf16[256,2048]{1,0:T(8,128)(2,1)S(1)} %collective-permute-done.2), channel_id=1, source_target_pairs={{0,2},{2,4},{4,6},{6,7},{7,5},{5,3},{3,1},{1,0},{8,10},{10,12},{12... | collective-permute-start | bytes 3145736 | tf_op jit(solution)/shard_map/ppermute | solution.py:77
  146.3 1.0 copy-start.6
  147.3 14.9 %collective-permute-start.4 = (bf16[256,2048]{1,0:T(8,128)(2,1)S(1)}, bf16[256,2048]{1,0:T(8,128)(2,1)}, u32[]{:S(2)}, u32[]{:S(2)}) collective-permute-start(bf16[256,2048]{1,0:T(8,128)(2,1)S(1)} %collective-permute-done.3), channel_id=1, source_target_pairs={{0,2},{2,4},{4,6},{6,7},{7,5},{5,3},{3,1},{1,0},{8,10},{10,12},{12... | collective-permute-start | bytes 3145736 | tf_op jit(solution)/shard_map/ppermute | solution.py:77
  162.2 24.2 %collective-permute-start.5 = (bf16[256,2048]{1,0:T(8,128)(2,1)}, bf16[256,2048]{1,0:T(8,128)(2,1)}, u32[]{:S(2)}, u32[]{:S(2)}) collective-permute-start(bf16[256,2048]{1,0:T(8,128)(2,1)} %collective-permute-done.4), channel_id=1, source_target_pairs={{0,2},{2,4},{4,6},{6,7},{7,5},{5,3},{3,1},{1,0},{8,10},{10,12},{12... | collective-permute-start | bytes 3145736 | tf_op jit(solution)/shard_map/ppermute | solution.py:77
  166.3 15.8 %all-to-all-start = ((f32[4,128,512]{2,1,0:T(8,128)}), f32[4,128,512]{2,1,0:T(8,128)S(1)}, u32[]{:S(2)}, u32[]{:S(2)}) async-start(f32[4,128,512]{2,1,0:T(8,128)} %fusion.3), calls=%async_computation | async-start | bytes 2097152 | tf_op jit(solution)/shard_map/all_to_all | solution.py:83
  182.1 8.7 %copy-start.1 = (f32[4,128,512]{2,1,0:T(8,128)}, f32[4,128,512]{2,1,0:T(8,128)S(1)}, u32[]{:S(2)}) copy-start(f32[4,128,512]{2,1,0:T(8,128)S(1)} %all-to-all-done) | copy-start | bytes 3145732
  182.1 17.4 %all-to-all-start.1 = ((f32[4,128,512]{2,1,0:T(8,128)}), f32[4,128,512]{2,1,0:T(8,128)}, u32[]{:S(2)}, u32[]{:S(2)}) async-start(f32[4,128,512]{2,1,0:T(8,128)} %fusion.6), calls=%async_computation.1 | async-start | bytes 2097152 | tf_op jit(solution)/shard_map/all_to_all | solution.py:83
  186.4 16.7 %collective-permute-start.6 = (bf16[256,2048]{1,0:T(8,128)(2,1)}, bf16[256,2048]{1,0:T(8,128)(2,1)}, u32[]{:S(2)}, u32[]{:S(2)}) collective-permute-start(bf16[256,2048]{1,0:T(8,128)(2,1)} %collective-permute-done.5), channel_id=1, source_target_pairs={{0,2},{2,4},{4,6},{6,7},{7,5},{5,3},{3,1},{1,0},{8,10},{10,12},{12... | collective-permute-start | bytes 3145736 | tf_op jit(solution)/shard_map/ppermute | solution.py:77
  199.5 16.6 %all-to-all-start.2 = ((f32[4,128,512]{2,1,0:T(8,128)}), f32[4,128,512]{2,1,0:T(8,128)S(1)}, u32[]{:S(2)}, u32[]{:S(2)}) async-start(f32[4,128,512]{2,1,0:T(8,128)} %fusion.9), calls=%async_computation.2 | async-start | bytes 2097152 | tf_op jit(solution)/shard_map/all_to_all | solution.py:83
  207.5 13.2 %copy-start.3 = (s32[128,2]{0,1:T(2,128)S(1)}, s32[128,2]{0,1:T(2,128)}, u32[]{:S(2)}) copy-start(s32[128,2]{0,1:T(2,128)} %param.8) | copy-start | bytes 3076
  207.5 13.5 %copy-start.8 = (s32[8]{0:T(128)S(1)}, s32[8]{0:T(128)}, u32[]{:S(2)}) copy-start(s32[8]{0:T(128)} %constant.104.clone) | copy-start | bytes 100
  207.5 14.1 %copy-start.4 = (s32[8]{0:T(128)S(1)}, s32[8]{0:T(128)}, u32[]{:S(2)}) copy-start(s32[8]{0:T(128)} %constant.107) | copy-start | bytes 100
  216.1 4.7 %copy-start.2 = (f32[4,128,512]{2,1,0:T(8,128)}, f32[4,128,512]{2,1,0:T(8,128)S(1)}, u32[]{:S(2)}) copy-start(f32[4,128,512]{2,1,0:T(8,128)S(1)} %all-to-all-done.2) | copy-start | bytes 3145732
  216.1 17.4 %all-to-all-start.3 = ((f32[4,128,512]{2,1,0:T(8,128)}), f32[4,128,512]{2,1,0:T(8,128)}, u32[]{:S(2)}, u32[]{:S(2)}) async-start(f32[4,128,512]{2,1,0:T(8,128)} %fusion.12), calls=%async_computation.3 | async-start | bytes 2097152 | tf_op jit(solution)/shard_map/all_to_all | solution.py:83
Sparse Core Ops, SparseCore 0:
  45.9 97.6 reduce-scatter.1

commit v7 on v2

--- a/solution.py
+++ b/solution.py
@@ -27,6 +27,12 @@
 SWAP = [(0, 1), (1, 0)]
 
 
+def flood_pairs(n_z, t):
+    up = [(z * CORES, (z + 1) * CORES) for z in range(t - 1, n_z - 1)]
+    down = [(z * CORES + 1, (z - 1) * CORES + 1) for z in range(1, n_z - t + 1)]
+    return up + down
+
+
 def shards(routes, expert_inputs, hidden_grad, weight, moment_one, moment_two):
     n_expert = lax.axis_size("expert")
     n_z = lax.axis_size("z")
@@ -38,6 +44,7 @@
     tok_count = routes.shape[0]
     top_count = routes.shape[1]
     me_c = lax.axis_index("core")
+    me_z = lax.axis_index("z")
     flat_routes = routes.reshape(-1)
     onehot = (flat_routes[:, None] == jnp.arange(experts, dtype=jnp.int32)[None, :]).astype(
         jnp.int32
@@ -55,20 +62,32 @@
     masked = jnp.where(valid[:, None], grad_flat, jnp.zeros_like(grad_flat))
 
     wbf = weight.astype(jnp.bfloat16)
-    w_mine = lax.all_gather(wbf, "z", axis=0, tiled=True)
-    w_other = lax.ppermute(w_mine, "core", SWAP)
-    w_rel = jnp.concatenate([w_mine, w_other], axis=0)
-    partial_rows = lax.dot_general(
-        masked, w_rel, (((1,), (1,)), ((), ())), preferred_element_type=jnp.float32
+    partner = lax.ppermute(wbf, "core", SWAP)
+    chip_w = jnp.where(
+        me_c == 0, jnp.concatenate([wbf, partner], axis=0), jnp.concatenate([partner, wbf], axis=0)
     )
+    held = []
+    cur = chip_w
+    for t in range(1, n_z):
+        cur = lax.ppermute(cur, DP, flood_pairs(n_z, t))
+        held.append(cur)
+    own_held = jnp.stack(held)
+    other_held = lax.ppermute(own_held, "core", SWAP)
+    down_side = jnp.where(me_c == 0, own_held, other_held)
+    up_side = jnp.where(me_c == 0, other_held, own_held)
+    parts = [chip_w]
+    for r in range(1, n_z):
+        parts.append(jnp.where(me_z + r < n_z, up_side[r - 1], down_side[n_z - r - 1]))
+    w_rel = jnp.concatenate(parts, axis=0)
+    cols = (((1,), (1,)), ((), ()))
+    partial_rows = lax.dot_general(masked, w_rel, cols, preferred_element_type=jnp.float32)
     sent = partial_rows.reshape(n_expert, capacity, width)
     received = lax.all_to_all(sent, "expert", split_axis=0, concat_axis=0, tiled=True)
     paired = jnp.sum(received.reshape(experts, 2, capacity, width), axis=1).astype(jnp.bfloat16)
     picked = paired[routes, slots]
     token_rel = jnp.sum(picked.astype(jnp.float32), axis=1).astype(jnp.bfloat16)
-    split = token_rel.reshape(tok_count, CORES, n_z, rows)
-    split = jnp.where(me_c == 0, split, split[:, ::-1])
-    token_grad = jnp.transpose(split, (0, 2, 1, 3)).reshape(tok_count, width)
+    token_grad = jnp.roll(token_rel.reshape(tok_count, n_z, CORES * rows), me_z, axis=1)
+    token_grad = token_grad.reshape(tok_count, width)
 
     by_class = inputs_flat.reshape(slot_rows, n_z, CORES, rows)
     in_mine = lax.dynamic_index_in_dim(by_class, me_c, axis=2, keepdims=False)
@@ -82,7 +101,9 @@
         in_mine.reshape(slot_rows, n_z * rows), masked, dims, preferred_element_type=jnp.float32
     )
     chip = (g_mine + g_recv.astype(jnp.float32)).astype(jnp.bfloat16)
-    owned = lax.psum_scatter(chip, "z", scatter_dimension=0, tiled=True).astype(jnp.float32)
+    owned = lax.psum_scatter(chip, "z", scatter_dimension=0, tiled=True)
+    token_grad, owned = lax.optimization_barrier((token_grad, owned))
+    owned = owned.astype(jnp.float32)
     new_weight, new_first, new_second = adamw(weight, moment_one, moment_two, owned / loss_scale)
     return (token_grad, new_weight, new_first, new_second)
 

time: 294 us -> 212 us (0.72); the launches traced: 289 us -> 211 us
  waiting for transfers between devices: 218 us -> 119 us
  other arithmetic: 13.7 us -> 30.5 us
  starting transfers between devices: 5.38 us -> 9.07 us
    all_gather x1 -> x0, waiting for transfers between devices: 79.4 us -> none  [shards(): w_mine = lax.all_gather(wbf, 'z', axis=0, tiled=True)]
    reduce_scatter x1, waiting for transfers between devices: 76.1 us -> 0.01 us  [shards(): owned = lax.psum_scatter(chip, 'z', scatter_dimension=0, tiled=True)]
    ppermute x1 -> x5, waiting for transfers between devices: 7.31 us -> 71.3 us  [the longest x3 62.6 us: shards(): cur = lax.ppermute(cur, DP, flood_pairs(n_z, t))]
    select_n x0 -> x3, other arithmetic: none -> 8.21 us  [the longest x1 5.42 us: shards(): up_side = jnp.where(me_c == 0, other_held, own_held)]
    ppermute x1, waiting for transfers between devices: 7.15 us -> 0.01 us  [shards(): g_recv = lax.ppermute(g_other.astype(jnp.bfloat16), 'core', SWAP)]
    another operation x2 -> x3, other arithmetic: 0.8 us -> 6.29 us  [the longest x1 5.49 us: shards(): own_held = jnp.stack(held)]
    ppermute x1 -> x5, starting transfers between devices: 0.05 us -> 3.93 us  [the longest x3 3.85 us: shards(): cur = lax.ppermute(cur, DP, flood_pairs(n_z, t))]
    unnamed x12 -> x22, local copies, waits for them, and re-layouts: 7.5 us -> 7.52 us
  transfers between devices with their start and end apart: 5 -> 8, of which waited for: 5 -> 6; matrix products, arithmetic and copies ran while one was open for 0% -> 23% of each run, Pallas kernels for 0% -> 0%
where the time goes in v7:
time: 212 us; the launch traced here: 211 us
  waiting for transfers between devices  119 us (56%)
  other arithmetic  30.5 us (14%)
  matrix products  15.6 us (7%)
  local copies, waits for them, and re-layouts  15.2 us (7%)
  between operations  15 us (7%)
  starting transfers between devices  9.07 us (4%)
  blocking collectives  7.37 us (3%)
    ppermute x3, waiting for transfers between devices, shards(): cur = lax.ppermute(cur, DP, flood_pairs(n_z, t))  62.6 us
    all_to_all x1, waiting for transfers between devices, shards(): lax.all_to_all(sent, 'expert', split_axis=0, concat_axis=0, tiled=True)  47.3 us
    dot_general x1, matrix products, shards(): lax.dot_general(masked, w_rel, cols, preferred_element_type=jnp.float32)  8.81 us
    unnamed x22, local copies, waits for them, and re-layouts  7.52 us
    unnamed x1, blocking collectives  7.37 us
    sub x1, other arithmetic, adamw(): new_weight = weight - learn_rate * (update + decay * weight)  6.42 us
    ppermute x1, waiting for transfers between devices, shards(): other_held = lax.ppermute(own_held, 'core', SWAP)  6.06 us
    another operation x1, other arithmetic, shards(): own_held = jnp.stack(held)  5.49 us
  transfers between devices with their start and end apart: 8, of which 6 were waited for; matrix products, arithmetic and copies ran while one was open for 23% of the time, Pallas kernels for 0%

profile of v7, /device:TPU:24, one launch (start us, length us, event | category | flops | bytes accessed | tf_op | source)
XLA Modules:
  0.0 211.5 jit_solution(13289101300875547026)
XLA Ops:
  7.2 1.7 convert_element_type.28
  9.1 2.6 %collective-permute-done = bf16[256,2048]{1,0:T(8,128)(2,1)S(1)} collective-permute-done((bf16[256,2048]{1,0:T(8,128)(2,1)S(1)}, bf16[256,2048]{1,0:T(8,128)(2,1)S(1)}, u32[]{:S(2)}, u32[]{:S(2)}) %collective-permute-start) | collective-permute-done | bytes 1048608 | tf_op jit(solution)/shard_map/ppermute | solution.py:65
  11.7 1.0 maximum_select_fusion
  12.7 1.3 collective-permute-start.1
  14.0 26.6 %collective-permute-done.1 = bf16[512,2048]{1,0:T(8,128)(2,1)S(1)} collective-permute-done((bf16[512,2048]{1,0:T(8,128)(2,1)S(1)}, bf16[512,2048]{1,0:T(8,128)(2,1)S(1)}, u32[]{:S(2)}, u32[]{:S(2)}) %collective-permute-start.1) | collective-permute-done | bytes 2097184 | tf_op jit(solution)/shard_map/ppermute | solution.py:72
  40.6 1.3 copy-done.1
  41.9 1.3 collective-permute-start.2
  43.2 26.7 %collective-permute-done.2 = bf16[512,2048]{1,0:T(8,128)(2,1)} collective-permute-done((bf16[512,2048]{1,0:T(8,128)(2,1)S(1)}, bf16[512,2048]{1,0:T(8,128)(2,1)}, u32[]{:S(2)}, u32[]{:S(2)}) %collective-permute-start.2) | collective-permute-done | bytes 2097184 | tf_op jit(solution)/shard_map/ppermute | solution.py:72
  69.9 1.3 collective-permute-start.3
  71.6 0.6 reduce-window.6
  72.7 0.6 dynamic-slice
  74.3 7.4 %all-reduce = s32[8]{0:T(128)S(1)} all-reduce(s32[8]{0:T(128)S(1)} %dynamic-update-slice), channel_id=2, replica_groups=mesh['expert'=4,'z'=4,'core'=2] {'expert'}, use_global_device_ids=true, to_apply=%add | all-reduce | flops 8 | bytes 64
  81.8 2.9 %copy.31 = bf16[1,1,512,2048]{2,3,1,0:T(8,128)(2,1)S(1)} copy(bf16[1,1,512,2048]{3,2,1,0:T(8,128)(2,1)} %param.7) | data formatting | bytes 4194304 | tf_op args[1]
  85.1 1.3 copy-done.6
  86.4 2.4 %convolution_convert_fusion = bf16[1024,2048]{1,0:T(8,128)(2,1)S(1)} fusion(bf16[512,1024]{0,1:T(8,128)(2,1)S(1)} %bitcast.58, bf16[1,1,512,2048]{3,2,1,0:T(8,128)(2,1)S(1)} %copy-done.6, pred[512]{0:T(512)(128)(4,1)S(1)} %get-tuple-element.20), kind=kOutput, calls=%fused_computation.14 | convolution fusion | flops 2150629376 | bytes 7340544 | tf_op jit(solution)/shard_map/dot_general | solution.py:96
  88.9 9.3 %collective-permute-done.3 = bf16[512,2048]{1,0:T(8,128)(2,1)} collective-permute-done((bf16[512,2048]{1,0:T(8,128)(2,1)}, bf16[512,2048]{1,0:T(8,128)(2,1)}, u32[]{:S(2)}, u32[]{:S(2)}) %collective-permute-start.3) | collective-permute-done | bytes 2097184 | tf_op jit(solution)/shard_map/ppermute | solution.py:72
  98.2 5.5 %pad_maximum_fusion = bf16[3,512,2048]{2,1,0:T(8,128)(2,1)} fusion(bf16[1,512,2048]{2,1,0:T(8,128)(2,1)} %bitcast.4, bf16[1,512,2048]{2,1,0:T(8,128)(2,1)} %bitcast.3, bf16[1,512,2048]{2,1,0:T(8,128)(2,1)S(1)} %bitcast.54), kind=kLoop, calls=%fused_computation.10 | loop fusion | flops 6291456 | bytes 12582912 | tf_op jit(solution)/shard_map/stack | solution.py:74
  103.7 4.4 %add_convert_fusion = bf16[1024,2048]{1,0:T(8,128)(2,1)} fusion(bf16[1024,2048]{1,0:T(8,128)(2,1)S(1)} %collective-permute-done.5, bf16[512,1024]{0,1:T(8,128)(2,1)S(1)} %bitcast.57, bf16[1,1,512,2048]{3,2,1,0:T(8,128)(2,1)S(1)} %copy-done.6, pred[512]{0:T(512)(128)(4,1)S(1)} %get-tuple-element.20), kind=kOutput, calls=%fused_computation.9 | convolution fusion | flops 2154823680 | bytes 11534848 | tf_op jit(solution)/shard_map/dot_general | solution.py:100
  108.1 6.1 %collective-permute-done.4 = bf16[3,512,2048]{2,1,0:T(8,128)(2,1)} collective-permute-done((bf16[3,512,2048]{2,1,0:T(8,128)(2,1)}, bf16[3,512,2048]{2,1,0:T(8,128)(2,1)}, u32[]{:S(2)}, u32[]{:S(2)}) %collective-permute-start.4) | collective-permute-done | bytes 6291488 | tf_op jit(solution)/shard_map/ppermute | solution.py:75
  114.2 5.4 %broadcast_select_fusion.1 = (bf16[3,512,2048]{2,1,0:T(8,128)(2,1)S(1)}, bf16[3,512,2048]{2,1,0:T(8,128)(2,1)S(1)}) fusion(bf16[3,512,2048]{2,1,0:T(8,128)(2,1)} %collective-permute-done.4, pred[]{:T(512)S(6)} %eq.50, bf16[1,512,2048]{2,1,0:T(8,128)(2,1)} %bitcast.4, bf16[1,512,2048]{2,1,0:T(8,128)(2,1)} %bitcast.3, bf16[1,512,2048]{2,1,0:T(8,128)(2,1)S(1)} %bitcast.55), kind=kLoop, calls=%fused_computation.12 | loop fusion | flops 12582912 | bytes 25165824 | tf_op jit(solution)/shard_map/jit(_where)/select_n | solution.py:77
  119.6 1.8 fusion.12
  121.6 8.8 %fusion = f32[4,128,2048]{2,1,0:T(8,128)} fusion(bf16[512,2048]{1,0:T(8,128)(2,1)S(1)} %get-tuple-element.14, bf16[512,2048]{1,0:T(8,128)(2,1)} %get-tuple-element.15, bf16[512,2048]{1,0:T(8,128)(2,1)S(1)} %get-tuple-element.13, bf16[512,2048]{1,0:T(8,128)(2,1)S(1)} %copy-done.4, bf16[4,128,2048]{2,1,0:T(8,128)(2,1)} %bitcast.61, ...), kind=kOutput, calls=%fused_computation.2 | convolution fusion | flops 4329570304 | bytes 14680576 | tf_op jit(solution)/shard_map/dot_general | solution.py:83
  130.4 5.0 %all-to-all-start = ((f32[4,128,2048]{2,1,0:T(8,128)}), f32[4,128,2048]{2,1,0:T(8,128)}, u32[]{:S(2)}, u32[]{:S(2)}) async-start(f32[4,128,2048]{2,1,0:T(8,128)} %fusion), calls=%async_computation | async-start | bytes 8388608 | tf_op jit(solution)/shard_map/all_to_all | solution.py:85
  136.0 47.3 %all-to-all-done = f32[4,128,2048]{2,1,0:T(8,128)} async-done(((f32[4,128,2048]{2,1,0:T(8,128)}), f32[4,128,2048]{2,1,0:T(8,128)}, u32[]{:S(2)}, u32[]{:S(2)}) %all-to-all-start) | async-done | bytes 4194336 | tf_op jit(solution)/shard_map/all_to_all | solution.py:85
  183.3 2.8 %bitcast_reduce_fusion = bf16[2,128,2048]{2,1,0:T(8,128)(2,1)S(1)} fusion(f32[4,128,2048]{2,1,0:T(8,128)} %all-to-all-done), kind=kLoop, calls=%fused_computation.13 | loop fusion | flops 524288 | bytes 5242880 | tf_op jit(solution)/shard_map/reduce_sum | solution.py:86
  186.1 4.3 %gather_fusion = bf16[256,2048]{1,0:T(8,128)(2,1)S(1)} fusion(bf16[2,128,2048]{2,1,0:T(8,128)(2,1)S(1)} %bitcast_reduce_fusion, s32[256]{0:T(256)S(1)} %reshape.136), kind=kCustom, calls=%fused_computation | custom fusion | bytes 2099200 | tf_op jit(solution)/shard_map/gather | solution.py:87
  190.4 0.7 reshape.139
  191.2 3.7 %reduce_sum.52 = bf16[128,2048]{1,0:T(8,128)(2,1)} reduce(bf16[128,2,2048]{2,1,0:T(2,128)(2,1)S(1)} %reshape.139, bf16[]{:T(256)} %constant.79.clone.1), dimensions={1}, to_apply=%region_6.7 | reduce | flops 262144 | bytes 1572866 | tf_op jit(solution)/shard_map/reduce_sum | solution.py:88
  194.9 1.4 reshape.132
  196.3 1.0 fusion.21
  197.3 0.9 copy.33
  198.2 6.4 %multiply_subtract_fusion = (f32[256,2048]{1,0:T(8,128)}, f32[256,2048]{1,0:T(8,128)}, f32[256,2048]{1,0:T(8,128)}) fusion(f32[256,2048]{1,0:T(8,128)S(1)} %copy-done, bf16[256,2048]{1,0:T(8,128)(2,1)} %reduce-scatter.2.cloned.1.call-done, f32[256,2048]{1,0:T(8,128)} %param.10, f32[256,2048]{1,0:T(8,128)} %param.11), kind=kLoop, calls=%fused_computation.31 | loop fusion | flops 8912896 | bytes 13631488 | tf_op jit(solution)/shard_map/sub | solution.py:23
  (41 shorter events, 2.6 us)
Async XLA Ops:
  7.2 191.1 %reduce-scatter.2.cloned.1.call-start = ((), (), s32[]{:S(2)}) async-start(), calls=%async_computation.2 | async-start | bytes 5242880 | tf_op jit(solution)/shard_map/reduce_scatter | solution.py:104
  8.9 2.7 %collective-permute-start = (bf16[256,2048]{1,0:T(8,128)(2,1)S(1)}, bf16[256,2048]{1,0:T(8,128)(2,1)S(1)}, u32[]{:S(2)}, u32[]{:S(2)}) collective-permute-start(bf16[256,2048]{1,0:T(8,128)(2,1)S(1)} %convert_element_type.28), channel_id=1, source_target_pairs={{0,1},{1,0},{2,3},{3,2},{4,5},{5,4},{6,7},{7,6},{8,9},{9,8},{10,11... | collective-permute-start | bytes 3145736 | tf_op jit(solution)/shard_map/ppermute | solution.py:65
  9.0 62.2 %copy-start.5 = (s32[128,2]{0,1:T(2,128)S(1)}, s32[128,2]{0,1:T(2,128)}, u32[]{:S(2)}) copy-start(s32[128,2]{0,1:T(2,128)} %param.6) | copy-start | bytes 3076
  9.0 63.6 %copy-start.7 = (u32[32]{0:T(128)S(1)}, u32[32]{0:T(128)}, u32[]{:S(2)}) copy-start(u32[32]{0:T(128)} %constant.114) | copy-start | bytes 388
  12.7 57.3 %copy-start.3 = (bf16[512,2048]{1,0:T(8,128)(2,1)}, bf16[512,2048]{1,0:T(8,128)(2,1)S(1)}, u32[]{:S(2)}) copy-start(bf16[512,2048]{1,0:T(8,128)(2,1)S(1)} %maximum_select_fusion) | copy-start | bytes 6291460
  12.7 27.9 %collective-permute-start.1 = (bf16[512,2048]{1,0:T(8,128)(2,1)S(1)}, bf16[512,2048]{1,0:T(8,128)(2,1)S(1)}, u32[]{:S(2)}, u32[]{:S(2)}) collective-permute-start(bf16[512,2048]{1,0:T(8,128)(2,1)S(1)} %maximum_select_fusion), channel_id=1, source_target_pairs={{0,2},{2,4},{4,6},{3,1},{5,3},{7,5},{8,10},{10,12},{12,14},{11,9},... | collective-permute-start | bytes 6291464 | tf_op jit(solution)/shard_map/ppermute | solution.py:72
  40.6 1.3 copy-start.1
  41.9 28.0 %collective-permute-start.2 = (bf16[512,2048]{1,0:T(8,128)(2,1)S(1)}, bf16[512,2048]{1,0:T(8,128)(2,1)}, u32[]{:S(2)}, u32[]{:S(2)}) collective-permute-start(bf16[512,2048]{1,0:T(8,128)(2,1)S(1)} %collective-permute-done.1), channel_id=1, source_target_pairs={{2,4},{4,6},{3,1},{5,3},{10,12},{12,14},{11,9},{13,11},{18,20},{20... | collective-permute-start | bytes 6291464 | tf_op jit(solution)/shard_map/ppermute | solution.py:72
  69.9 28.2 %collective-permute-start.3 = (bf16[512,2048]{1,0:T(8,128)(2,1)}, bf16[512,2048]{1,0:T(8,128)(2,1)}, u32[]{:S(2)}, u32[]{:S(2)}) collective-permute-start(bf16[512,2048]{1,0:T(8,128)(2,1)} %collective-permute-done.2), channel_id=1, source_target_pairs={{4,6},{3,1},{12,14},{11,9},{20,22},{19,17},{28,30},{27,25}} | collective-permute-start | bytes 6291464 | tf_op jit(solution)/shard_map/ppermute | solution.py:72
  84.8 1.6 copy-start.6
  86.4 11.8 %copy-start.2 = (bf16[512,2048]{1,0:T(8,128)(2,1)S(1)}, bf16[512,2048]{1,0:T(8,128)(2,1)}, u32[]{:S(2)}) copy-start(bf16[512,2048]{1,0:T(8,128)(2,1)} %copy-done.1) | copy-start | bytes 6291460
  88.8 14.8 %collective-permute-start.5 = (bf16[1024,2048]{1,0:T(8,128)(2,1)S(1)}, bf16[1024,2048]{1,0:T(8,128)(2,1)S(1)}, u32[]{:S(2)}, u32[]{:S(2)}) collective-permute-start(bf16[1024,2048]{1,0:T(8,128)(2,1)S(1)} %convolution_convert_fusion), channel_id=1, source_target_pairs={{0,1},{1,0},{2,3},{3,2},{4,5},{5,4},{6,7},{7,6},{8,9},{9,8},{10,11... | collective-permute-start | bytes 12582920 | tf_op jit(solution)/shard_map/ppermute | solution.py:99
  103.7 10.5 %collective-permute-start.4 = (bf16[3,512,2048]{2,1,0:T(8,128)(2,1)}, bf16[3,512,2048]{2,1,0:T(8,128)(2,1)}, u32[]{:S(2)}, u32[]{:S(2)}) collective-permute-start(bf16[3,512,2048]{2,1,0:T(8,128)(2,1)} %pad_maximum_fusion), channel_id=1, source_target_pairs={{0,1},{1,0},{2,3},{3,2},{4,5},{5,4},{6,7},{7,6},{8,9},{9,8},{10,11... | collective-permute-start | bytes 18874376 | tf_op jit(solution)/shard_map/ppermute | solution.py:75
  119.6 2.0 copy-start.4
  130.4 52.9 %all-to-all-start = ((f32[4,128,2048]{2,1,0:T(8,128)}), f32[4,128,2048]{2,1,0:T(8,128)}, u32[]{:S(2)}, u32[]{:S(2)}) async-start(f32[4,128,2048]{2,1,0:T(8,128)} %fusion), calls=%async_computation | async-start | bytes 8388608 | tf_op jit(solution)/shard_map/all_to_all | solution.py:85
  191.2 7.1 %copy-start = (f32[256,2048]{1,0:T(8,128)S(1)}, f32[256,2048]{1,0:T(8,128)}, u32[]{:S(2)}) copy-start(f32[256,2048]{1,0:T(8,128)} %param.9) | copy-start | bytes 6291460
Sparse Core Ops, SparseCore 0:
  108.2 77.1 reduce-scatter.1

commit v8 on v7

--- a/solution.py
+++ b/solution.py
@@ -84,8 +84,13 @@
     sent = partial_rows.reshape(n_expert, capacity, width)
     received = lax.all_to_all(sent, "expert", split_axis=0, concat_axis=0, tiled=True)
     paired = jnp.sum(received.reshape(experts, 2, capacity, width), axis=1).astype(jnp.bfloat16)
-    picked = paired[routes, slots]
-    token_rel = jnp.sum(picked.astype(jnp.float32), axis=1).astype(jnp.bfloat16)
+    target = (routes * capacity + slots).reshape(tok_count, top_count, 1)
+    choose = jnp.sum(
+        (target == jnp.arange(experts * capacity, dtype=jnp.int32)).astype(jnp.int32), axis=1
+    ).astype(jnp.bfloat16)
+    token_rel = jnp.dot(
+        choose, paired.reshape(experts * capacity, width), preferred_element_type=jnp.float32
+    ).astype(jnp.bfloat16)
     token_grad = jnp.roll(token_rel.reshape(tok_count, n_z, CORES * rows), me_z, axis=1)
     token_grad = token_grad.reshape(tok_count, width)
 

time: 212 us -> 203 us (0.958)
  local copies, waits for them, and re-layouts: 15.2 us -> 8.89 us
  other arithmetic: 30.5 us -> 26.9 us
    gather x2 -> x0, local copies, waits for them, and re-layouts: 5.04 us -> none  [shards(): picked = paired[routes, slots]]
    reduce_sum x1, other arithmetic: 3.74 us -> 0.13 us  [shards(): jnp.sum((target == jnp.arange(experts * capacity, dtype=jnp.int32)).astyp...]
  transfers between devices with their start and end apart: 8 -> 8, of which waited for: 6 -> 6; matrix products, arithmetic and copies ran while one was open for 23% -> 20% of each run, Pallas kernels for 0% -> 0%
where the time goes in v8:
time: 203 us; the launch traced here: 202 us
  waiting for transfers between devices  119 us (59%)
  other arithmetic  26.9 us (13%)
  matrix products  15.9 us (8%)
  between operations  14.9 us (7%)
  starting transfers between devices  9.07 us (4%)
  local copies, waits for them, and re-layouts  8.89 us (4%)
  blocking collectives  7.37 us (4%)
    ppermute x3, waiting for transfers between devices, shards(): cur = lax.ppermute(cur, DP, flood_pairs(n_z, t))  62.6 us
    all_to_all x1, waiting for transfers between devices, shards(): lax.all_to_all(sent, 'expert', split_axis=0, concat_axis=0, tiled=True)  47.5 us
    dot_general x1, matrix products, shards(): lax.dot_general(masked, w_rel, cols, preferred_element_type=jnp.float32)  8.81 us
    unnamed x22, local copies, waits for them, and re-layouts  7.52 us
    unnamed x1, blocking collectives  7.37 us
    sub x1, other arithmetic, adamw(): new_weight = weight - learn_rate * (update + decay * weight)  6.42 us
    ppermute x1, waiting for transfers between devices, shards(): other_held = lax.ppermute(own_held, 'core', SWAP)  6.06 us
    another operation x1, other arithmetic, shards(): own_held = jnp.stack(held)  5.49 us
  transfers between devices with their start and end apart: 8, of which 6 were waited for; matrix products, arithmetic and copies ran while one was open for 20% of the time, Pallas kernels for 0%

profile of v8, /device:TPU:24, one launch (start us, length us, event | category | flops | bytes accessed | tf_op | source)
XLA Modules:
  0.0 202.0 jit_solution(17847128010941175234)
XLA Ops:
  7.2 1.7 convert_element_type.42
  9.1 2.6 %collective-permute-done = bf16[256,2048]{1,0:T(8,128)(2,1)S(1)} collective-permute-done((bf16[256,2048]{1,0:T(8,128)(2,1)S(1)}, bf16[256,2048]{1,0:T(8,128)(2,1)S(1)}, u32[]{:S(2)}, u32[]{:S(2)}) %collective-permute-start) | collective-permute-done | bytes 1048608 | tf_op jit(solution)/shard_map/ppermute | solution.py:65
  11.7 1.0 maximum_select_fusion
  12.7 1.3 collective-permute-start.1
  14.0 26.6 %collective-permute-done.1 = bf16[512,2048]{1,0:T(8,128)(2,1)S(1)} collective-permute-done((bf16[512,2048]{1,0:T(8,128)(2,1)S(1)}, bf16[512,2048]{1,0:T(8,128)(2,1)S(1)}, u32[]{:S(2)}, u32[]{:S(2)}) %collective-permute-start.1) | collective-permute-done | bytes 2097184 | tf_op jit(solution)/shard_map/ppermute | solution.py:72
  40.6 1.3 copy-done.1
  41.9 1.3 collective-permute-start.2
  43.2 26.7 %collective-permute-done.2 = bf16[512,2048]{1,0:T(8,128)(2,1)} collective-permute-done((bf16[512,2048]{1,0:T(8,128)(2,1)S(1)}, bf16[512,2048]{1,0:T(8,128)(2,1)}, u32[]{:S(2)}, u32[]{:S(2)}) %collective-permute-start.2) | collective-permute-done | bytes 2097184 | tf_op jit(solution)/shard_map/ppermute | solution.py:72
  69.9 1.3 collective-permute-start.3
  71.6 0.6 reduce-window.6
  72.7 0.6 dynamic-slice
  74.1 0.2 dynamic-update-slice
  74.3 7.4 %all-reduce = s32[8]{0:T(128)S(1)} all-reduce(s32[8]{0:T(128)S(1)} %dynamic-update-slice), channel_id=2, replica_groups=mesh['expert'=4,'z'=4,'core'=2] {'expert'}, use_global_device_ids=true, to_apply=%add | all-reduce | flops 8 | bytes 64
  81.8 2.9 %copy.29 = bf16[1,1,512,2048]{2,3,1,0:T(8,128)(2,1)S(1)} copy(bf16[1,1,512,2048]{3,2,1,0:T(8,128)(2,1)} %param.7) | data formatting | bytes 4194304 | tf_op args[1]
  84.8 0.2 constant_dynamic-slice_fusion.1
  85.1 1.3 copy-done.6
  86.4 2.4 %convolution_convert_fusion = bf16[1024,2048]{1,0:T(8,128)(2,1)S(1)} fusion(bf16[512,1024]{0,1:T(8,128)(2,1)S(1)} %bitcast.55, bf16[1,1,512,2048]{3,2,1,0:T(8,128)(2,1)S(1)} %copy-done.6, pred[512]{0:T(512)(128)(4,1)S(1)} %get-tuple-element.20), kind=kOutput, calls=%fused_computation.13 | convolution fusion | flops 2150629376 | bytes 7340544 | tf_op jit(solution)/shard_map/dot_general | solution.py:101
  88.9 9.3 %collective-permute-done.3 = bf16[512,2048]{1,0:T(8,128)(2,1)} collective-permute-done((bf16[512,2048]{1,0:T(8,128)(2,1)}, bf16[512,2048]{1,0:T(8,128)(2,1)}, u32[]{:S(2)}, u32[]{:S(2)}) %collective-permute-start.3) | collective-permute-done | bytes 2097184 | tf_op jit(solution)/shard_map/ppermute | solution.py:72
  98.2 5.5 %pad_maximum_fusion = bf16[3,512,2048]{2,1,0:T(8,128)(2,1)} fusion(bf16[1,512,2048]{2,1,0:T(8,128)(2,1)} %bitcast.5, bf16[1,512,2048]{2,1,0:T(8,128)(2,1)} %bitcast.4, bf16[1,512,2048]{2,1,0:T(8,128)(2,1)S(1)} %bitcast.50), kind=kLoop, calls=%fused_computation.9 | loop fusion | flops 6291456 | bytes 12582912 | tf_op jit(solution)/shard_map/stack | solution.py:74
  103.7 4.4 %add_convert_fusion = bf16[1024,2048]{1,0:T(8,128)(2,1)} fusion(bf16[1024,2048]{1,0:T(8,128)(2,1)S(1)} %collective-permute-done.5, bf16[512,1024]{0,1:T(8,128)(2,1)S(1)} %bitcast.54, bf16[1,1,512,2048]{3,2,1,0:T(8,128)(2,1)S(1)} %copy-done.6, pred[512]{0:T(512)(128)(4,1)S(1)} %get-tuple-element.20), kind=kOutput, calls=%fused_computation.8 | convolution fusion | flops 2154823680 | bytes 11534848 | tf_op jit(solution)/shard_map/dot_general | solution.py:105
  108.1 6.1 %collective-permute-done.4 = bf16[3,512,2048]{2,1,0:T(8,128)(2,1)} collective-permute-done((bf16[3,512,2048]{2,1,0:T(8,128)(2,1)}, bf16[3,512,2048]{2,1,0:T(8,128)(2,1)}, u32[]{:S(2)}, u32[]{:S(2)}) %collective-permute-start.4) | collective-permute-done | bytes 6291488 | tf_op jit(solution)/shard_map/ppermute | solution.py:75
  114.2 5.4 %broadcast_select_fusion.1 = (bf16[3,512,2048]{2,1,0:T(8,128)(2,1)S(1)}, bf16[3,512,2048]{2,1,0:T(8,128)(2,1)S(1)}) fusion(bf16[3,512,2048]{2,1,0:T(8,128)(2,1)} %collective-permute-done.4, pred[]{:T(512)S(6)} %eq.70, bf16[1,512,2048]{2,1,0:T(8,128)(2,1)} %bitcast.5, bf16[1,512,2048]{2,1,0:T(8,128)(2,1)} %bitcast.4, bf16[1,512,2048]{2,1,0:T(8,128)(2,1)S(1)} %bitcast.51), kind=kLoop, calls=%fused_computation.11 | loop fusion | flops 12582912 | bytes 25165824 | tf_op jit(solution)/shard_map/jit(_where)/select_n | solution.py:77
  119.6 1.8 fusion.12
  121.6 8.8 %fusion = f32[4,128,2048]{2,1,0:T(8,128)} fusion(bf16[512,2048]{1,0:T(8,128)(2,1)S(1)} %get-tuple-element.14, bf16[512,2048]{1,0:T(8,128)(2,1)} %get-tuple-element.15, bf16[512,2048]{1,0:T(8,128)(2,1)S(1)} %get-tuple-element.13, bf16[512,2048]{1,0:T(8,128)(2,1)S(1)} %copy-done.4, bf16[4,128,2048]{2,1,0:T(8,128)(2,1)} %bitcast.58, ...), kind=kOutput, calls=%fused_computation.1 | convolution fusion | flops 4329570304 | bytes 14680576 | tf_op jit(solution)/shard_map/dot_general | solution.py:83
  130.4 5.0 %all-to-all-start = ((f32[4,128,2048]{2,1,0:T(8,128)}), f32[4,128,2048]{2,1,0:T(8,128)}, u32[]{:S(2)}, u32[]{:S(2)}) async-start(f32[4,128,2048]{2,1,0:T(8,128)} %fusion), calls=%async_computation | async-start | bytes 8388608 | tf_op jit(solution)/shard_map/all_to_all | solution.py:85
  135.8 47.5 %all-to-all-done = f32[4,128,2048]{2,1,0:T(8,128)} async-done(((f32[4,128,2048]{2,1,0:T(8,128)}), f32[4,128,2048]{2,1,0:T(8,128)}, u32[]{:S(2)}, u32[]{:S(2)}) %all-to-all-start) | async-done | bytes 4194336 | tf_op jit(solution)/shard_map/all_to_all | solution.py:85
  183.3 2.8 %bitcast_reduce_fusion = bf16[2,128,2048]{2,1,0:T(8,128)(2,1)S(1)} fusion(f32[4,128,2048]{2,1,0:T(8,128)} %all-to-all-done), kind=kLoop, calls=%fused_computation.12 | loop fusion | flops 524288 | bytes 5242880 | tf_op jit(solution)/shard_map/reduce_sum | solution.py:86
  186.1 0.3 convolution_convert_fusion.1
  186.4 0.4 reshape.109
  186.8 1.0 fusion.21
  187.8 0.9 copy.31
  188.7 6.4 %multiply_subtract_fusion = (f32[256,2048]{1,0:T(8,128)}, f32[256,2048]{1,0:T(8,128)}, f32[256,2048]{1,0:T(8,128)}) fusion(f32[256,2048]{1,0:T(8,128)S(1)} %copy-done, bf16[256,2048]{1,0:T(8,128)(2,1)} %reduce-scatter.2.cloned.1.call-done, f32[256,2048]{1,0:T(8,128)} %param.10, f32[256,2048]{1,0:T(8,128)} %param.11), kind=kLoop, calls=%fused_computation.31 | loop fusion | flops 8912896 | bytes 13631488 | tf_op jit(solution)/shard_map/sub | solution.py:23
  (38 shorter events, 2.0 us)
Async XLA Ops:
  7.2 181.5 %reduce-scatter.2.cloned.1.call-start = ((), (), s32[]{:S(2)}) async-start(), calls=%async_computation.2 | async-start | bytes 5242880 | tf_op jit(solution)/shard_map/reduce_scatter | solution.py:109
  8.9 2.7 %collective-permute-start = (bf16[256,2048]{1,0:T(8,128)(2,1)S(1)}, bf16[256,2048]{1,0:T(8,128)(2,1)S(1)}, u32[]{:S(2)}, u32[]{:S(2)}) collective-permute-start(bf16[256,2048]{1,0:T(8,128)(2,1)S(1)} %convert_element_type.42), channel_id=1, source_target_pairs={{0,1},{1,0},{2,3},{3,2},{4,5},{5,4},{6,7},{7,6},{8,9},{9,8},{10,11... | collective-permute-start | bytes 3145736 | tf_op jit(solution)/shard_map/ppermute | solution.py:65
  9.0 62.2 %copy-start.5 = (s32[128,2]{0,1:T(2,128)S(1)}, s32[128,2]{0,1:T(2,128)}, u32[]{:S(2)}) copy-start(s32[128,2]{0,1:T(2,128)} %param.6) | copy-start | bytes 3076
  9.0 63.6 %copy-start.7 = (u32[32]{0:T(128)S(1)}, u32[32]{0:T(128)}, u32[]{:S(2)}) copy-start(u32[32]{0:T(128)} %constant.98) | copy-start | bytes 388
  12.7 57.3 %copy-start.3 = (bf16[512,2048]{1,0:T(8,128)(2,1)}, bf16[512,2048]{1,0:T(8,128)(2,1)S(1)}, u32[]{:S(2)}) copy-start(bf16[512,2048]{1,0:T(8,128)(2,1)S(1)} %maximum_select_fusion) | copy-start | bytes 6291460
  12.7 27.9 %collective-permute-start.1 = (bf16[512,2048]{1,0:T(8,128)(2,1)S(1)}, bf16[512,2048]{1,0:T(8,128)(2,1)S(1)}, u32[]{:S(2)}, u32[]{:S(2)}) collective-permute-start(bf16[512,2048]{1,0:T(8,128)(2,1)S(1)} %maximum_select_fusion), channel_id=1, source_target_pairs={{0,2},{2,4},{4,6},{3,1},{5,3},{7,5},{8,10},{10,12},{12,14},{11,9},... | collective-permute-start | bytes 6291464 | tf_op jit(solution)/shard_map/ppermute | solution.py:72
  40.6 1.3 copy-start.1
  41.9 28.0 %collective-permute-start.2 = (bf16[512,2048]{1,0:T(8,128)(2,1)S(1)}, bf16[512,2048]{1,0:T(8,128)(2,1)}, u32[]{:S(2)}, u32[]{:S(2)}) collective-permute-start(bf16[512,2048]{1,0:T(8,128)(2,1)S(1)} %collective-permute-done.1), channel_id=1, source_target_pairs={{2,4},{4,6},{3,1},{5,3},{10,12},{12,14},{11,9},{13,11},{18,20},{20... | collective-permute-start | bytes 6291464 | tf_op jit(solution)/shard_map/ppermute | solution.py:72
  69.9 28.2 %collective-permute-start.3 = (bf16[512,2048]{1,0:T(8,128)(2,1)}, bf16[512,2048]{1,0:T(8,128)(2,1)}, u32[]{:S(2)}, u32[]{:S(2)}) collective-permute-start(bf16[512,2048]{1,0:T(8,128)(2,1)} %collective-permute-done.2), channel_id=1, source_target_pairs={{4,6},{3,1},{12,14},{11,9},{20,22},{19,17},{28,30},{27,25}} | collective-permute-start | bytes 6291464 | tf_op jit(solution)/shard_map/ppermute | solution.py:72
  84.8 1.6 copy-start.6
  86.4 11.8 %copy-start.2 = (bf16[512,2048]{1,0:T(8,128)(2,1)S(1)}, bf16[512,2048]{1,0:T(8,128)(2,1)}, u32[]{:S(2)}) copy-start(bf16[512,2048]{1,0:T(8,128)(2,1)} %copy-done.1) | copy-start | bytes 6291460
  88.8 14.8 %collective-permute-start.5 = (bf16[1024,2048]{1,0:T(8,128)(2,1)S(1)}, bf16[1024,2048]{1,0:T(8,128)(2,1)S(1)}, u32[]{:S(2)}, u32[]{:S(2)}) collective-permute-start(bf16[1024,2048]{1,0:T(8,128)(2,1)S(1)} %convolution_convert_fusion), channel_id=1, source_target_pairs={{0,1},{1,0},{2,3},{3,2},{4,5},{5,4},{6,7},{7,6},{8,9},{9,8},{10,11... | collective-permute-start | bytes 12582920 | tf_op jit(solution)/shard_map/ppermute | solution.py:104
  103.7 10.5 %collective-permute-start.4 = (bf16[3,512,2048]{2,1,0:T(8,128)(2,1)}, bf16[3,512,2048]{2,1,0:T(8,128)(2,1)}, u32[]{:S(2)}, u32[]{:S(2)}) collective-permute-start(bf16[3,512,2048]{2,1,0:T(8,128)(2,1)} %pad_maximum_fusion), channel_id=1, source_target_pairs={{0,1},{1,0},{2,3},{3,2},{4,5},{5,4},{6,7},{7,6},{8,9},{9,8},{10,11... | collective-permute-start | bytes 18874376 | tf_op jit(solution)/shard_map/ppermute | solution.py:75
  119.6 2.0 %copy-start.4 = (bf16[512,2048]{1,0:T(8,128)(2,1)S(1)}, bf16[512,2048]{1,0:T(8,128)(2,1)}, u32[]{:S(2)}) copy-start(bf16[512,2048]{1,0:T(8,128)(2,1)} %copy-done.3) | copy-start | bytes 6291460
  130.4 52.9 %all-to-all-start = ((f32[4,128,2048]{2,1,0:T(8,128)}), f32[4,128,2048]{2,1,0:T(8,128)}, u32[]{:S(2)}, u32[]{:S(2)}) async-start(f32[4,128,2048]{2,1,0:T(8,128)} %fusion), calls=%async_computation | async-start | bytes 8388608 | tf_op jit(solution)/shard_map/all_to_all | solution.py:85
  186.1 2.6 %copy-start = (f32[256,2048]{1,0:T(8,128)S(1)}, f32[256,2048]{1,0:T(8,128)}, u32[]{:S(2)}) copy-start(f32[256,2048]{1,0:T(8,128)} %param.9) | copy-start | bytes 6291460
Sparse Core Ops, SparseCore 0:
  108.2 77.1 reduce-scatter.1

commit v9 on v8

--- a/solution.py
+++ b/solution.py
@@ -71,13 +71,12 @@
     for t in range(1, n_z):
         cur = lax.ppermute(cur, DP, flood_pairs(n_z, t))
         held.append(cur)
-    own_held = jnp.stack(held)
-    other_held = lax.ppermute(own_held, "core", SWAP)
-    down_side = jnp.where(me_c == 0, own_held, other_held)
-    up_side = jnp.where(me_c == 0, other_held, own_held)
+    other_held = lax.ppermute(tuple(held), "core", SWAP)
     parts = [chip_w]
     for r in range(1, n_z):
-        parts.append(jnp.where(me_z + r < n_z, up_side[r - 1], down_side[n_z - r - 1]))
+        up = jnp.where(me_c == 0, other_held[r - 1], held[r - 1])
+        down = jnp.where(me_c == 0, held[n_z - r - 1], other_held[n_z - r - 1])
+        parts.append(jnp.where(me_z + r < n_z, up, down))
     w_rel = jnp.concatenate(parts, axis=0)
     cols = (((1,), (1,)), ((), ()))
     partial_rows = lax.dot_general(masked, w_rel, cols, preferred_element_type=jnp.float32)

time: 203 us -> 255 us (1.26)
  waiting for transfers between devices: 119 us -> 178 us
  other arithmetic: 26.9 us -> 21.2 us
    ppermute x3, waiting for transfers between devices: 62.6 us -> 128 us  [shards(): cur = lax.ppermute(cur, DP, flood_pairs(n_z, t))]
    another operation x3 -> x2, other arithmetic: 6.29 us -> 0.8 us  [the longest x1 5.49 us: shards(): own_held = jnp.stack(held)]
    ppermute x1 -> x3, waiting for transfers between devices: 6.06 us -> 1.93 us  [shards(): other_held = lax.ppermute(tuple(held), 'core', SWAP)]
    ppermute x1, waiting for transfers between devices: 2.61 us -> 0.01 us  [shards(): partner = lax.ppermute(wbf, 'core', SWAP)]
    unnamed x22 -> x24, local copies, waits for them, and re-layouts: 7.52 us -> 8.98 us
  transfers between devices with their start and end apart: 8 -> 10, of which waited for: 6 -> 5; matrix products, arithmetic and copies ran while one was open for 20% -> 12% of each run, Pallas kernels for 0% -> 0%
where the time goes in v9:
time: 255 us
  waiting for transfers between devices  178 us (70%)
  other arithmetic  21.2 us (8%)
  between operations  15 us (6%)
  matrix products  13.7 us (5%)
  local copies, waits for them, and re-layouts  10.3 us (4%)
  starting transfers between devices  9.62 us (4%)
  blocking collectives  7.37 us (3%)
    ppermute x3, waiting for transfers between devices, shards(): cur = lax.ppermute(cur, DP, flood_pairs(n_z, t))  128 us
    all_to_all x1, waiting for transfers between devices, shards(): lax.all_to_all(sent, 'expert', split_axis=0, concat_axis=0, tiled=True)  47.5 us
    unnamed x24, local copies, waits for them, and re-layouts  8.98 us
    unnamed x1, blocking collectives  7.37 us
    dot_general x1, matrix products, shards(): lax.dot_general(masked, w_rel, cols, preferred_element_type=jnp.float32)  6.6 us
    sub x1, other arithmetic, adamw(): new_weight = weight - learn_rate * (update + decay * weight)  6.42 us
    select_n x2, other arithmetic, shards(): parts.append(jnp.where(me_z + r < n_z, up, down))  5.59 us
  transfers between devices with their start and end apart: 10, of which 5 were waited for; matrix products, arithmetic and copies ran while one was open for 12% of the time, Pallas kernels for 0%

profile of v9, /device:TPU:24, one launch (start us, length us, event | category | flops | bytes accessed | tf_op | source)
XLA Modules:
  0.0 254.8 jit_solution(5102760433864653727)
XLA Ops:
  7.2 1.7 convert_element_type.42
  9.5 0.6 reduce-window.6
  10.1 0.2 slice_reduce_fusion
  10.5 0.6 dynamic-slice
  11.9 0.2 dynamic-update-slice
  12.2 7.4 %all-reduce = s32[8]{0:T(128)S(1)} all-reduce(s32[8]{0:T(128)S(1)} %dynamic-update-slice), channel_id=2, replica_groups=mesh['expert'=4,'z'=4,'core'=2] {'expert'}, use_global_device_ids=true, to_apply=%add | all-reduce | flops 8 | bytes 64
  19.6 2.9 %copy.29 = bf16[1,1,512,2048]{2,3,1,0:T(8,128)(2,1)S(1)} copy(bf16[1,1,512,2048]{3,2,1,0:T(8,128)(2,1)} %param.7) | data formatting | bytes 4194304 | tf_op args[1]
  22.5 2.4 maximum_select_fusion
  24.9 1.3 collective-permute-start.1
  26.6 1.4 copy-done.6
  27.9 2.4 convolution_convert_fusion
  30.5 22.4 %collective-permute-done.1 = bf16[512,2048]{1,0:T(8,128)(2,1)S(1)} collective-permute-done((bf16[512,2048]{1,0:T(8,128)(2,1)S(1)}, bf16[512,2048]{1,0:T(8,128)(2,1)S(1)}, u32[]{:S(2)}, u32[]{:S(2)}) %collective-permute-start.1) | collective-permute-done | bytes 2097184 | tf_op jit(solution)/shard_map/ppermute | solution.py:72
  52.9 1.3 copy-done.1
  54.2 1.3 collective-permute-start.3
  55.5 26.7 %collective-permute-done.3 = bf16[512,2048]{1,0:T(8,128)(2,1)} collective-permute-done((bf16[512,2048]{1,0:T(8,128)(2,1)S(1)}, bf16[512,2048]{1,0:T(8,128)(2,1)}, u32[]{:S(2)}, u32[]{:S(2)}) %collective-permute-start.3) | collective-permute-done | bytes 2097184 | tf_op jit(solution)/shard_map/ppermute | solution.py:72
  82.2 1.3 collective-permute-start.4
  83.6 4.4 %add_convert_fusion = bf16[1024,2048]{1,0:T(8,128)(2,1)} fusion(bf16[1024,2048]{1,0:T(8,128)(2,1)S(1)} %collective-permute-done.7, bf16[512,1024]{0,1:T(8,128)(2,1)S(1)} %bitcast.43, bf16[1,1,512,2048]{3,2,1,0:T(8,128)(2,1)S(1)} %copy-done.6, pred[512]{0:T(512)(128)(4,1)S(1)} %get-tuple-element.17), kind=kOutput, calls=%fused_computation.8 | convolution fusion | flops 2154823680 | bytes 11534848 | tf_op jit(solution)/shard_map/dot_general | solution.py:104
  88.0 1.6 copy-done.2
  89.5 0.5 collective-permute-start.2
  90.0 79.1 %collective-permute-done.4 = bf16[512,2048]{1,0:T(8,128)(2,1)} collective-permute-done((bf16[512,2048]{1,0:T(8,128)(2,1)}, bf16[512,2048]{1,0:T(8,128)(2,1)}, u32[]{:S(2)}, u32[]{:S(2)}) %collective-permute-start.4) | collective-permute-done | bytes 2097184 | tf_op jit(solution)/shard_map/ppermute | solution.py:72
  169.1 2.5 select_select_fusion.1
  171.7 1.9 collective-permute-done.5
  173.6 3.1 %select_select_fusion.2 = (bf16[512,2048]{1,0:T(8,128)(2,1)S(1)}, bf16[512,2048]{1,0:T(8,128)(2,1)S(1)}) fusion(bf16[512,2048]{1,0:T(8,128)(2,1)} %collective-permute-done.4, bf16[512,2048]{1,0:T(8,128)(2,1)} %collective-permute-done.5, bf16[512,2048]{1,0:T(8,128)(2,1)} %collective-permute-done.2, bf16[512,2048]{1,0:T(8,128)(2,1)S(1)} %copy-done.2, ...), kind=kLoop, calls=%fused_computation.25 | loop fusion | flops 6291456 | bytes 12582915 | tf_op jit(solution)/shard_map/jit(_where)/select_n | solution.py:79
  176.7 6.6 %fusion = f32[4,128,2048]{2,1,0:T(8,128)} fusion(bf16[512,2048]{1,0:T(8,128)(2,1)S(1)} %get-tuple-element.14, bf16[512,2048]{1,0:T(8,128)(2,1)S(1)} %select_select_fusion.1, bf16[512,2048]{1,0:T(8,128)(2,1)S(1)} %get-tuple-element.13, bf16[512,2048]{1,0:T(8,128)(2,1)S(1)} %copy-done.4, bf16[4,128,2048]{2,1,0:T(8,128)(2,1)S(1)} %bitcast.47, ...), kind=kOutput, calls=%fused_computation.1 | convolution fusion | flops 4329570304 | bytes 14680576 | tf_op jit(solution)/shard_map/dot_general | solution.py:82
  183.3 5.0 %all-to-all-start = ((f32[4,128,2048]{2,1,0:T(8,128)}), f32[4,128,2048]{2,1,0:T(8,128)}, u32[]{:S(2)}, u32[]{:S(2)}) async-start(f32[4,128,2048]{2,1,0:T(8,128)} %fusion), calls=%async_computation | async-start | bytes 8388608 | tf_op jit(solution)/shard_map/all_to_all | solution.py:84
  188.7 47.5 %all-to-all-done = f32[4,128,2048]{2,1,0:T(8,128)} async-done(((f32[4,128,2048]{2,1,0:T(8,128)}), f32[4,128,2048]{2,1,0:T(8,128)}, u32[]{:S(2)}, u32[]{:S(2)}) %all-to-all-start) | async-done | bytes 4194336 | tf_op jit(solution)/shard_map/all_to_all | solution.py:84
  236.2 2.7 %bitcast_reduce_fusion = bf16[2,128,2048]{2,1,0:T(8,128)(2,1)S(1)} fusion(f32[4,128,2048]{2,1,0:T(8,128)} %all-to-all-done), kind=kLoop, calls=%fused_computation.9 | loop fusion | flops 524288 | bytes 5242880 | tf_op jit(solution)/shard_map/reduce_sum | solution.py:85
  239.0 0.3 convolution_convert_fusion.1
  239.3 0.4 reshape.103
  239.7 1.0 fusion.18
  240.6 0.9 copy.31
  241.5 6.4 %multiply_subtract_fusion = (f32[256,2048]{1,0:T(8,128)}, f32[256,2048]{1,0:T(8,128)}, f32[256,2048]{1,0:T(8,128)}) fusion(f32[256,2048]{1,0:T(8,128)S(1)} %copy-done, bf16[256,2048]{1,0:T(8,128)(2,1)} %reduce-scatter.2.cloned.1.call-done, f32[256,2048]{1,0:T(8,128)} %param.10, f32[256,2048]{1,0:T(8,128)} %param.11), kind=kLoop, calls=%fused_computation.22 | loop fusion | flops 8912896 | bytes 13631488 | tf_op jit(solution)/shard_map/sub | solution.py:23
  (43 shorter events, 1.8 us)
Async XLA Ops:
  7.2 3.3 %copy-start.8 = (u32[32]{0:T(128)S(1)}, u32[32]{0:T(128)}, u32[]{:S(2)}) copy-start(u32[32]{0:T(128)} %constant.98) | copy-start | bytes 388
  7.2 1.9 copy-start.5
  7.2 234.3 %reduce-scatter.2.cloned.1.call-start = ((), (), s32[]{:S(2)}) async-start(), calls=%async_computation.2 | async-start | bytes 5242880 | tf_op jit(solution)/shard_map/reduce_scatter | solution.py:108
  9.0 13.5 %collective-permute-start = (bf16[256,2048]{1,0:T(8,128)(2,1)S(1)}, bf16[256,2048]{1,0:T(8,128)(2,1)}, u32[]{:S(2)}, u32[]{:S(2)}) collective-permute-start(bf16[256,2048]{1,0:T(8,128)(2,1)S(1)} %convert_element_type.42), channel_id=1, source_target_pairs={{0,1},{1,0},{2,3},{3,2},{4,5},{5,4},{6,7},{7,6},{8,9},{9,8},{10,11... | collective-permute-start | bytes 3145736 | tf_op jit(solution)/shard_map/ppermute | solution.py:65
  24.9 1.6 copy-start.3
  24.9 27.9 %collective-permute-start.1 = (bf16[512,2048]{1,0:T(8,128)(2,1)S(1)}, bf16[512,2048]{1,0:T(8,128)(2,1)S(1)}, u32[]{:S(2)}, u32[]{:S(2)}) collective-permute-start(bf16[512,2048]{1,0:T(8,128)(2,1)S(1)} %maximum_select_fusion), channel_id=1, source_target_pairs={{0,2},{2,4},{4,6},{3,1},{5,3},{7,5},{8,10},{10,12},{12,14},{11,9},... | collective-permute-start | bytes 6291464 | tf_op jit(solution)/shard_map/ppermute | solution.py:72
  26.4 1.6 copy-start.6
  30.4 53.2 %collective-permute-start.7 = (bf16[1024,2048]{1,0:T(8,128)(2,1)S(1)}, bf16[1024,2048]{1,0:T(8,128)(2,1)S(1)}, u32[]{:S(2)}, u32[]{:S(2)}) collective-permute-start(bf16[1024,2048]{1,0:T(8,128)(2,1)S(1)} %convolution_convert_fusion), channel_id=1, source_target_pairs={{0,1},{1,0},{2,3},{3,2},{4,5},{5,4},{6,7},{7,6},{8,9},{9,8},{10,11... | collective-permute-start | bytes 12582920 | tf_op jit(solution)/shard_map/ppermute | solution.py:103
  52.9 1.3 copy-start.1
  54.2 28.0 %collective-permute-start.3 = (bf16[512,2048]{1,0:T(8,128)(2,1)S(1)}, bf16[512,2048]{1,0:T(8,128)(2,1)}, u32[]{:S(2)}, u32[]{:S(2)}) collective-permute-start(bf16[512,2048]{1,0:T(8,128)(2,1)S(1)} %collective-permute-done.1), channel_id=1, source_target_pairs={{2,4},{4,6},{3,1},{5,3},{10,12},{12,14},{11,9},{13,11},{18,20},{20... | collective-permute-start | bytes 6291464 | tf_op jit(solution)/shard_map/ppermute | solution.py:72
  82.2 86.9 %collective-permute-start.4 = (bf16[512,2048]{1,0:T(8,128)(2,1)}, bf16[512,2048]{1,0:T(8,128)(2,1)}, u32[]{:S(2)}, u32[]{:S(2)}) collective-permute-start(bf16[512,2048]{1,0:T(8,128)(2,1)} %collective-permute-done.3), channel_id=1, source_target_pairs={{4,6},{3,1},{12,14},{11,9},{20,22},{19,17},{28,30},{27,25}} | collective-permute-start | bytes 6291464 | tf_op jit(solution)/shard_map/ppermute | solution.py:72
  83.5 85.7 %collective-permute-start.6 = (bf16[512,2048]{1,0:T(8,128)(2,1)}, bf16[512,2048]{1,0:T(8,128)(2,1)}, u32[]{:S(2)}, u32[]{:S(2)}) collective-permute-start(bf16[512,2048]{1,0:T(8,128)(2,1)} %collective-permute-done.3), channel_id=1, source_target_pairs={{0,1},{1,0},{2,3},{3,2},{4,5},{5,4},{6,7},{7,6},{8,9},{9,8},{10,11... | collective-permute-start | bytes 6291464 | tf_op jit(solution)/shard_map/ppermute | solution.py:74
  87.9 1.6 copy-start.2
  89.5 82.2 %collective-permute-start.2 = (bf16[512,2048]{1,0:T(8,128)(2,1)S(1)}, bf16[512,2048]{1,0:T(8,128)(2,1)}, u32[]{:S(2)}, u32[]{:S(2)}) collective-permute-start(bf16[512,2048]{1,0:T(8,128)(2,1)S(1)} %copy-done.2), channel_id=1, source_target_pairs={{0,1},{1,0},{2,3},{3,2},{4,5},{5,4},{6,7},{7,6},{8,9},{9,8},{10,11... | collective-permute-start | bytes 6291464 | tf_op jit(solution)/shard_map/ppermute | solution.py:74
  169.1 4.5 %collective-permute-start.5 = (bf16[512,2048]{1,0:T(8,128)(2,1)}, bf16[512,2048]{1,0:T(8,128)(2,1)}, u32[]{:S(2)}, u32[]{:S(2)}) collective-permute-start(bf16[512,2048]{1,0:T(8,128)(2,1)} %collective-permute-done.4), channel_id=1, source_target_pairs={{0,1},{1,0},{2,3},{3,2},{4,5},{5,4},{6,7},{7,6},{8,9},{9,8},{10,11... | collective-permute-start | bytes 6291464 | tf_op jit(solution)/shard_map/ppermute | solution.py:74
  171.7 5.0 %copy-start.4 = (bf16[512,2048]{1,0:T(8,128)(2,1)S(1)}, bf16[512,2048]{1,0:T(8,128)(2,1)}, u32[]{:S(2)}) copy-start(bf16[512,2048]{1,0:T(8,128)(2,1)} %copy-done.3) | copy-start | bytes 6291460
  171.7 5.0 %copy-start.7 = (bf16[1,1,512,2048]{3,2,1,0:T(8,128)(2,1)S(1)}, bf16[1,1,512,2048]{3,2,1,0:T(8,128)(2,1)}, u32[]{:S(2)}) copy-start(bf16[1,1,512,2048]{3,2,1,0:T(8,128)(2,1)} %param.8) | copy-start | bytes 6291460
  183.3 52.9 %all-to-all-start = ((f32[4,128,2048]{2,1,0:T(8,128)}), f32[4,128,2048]{2,1,0:T(8,128)}, u32[]{:S(2)}, u32[]{:S(2)}) async-start(f32[4,128,2048]{2,1,0:T(8,128)} %fusion), calls=%async_computation | async-start | bytes 8388608 | tf_op jit(solution)/shard_map/all_to_all | solution.py:84
  239.0 2.6 %copy-start = (f32[256,2048]{1,0:T(8,128)S(1)}, f32[256,2048]{1,0:T(8,128)}, u32[]{:S(2)}) copy-start(f32[256,2048]{1,0:T(8,128)} %param.9) | copy-start | bytes 6291460
Sparse Core Ops, SparseCore 0:
  88.1 90.9 reduce-scatter.1

commit v10 on v9

--- a/solution.py
+++ b/solution.py
@@ -71,7 +71,8 @@
     for t in range(1, n_z):
         cur = lax.ppermute(cur, DP, flood_pairs(n_z, t))
         held.append(cur)
-    other_held = lax.ppermute(tuple(held), "core", SWAP)
+    held = lax.optimization_barrier(tuple(held))
+    other_held = lax.ppermute(held, "core", SWAP)
     parts = [chip_w]
     for r in range(1, n_z):
         up = jnp.where(me_c == 0, other_held[r - 1], held[r - 1])

time: 255 us -> 196 us (0.77)
  waiting for transfers between devices: 178 us -> 119 us
  local copies, waits for them, and re-layouts: 10.3 us -> 6.11 us
    ppermute x3, waiting for transfers between devices: 128 us -> 64.3 us  [shards(): cur = lax.ppermute(cur, DP, flood_pairs(n_z, t))]
    unnamed x24 -> x16, local copies, waits for them, and re-layouts: 8.98 us -> 4.73 us
    ppermute x1, waiting for transfers between devices: 0.01 us -> 2.61 us  [shards(): partner = lax.ppermute(wbf, 'core', SWAP)]
  transfers between devices with their start and end apart: 10 -> 10, of which waited for: 5 -> 7; matrix products, arithmetic and copies ran while one was open for 12% -> 17% of each run, Pallas kernels for 0% -> 0%
where the time goes in v10:
time: 196 us; the launch traced here: 194 us
  waiting for transfers between devices  119 us (61%)
  other arithmetic  21.3 us (11%)
  matrix products  15.3 us (8%)
  between operations  14.9 us (8%)
  starting transfers between devices  9.72 us (5%)
  blocking collectives  7.37 us (4%)
  local copies, waits for them, and re-layouts  6.11 us (3%)
    ppermute x3, waiting for transfers between devices, shards(): cur = lax.ppermute(cur, DP, flood_pairs(n_z, t))  64.3 us
    all_to_all x1, waiting for transfers between devices, shards(): lax.all_to_all(sent, 'expert', split_axis=0, concat_axis=0, tiled=True)  47.6 us
    dot_general x1, matrix products, shards(): lax.dot_general(masked, w_rel, cols, preferred_element_type=jnp.float32)  8.19 us
    unnamed x1, blocking collectives  7.37 us
    sub x1, other arithmetic, adamw(): new_weight = weight - learn_rate * (update + decay * weight)  6.42 us
    select_n x2, other arithmetic, shards(): parts.append(jnp.where(me_z + r < n_z, up, down))  5.83 us
    all_to_all x1, starting transfers between devices, shards(): lax.all_to_all(sent, 'expert', split_axis=0, concat_axis=0, tiled=True)  5.05 us
    unnamed x16, local copies, waits for them, and re-layouts  4.73 us
  transfers between devices with their start and end apart: 10, of which 7 were waited for; matrix products, arithmetic and copies ran while one was open for 17% of the time, Pallas kernels for 0%

profile of v10, /device:TPU:24, one launch (start us, length us, event | category | flops | bytes accessed | tf_op | source)
XLA Modules:
  0.0 193.6 jit_solution(7766791040396405451)
XLA Ops:
  7.2 1.7 convert_element_type.42
  9.1 2.6 %collective-permute-done = bf16[256,2048]{1,0:T(8,128)(2,1)S(1)} collective-permute-done((bf16[256,2048]{1,0:T(8,128)(2,1)S(1)}, bf16[256,2048]{1,0:T(8,128)(2,1)S(1)}, u32[]{:S(2)}, u32[]{:S(2)}) %collective-permute-start) | collective-permute-done | bytes 1048608 | tf_op jit(solution)/shard_map/ppermute | solution.py:65
  11.7 2.3 %maximum_select_fusion = bf16[512,2048]{1,0:T(8,128)(2,1)} fusion(bf16[256,2048]{1,0:T(8,128)(2,1)S(1)} %collective-permute-done, bf16[256,2048]{1,0:T(8,128)(2,1)S(1)} %convert_element_type.42, pred[]{:T(512)S(6)} %eq.74), kind=kLoop, calls=%fused_computation.18 | loop fusion | flops 9437184 | bytes 4194305 | tf_op jit(solution)/shard_map/jit(_where)/select_n | solution.py:66
  14.0 1.3 collective-permute-start.1
  15.7 0.6 reduce-window.6
  16.3 0.2 slice_reduce_fusion
  16.7 0.6 dynamic-slice
  18.2 0.2 dynamic-update-slice
  18.4 7.4 %all-reduce = s32[8]{0:T(128)S(1)} all-reduce(s32[8]{0:T(128)S(1)} %dynamic-update-slice), channel_id=2, replica_groups=mesh['expert'=4,'z'=4,'core'=2] {'expert'}, use_global_device_ids=true, to_apply=%add | all-reduce | flops 8 | bytes 64
  25.9 2.9 %copy.29 = bf16[1,1,512,2048]{2,3,1,0:T(8,128)(2,1)S(1)} copy(bf16[1,1,512,2048]{3,2,1,0:T(8,128)(2,1)} %param.7) | data formatting | bytes 4194304 | tf_op args[1]
  28.9 0.2 constant_dynamic-slice_fusion.1
  29.2 13.0 %collective-permute-done.1 = bf16[512,2048]{1,0:T(8,128)(2,1)} collective-permute-done((bf16[512,2048]{1,0:T(8,128)(2,1)}, bf16[512,2048]{1,0:T(8,128)(2,1)}, u32[]{:S(2)}, u32[]{:S(2)}) %collective-permute-start.1) | collective-permute-done | bytes 2097184 | tf_op jit(solution)/shard_map/ppermute | solution.py:72
  42.2 1.3 collective-permute-start.2
  43.5 2.4 %convolution_convert_fusion = bf16[1024,2048]{1,0:T(8,128)(2,1)S(1)} fusion(bf16[512,1024]{0,1:T(8,128)(2,1)S(1)} %bitcast.44, bf16[1,1,512,2048]{3,2,1,0:T(8,128)(2,1)S(1)} %copy-done.2, pred[512]{0:T(512)(128)(4,1)S(1)} %get-tuple-element.23), kind=kOutput, calls=%fused_computation.10 | convolution fusion | flops 2150629376 | bytes 7340544 | tf_op jit(solution)/shard_map/dot_general | solution.py:101
  46.0 24.4 %collective-permute-done.2 = bf16[512,2048]{1,0:T(8,128)(2,1)} collective-permute-done((bf16[512,2048]{1,0:T(8,128)(2,1)}, bf16[512,2048]{1,0:T(8,128)(2,1)}, u32[]{:S(2)}, u32[]{:S(2)}) %collective-permute-start.2) | collective-permute-done | bytes 2097184 | tf_op jit(solution)/shard_map/ppermute | solution.py:72
  70.5 1.3 collective-permute-start.3
  71.8 26.8 %collective-permute-done.3 = bf16[512,2048]{1,0:T(8,128)(2,1)S(1)} collective-permute-done((bf16[512,2048]{1,0:T(8,128)(2,1)}, bf16[512,2048]{1,0:T(8,128)(2,1)S(1)}, u32[]{:S(2)}, u32[]{:S(2)}) %collective-permute-start.3) | collective-permute-done | bytes 2097184 | tf_op jit(solution)/shard_map/ppermute | solution.py:72
  98.6 4.4 %add_convert_fusion = bf16[1024,2048]{1,0:T(8,128)(2,1)} fusion(bf16[1024,2048]{1,0:T(8,128)(2,1)S(1)} %collective-permute-done.7, bf16[512,1024]{0,1:T(8,128)(2,1)S(1)} %bitcast.43, bf16[1,1,512,2048]{3,2,1,0:T(8,128)(2,1)S(1)} %copy-done.2, pred[512]{0:T(512)(128)(4,1)S(1)} %get-tuple-element.23), kind=kOutput, calls=%fused_computation.8 | convolution fusion | flops 2154823680 | bytes 11534848 | tf_op jit(solution)/shard_map/dot_general | solution.py:105
  103.0 0.6 collective-permute-start.4
  103.6 2.4 %select_select_fusion.1 = bf16[512,2048]{1,0:T(8,128)(2,1)S(1)} fusion(bf16[512,2048]{1,0:T(8,128)(2,1)} %collective-permute-done.2, bf16[512,2048]{1,0:T(8,128)(2,1)} %collective-permute-done.6, pred[]{:T(512)S(6)} %lt.53, pred[]{:T(512)S(6)} %eq.74), kind=kLoop, calls=%fused_computation.24 | loop fusion | flops 3145728 | bytes 6291458 | tf_op jit(solution)/shard_map/jit(_where)/select_n | solution.py:80
  106.1 3.8 %collective-permute-done.4 = bf16[512,2048]{1,0:T(8,128)(2,1)} collective-permute-done((bf16[512,2048]{1,0:T(8,128)(2,1)}, bf16[512,2048]{1,0:T(8,128)(2,1)}, u32[]{:S(2)}, u32[]{:S(2)}) %collective-permute-start.4) | collective-permute-done | bytes 2097184 | tf_op jit(solution)/shard_map/ppermute | solution.py:75
  109.9 0.6 collective-permute-done.5
  110.5 3.4 %select_select_fusion.2 = (bf16[512,2048]{1,0:T(8,128)(2,1)S(1)}, bf16[512,2048]{1,0:T(8,128)(2,1)S(1)}) fusion(bf16[512,2048]{1,0:T(8,128)(2,1)S(1)} %collective-permute-done.3, bf16[512,2048]{1,0:T(8,128)(2,1)} %collective-permute-done.5, bf16[512,2048]{1,0:T(8,128)(2,1)} %collective-permute-done.4, bf16[512,2048]{1,0:T(8,128)(2,1)} %collective-permute-done.1, ...), kind=kLoop, calls=%fused_computation.25 | loop fusion | flops 6291456 | bytes 12582915 | tf_op jit(solution)/shard_map/jit(_where)/select_n | solution.py:80
  113.9 8.2 %fusion = f32[4,128,2048]{2,1,0:T(8,128)} fusion(bf16[512,2048]{1,0:T(8,128)(2,1)S(1)} %get-tuple-element.20, bf16[512,2048]{1,0:T(8,128)(2,1)S(1)} %select_select_fusion.1, bf16[512,2048]{1,0:T(8,128)(2,1)S(1)} %get-tuple-element.19, bf16[512,2048]{1,0:T(8,128)(2,1)} %maximum_select_fusion, bf16[4,128,2048]{2,1,0:T(8,128)(2,1)S(1)} %bitcast.47, ...), kind=kOutput, calls=%fused_computation.1 | convolution fusion | flops 4329570304 | bytes 14680576 | tf_op jit(solution)/shard_map/dot_general | solution.py:83
  122.1 5.0 %all-to-all-start = ((f32[4,128,2048]{2,1,0:T(8,128)}), f32[4,128,2048]{2,1,0:T(8,128)}, u32[]{:S(2)}, u32[]{:S(2)}) async-start(f32[4,128,2048]{2,1,0:T(8,128)} %fusion), calls=%async_computation | async-start | bytes 8388608 | tf_op jit(solution)/shard_map/all_to_all | solution.py:85
  127.5 47.6 %all-to-all-done = f32[4,128,2048]{2,1,0:T(8,128)} async-done(((f32[4,128,2048]{2,1,0:T(8,128)}), f32[4,128,2048]{2,1,0:T(8,128)}, u32[]{:S(2)}, u32[]{:S(2)}) %all-to-all-start) | async-done | bytes 4194336 | tf_op jit(solution)/shard_map/all_to_all | solution.py:85
  175.0 2.7 %bitcast_reduce_fusion = bf16[2,128,2048]{2,1,0:T(8,128)(2,1)S(1)} fusion(f32[4,128,2048]{2,1,0:T(8,128)} %all-to-all-done), kind=kLoop, calls=%fused_computation.9 | loop fusion | flops 524288 | bytes 5242880 | tf_op jit(solution)/shard_map/reduce_sum | solution.py:86
  177.8 0.3 convolution_convert_fusion.1
  178.1 0.4 reshape.103
  178.5 1.0 fusion.18
  179.5 0.9 copy.31
  180.4 6.4 %multiply_subtract_fusion = (f32[256,2048]{1,0:T(8,128)}, f32[256,2048]{1,0:T(8,128)}, f32[256,2048]{1,0:T(8,128)}) fusion(f32[256,2048]{1,0:T(8,128)S(1)} %copy-done, bf16[256,2048]{1,0:T(8,128)(2,1)} %reduce-scatter.2.cloned.1.call-done, f32[256,2048]{1,0:T(8,128)} %param.10, f32[256,2048]{1,0:T(8,128)} %param.11), kind=kLoop, calls=%fused_computation.22 | loop fusion | flops 8912896 | bytes 13631488 | tf_op jit(solution)/shard_map/sub | solution.py:23
  (35 shorter events, 1.7 us)
Async XLA Ops:
  7.2 173.2 %reduce-scatter.2.cloned.1.call-start = ((), (), s32[]{:S(2)}) async-start(), calls=%async_computation.2 | async-start | bytes 5242880 | tf_op jit(solution)/shard_map/reduce_scatter | solution.py:109
  8.9 2.7 %collective-permute-start = (bf16[256,2048]{1,0:T(8,128)(2,1)S(1)}, bf16[256,2048]{1,0:T(8,128)(2,1)S(1)}, u32[]{:S(2)}, u32[]{:S(2)}) collective-permute-start(bf16[256,2048]{1,0:T(8,128)(2,1)S(1)} %convert_element_type.42), channel_id=1, source_target_pairs={{0,1},{1,0},{2,3},{3,2},{4,5},{5,4},{6,7},{7,6},{8,9},{9,8},{10,11... | collective-permute-start | bytes 3145736 | tf_op jit(solution)/shard_map/ppermute | solution.py:65
  9.0 6.3 %copy-start.1 = (s32[128,2]{0,1:T(2,128)S(1)}, s32[128,2]{0,1:T(2,128)}, u32[]{:S(2)}) copy-start(s32[128,2]{0,1:T(2,128)} %param.6) | copy-start | bytes 3076
  9.0 7.7 %copy-start.4 = (u32[32]{0:T(128)S(1)}, u32[32]{0:T(128)}, u32[]{:S(2)}) copy-start(u32[32]{0:T(128)} %constant.98) | copy-start | bytes 388
  14.0 28.2 %collective-permute-start.1 = (bf16[512,2048]{1,0:T(8,128)(2,1)}, bf16[512,2048]{1,0:T(8,128)(2,1)}, u32[]{:S(2)}, u32[]{:S(2)}) collective-permute-start(bf16[512,2048]{1,0:T(8,128)(2,1)} %maximum_select_fusion), channel_id=1, source_target_pairs={{0,2},{2,4},{4,6},{3,1},{5,3},{7,5},{8,10},{10,12},{12,14},{11,9},... | collective-permute-start | bytes 6291464 | tf_op jit(solution)/shard_map/ppermute | solution.py:72
  28.9 14.6 %copy-start.2 = (bf16[1,1,512,2048]{3,2,1,0:T(8,128)(2,1)S(1)}, bf16[1,1,512,2048]{3,2,1,0:T(8,128)(2,1)}, u32[]{:S(2)}) copy-start(bf16[1,1,512,2048]{3,2,1,0:T(8,128)(2,1)} %param.8) | copy-start | bytes 6291460
  42.2 28.2 %collective-permute-start.2 = (bf16[512,2048]{1,0:T(8,128)(2,1)}, bf16[512,2048]{1,0:T(8,128)(2,1)}, u32[]{:S(2)}, u32[]{:S(2)}) collective-permute-start(bf16[512,2048]{1,0:T(8,128)(2,1)} %collective-permute-done.1), channel_id=1, source_target_pairs={{2,4},{4,6},{3,1},{5,3},{10,12},{12,14},{11,9},{13,11},{18,20},{20... | collective-permute-start | bytes 6291464 | tf_op jit(solution)/shard_map/ppermute | solution.py:72
  46.0 52.6 %collective-permute-start.7 = (bf16[1024,2048]{1,0:T(8,128)(2,1)S(1)}, bf16[1024,2048]{1,0:T(8,128)(2,1)S(1)}, u32[]{:S(2)}, u32[]{:S(2)}) collective-permute-start(bf16[1024,2048]{1,0:T(8,128)(2,1)S(1)} %convolution_convert_fusion), channel_id=1, source_target_pairs={{0,1},{1,0},{2,3},{3,2},{4,5},{5,4},{6,7},{7,6},{8,9},{9,8},{10,11... | collective-permute-start | bytes 12582920 | tf_op jit(solution)/shard_map/ppermute | solution.py:104
  70.5 28.1 %collective-permute-start.3 = (bf16[512,2048]{1,0:T(8,128)(2,1)}, bf16[512,2048]{1,0:T(8,128)(2,1)S(1)}, u32[]{:S(2)}, u32[]{:S(2)}) collective-permute-start(bf16[512,2048]{1,0:T(8,128)(2,1)} %collective-permute-done.2), channel_id=1, source_target_pairs={{4,6},{3,1},{12,14},{11,9},{20,22},{19,17},{28,30},{27,25}} | collective-permute-start | bytes 6291464 | tf_op jit(solution)/shard_map/ppermute | solution.py:72
  98.6 5.0 %collective-permute-start.6 = (bf16[512,2048]{1,0:T(8,128)(2,1)}, bf16[512,2048]{1,0:T(8,128)(2,1)}, u32[]{:S(2)}, u32[]{:S(2)}) collective-permute-start(bf16[512,2048]{1,0:T(8,128)(2,1)} %collective-permute-done.2), channel_id=1, source_target_pairs={{0,1},{1,0},{2,3},{3,2},{4,5},{5,4},{6,7},{7,6},{8,9},{9,8},{10,11... | collective-permute-start | bytes 6291464 | tf_op jit(solution)/shard_map/ppermute | solution.py:75
  103.0 6.9 %collective-permute-start.4 = (bf16[512,2048]{1,0:T(8,128)(2,1)}, bf16[512,2048]{1,0:T(8,128)(2,1)}, u32[]{:S(2)}, u32[]{:S(2)}) collective-permute-start(bf16[512,2048]{1,0:T(8,128)(2,1)} %collective-permute-done.1), channel_id=1, source_target_pairs={{0,1},{1,0},{2,3},{3,2},{4,5},{5,4},{6,7},{7,6},{8,9},{9,8},{10,11... | collective-permute-start | bytes 6291464 | tf_op jit(solution)/shard_map/ppermute | solution.py:75
  103.6 6.9 %collective-permute-start.5 = (bf16[512,2048]{1,0:T(8,128)(2,1)S(1)}, bf16[512,2048]{1,0:T(8,128)(2,1)}, u32[]{:S(2)}, u32[]{:S(2)}) collective-permute-start(bf16[512,2048]{1,0:T(8,128)(2,1)S(1)} %collective-permute-done.3), channel_id=1, source_target_pairs={{0,1},{1,0},{2,3},{3,2},{4,5},{5,4},{6,7},{7,6},{8,9},{9,8},{10,11... | collective-permute-start | bytes 6291464 | tf_op jit(solution)/shard_map/ppermute | solution.py:75
  106.1 7.8 %copy-start.3 = (bf16[1,1,512,2048]{3,2,1,0:T(8,128)(2,1)S(1)}, bf16[1,1,512,2048]{3,2,1,0:T(8,128)(2,1)}, u32[]{:S(2)}) copy-start(bf16[1,1,512,2048]{3,2,1,0:T(8,128)(2,1)} %param.8) | copy-start | bytes 6291460
  122.1 53.0 %all-to-all-start = ((f32[4,128,2048]{2,1,0:T(8,128)}), f32[4,128,2048]{2,1,0:T(8,128)}, u32[]{:S(2)}, u32[]{:S(2)}) async-start(f32[4,128,2048]{2,1,0:T(8,128)} %fusion), calls=%async_computation | async-start | bytes 8388608 | tf_op jit(solution)/shard_map/all_to_all | solution.py:85
  177.8 2.6 %copy-start = (f32[256,2048]{1,0:T(8,128)S(1)}, f32[256,2048]{1,0:T(8,128)}, u32[]{:S(2)}) copy-start(f32[256,2048]{1,0:T(8,128)} %param.9) | copy-start | bytes 6291460
Sparse Core Ops, SparseCore 0:
  103.1 77.1 reduce-scatter.1

commit v11 on v10

--- a/solution.py
+++ b/solution.py
@@ -71,7 +71,20 @@
     for t in range(1, n_z):
         cur = lax.ppermute(cur, DP, flood_pairs(n_z, t))
         held.append(cur)
-    held = lax.optimization_barrier(tuple(held))
+    by_class = inputs_flat.reshape(slot_rows, n_z, CORES, rows)
+    in_mine = lax.dynamic_index_in_dim(by_class, me_c, axis=2, keepdims=False)
+    in_other = lax.dynamic_index_in_dim(by_class, 1 - me_c, axis=2, keepdims=False)
+    dims = (((0,), (0,)), ((), ()))
+    g_other = lax.dot_general(
+        in_other.reshape(slot_rows, n_z * rows), masked, dims, preferred_element_type=jnp.float32
+    )
+    g_recv = lax.ppermute(g_other.astype(jnp.bfloat16), "core", SWAP)
+    g_mine = lax.dot_general(
+        in_mine.reshape(slot_rows, n_z * rows), masked, dims, preferred_element_type=jnp.float32
+    )
+    chip = (g_mine + g_recv.astype(jnp.float32)).astype(jnp.bfloat16)
+    held, chip = lax.optimization_barrier((tuple(held), chip))
+    owned = lax.psum_scatter(chip, "z", scatter_dimension=0, tiled=True)
     other_held = lax.ppermute(held, "core", SWAP)
     parts = [chip_w]
     for r in range(1, n_z):
@@ -94,19 +107,6 @@
     token_grad = jnp.roll(token_rel.reshape(tok_count, n_z, CORES * rows), me_z, axis=1)
     token_grad = token_grad.reshape(tok_count, width)
 
-    by_class = inputs_flat.reshape(slot_rows, n_z, CORES, rows)
-    in_mine = lax.dynamic_index_in_dim(by_class, me_c, axis=2, keepdims=False)
-    in_other = lax.dynamic_index_in_dim(by_class, 1 - me_c, axis=2, keepdims=False)
-    dims = (((0,), (0,)), ((), ()))
-    g_other = lax.dot_general(
-        in_other.reshape(slot_rows, n_z * rows), masked, dims, preferred_element_type=jnp.float32
-    )
-    g_recv = lax.ppermute(g_other.astype(jnp.bfloat16), "core", SWAP)
-    g_mine = lax.dot_general(
-        in_mine.reshape(slot_rows, n_z * rows), masked, dims, preferred_element_type=jnp.float32
-    )
-    chip = (g_mine + g_recv.astype(jnp.float32)).astype(jnp.bfloat16)
-    owned = lax.psum_scatter(chip, "z", scatter_dimension=0, tiled=True)
     token_grad, owned = lax.optimization_barrier((token_grad, owned))
     owned = owned.astype(jnp.float32)
     new_weight, new_first, new_second = adamw(weight, moment_one, moment_two, owned / loss_scale)

time: 196 us -> 192 us (0.980); the launches traced: 194 us -> 192 us
  waiting for transfers between devices: 119 us -> 115 us
    ppermute x3, waiting for transfers between devices: 64.3 us -> 60 us  [shards(): cur = lax.ppermute(cur, DP, flood_pairs(n_z, t))]
    ppermute x3, waiting for transfers between devices: 4.38 us -> 7.36 us  [shards(): other_held = lax.ppermute(held, 'core', SWAP)]
    ppermute x1, waiting for transfers between devices: 2.61 us -> 0.01 us  [shards(): partner = lax.ppermute(wbf, 'core', SWAP)]
  transfers between devices with their start and end apart: 10 -> 10, of which waited for: 7 -> 6; matrix products, arithmetic and copies ran while one was open for 17% -> 17% of each run, Pallas kernels for 0% -> 0%
where the time goes in v11:
time: 192 us
  waiting for transfers between devices  115 us (60%)
  other arithmetic  21 us (11%)
  matrix products  15.3 us (8%)
  between operations  14.9 us (8%)
  starting transfers between devices  11.1 us (6%)
  local copies, waits for them, and re-layouts  7.38 us (4%)
  blocking collectives  7.37 us (4%)
    ppermute x3, waiting for transfers between devices, shards(): cur = lax.ppermute(cur, DP, flood_pairs(n_z, t))  60 us
    all_to_all x1, waiting for transfers between devices, shards(): lax.all_to_all(sent, 'expert', split_axis=0, concat_axis=0, tiled=True)  47.4 us
    dot_general x1, matrix products, shards(): lax.dot_general(masked, w_rel, cols, preferred_element_type=jnp.float32)  8.17 us
    unnamed x1, blocking collectives  7.37 us
    ppermute x3, waiting for transfers between devices, shards(): other_held = lax.ppermute(held, 'core', SWAP)  7.36 us
    sub x1, other arithmetic, adamw(): new_weight = weight - learn_rate * (update + decay * weight)  6.42 us
    unnamed x16, local copies, waits for them, and re-layouts  6.01 us
    select_n x2, other arithmetic, shards(): parts.append(jnp.where(me_z + r < n_z, up, down))  5.49 us
  transfers between devices with their start and end apart: 10, of which 6 were waited for; matrix products, arithmetic and copies ran while one was open for 17% of the time, Pallas kernels for 0%

profile of v11, /device:TPU:24, one launch (start us, length us, event | category | flops | bytes accessed | tf_op | source)
XLA Modules:
  0.0 191.9 jit_solution(9243755224354259718)
XLA Ops:
  7.2 1.7 convert_element_type.42
  9.5 0.6 reduce-window.6
  10.5 0.6 dynamic-slice
  11.8 2.3 %maximum_select_fusion = bf16[512,2048]{1,0:T(8,128)(2,1)} fusion(bf16[256,2048]{1,0:T(8,128)(2,1)S(1)} %collective-permute-done, bf16[256,2048]{1,0:T(8,128)(2,1)S(1)} %convert_element_type.42, pred[]{:T(512)S(6)} %eq.74), kind=kLoop, calls=%fused_computation.18 | loop fusion | flops 9437184 | bytes 4194305 | tf_op jit(solution)/shard_map/jit(_where)/select_n | solution.py:66
  14.1 1.3 collective-permute-start.1
  15.6 0.2 dynamic-update-slice
  15.8 7.4 %all-reduce = s32[8]{0:T(128)S(1)} all-reduce(s32[8]{0:T(128)S(1)} %dynamic-update-slice), channel_id=2, replica_groups=mesh['expert'=4,'z'=4,'core'=2] {'expert'}, use_global_device_ids=true, to_apply=%add | all-reduce | flops 8 | bytes 64
  23.3 2.9 %copy.29 = bf16[1,1,512,2048]{2,3,1,0:T(8,128)(2,1)S(1)} copy(bf16[1,1,512,2048]{3,2,1,0:T(8,128)(2,1)} %param.7) | data formatting | bytes 4194304 | tf_op args[1]
  26.3 0.2 constant_dynamic-slice_fusion.1
  26.6 1.3 copy-done.2
  27.9 2.4 %convolution_convert_fusion = bf16[1024,2048]{1,0:T(8,128)(2,1)S(1)} fusion(bf16[512,1024]{0,1:T(8,128)(2,1)S(1)} %bitcast.44, bf16[1,1,512,2048]{3,2,1,0:T(8,128)(2,1)S(1)} %copy-done.2, pred[512]{0:T(512)(128)(4,1)S(1)} %get-tuple-element.26), kind=kOutput, calls=%fused_computation.10 | convolution fusion | flops 2150629376 | bytes 7340544 | tf_op jit(solution)/shard_map/dot_general | solution.py:78
  30.3 1.4 collective-permute-start.4
  31.7 10.6 %collective-permute-done.1 = bf16[512,2048]{1,0:T(8,128)(2,1)} collective-permute-done((bf16[512,2048]{1,0:T(8,128)(2,1)}, bf16[512,2048]{1,0:T(8,128)(2,1)}, u32[]{:S(2)}, u32[]{:S(2)}) %collective-permute-start.1) | collective-permute-done | bytes 2097184 | tf_op jit(solution)/shard_map/ppermute | solution.py:72
  42.3 1.3 collective-permute-start.2
  43.6 26.9 %collective-permute-done.2 = bf16[512,2048]{1,0:T(8,128)(2,1)} collective-permute-done((bf16[512,2048]{1,0:T(8,128)(2,1)}, bf16[512,2048]{1,0:T(8,128)(2,1)}, u32[]{:S(2)}, u32[]{:S(2)}) %collective-permute-start.2) | collective-permute-done | bytes 2097184 | tf_op jit(solution)/shard_map/ppermute | solution.py:72
  70.6 1.3 collective-permute-start.3
  71.9 4.4 %add_convert_fusion = bf16[1024,2048]{1,0:T(8,128)(2,1)} fusion(bf16[1024,2048]{1,0:T(8,128)(2,1)S(1)} %collective-permute-done.4, bf16[512,1024]{0,1:T(8,128)(2,1)S(1)} %bitcast.43, bf16[1,1,512,2048]{3,2,1,0:T(8,128)(2,1)S(1)} %copy-done.2, pred[512]{0:T(512)(128)(4,1)S(1)} %get-tuple-element.26), kind=kOutput, calls=%fused_computation.8 | convolution fusion | flops 2154823680 | bytes 11534848 | tf_op jit(solution)/shard_map/dot_general | solution.py:82
  76.2 22.5 %collective-permute-done.3 = bf16[512,2048]{1,0:T(8,128)(2,1)S(1)} collective-permute-done((bf16[512,2048]{1,0:T(8,128)(2,1)}, bf16[512,2048]{1,0:T(8,128)(2,1)S(1)}, u32[]{:S(2)}, u32[]{:S(2)}) %collective-permute-start.3) | collective-permute-done | bytes 2097184 | tf_op jit(solution)/shard_map/ppermute | solution.py:72
  98.7 0.6 collective-permute-start.5
  99.4 3.8 %collective-permute-done.7 = bf16[512,2048]{1,0:T(8,128)(2,1)} collective-permute-done((bf16[512,2048]{1,0:T(8,128)(2,1)}, bf16[512,2048]{1,0:T(8,128)(2,1)}, u32[]{:S(2)}, u32[]{:S(2)}) %collective-permute-start.7) | collective-permute-done | bytes 2097184 | tf_op jit(solution)/shard_map/ppermute | solution.py:88
  103.2 2.4 %select_select_fusion.1 = bf16[512,2048]{1,0:T(8,128)(2,1)S(1)} fusion(bf16[512,2048]{1,0:T(8,128)(2,1)} %collective-permute-done.2, bf16[512,2048]{1,0:T(8,128)(2,1)} %collective-permute-done.7, pred[]{:T(512)S(6)} %lt.56, pred[]{:T(512)S(6)} %eq.74), kind=kLoop, calls=%fused_computation.24 | loop fusion | flops 3145728 | bytes 6291458 | tf_op jit(solution)/shard_map/jit(_where)/select_n | solution.py:93
  105.6 3.5 %collective-permute-done.5 = bf16[512,2048]{1,0:T(8,128)(2,1)} collective-permute-done((bf16[512,2048]{1,0:T(8,128)(2,1)}, bf16[512,2048]{1,0:T(8,128)(2,1)}, u32[]{:S(2)}, u32[]{:S(2)}) %collective-permute-start.5) | collective-permute-done | bytes 2097184 | tf_op jit(solution)/shard_map/ppermute | solution.py:88
  109.2 3.0 %select_select_fusion.2 = (bf16[512,2048]{1,0:T(8,128)(2,1)S(1)}, bf16[512,2048]{1,0:T(8,128)(2,1)S(1)}) fusion(bf16[512,2048]{1,0:T(8,128)(2,1)S(1)} %collective-permute-done.3, bf16[512,2048]{1,0:T(8,128)(2,1)} %collective-permute-done.6, bf16[512,2048]{1,0:T(8,128)(2,1)} %collective-permute-done.5, bf16[512,2048]{1,0:T(8,128)(2,1)} %collective-permute-done.1, ...), kind=kLoop, calls=%fused_computation.25 | loop fusion | flops 6291456 | bytes 12582915 | tf_op jit(solution)/shard_map/jit(_where)/select_n | solution.py:93
  112.2 8.2 %fusion = f32[4,128,2048]{2,1,0:T(8,128)} fusion(bf16[512,2048]{1,0:T(8,128)(2,1)S(1)} %get-tuple-element.22, bf16[512,2048]{1,0:T(8,128)(2,1)S(1)} %select_select_fusion.1, bf16[512,2048]{1,0:T(8,128)(2,1)S(1)} %get-tuple-element.21, bf16[512,2048]{1,0:T(8,128)(2,1)} %maximum_select_fusion, bf16[4,128,2048]{2,1,0:T(8,128)(2,1)S(1)} %bitcast.47, ...), kind=kOutput, calls=%fused_computation.1 | convolution fusion | flops 4329570304 | bytes 14680576 | tf_op jit(solution)/shard_map/dot_general | solution.py:96
  120.4 5.0 %all-to-all-start = ((f32[4,128,2048]{2,1,0:T(8,128)}), f32[4,128,2048]{2,1,0:T(8,128)}, u32[]{:S(2)}, u32[]{:S(2)}) async-start(f32[4,128,2048]{2,1,0:T(8,128)} %fusion), calls=%async_computation | async-start | bytes 8388608 | tf_op jit(solution)/shard_map/all_to_all | solution.py:98
  125.8 47.4 %all-to-all-done = f32[4,128,2048]{2,1,0:T(8,128)} async-done(((f32[4,128,2048]{2,1,0:T(8,128)}), f32[4,128,2048]{2,1,0:T(8,128)}, u32[]{:S(2)}, u32[]{:S(2)}) %all-to-all-start) | async-done | bytes 4194336 | tf_op jit(solution)/shard_map/all_to_all | solution.py:98
  173.3 2.7 %bitcast_reduce_fusion = bf16[2,128,2048]{2,1,0:T(8,128)(2,1)S(1)} fusion(f32[4,128,2048]{2,1,0:T(8,128)} %all-to-all-done), kind=kLoop, calls=%fused_computation.9 | loop fusion | flops 524288 | bytes 5242880 | tf_op jit(solution)/shard_map/reduce_sum | solution.py:99
  176.0 0.3 convolution_convert_fusion.1
  176.3 0.4 reshape.105
  176.7 1.0 fusion.18
  177.7 0.9 copy.31
  178.6 6.4 %multiply_subtract_fusion = (f32[256,2048]{1,0:T(8,128)}, f32[256,2048]{1,0:T(8,128)}, f32[256,2048]{1,0:T(8,128)}) fusion(f32[256,2048]{1,0:T(8,128)S(1)} %copy-done, bf16[256,2048]{1,0:T(8,128)(2,1)} %reduce-scatter.2.cloned.1.call-done, f32[256,2048]{1,0:T(8,128)} %param.10, f32[256,2048]{1,0:T(8,128)} %param.11), kind=kLoop, calls=%fused_computation.22 | loop fusion | flops 8912896 | bytes 13631488 | tf_op jit(solution)/shard_map/sub | solution.py:23
  (35 shorter events, 1.8 us)
Async XLA Ops:
  7.2 3.3 %copy-start.4 = (u32[32]{0:T(128)S(1)}, u32[32]{0:T(128)}, u32[]{:S(2)}) copy-start(u32[32]{0:T(128)} %constant.98) | copy-start | bytes 388
  7.2 1.9 copy-start.1
  7.2 171.4 %reduce-scatter.2.cloned.1.call-start = ((), (), s32[]{:S(2)}) async-start(), calls=%async_computation.2 | async-start | bytes 5242880 | tf_op jit(solution)/shard_map/reduce_scatter | solution.py:87
  9.0 2.8 %collective-permute-start = (bf16[256,2048]{1,0:T(8,128)(2,1)S(1)}, bf16[256,2048]{1,0:T(8,128)(2,1)S(1)}, u32[]{:S(2)}, u32[]{:S(2)}) collective-permute-start(bf16[256,2048]{1,0:T(8,128)(2,1)S(1)} %convert_element_type.42), channel_id=1, source_target_pairs={{0,1},{1,0},{2,3},{3,2},{4,5},{5,4},{6,7},{7,6},{8,9},{9,8},{10,11... | collective-permute-start | bytes 3145736 | tf_op jit(solution)/shard_map/ppermute | solution.py:65
  14.1 28.2 %collective-permute-start.1 = (bf16[512,2048]{1,0:T(8,128)(2,1)}, bf16[512,2048]{1,0:T(8,128)(2,1)}, u32[]{:S(2)}, u32[]{:S(2)}) collective-permute-start(bf16[512,2048]{1,0:T(8,128)(2,1)} %maximum_select_fusion), channel_id=1, source_target_pairs={{0,2},{2,4},{4,6},{3,1},{5,3},{7,5},{8,10},{10,12},{12,14},{11,9},... | collective-permute-start | bytes 6291464 | tf_op jit(solution)/shard_map/ppermute | solution.py:72
  26.3 1.6 copy-start.2
  30.3 41.6 %collective-permute-start.4 = (bf16[1024,2048]{1,0:T(8,128)(2,1)S(1)}, bf16[1024,2048]{1,0:T(8,128)(2,1)S(1)}, u32[]{:S(2)}, u32[]{:S(2)}) collective-permute-start(bf16[1024,2048]{1,0:T(8,128)(2,1)S(1)} %convolution_convert_fusion), channel_id=1, source_target_pairs={{0,1},{1,0},{2,3},{3,2},{4,5},{5,4},{6,7},{7,6},{8,9},{9,8},{10,11... | collective-permute-start | bytes 12582920 | tf_op jit(solution)/shard_map/ppermute | solution.py:81
  42.3 28.2 %collective-permute-start.2 = (bf16[512,2048]{1,0:T(8,128)(2,1)}, bf16[512,2048]{1,0:T(8,128)(2,1)}, u32[]{:S(2)}, u32[]{:S(2)}) collective-permute-start(bf16[512,2048]{1,0:T(8,128)(2,1)} %collective-permute-done.1), channel_id=1, source_target_pairs={{2,4},{4,6},{3,1},{5,3},{10,12},{12,14},{11,9},{13,11},{18,20},{20... | collective-permute-start | bytes 6291464 | tf_op jit(solution)/shard_map/ppermute | solution.py:72
  70.6 28.1 %collective-permute-start.3 = (bf16[512,2048]{1,0:T(8,128)(2,1)}, bf16[512,2048]{1,0:T(8,128)(2,1)S(1)}, u32[]{:S(2)}, u32[]{:S(2)}) collective-permute-start(bf16[512,2048]{1,0:T(8,128)(2,1)} %collective-permute-done.2), channel_id=1, source_target_pairs={{4,6},{3,1},{12,14},{11,9},{20,22},{19,17},{28,30},{27,25}} | collective-permute-start | bytes 6291464 | tf_op jit(solution)/shard_map/ppermute | solution.py:72
  98.7 4.5 %collective-permute-start.7 = (bf16[512,2048]{1,0:T(8,128)(2,1)}, bf16[512,2048]{1,0:T(8,128)(2,1)}, u32[]{:S(2)}, u32[]{:S(2)}) collective-permute-start(bf16[512,2048]{1,0:T(8,128)(2,1)} %collective-permute-done.2), channel_id=1, source_target_pairs={{0,1},{1,0},{2,3},{3,2},{4,5},{5,4},{6,7},{7,6},{8,9},{9,8},{10,11... | collective-permute-start | bytes 6291464 | tf_op jit(solution)/shard_map/ppermute | solution.py:88
  98.7 10.5 %collective-permute-start.5 = (bf16[512,2048]{1,0:T(8,128)(2,1)}, bf16[512,2048]{1,0:T(8,128)(2,1)}, u32[]{:S(2)}, u32[]{:S(2)}) collective-permute-start(bf16[512,2048]{1,0:T(8,128)(2,1)} %collective-permute-done.1), channel_id=1, source_target_pairs={{0,1},{1,0},{2,3},{3,2},{4,5},{5,4},{6,7},{7,6},{8,9},{9,8},{10,11... | collective-permute-start | bytes 6291464 | tf_op jit(solution)/shard_map/ppermute | solution.py:88
  99.3 9.9 %collective-permute-start.6 = (bf16[512,2048]{1,0:T(8,128)(2,1)S(1)}, bf16[512,2048]{1,0:T(8,128)(2,1)}, u32[]{:S(2)}, u32[]{:S(2)}) collective-permute-start(bf16[512,2048]{1,0:T(8,128)(2,1)S(1)} %collective-permute-done.3), channel_id=1, source_target_pairs={{0,1},{1,0},{2,3},{3,2},{4,5},{5,4},{6,7},{7,6},{8,9},{9,8},{10,11... | collective-permute-start | bytes 6291464 | tf_op jit(solution)/shard_map/ppermute | solution.py:88
  105.6 6.6 %copy-start.3 = (bf16[1,1,512,2048]{3,2,1,0:T(8,128)(2,1)S(1)}, bf16[1,1,512,2048]{3,2,1,0:T(8,128)(2,1)}, u32[]{:S(2)}) copy-start(bf16[1,1,512,2048]{3,2,1,0:T(8,128)(2,1)} %param.8) | copy-start | bytes 6291460
  120.4 52.8 %all-to-all-start = ((f32[4,128,2048]{2,1,0:T(8,128)}), f32[4,128,2048]{2,1,0:T(8,128)}, u32[]{:S(2)}, u32[]{:S(2)}) async-start(f32[4,128,2048]{2,1,0:T(8,128)} %fusion), calls=%async_computation | async-start | bytes 8388608 | tf_op jit(solution)/shard_map/all_to_all | solution.py:98
  176.0 2.6 %copy-start = (f32[256,2048]{1,0:T(8,128)S(1)}, f32[256,2048]{1,0:T(8,128)}, u32[]{:S(2)}) copy-start(f32[256,2048]{1,0:T(8,128)} %param.9) | copy-start | bytes 6291460
Sparse Core Ops, SparseCore 0:
  98.8 77.1 reduce-scatter.1

commit v12 on v11

--- a/solution.py
+++ b/solution.py
@@ -86,16 +86,22 @@
     held, chip = lax.optimization_barrier((tuple(held), chip))
     owned = lax.psum_scatter(chip, "z", scatter_dimension=0, tiled=True)
     other_held = lax.ppermute(held, "core", SWAP)
-    parts = [chip_w]
+    cols = (((1,), (1,)), ((), ()))
+    own_rows = lax.dot_general(masked, chip_w, cols, preferred_element_type=jnp.float32)
+    recv_own = lax.all_to_all(
+        own_rows.reshape(n_expert, capacity, CORES * rows), "expert", 0, 0, tiled=True
+    )
+    parts = []
     for r in range(1, n_z):
         up = jnp.where(me_c == 0, other_held[r - 1], held[r - 1])
         down = jnp.where(me_c == 0, held[n_z - r - 1], other_held[n_z - r - 1])
         parts.append(jnp.where(me_z + r < n_z, up, down))
-    w_rel = jnp.concatenate(parts, axis=0)
-    cols = (((1,), (1,)), ((), ()))
-    partial_rows = lax.dot_general(masked, w_rel, cols, preferred_element_type=jnp.float32)
-    sent = partial_rows.reshape(n_expert, capacity, width)
-    received = lax.all_to_all(sent, "expert", split_axis=0, concat_axis=0, tiled=True)
+    w_rest = jnp.concatenate(parts, axis=0)
+    rest_rows = lax.dot_general(masked, w_rest, cols, preferred_element_type=jnp.float32)
+    recv_rest = lax.all_to_all(
+        rest_rows.reshape(n_expert, capacity, width - CORES * rows), "expert", 0, 0, tiled=True
+    )
+    received = jnp.concatenate([recv_own, recv_rest], axis=2)
     paired = jnp.sum(received.reshape(experts, 2, capacity, width), axis=1).astype(jnp.bfloat16)
     target = (routes * capacity + slots).reshape(tok_count, top_count, 1)
     choose = jnp.sum(

time: 192 us -> 192 us (level); the launches traced: 192 us -> 189 us
  waiting for transfers between devices: 115 us -> 108 us
  starting transfers between devices: 11.1 us -> 13.7 us
    reduce_scatter x1, waiting for transfers between devices: 0.01 us -> 8.78 us  [shards(): owned = lax.psum_scatter(chip, 'z', scatter_dimension=0, tiled=True)]
    all_to_all x1 -> x2, waiting for transfers between devices: 47.4 us -> 38.7 us  [the longest x1 35.5 us: shards(): lax.all_to_all(rest_rows.reshape(n_expert, capacity, width - CORES * rows...]
    ppermute x3, waiting for transfers between devices: 7.36 us -> 0.01 us  [shards(): other_held = lax.ppermute(held, 'core', SWAP)]
    all_to_all x1 -> x2, starting transfers between devices: 5.02 us -> 7.63 us  [the longest x1 3.9 us: shards(): lax.all_to_all(rest_rows.reshape(n_expert, capacity, width - CORES * rows...]
    dot_general x1 -> x2, matrix products: 8.17 us -> 9.74 us  [the longest x1 5.25 us: shards(): lax.dot_general(masked, w_rest, cols, preferred_element_type=jnp.float32)]
    unnamed x16 -> x18, local copies, waits for them, and re-layouts: 6.01 us -> 7.21 us
  transfers between devices with their start and end apart: 10 -> 11, of which waited for: 6 -> 6; matrix products, arithmetic and copies ran while one was open for 17% -> 17% of each run, Pallas kernels for 0% -> 0%
where the time goes in v12:
time: 192 us; the launch traced here: 189 us
  waiting for transfers between devices  108 us (56%)
  other arithmetic  20.2 us (11%)
  matrix products  16.8 us (9%)
  between operations  15 us (8%)
  starting transfers between devices  13.7 us (7%)
  local copies, waits for them, and re-layouts  8.59 us (4%)
  blocking collectives  7.37 us (4%)
    ppermute x3, waiting for transfers between devices, shards(): cur = lax.ppermute(cur, DP, flood_pairs(n_z, t))  60 us
    all_to_all x1, waiting for transfers between devices, shards(): lax.all_to_all(rest_rows.reshape(n_expert, capacity, width - CORES * rows...  35.5 us
    reduce_scatter x1, waiting for transfers between devices, shards(): owned = lax.psum_scatter(chip, 'z', scatter_dimension=0, tiled=True)  8.78 us
    unnamed x1, blocking collectives  7.37 us
    unnamed x18, local copies, waits for them, and re-layouts  7.21 us
    sub x1, other arithmetic, adamw(): new_weight = weight - learn_rate * (update + decay * weight)  6.42 us
    select_n x2, other arithmetic, shards(): parts.append(jnp.where(me_z + r < n_z, up, down))  5.63 us
    dot_general x1, matrix products, shards(): lax.dot_general(masked, w_rest, cols, preferred_element_type=jnp.float32)  5.25 us
  transfers between devices with their start and end apart: 11, of which 6 were waited for; matrix products, arithmetic and copies ran while one was open for 17% of the time, Pallas kernels for 0%

profile of v12, /device:TPU:24, one launch (start us, length us, event | category | flops | bytes accessed | tf_op | source)
XLA Modules:
  0.0 189.1 jit_solution(14724514678075123512)
XLA Ops:
  7.2 1.7 convert_element_type.42
  9.5 0.6 reduce-window.6
  10.5 0.6 dynamic-slice
  11.8 2.3 %maximum_select_fusion = bf16[512,2048]{1,0:T(8,128)(2,1)} fusion(bf16[256,2048]{1,0:T(8,128)(2,1)S(1)} %collective-permute-done, bf16[256,2048]{1,0:T(8,128)(2,1)S(1)} %convert_element_type.42, pred[]{:T(512)S(6)} %eq.74), kind=kLoop, calls=%fused_computation.17 | loop fusion | flops 9437184 | bytes 4194305 | tf_op jit(solution)/shard_map/jit(_where)/select_n | solution.py:66
  14.1 1.3 collective-permute-start.1
  15.8 7.4 %all-reduce = s32[8]{0:T(128)S(1)} all-reduce(s32[8]{0:T(128)S(1)} %dynamic-update-slice), channel_id=2, replica_groups=mesh['expert'=4,'z'=4,'core'=2] {'expert'}, use_global_device_ids=true, to_apply=%add | all-reduce | flops 8 | bytes 64
  23.3 2.9 %copy.29 = bf16[1,1,512,2048]{2,3,1,0:T(8,128)(2,1)S(1)} copy(bf16[1,1,512,2048]{3,2,1,0:T(8,128)(2,1)} %param.7) | data formatting | bytes 4194304 | tf_op args[1]
  26.6 1.3 copy-done.3
  27.9 2.4 %convolution_convert_fusion = bf16[1024,2048]{1,0:T(8,128)(2,1)S(1)} fusion(bf16[512,1024]{0,1:T(8,128)(2,1)S(1)} %bitcast.47, bf16[1,1,512,2048]{3,2,1,0:T(8,128)(2,1)S(1)} %copy-done.3, pred[512]{0:T(512)(128)(4,1)S(1)} %get-tuple-element.26), kind=kOutput, calls=%fused_computation.9 | convolution fusion | flops 2150629376 | bytes 7340544 | tf_op jit(solution)/shard_map/dot_general | solution.py:78
  30.3 1.4 collective-permute-start.4
  31.7 10.6 %collective-permute-done.1 = bf16[512,2048]{1,0:T(8,128)(2,1)} collective-permute-done((bf16[512,2048]{1,0:T(8,128)(2,1)}, bf16[512,2048]{1,0:T(8,128)(2,1)}, u32[]{:S(2)}, u32[]{:S(2)}) %collective-permute-start.1) | collective-permute-done | bytes 2097184 | tf_op jit(solution)/shard_map/ppermute | solution.py:72
  42.3 1.3 collective-permute-start.2
  43.6 26.9 %collective-permute-done.2 = bf16[512,2048]{1,0:T(8,128)(2,1)} collective-permute-done((bf16[512,2048]{1,0:T(8,128)(2,1)}, bf16[512,2048]{1,0:T(8,128)(2,1)}, u32[]{:S(2)}, u32[]{:S(2)}) %collective-permute-start.2) | collective-permute-done | bytes 2097184 | tf_op jit(solution)/shard_map/ppermute | solution.py:72
  70.6 1.3 collective-permute-start.3
  71.9 4.4 %add_convert_fusion = bf16[1024,2048]{1,0:T(8,128)(2,1)} fusion(bf16[1024,2048]{1,0:T(8,128)(2,1)S(1)} %collective-permute-done.4, bf16[512,1024]{0,1:T(8,128)(2,1)S(1)} %bitcast.46, bf16[1,1,512,2048]{3,2,1,0:T(8,128)(2,1)S(1)} %copy-done.3, pred[512]{0:T(512)(128)(4,1)S(1)} %get-tuple-element.26), kind=kOutput, calls=%fused_computation | convolution fusion | flops 2154823680 | bytes 11534848 | tf_op jit(solution)/shard_map/dot_general | solution.py:82
  76.2 22.5 %collective-permute-done.3 = bf16[512,2048]{1,0:T(8,128)(2,1)S(1)} collective-permute-done((bf16[512,2048]{1,0:T(8,128)(2,1)}, bf16[512,2048]{1,0:T(8,128)(2,1)S(1)}, u32[]{:S(2)}, u32[]{:S(2)}) %collective-permute-start.3) | collective-permute-done | bytes 2097184 | tf_op jit(solution)/shard_map/ppermute | solution.py:72
  98.8 0.5 collective-permute-start.5
  99.4 4.5 %fusion.13 = f32[4,128,512]{2,1,0:T(8,128)} fusion(bf16[512,2048]{1,0:T(8,128)(2,1)} %maximum_select_fusion, bf16[4,128,2048]{2,1,0:T(8,128)(2,1)} %bitcast.50, pred[4,128]{1,0:T(4,128)(4,1)S(1)} %get-tuple-element.25), kind=kOutput, calls=%fused_computation.21 | convolution fusion | flops 1074790400 | bytes 5243392 | tf_op jit(solution)/shard_map/dot_general | solution.py:90
  103.8 3.7 %all-to-all-start = ((f32[4,128,512]{2,1,0:T(8,128)}), f32[4,128,512]{2,1,0:T(8,128)S(1)}, u32[]{:S(2)}, u32[]{:S(2)}) async-start(f32[4,128,512]{2,1,0:T(8,128)} %fusion.13), calls=%async_computation | async-start | bytes 2097152 | tf_op jit(solution)/shard_map/all_to_all | solution.py:91
  107.6 2.4 %select_select_fusion.1 = bf16[512,2048]{1,0:T(8,128)(2,1)S(1)} fusion(bf16[512,2048]{1,0:T(8,128)(2,1)} %collective-permute-done.2, bf16[512,2048]{1,0:T(8,128)(2,1)} %collective-permute-done.7, pred[]{:T(512)S(6)} %lt.56, pred[]{:T(512)S(6)} %eq.74), kind=kLoop, calls=%fused_computation.25 | loop fusion | flops 3145728 | bytes 6291458 | tf_op jit(solution)/shard_map/jit(_where)/select_n | solution.py:98
  110.1 3.2 %select_select_fusion.2 = (bf16[512,2048]{1,0:T(8,128)(2,1)S(1)}, bf16[512,2048]{1,0:T(8,128)(2,1)S(1)}) fusion(bf16[512,2048]{1,0:T(8,128)(2,1)S(1)} %collective-permute-done.3, bf16[512,2048]{1,0:T(8,128)(2,1)} %collective-permute-done.6, bf16[512,2048]{1,0:T(8,128)(2,1)} %collective-permute-done.5, bf16[512,2048]{1,0:T(8,128)(2,1)} %collective-permute-done.1, ...), kind=kLoop, calls=%fused_computation.26 | loop fusion | flops 6291456 | bytes 12582915 | tf_op jit(solution)/shard_map/jit(_where)/select_n | solution.py:98
  113.5 5.3 %fusion = f32[4,128,1536]{2,1,0:T(8,128)} fusion(bf16[512,2048]{1,0:T(8,128)(2,1)S(1)} %get-tuple-element.22, bf16[512,2048]{1,0:T(8,128)(2,1)S(1)} %select_select_fusion.1, bf16[512,2048]{1,0:T(8,128)(2,1)S(1)} %get-tuple-element.21, bf16[4,128,2048]{2,1,0:T(8,128)(2,1)S(1)} %bitcast.51, pred[4,128]{1,0:T(4,128)(4,1)S(1)} %get-tuple-element.25), kind=kOutput, calls=%fused_computation.2 | convolution fusion | flops 3241148416 | bytes 11534848 | tf_op jit(solution)/shard_map/dot_general | solution.py:100
  118.7 3.2 %all-to-all-done = f32[4,128,512]{2,1,0:T(8,128)S(1)} async-done(((f32[4,128,512]{2,1,0:T(8,128)}), f32[4,128,512]{2,1,0:T(8,128)S(1)}, u32[]{:S(2)}, u32[]{:S(2)}) %all-to-all-start) | async-done | bytes 1048608 | tf_op jit(solution)/shard_map/all_to_all | solution.py:91
  121.9 1.0 copy-done.1
  122.9 3.9 %all-to-all-start.1 = ((f32[4,128,1536]{2,1,0:T(8,128)}), f32[4,128,1536]{2,1,0:T(8,128)S(1)}, u32[]{:S(2)}, u32[]{:S(2)}) async-start(f32[4,128,1536]{2,1,0:T(8,128)} %fusion), calls=%async_computation.1 | async-start | bytes 6291456 | tf_op jit(solution)/shard_map/all_to_all | solution.py:101
  127.2 35.5 %all-to-all-done.1 = f32[4,128,1536]{2,1,0:T(8,128)S(1)} async-done(((f32[4,128,1536]{2,1,0:T(8,128)}), f32[4,128,1536]{2,1,0:T(8,128)S(1)}, u32[]{:S(2)}, u32[]{:S(2)}) %all-to-all-start.1) | async-done | bytes 3145760 | tf_op jit(solution)/shard_map/all_to_all | solution.py:101
  162.7 1.8 bitcast_reduce_fusion
  164.8 0.4 reshape.113
  165.2 1.0 fusion.17
  166.2 0.9 copy.31
  167.1 8.8 %reduce-scatter.2.cloned.1.call-done = bf16[256,2048]{1,0:T(8,128)(2,1)} async-done(((bf16[1024,2048]{1,0:T(8,128)(2,1)}), bf16[256,2048]{1,0:T(8,128)(2,1)}) %reduce-scatter.2.cloned.1.call-update) | async-done | bytes 1048592 | tf_op jit(solution)/shard_map/reduce_scatter | solution.py:87
  175.9 6.4 %multiply_subtract_fusion = (f32[256,2048]{1,0:T(8,128)}, f32[256,2048]{1,0:T(8,128)}, f32[256,2048]{1,0:T(8,128)}) fusion(f32[256,2048]{1,0:T(8,128)S(1)} %copy-done, bf16[256,2048]{1,0:T(8,128)(2,1)} %reduce-scatter.2.cloned.1.call-done, f32[256,2048]{1,0:T(8,128)} %param.10, f32[256,2048]{1,0:T(8,128)} %param.11), kind=kLoop, calls=%fused_computation.23 | loop fusion | flops 8912896 | bytes 13631488 | tf_op jit(solution)/shard_map/sub | solution.py:23
  (40 shorter events, 2.9 us)
Async XLA Ops:
  7.2 3.3 %copy-start.5 = (u32[32]{0:T(128)S(1)}, u32[32]{0:T(128)}, u32[]{:S(2)}) copy-start(u32[32]{0:T(128)} %constant.98) | copy-start | bytes 388
  7.2 1.9 copy-start.2
  7.2 168.7 %reduce-scatter.2.cloned.1.call-start = ((), (), s32[]{:S(2)}) async-start(), calls=%async_computation.3 | async-start | bytes 5242880 | tf_op jit(solution)/shard_map/reduce_scatter | solution.py:87
  9.0 2.8 %collective-permute-start = (bf16[256,2048]{1,0:T(8,128)(2,1)S(1)}, bf16[256,2048]{1,0:T(8,128)(2,1)S(1)}, u32[]{:S(2)}, u32[]{:S(2)}) collective-permute-start(bf16[256,2048]{1,0:T(8,128)(2,1)S(1)} %convert_element_type.42), channel_id=1, source_target_pairs={{0,1},{1,0},{2,3},{3,2},{4,5},{5,4},{6,7},{7,6},{8,9},{9,8},{10,11... | collective-permute-start | bytes 3145736 | tf_op jit(solution)/shard_map/ppermute | solution.py:65
  14.1 28.2 %collective-permute-start.1 = (bf16[512,2048]{1,0:T(8,128)(2,1)}, bf16[512,2048]{1,0:T(8,128)(2,1)}, u32[]{:S(2)}, u32[]{:S(2)}) collective-permute-start(bf16[512,2048]{1,0:T(8,128)(2,1)} %maximum_select_fusion), channel_id=1, source_target_pairs={{0,2},{2,4},{4,6},{3,1},{5,3},{7,5},{8,10},{10,12},{12,14},{11,9},... | collective-permute-start | bytes 6291464 | tf_op jit(solution)/shard_map/ppermute | solution.py:72
  26.3 1.6 copy-start.3
  30.3 41.6 %collective-permute-start.4 = (bf16[1024,2048]{1,0:T(8,128)(2,1)S(1)}, bf16[1024,2048]{1,0:T(8,128)(2,1)S(1)}, u32[]{:S(2)}, u32[]{:S(2)}) collective-permute-start(bf16[1024,2048]{1,0:T(8,128)(2,1)S(1)} %convolution_convert_fusion), channel_id=1, source_target_pairs={{0,1},{1,0},{2,3},{3,2},{4,5},{5,4},{6,7},{7,6},{8,9},{9,8},{10,11... | collective-permute-start | bytes 12582920 | tf_op jit(solution)/shard_map/ppermute | solution.py:81
  42.3 28.2 %collective-permute-start.2 = (bf16[512,2048]{1,0:T(8,128)(2,1)}, bf16[512,2048]{1,0:T(8,128)(2,1)}, u32[]{:S(2)}, u32[]{:S(2)}) collective-permute-start(bf16[512,2048]{1,0:T(8,128)(2,1)} %collective-permute-done.1), channel_id=1, source_target_pairs={{2,4},{4,6},{3,1},{5,3},{10,12},{12,14},{11,9},{13,11},{18,20},{20... | collective-permute-start | bytes 6291464 | tf_op jit(solution)/shard_map/ppermute | solution.py:72
  70.6 28.1 %collective-permute-start.3 = (bf16[512,2048]{1,0:T(8,128)(2,1)}, bf16[512,2048]{1,0:T(8,128)(2,1)S(1)}, u32[]{:S(2)}, u32[]{:S(2)}) collective-permute-start(bf16[512,2048]{1,0:T(8,128)(2,1)} %collective-permute-done.2), channel_id=1, source_target_pairs={{4,6},{3,1},{12,14},{11,9},{20,22},{19,17},{28,30},{27,25}} | collective-permute-start | bytes 6291464 | tf_op jit(solution)/shard_map/ppermute | solution.py:72
  98.7 8.9 %collective-permute-start.7 = (bf16[512,2048]{1,0:T(8,128)(2,1)}, bf16[512,2048]{1,0:T(8,128)(2,1)}, u32[]{:S(2)}, u32[]{:S(2)}) collective-permute-start(bf16[512,2048]{1,0:T(8,128)(2,1)} %collective-permute-done.2), channel_id=1, source_target_pairs={{0,1},{1,0},{2,3},{3,2},{4,5},{5,4},{6,7},{7,6},{8,9},{9,8},{10,11... | collective-permute-start | bytes 6291464 | tf_op jit(solution)/shard_map/ppermute | solution.py:88
  98.8 11.2 %collective-permute-start.5 = (bf16[512,2048]{1,0:T(8,128)(2,1)}, bf16[512,2048]{1,0:T(8,128)(2,1)}, u32[]{:S(2)}, u32[]{:S(2)}) collective-permute-start(bf16[512,2048]{1,0:T(8,128)(2,1)} %collective-permute-done.1), channel_id=1, source_target_pairs={{0,1},{1,0},{2,3},{3,2},{4,5},{5,4},{6,7},{7,6},{8,9},{9,8},{10,11... | collective-permute-start | bytes 6291464 | tf_op jit(solution)/shard_map/ppermute | solution.py:88
  99.3 10.8 %collective-permute-start.6 = (bf16[512,2048]{1,0:T(8,128)(2,1)S(1)}, bf16[512,2048]{1,0:T(8,128)(2,1)}, u32[]{:S(2)}, u32[]{:S(2)}) collective-permute-start(bf16[512,2048]{1,0:T(8,128)(2,1)S(1)} %collective-permute-done.3), channel_id=1, source_target_pairs={{0,1},{1,0},{2,3},{3,2},{4,5},{5,4},{6,7},{7,6},{8,9},{9,8},{10,11... | collective-permute-start | bytes 6291464 | tf_op jit(solution)/shard_map/ppermute | solution.py:88
  103.8 18.1 %all-to-all-start = ((f32[4,128,512]{2,1,0:T(8,128)}), f32[4,128,512]{2,1,0:T(8,128)S(1)}, u32[]{:S(2)}, u32[]{:S(2)}) async-start(f32[4,128,512]{2,1,0:T(8,128)} %fusion.13), calls=%async_computation | async-start | bytes 2097152 | tf_op jit(solution)/shard_map/all_to_all | solution.py:91
  110.0 3.5 %copy-start.4 = (bf16[1,1,512,2048]{3,2,1,0:T(8,128)(2,1)S(1)}, bf16[1,1,512,2048]{3,2,1,0:T(8,128)(2,1)}, u32[]{:S(2)}) copy-start(bf16[1,1,512,2048]{3,2,1,0:T(8,128)(2,1)} %param.8) | copy-start | bytes 6291460
  121.9 1.0 copy-start.1
  122.9 39.8 %all-to-all-start.1 = ((f32[4,128,1536]{2,1,0:T(8,128)}), f32[4,128,1536]{2,1,0:T(8,128)S(1)}, u32[]{:S(2)}, u32[]{:S(2)}) async-start(f32[4,128,1536]{2,1,0:T(8,128)} %fusion), calls=%async_computation.1 | async-start | bytes 6291456 | tf_op jit(solution)/shard_map/all_to_all | solution.py:101
  164.5 11.4 %copy-start = (f32[256,2048]{1,0:T(8,128)S(1)}, f32[256,2048]{1,0:T(8,128)}, u32[]{:S(2)}) copy-start(f32[256,2048]{1,0:T(8,128)} %param.9) | copy-start | bytes 6291460
Sparse Core Ops, SparseCore 0:
  98.8 76.9 reduce-scatter.1

commit v13 on v12

--- a/solution.py
+++ b/solution.py
@@ -31,6 +31,27 @@
     up = [(z * CORES, (z + 1) * CORES) for z in range(t - 1, n_z - 1)]
     down = [(z * CORES + 1, (z - 1) * CORES + 1) for z in range(1, n_z - t + 1)]
     return up + down
+
+
+def reduce_scatter_rows(full, axis, n, me, rows):
+    def own_block(q):
+        q = jnp.clip(q, 0, n - 1)
+        return lax.dynamic_slice_in_dim(full, q * rows, rows, axis=0)
+
+    recv_r = None
+    recv_l = None
+    for t in range(1, n):
+        pay_r = own_block(me + n - t)
+        pay_l = own_block(me - n + t)
+        if recv_r is not None:
+            pay_r = pay_r + recv_r.astype(jnp.float32)
+            pay_l = pay_l + recv_l.astype(jnp.float32)
+        recv_r = lax.ppermute(pay_r.astype(jnp.bfloat16), axis, [(p, p + 1) for p in range(0, t)])
+        recv_l = lax.ppermute(pay_l.astype(jnp.bfloat16), axis, [(p, p - 1) for p in range(n - t, n)])
+    total = own_block(me)
+    if recv_r is not None:
+        total = total + recv_r.astype(jnp.float32) + recv_l.astype(jnp.float32)
+    return total
 
 
 def shards(routes, expert_inputs, hidden_grad, weight, moment_one, moment_two):
@@ -82,9 +103,9 @@
     g_mine = lax.dot_general(
         in_mine.reshape(slot_rows, n_z * rows), masked, dims, preferred_element_type=jnp.float32
     )
-    chip = (g_mine + g_recv.astype(jnp.float32)).astype(jnp.bfloat16)
+    chip = g_mine + g_recv.astype(jnp.float32)
     held, chip = lax.optimization_barrier((tuple(held), chip))
-    owned = lax.psum_scatter(chip, "z", scatter_dimension=0, tiled=True)
+    owned = reduce_scatter_rows(chip, "z", n_z, me_z, rows)
     other_held = lax.ppermute(held, "core", SWAP)
     cols = (((1,), (1,)), ((), ()))
     own_rows = lax.dot_general(masked, chip_w, cols, preferred_element_type=jnp.float32)

time: 192 us -> 197 us (1.026)
  the two profiles are of different devices: /device:TPU:24 before, /device:TPU:11 now
where the time goes in v13:
time: 197 us
  waiting for transfers between devices  94.3 us (48%)
  other arithmetic  35.1 us (18%)
  starting transfers between devices  29.9 us (15%)
  matrix products  19.7 us (10%)
  local copies, waits for them, and re-layouts  9.89 us (5%)
  blocking collectives  6.16 us (3%)
    ppermute x3, waiting for transfers between devices, shards(): cur = lax.ppermute(cur, DP, flood_pairs(n_z, t))  50 us
    ppermute x3, waiting for transfers between devices, reduce_scatter_rows(): lax.ppermute(pay_r.astype(jnp.bfloat16), axis, [(p, p + 1) for p in range...  34 us
    ppermute x3, waiting for transfers between devices, reduce_scatter_rows(): lax.ppermute(pay_l.astype(jnp.bfloat16), axis, [(p, p - 1) for p in range...  10.2 us
    convert_element_type x2, other arithmetic, reduce_scatter_rows(): pay_r.astype(jnp.bfloat16)  8.02 us
    unnamed x22, local copies, waits for them, and re-layouts  7.26 us
    ppermute x3, starting transfers between devices, reduce_scatter_rows(): lax.ppermute(pay_r.astype(jnp.bfloat16), axis, [(p, p + 1) for p in range...  7.17 us
    unnamed x1, blocking collectives  6.16 us
    sub x1, other arithmetic, adamw(): new_weight = weight - learn_rate * (update + decay * weight)  6.07 us
  transfers between devices with their start and end apart: 16, of which 8 were waited for; matrix products, arithmetic and copies ran while one was open for 24% of the time, Pallas kernels for 0%

profile of v13, /device:TPU:11, one launch (start us, length us, event | category | flops | bytes accessed | tf_op | source)
XLA Modules:
  0.0 196.6 jit_solution(5978841190833072213)
XLA Ops:
  0.7 1.7 convert_element_type.72
  5.8 2.3 %maximum_select_fusion = bf16[512,2048]{1,0:T(8,128)(2,1)} fusion(bf16[256,2048]{1,0:T(8,128)(2,1)S(1)} %collective-permute-done, bf16[256,2048]{1,0:T(8,128)(2,1)S(1)} %convert_element_type.72, pred[]{:T(512)S(6)} %eq.74), kind=kLoop, calls=%fused_computation.11 | loop fusion | flops 9437184 | bytes 4194305 | tf_op jit(solution)/shard_map/jit(_where)/select_n | solution.py:87
  8.2 2.1 %collective-permute-start.1 = (bf16[512,2048]{1,0:T(8,128)(2,1)}, bf16[512,2048]{1,0:T(8,128)(2,1)}, u32[]{:S(2)}, u32[]{:S(2)}) collective-permute-start(bf16[512,2048]{1,0:T(8,128)(2,1)} %maximum_select_fusion), channel_id=1, source_target_pairs={{0,2},{2,4},{4,6},{3,1},{5,3},{7,5},{8,10},{10,12},{12,14},{11,9},... | collective-permute-start | bytes 6291464 | tf_op jit(solution)/shard_map/ppermute | solution.py:93
  10.7 6.2 %all-reduce = s32[8]{0:T(128)S(1)} all-reduce(s32[8]{0:T(128)S(1)} %dynamic-update-slice), channel_id=2, replica_groups=mesh['expert'=4,'z'=4,'core'=2] {'expert'}, use_global_device_ids=true, to_apply=%add | all-reduce | flops 8 | bytes 64
  16.9 2.9 %copy.29 = bf16[1,1,512,2048]{2,3,1,0:T(8,128)(2,1)S(1)} copy(bf16[1,1,512,2048]{3,2,1,0:T(8,128)(2,1)} %param.7) | data formatting | bytes 4194304 | tf_op args[1]
  21.5 4.4 %convolution_convert_fusion = bf16[1024,2048]{1,0:T(8,128)(2,1)} fusion(bf16[512,1024]{0,1:T(8,128)(2,1)S(1)} %bitcast.47, bf16[1,1,512,2048]{3,2,1,0:T(8,128)(2,1)S(1)} %copy-done.5, pred[512]{0:T(512)(128)(4,1)S(1)} %get-tuple-element.30), kind=kOutput, calls=%fused_computation.9 | convolution fusion | flops 2150629376 | bytes 7340544 | tf_op jit(solution)/shard_map/dot_general | solution.py:99
  25.9 2.7 %collective-permute-start.4 = (bf16[1024,2048]{1,0:T(8,128)(2,1)}, bf16[1024,2048]{1,0:T(8,128)(2,1)}, u32[]{:S(2)}, u32[]{:S(2)}) collective-permute-start(bf16[1024,2048]{1,0:T(8,128)(2,1)} %convolution_convert_fusion), channel_id=1, source_target_pairs={{0,1},{1,0},{2,3},{3,2},{4,5},{5,4},{6,7},{7,6},{8,9},{9,8},{10,11... | collective-permute-start | bytes 12582920 | tf_op jit(solution)/shard_map/ppermute | solution.py:102
  28.5 7.0 %collective-permute-done.1 = bf16[512,2048]{1,0:T(8,128)(2,1)} collective-permute-done((bf16[512,2048]{1,0:T(8,128)(2,1)}, bf16[512,2048]{1,0:T(8,128)(2,1)}, u32[]{:S(2)}, u32[]{:S(2)}) %collective-permute-start.1) | collective-permute-done | bytes 2097184 | tf_op jit(solution)/shard_map/ppermute | solution.py:93
  35.5 1.9 collective-permute-start.2
  37.5 25.2 %collective-permute-done.2 = bf16[512,2048]{1,0:T(8,128)(2,1)} collective-permute-done((bf16[512,2048]{1,0:T(8,128)(2,1)}, bf16[512,2048]{1,0:T(8,128)(2,1)}, u32[]{:S(2)}, u32[]{:S(2)}) %collective-permute-start.2) | collective-permute-done | bytes 2097184 | tf_op jit(solution)/shard_map/ppermute | solution.py:93
  62.6 2.0 %collective-permute-start.3 = (bf16[512,2048]{1,0:T(8,128)(2,1)}, bf16[512,2048]{1,0:T(8,128)(2,1)S(1)}, u32[]{:S(2)}, u32[]{:S(2)}) collective-permute-start(bf16[512,2048]{1,0:T(8,128)(2,1)} %collective-permute-done.2), channel_id=1, source_target_pairs={{4,6},{3,1},{12,14},{11,9},{20,22},{19,17},{28,30},{27,25}} | collective-permute-start | bytes 6291464 | tf_op jit(solution)/shard_map/ppermute | solution.py:93
  64.7 5.2 %convert_add_fusion = f32[1024,2048]{1,0:T(8,128)S(1)} fusion(bf16[1024,2048]{1,0:T(8,128)(2,1)} %collective-permute-done.4, bf16[512,1024]{0,1:T(8,128)(2,1)S(1)} %bitcast.46, bf16[1,1,512,2048]{3,2,1,0:T(8,128)(2,1)} %param.8, pred[512]{0:T(512)(128)(4,1)S(1)} %get-tuple-element.30), kind=kOutput, calls=%fused_computation | convolution fusion | flops 2152726528 | bytes 15729152 | tf_op jit(solution)/shard_map/dot_general | solution.py:103
  70.0 17.9 %collective-permute-done.3 = bf16[512,2048]{1,0:T(8,128)(2,1)S(1)} collective-permute-done((bf16[512,2048]{1,0:T(8,128)(2,1)}, bf16[512,2048]{1,0:T(8,128)(2,1)S(1)}, u32[]{:S(2)}, u32[]{:S(2)}) %collective-permute-start.3) | collective-permute-done | bytes 2097184 | tf_op jit(solution)/shard_map/ppermute | solution.py:93
  92.1 16.1 %collective-permute-done.8 = bf16[256,2048]{1,0:T(8,128)(2,1)} collective-permute-done((bf16[256,2048]{1,0:T(8,128)(2,1)S(1)}, bf16[256,2048]{1,0:T(8,128)(2,1)}, u32[]{:S(2)}, u32[]{:S(2)}) %collective-permute-start.8) | collective-permute-done | bytes 1048608 | tf_op jit(solution)/shard_map/ppermute | solution.py:49
  108.1 3.2 %add_convert_fusion.3 = bf16[256,2048]{1,0:T(8,128)(2,1)} fusion(bf16[256,2048]{1,0:T(8,128)(2,1)} %collective-permute-done.8, f32[1024,2048]{1,0:T(8,128)} %copy-done, s32[]{:T(128)S(6)} %select_n.136), kind=kLoop, calls=%fused_computation.25 | loop fusion | flops 1572864 | bytes 4194308 | tf_op jit(solution)/shard_map/convert_element_type | solution.py:49
  111.3 1.9 collective-permute-start.9
  113.8 4.5 %fusion.10 = f32[4,128,512]{2,1,0:T(8,128)} fusion(bf16[512,2048]{1,0:T(8,128)(2,1)} %maximum_select_fusion, bf16[4,128,2048]{2,1,0:T(8,128)(2,1)} %bitcast.50, pred[4,128]{1,0:T(4,128)(4,1)S(1)} %get-tuple-element.29), kind=kOutput, calls=%fused_computation.15 | convolution fusion | flops 1074790400 | bytes 5243392 | tf_op jit(solution)/shard_map/dot_general | solution.py:111
  118.3 3.7 %all-to-all-start = ((f32[4,128,512]{2,1,0:T(8,128)}), f32[4,128,512]{2,1,0:T(8,128)S(1)}, u32[]{:S(2)}, u32[]{:S(2)}) async-start(f32[4,128,512]{2,1,0:T(8,128)} %fusion.10), calls=%async_computation | async-start | bytes 2097152 | tf_op jit(solution)/shard_map/all_to_all | solution.py:112
  122.1 5.3 %collective-permute-done.9 = bf16[256,2048]{1,0:T(8,128)(2,1)} collective-permute-done((bf16[256,2048]{1,0:T(8,128)(2,1)}, bf16[256,2048]{1,0:T(8,128)(2,1)}, u32[]{:S(2)}, u32[]{:S(2)}) %collective-permute-start.9) | collective-permute-done | bytes 1048608 | tf_op jit(solution)/shard_map/ppermute | solution.py:49
  127.4 4.8 %add_convert_fusion.2 = (bf16[256,2048]{1,0:T(8,128)(2,1)}, bf16[256,2048]{1,0:T(8,128)(2,1)}) fusion(bf16[256,2048]{1,0:T(8,128)(2,1)} %collective-permute-done.9, f32[1024,2048]{1,0:T(8,128)} %copy-done, s32[]{:T(128)S(6)} %select_n.135, bf16[256,2048]{1,0:T(8,128)(2,1)} %collective-permute-done.11, s32[]{:T(128)S(6)} %select_n.139), kind=kLoop, calls=%fused_computation.24 | loop fusion | flops 3145728 | bytes 8388616 | tf_op jit(solution)/shard_map/convert_element_type | solution.py:49
  133.7 2.4 %select_select_fusion.1 = bf16[512,2048]{1,0:T(8,128)(2,1)S(1)} fusion(bf16[512,2048]{1,0:T(8,128)(2,1)} %collective-permute-done.2, bf16[512,2048]{1,0:T(8,128)(2,1)} %collective-permute-done.7, pred[]{:T(512)S(6)} %lt.77, pred[]{:T(512)S(6)} %eq.74), kind=kLoop, calls=%fused_computation.28 | loop fusion | flops 3145728 | bytes 6291458 | tf_op jit(solution)/shard_map/jit(_where)/select_n | solution.py:119
  136.2 3.2 %select_select_fusion.2 = (bf16[512,2048]{1,0:T(8,128)(2,1)S(1)}, bf16[512,2048]{1,0:T(8,128)(2,1)S(1)}) fusion(bf16[512,2048]{1,0:T(8,128)(2,1)S(1)} %collective-permute-done.3, bf16[512,2048]{1,0:T(8,128)(2,1)} %collective-permute-done.6, bf16[512,2048]{1,0:T(8,128)(2,1)} %collective-permute-done.5, bf16[512,2048]{1,0:T(8,128)(2,1)} %collective-permute-done.1, ...), kind=kLoop, calls=%fused_computation.29 | loop fusion | flops 6291456 | bytes 12582915 | tf_op jit(solution)/shard_map/jit(_where)/select_n | solution.py:119
  139.6 5.3 %fusion = f32[4,128,1536]{2,1,0:T(8,128)} fusion(bf16[512,2048]{1,0:T(8,128)(2,1)S(1)} %get-tuple-element.26, bf16[512,2048]{1,0:T(8,128)(2,1)S(1)} %select_select_fusion.1, bf16[512,2048]{1,0:T(8,128)(2,1)S(1)} %get-tuple-element.25, bf16[4,128,2048]{2,1,0:T(8,128)(2,1)S(1)} %bitcast.51, pred[4,128]{1,0:T(4,128)(4,1)S(1)} %get-tuple-element.29), kind=kOutput, calls=%fused_computation.2 | convolution fusion | flops 3241148416 | bytes 11534848 | tf_op jit(solution)/shard_map/dot_general | solution.py:121
  145.9 3.9 %all-to-all-start.1 = ((f32[4,128,1536]{2,1,0:T(8,128)}), f32[4,128,1536]{2,1,0:T(8,128)S(1)}, u32[]{:S(2)}, u32[]{:S(2)}) async-start(f32[4,128,1536]{2,1,0:T(8,128)} %fusion), calls=%async_computation.1 | async-start | bytes 6291456 | tf_op jit(solution)/shard_map/all_to_all | solution.py:122
  149.8 4.0 %collective-permute-start.10 = (bf16[256,2048]{1,0:T(8,128)(2,1)}, bf16[256,2048]{1,0:T(8,128)(2,1)}, u32[]{:S(2)}, u32[]{:S(2)}) collective-permute-start(bf16[256,2048]{1,0:T(8,128)(2,1)} %get-tuple-element.21), channel_id=1, source_target_pairs={{0,2},{2,4},{4,6},{1,3},{3,5},{5,7},{8,10},{10,12},{12,14},{9,11},... | collective-permute-start | bytes 3145736 | tf_op jit(solution)/shard_map/ppermute | solution.py:49
  155.3 3.2 %add_convert_fusion = bf16[256,2048]{1,0:T(8,128)(2,1)} fusion(bf16[256,2048]{1,0:T(8,128)(2,1)} %collective-permute-done.12, f32[1024,2048]{1,0:T(8,128)} %copy-done, s32[]{:T(128)S(6)} %select_n.138), kind=kLoop, calls=%fused_computation.21 | loop fusion | flops 1572864 | bytes 4194308 | tf_op jit(solution)/shard_map/convert_element_type | solution.py:50
  158.5 1.9 collective-permute-start.13
  160.8 12.6 %collective-permute-done.10 = bf16[256,2048]{1,0:T(8,128)(2,1)} collective-permute-done((bf16[256,2048]{1,0:T(8,128)(2,1)}, bf16[256,2048]{1,0:T(8,128)(2,1)}, u32[]{:S(2)}, u32[]{:S(2)}) %collective-permute-start.10) | collective-permute-done | bytes 1048608 | tf_op jit(solution)/shard_map/ppermute | solution.py:49
  173.4 8.7 %collective-permute-done.13 = bf16[256,2048]{1,0:T(8,128)(2,1)} collective-permute-done((bf16[256,2048]{1,0:T(8,128)(2,1)}, bf16[256,2048]{1,0:T(8,128)(2,1)}, u32[]{:S(2)}, u32[]{:S(2)}) %collective-permute-start.13) | collective-permute-done | bytes 1048608 | tf_op jit(solution)/shard_map/ppermute | solution.py:50
  182.1 4.0 %convert_add_fusion.1 = f32[256,2048]{1,0:T(8,128)} fusion(bf16[256,2048]{1,0:T(8,128)(2,1)} %collective-permute-done.13, bf16[256,2048]{1,0:T(8,128)(2,1)} %collective-permute-done.10, f32[1024,2048]{1,0:T(8,128)} %copy-done, s32[]{:T(128)S(6)} %select_n.134), kind=kLoop, calls=%fused_computation.20 | loop fusion | flops 2097152 | bytes 6291460 | tf_op jit(solution)/shard_map/add | solution.py:53
  186.1 1.8 bitcast_reduce_fusion
  190.5 6.1 %multiply_subtract_fusion = (f32[256,2048]{1,0:T(8,128)}, f32[256,2048]{1,0:T(8,128)}, f32[256,2048]{1,0:T(8,128)}) fusion(f32[256,2048]{1,0:T(8,128)S(1)} %copy-done.2, f32[256,2048]{1,0:T(8,128)S(1)} %copy-done.1, f32[256,2048]{1,0:T(8,128)} %param.10, f32[256,2048]{1,0:T(8,128)} %param.11), kind=kLoop, calls=%fused_computation.17 | loop fusion | flops 8388608 | bytes 14680064 | tf_op jit(solution)/shard_map/sub | solution.py:23
  (58 shorter events, 16.9 us)
Async XLA Ops:
  0.6 3.9 %copy-start.7 = (u32[32]{0:T(128)S(1)}, u32[32]{0:T(128)}, u32[]{:S(2)}) copy-start(u32[32]{0:T(128)} %constant.114) | copy-start | bytes 388
  0.6 2.5 %copy-start.4 = (s32[128,2]{0,1:T(2,128)S(1)}, s32[128,2]{0,1:T(2,128)}, u32[]{:S(2)}) copy-start(s32[128,2]{0,1:T(2,128)} %param.6) | copy-start | bytes 3076
  2.4 3.4 %collective-permute-start = (bf16[256,2048]{1,0:T(8,128)(2,1)S(1)}, bf16[256,2048]{1,0:T(8,128)(2,1)S(1)}, u32[]{:S(2)}, u32[]{:S(2)}) collective-permute-start(bf16[256,2048]{1,0:T(8,128)(2,1)S(1)} %convert_element_type.72), channel_id=1, source_target_pairs={{0,1},{1,0},{2,3},{3,2},{4,5},{5,4},{6,7},{7,6},{8,9},{9,8},{10,11... | collective-permute-start | bytes 3145736 | tf_op jit(solution)/shard_map/ppermute | solution.py:86
  8.2 27.4 %collective-permute-start.1 = (bf16[512,2048]{1,0:T(8,128)(2,1)}, bf16[512,2048]{1,0:T(8,128)(2,1)}, u32[]{:S(2)}, u32[]{:S(2)}) collective-permute-start(bf16[512,2048]{1,0:T(8,128)(2,1)} %maximum_select_fusion), channel_id=1, source_target_pairs={{0,2},{2,4},{4,6},{3,1},{5,3},{7,5},{8,10},{10,12},{12,14},{11,9},... | collective-permute-start | bytes 6291464 | tf_op jit(solution)/shard_map/ppermute | solution.py:93
  19.9 1.6 copy-start.5
  25.9 38.8 %collective-permute-start.4 = (bf16[1024,2048]{1,0:T(8,128)(2,1)}, bf16[1024,2048]{1,0:T(8,128)(2,1)}, u32[]{:S(2)}, u32[]{:S(2)}) collective-permute-start(bf16[1024,2048]{1,0:T(8,128)(2,1)} %convolution_convert_fusion), channel_id=1, source_target_pairs={{0,1},{1,0},{2,3},{3,2},{4,5},{5,4},{6,7},{7,6},{8,9},{9,8},{10,11... | collective-permute-start | bytes 12582920 | tf_op jit(solution)/shard_map/ppermute | solution.py:102
  35.5 27.1 %collective-permute-start.2 = (bf16[512,2048]{1,0:T(8,128)(2,1)}, bf16[512,2048]{1,0:T(8,128)(2,1)}, u32[]{:S(2)}, u32[]{:S(2)}) collective-permute-start(bf16[512,2048]{1,0:T(8,128)(2,1)} %collective-permute-done.1), channel_id=1, source_target_pairs={{2,4},{4,6},{3,1},{5,3},{10,12},{12,14},{11,9},{13,11},{18,20},{20... | collective-permute-start | bytes 6291464 | tf_op jit(solution)/shard_map/ppermute | solution.py:93
  62.6 25.2 %collective-permute-start.3 = (bf16[512,2048]{1,0:T(8,128)(2,1)}, bf16[512,2048]{1,0:T(8,128)(2,1)S(1)}, u32[]{:S(2)}, u32[]{:S(2)}) collective-permute-start(bf16[512,2048]{1,0:T(8,128)(2,1)} %collective-permute-done.2), channel_id=1, source_target_pairs={{4,6},{3,1},{12,14},{11,9},{20,22},{19,17},{28,30},{27,25}} | collective-permute-start | bytes 6291464 | tf_op jit(solution)/shard_map/ppermute | solution.py:93
  69.9 17.9 %copy-start = (f32[1024,2048]{1,0:T(8,128)}, f32[1024,2048]{1,0:T(8,128)S(1)}, u32[]{:S(2)}) copy-start(f32[1024,2048]{1,0:T(8,128)S(1)} %convert_add_fusion) | copy-start | bytes 25165828
  89.1 19.0 %collective-permute-start.8 = (bf16[256,2048]{1,0:T(8,128)(2,1)S(1)}, bf16[256,2048]{1,0:T(8,128)(2,1)}, u32[]{:S(2)}, u32[]{:S(2)}) collective-permute-start(bf16[256,2048]{1,0:T(8,128)(2,1)S(1)} %get-tuple-element.23), channel_id=1, source_target_pairs={{0,2},{1,3},{8,10},{9,11},{16,18},{17,19},{24,26},{25,27}} | collective-permute-start | bytes 3145736 | tf_op jit(solution)/shard_map/ppermute | solution.py:49
  90.4 31.7 %collective-permute-start.11 = (bf16[256,2048]{1,0:T(8,128)(2,1)}, bf16[256,2048]{1,0:T(8,128)(2,1)}, u32[]{:S(2)}, u32[]{:S(2)}) collective-permute-start(bf16[256,2048]{1,0:T(8,128)(2,1)} %get-tuple-element.24), channel_id=1, source_target_pairs={{6,4},{7,5},{14,12},{15,13},{22,20},{23,21},{30,28},{31,29}} | collective-permute-start | bytes 3145736 | tf_op jit(solution)/shard_map/ppermute | solution.py:50
  92.1 41.6 %collective-permute-start.7 = (bf16[512,2048]{1,0:T(8,128)(2,1)}, bf16[512,2048]{1,0:T(8,128)(2,1)}, u32[]{:S(2)}, u32[]{:S(2)}) collective-permute-start(bf16[512,2048]{1,0:T(8,128)(2,1)} %collective-permute-done.2), channel_id=1, source_target_pairs={{0,1},{1,0},{2,3},{3,2},{4,5},{5,4},{6,7},{7,6},{8,9},{9,8},{10,11... | collective-permute-start | bytes 6291464 | tf_op jit(solution)/shard_map/ppermute | solution.py:109
  111.3 16.1 %collective-permute-start.9 = (bf16[256,2048]{1,0:T(8,128)(2,1)}, bf16[256,2048]{1,0:T(8,128)(2,1)}, u32[]{:S(2)}, u32[]{:S(2)}) collective-permute-start(bf16[256,2048]{1,0:T(8,128)(2,1)} %add_convert_fusion.3), channel_id=1, source_target_pairs={{0,2},{2,4},{1,3},{3,5},{8,10},{10,12},{9,11},{11,13},{16,18},{18,... | collective-permute-start | bytes 3145736 | tf_op jit(solution)/shard_map/ppermute | solution.py:49
  113.3 22.9 %collective-permute-start.5 = (bf16[512,2048]{1,0:T(8,128)(2,1)}, bf16[512,2048]{1,0:T(8,128)(2,1)}, u32[]{:S(2)}, u32[]{:S(2)}) collective-permute-start(bf16[512,2048]{1,0:T(8,128)(2,1)} %collective-permute-done.1), channel_id=1, source_target_pairs={{0,1},{1,0},{2,3},{3,2},{4,5},{5,4},{6,7},{7,6},{8,9},{9,8},{10,11... | collective-permute-start | bytes 6291464 | tf_op jit(solution)/shard_map/ppermute | solution.py:109
  113.3 22.8 %collective-permute-start.6 = (bf16[512,2048]{1,0:T(8,128)(2,1)S(1)}, bf16[512,2048]{1,0:T(8,128)(2,1)}, u32[]{:S(2)}, u32[]{:S(2)}) collective-permute-start(bf16[512,2048]{1,0:T(8,128)(2,1)S(1)} %collective-permute-done.3), channel_id=1, source_target_pairs={{0,1},{1,0},{2,3},{3,2},{4,5},{5,4},{6,7},{7,6},{8,9},{9,8},{10,11... | collective-permute-start | bytes 6291464 | tf_op jit(solution)/shard_map/ppermute | solution.py:109
  118.3 26.6 %all-to-all-start = ((f32[4,128,512]{2,1,0:T(8,128)}), f32[4,128,512]{2,1,0:T(8,128)S(1)}, u32[]{:S(2)}, u32[]{:S(2)}) async-start(f32[4,128,512]{2,1,0:T(8,128)} %fusion.10), calls=%async_computation | async-start | bytes 2097152 | tf_op jit(solution)/shard_map/all_to_all | solution.py:112
  132.2 23.1 %collective-permute-start.12 = (bf16[256,2048]{1,0:T(8,128)(2,1)}, bf16[256,2048]{1,0:T(8,128)(2,1)}, u32[]{:S(2)}, u32[]{:S(2)}) collective-permute-start(bf16[256,2048]{1,0:T(8,128)(2,1)} %get-tuple-element.22), channel_id=1, source_target_pairs={{4,2},{6,4},{5,3},{7,5},{12,10},{14,12},{13,11},{15,13},{20,18},{2... | collective-permute-start | bytes 3145736 | tf_op jit(solution)/shard_map/ppermute | solution.py:50
  136.1 3.5 %copy-start.6 = (bf16[1,1,512,2048]{3,2,1,0:T(8,128)(2,1)S(1)}, bf16[1,1,512,2048]{3,2,1,0:T(8,128)(2,1)}, u32[]{:S(2)}) copy-start(bf16[1,1,512,2048]{3,2,1,0:T(8,128)(2,1)} %param.8) | copy-start | bytes 6291460
  144.9 1.0 copy-start.3
  145.9 40.2 %all-to-all-start.1 = ((f32[4,128,1536]{2,1,0:T(8,128)}), f32[4,128,1536]{2,1,0:T(8,128)S(1)}, u32[]{:S(2)}, u32[]{:S(2)}) async-start(f32[4,128,1536]{2,1,0:T(8,128)} %fusion), calls=%async_computation.1 | async-start | bytes 6291456 | tf_op jit(solution)/shard_map/all_to_all | solution.py:122
  149.8 23.5 %collective-permute-start.10 = (bf16[256,2048]{1,0:T(8,128)(2,1)}, bf16[256,2048]{1,0:T(8,128)(2,1)}, u32[]{:S(2)}, u32[]{:S(2)}) collective-permute-start(bf16[256,2048]{1,0:T(8,128)(2,1)} %get-tuple-element.21), channel_id=1, source_target_pairs={{0,2},{2,4},{4,6},{1,3},{3,5},{5,7},{8,10},{10,12},{12,14},{9,11},... | collective-permute-start | bytes 3145736 | tf_op jit(solution)/shard_map/ppermute | solution.py:49
  158.5 23.6 %collective-permute-start.13 = (bf16[256,2048]{1,0:T(8,128)(2,1)}, bf16[256,2048]{1,0:T(8,128)(2,1)}, u32[]{:S(2)}, u32[]{:S(2)}) collective-permute-start(bf16[256,2048]{1,0:T(8,128)(2,1)} %add_convert_fusion), channel_id=1, source_target_pairs={{2,0},{4,2},{6,4},{3,1},{5,3},{7,5},{10,8},{12,10},{14,12},{11,9},... | collective-permute-start | bytes 3145736 | tf_op jit(solution)/shard_map/ppermute | solution.py:50
  187.9 2.6 %copy-start.1 = (f32[256,2048]{1,0:T(8,128)S(1)}, f32[256,2048]{1,0:T(8,128)}, u32[]{:S(2)}) copy-start(f32[256,2048]{1,0:T(8,128)} %convert_add_fusion.1) | copy-start | bytes 6291460
  188.6 1.9 copy-start.2

commit v14 on v12

--- a/solution.py
+++ b/solution.py
@@ -71,20 +71,12 @@
     for t in range(1, n_z):
         cur = lax.ppermute(cur, DP, flood_pairs(n_z, t))
         held.append(cur)
-    by_class = inputs_flat.reshape(slot_rows, n_z, CORES, rows)
-    in_mine = lax.dynamic_index_in_dim(by_class, me_c, axis=2, keepdims=False)
-    in_other = lax.dynamic_index_in_dim(by_class, 1 - me_c, axis=2, keepdims=False)
     dims = (((0,), (0,)), ((), ()))
-    g_other = lax.dot_general(
-        in_other.reshape(slot_rows, n_z * rows), masked, dims, preferred_element_type=jnp.float32
-    )
-    g_recv = lax.ppermute(g_other.astype(jnp.bfloat16), "core", SWAP)
-    g_mine = lax.dot_general(
-        in_mine.reshape(slot_rows, n_z * rows), masked, dims, preferred_element_type=jnp.float32
-    )
-    chip = (g_mine + g_recv.astype(jnp.float32)).astype(jnp.bfloat16)
+    chip = lax.dot_general(
+        inputs_flat, masked, dims, preferred_element_type=jnp.float32
+    ).astype(jnp.bfloat16)
     held, chip = lax.optimization_barrier((tuple(held), chip))
-    owned = lax.psum_scatter(chip, "z", scatter_dimension=0, tiled=True)
+    owned = lax.psum_scatter(chip, DP, scatter_dimension=0, tiled=True)
     other_held = lax.ppermute(held, "core", SWAP)
     cols = (((1,), (1,)), ((), ()))
     own_rows = lax.dot_general(masked, chip_w, cols, preferred_element_type=jnp.float32)

time: 192 us -> 214 us (1.11)
  the two profiles are of different devices: /device:TPU:24 before, /device:TPU:0 now
where the time goes in v14:
time: 214 us
  waiting for transfers between devices  80 us (37%)
  starting transfers between devices  49.8 us (23%)
  local copies, waits for them, and re-layouts  22.1 us (10%)
  other arithmetic  20.8 us (10%)
  matrix products  18.8 us (9%)
  between operations  14.9 us (7%)
  blocking collectives  7.37 us (3%)
    ppermute x3, starting transfers between devices, shards(): other_held = lax.ppermute(held, 'core', SWAP)  31.5 us
    reduce_scatter x1, waiting for transfers between devices, shards(): owned = lax.psum_scatter(chip, DP, scatter_dimension=0, tiled=True)  26.7 us
    all_to_all x1, waiting for transfers between devices, shards(): lax.all_to_all(rest_rows.reshape(n_expert, capacity, width - CORES * rows...  26.5 us
    ppermute x3, waiting for transfers between devices, shards(): cur = lax.ppermute(cur, DP, flood_pairs(n_z, t))  22.1 us
    unnamed x29, local copies, waits for them, and re-layouts  20.9 us
    ppermute x3, starting transfers between devices, shards(): cur = lax.ppermute(cur, DP, flood_pairs(n_z, t))  10.2 us
    dot_general x1, matrix products, shards(): lax.dot_general(inputs_flat, masked, dims, preferred_element_type=jnp.flo...  8.64 us
    unnamed x1, blocking collectives  7.37 us
  transfers between devices with their start and end apart: 10, of which 5 were waited for; matrix products, arithmetic and copies ran while one was open for 19% of the time, Pallas kernels for 0%

profile of v14, /device:TPU:0, one launch (start us, length us, event | category | flops | bytes accessed | tf_op | source)
XLA Modules:
  0.0 213.7 jit_solution(13337411120171520097)
XLA Ops:
  7.2 1.9 convert_element_type.39
  9.6 2.4 %collective-permute-done = bf16[256,2048]{1,0:T(8,128)(2,1)} collective-permute-done((bf16[256,2048]{1,0:T(8,128)(2,1)S(1)}, bf16[256,2048]{1,0:T(8,128)(2,1)}, u32[]{:S(2)}, u32[]{:S(2)}) %collective-permute-start) | collective-permute-done | bytes 1048608 | tf_op jit(solution)/shard_map/ppermute | solution.py:65
  12.0 2.4 %maximum_select_fusion = bf16[512,2048]{1,0:T(8,128)(2,1)S(1)} fusion(bf16[256,2048]{1,0:T(8,128)(2,1)} %collective-permute-done, bf16[256,2048]{1,0:T(8,128)(2,1)S(1)} %convert_element_type.39, pred[]{:T(512)S(6)} %eq.74), kind=kLoop, calls=%fused_computation.16 | loop fusion | flops 9437184 | bytes 4194305 | tf_op jit(solution)/shard_map/jit(_where)/select_n | solution.py:66
  14.4 1.3 copy-done.5
  15.8 6.2 %collective-permute-start.1 = (bf16[512,2048]{1,0:T(8,128)(2,1)S(1)}, bf16[512,2048]{1,0:T(8,128)(2,1)}, u32[]{:S(2)}, u32[]{:S(2)}) collective-permute-start(bf16[512,2048]{1,0:T(8,128)(2,1)S(1)} %maximum_select_fusion), channel_id=1, source_target_pairs={{0,2},{2,4},{4,6},{3,1},{5,3},{7,5},{8,10},{10,12},{12,14},{11,9},... | collective-permute-start | bytes 6291464 | tf_op jit(solution)/shard_map/ppermute | solution.py:72
  22.0 22.1 %collective-permute-done.1 = bf16[512,2048]{1,0:T(8,128)(2,1)} collective-permute-done((bf16[512,2048]{1,0:T(8,128)(2,1)S(1)}, bf16[512,2048]{1,0:T(8,128)(2,1)}, u32[]{:S(2)}, u32[]{:S(2)}) %collective-permute-start.1) | collective-permute-done | bytes 2097184 | tf_op jit(solution)/shard_map/ppermute | solution.py:72
  44.1 2.0 collective-permute-start.2
  46.6 0.6 reduce-window.6
  48.8 2.0 collective-permute-start.3
  51.2 7.4 %all-reduce = s32[8]{0:T(128)S(1)} all-reduce(s32[8]{0:T(128)S(1)} %dynamic-update-slice), channel_id=2, replica_groups=mesh['expert'=4,'z'=4,'core'=2] {'expert'}, use_global_device_ids=true, to_apply=%add | all-reduce | flops 8 | bytes 64
  58.9 8.6 %convert_bitcast_fusion = bf16[2048,2048]{0,1:T(8,128)(2,1)} fusion(bf16[1,1,512,2048]{3,2,1,0:T(8,128)(2,1)S(1)} %copy-done, bf16[1,1,512,2048]{3,2,1,0:T(8,128)(2,1)} %param.8, pred[512]{0:T(512)(128)(4,1)S(1)} %get-tuple-element.40), kind=kOutput, calls=%fused_computation | convolution fusion | flops 4300210176 | bytes 12583424 | tf_op jit(solution)/shard_map/dot_general | solution.py:75
  67.6 30.9 %collective-permute-start.6 = (bf16[512,2048]{1,0:T(8,128)(2,1)}, bf16[512,2048]{1,0:T(8,128)(2,1)}, u32[]{:S(2)}, u32[]{:S(2)}) collective-permute-start(bf16[512,2048]{1,0:T(8,128)(2,1)} %collective-permute-done.2), channel_id=1, source_target_pairs={{0,1},{1,0},{2,3},{3,2},{4,5},{5,4},{6,7},{7,6},{8,9},{9,8},{10,11... | collective-permute-start | bytes 6291464 | tf_op jit(solution)/shard_map/ppermute | solution.py:80
  99.0 4.5 %fusion.10 = f32[4,128,512]{2,1,0:T(8,128)} fusion(bf16[512,2048]{1,0:T(8,128)(2,1)} %copy-done.5, bf16[4,128,2048]{2,1,0:T(8,128)(2,1)} %bitcast.43, pred[4,128]{1,0:T(4,128)(4,1)S(1)} %get-tuple-element.39), kind=kOutput, calls=%fused_computation.19 | convolution fusion | flops 1074790400 | bytes 5243392 | tf_op jit(solution)/shard_map/dot_general | solution.py:82
  103.5 3.7 %all-to-all-start = ((f32[4,128,512]{2,1,0:T(8,128)}), f32[4,128,512]{2,1,0:T(8,128)S(1)}, u32[]{:S(2)}, u32[]{:S(2)}) async-start(f32[4,128,512]{2,1,0:T(8,128)} %fusion.10), calls=%async_computation | async-start | bytes 2097152 | tf_op jit(solution)/shard_map/all_to_all | solution.py:83
  107.2 3.0 %select_select_fusion.1 = bf16[512,2048]{1,0:T(8,128)(2,1)S(1)} fusion(bf16[512,2048]{1,0:T(8,128)(2,1)} %collective-permute-done.2, bf16[512,2048]{1,0:T(8,128)(2,1)} %collective-permute-done.6, pred[]{:T(512)S(6)} %lt.47, pred[]{:T(512)S(6)} %eq.74), kind=kLoop, calls=%fused_computation.23 | loop fusion | flops 3145728 | bytes 6291458 | tf_op jit(solution)/shard_map/jit(_where)/select_n | solution.py:90
  110.2 3.2 %select_select_fusion.2 = (bf16[512,2048]{1,0:T(8,128)(2,1)S(1)}, bf16[512,2048]{1,0:T(8,128)(2,1)S(1)}) fusion(bf16[512,2048]{1,0:T(8,128)(2,1)} %collective-permute-done.3, bf16[512,2048]{1,0:T(8,128)(2,1)} %collective-permute-done.5, bf16[512,2048]{1,0:T(8,128)(2,1)S(1)} %collective-permute-done.4, bf16[512,2048]{1,0:T(8,128)(2,1)} %collective-permute-done.1, ...), kind=kLoop, calls=%fused_computation.24 | loop fusion | flops 6291456 | bytes 12582915 | tf_op jit(solution)/shard_map/jit(_where)/select_n | solution.py:90
  113.7 5.3 %fusion = f32[4,128,1536]{2,1,0:T(8,128)} fusion(bf16[512,2048]{1,0:T(8,128)(2,1)S(1)} %get-tuple-element.38, bf16[512,2048]{1,0:T(8,128)(2,1)S(1)} %select_select_fusion.1, bf16[512,2048]{1,0:T(8,128)(2,1)S(1)} %get-tuple-element.37, bf16[4,128,2048]{2,1,0:T(8,128)(2,1)S(1)} %bitcast.44, pred[4,128]{1,0:T(4,128)(4,1)S(1)} %get-tuple-element.39), kind=kOutput, calls=%fused_computation.2 | convolution fusion | flops 3241148416 | bytes 11534848 | tf_op jit(solution)/shard_map/dot_general | solution.py:92
  119.0 2.2 %all-to-all-done = f32[4,128,512]{2,1,0:T(8,128)S(1)} async-done(((f32[4,128,512]{2,1,0:T(8,128)}), f32[4,128,512]{2,1,0:T(8,128)S(1)}, u32[]{:S(2)}, u32[]{:S(2)}) %all-to-all-start) | async-done | bytes 1048608 | tf_op jit(solution)/shard_map/all_to_all | solution.py:83
  121.2 1.0 copy-done.4
  122.2 3.9 %all-to-all-start.1 = ((f32[4,128,1536]{2,1,0:T(8,128)}), f32[4,128,1536]{2,1,0:T(8,128)S(1)}, u32[]{:S(2)}, u32[]{:S(2)}) async-start(f32[4,128,1536]{2,1,0:T(8,128)} %fusion), calls=%async_computation.1 | async-start | bytes 6291456 | tf_op jit(solution)/shard_map/all_to_all | solution.py:93
  126.0 2.9 %copy.47 = f32[256,2048]{0,1:T(8,128)} copy(f32[256,2048]{1,0:T(8,128)} %param.9) | data formatting | bytes 4194304 | tf_op args[3]
  129.1 2.9 %copy.44 = f32[256,2048]{0,1:T(8,128)} copy(f32[256,2048]{1,0:T(8,128)} %param.10) | data formatting | bytes 4194304 | tf_op args[4]
  132.0 2.9 %copy.45 = f32[256,2048]{0,1:T(8,128)} copy(f32[256,2048]{1,0:T(8,128)} %param.11) | data formatting | bytes 4194304 | tf_op args[5]
  135.0 26.5 %all-to-all-done.1 = f32[4,128,1536]{2,1,0:T(8,128)S(1)} async-done(((f32[4,128,1536]{2,1,0:T(8,128)}), f32[4,128,1536]{2,1,0:T(8,128)S(1)}, u32[]{:S(2)}, u32[]{:S(2)}) %all-to-all-start.1) | async-done | bytes 3145760 | tf_op jit(solution)/shard_map/all_to_all | solution.py:93
  161.6 1.8 bitcast_reduce_fusion
  164.1 1.0 fusion.17
  165.1 0.9 copy.52
  165.9 26.7 %reduce-scatter.2.cloned.1.call-done = bf16[256,2048]{0,1:T(8,128)(2,1)} async-done(((bf16[2048,2048]{0,1:T(8,128)(2,1)}), bf16[256,2048]{0,1:T(8,128)(2,1)}) %reduce-scatter.2.cloned.1.call-update) | async-done | bytes 1048592 | tf_op jit(solution)/shard_map/reduce_scatter | solution.py:79
  192.6 6.3 %multiply_subtract_fusion = (f32[256,2048]{0,1:T(8,128)}, f32[256,2048]{0,1:T(8,128)}, f32[256,2048]{0,1:T(8,128)}) fusion(f32[256,2048]{0,1:T(8,128)S(1)} %copy-done.2, bf16[256,2048]{0,1:T(8,128)(2,1)} %reduce-scatter.2.cloned.1.call-done, f32[256,2048]{0,1:T(8,128)} %copy.44, f32[256,2048]{0,1:T(8,128)} %copy.45), kind=kLoop, calls=%fused_computation.21 | loop fusion | flops 8912896 | bytes 13631488 | tf_op jit(solution)/shard_map/sub | solution.py:23
  199.0 3.0 %copy.48 = f32[256,2048]{1,0:T(8,128)} copy(f32[256,2048]{0,1:T(8,128)} %get-tuple-element.34) | data formatting | bytes 4194304
  202.0 1.8 copy.49
  203.8 3.0 %copy.50 = f32[256,2048]{1,0:T(8,128)} copy(f32[256,2048]{0,1:T(8,128)} %get-tuple-element.36) | data formatting | bytes 4194304
  (47 shorter events, 4.5 us)
Async XLA Ops:
  7.2 51.7 %copy-start = (bf16[1,1,512,2048]{3,2,1,0:T(8,128)(2,1)S(1)}, bf16[1,1,512,2048]{3,2,1,0:T(8,128)(2,1)}, u32[]{:S(2)}) copy-start(bf16[1,1,512,2048]{3,2,1,0:T(8,128)(2,1)} %param.7) | copy-start | bytes 6291460
  7.2 185.5 %reduce-scatter.2.cloned.1.call-start = ((), (), s32[]{:S(2)}) async-start(), calls=%async_computation.3 | async-start | bytes 9437184 | tf_op jit(solution)/shard_map/reduce_scatter | solution.py:79
  9.1 2.9 %collective-permute-start = (bf16[256,2048]{1,0:T(8,128)(2,1)S(1)}, bf16[256,2048]{1,0:T(8,128)(2,1)}, u32[]{:S(2)}, u32[]{:S(2)}) collective-permute-start(bf16[256,2048]{1,0:T(8,128)(2,1)S(1)} %convert_element_type.39), channel_id=1, source_target_pairs={{0,1},{1,0},{2,3},{3,2},{4,5},{5,4},{6,7},{7,6},{8,9},{9,8},{10,11... | collective-permute-start | bytes 3145736 | tf_op jit(solution)/shard_map/ppermute | solution.py:65
  9.6 36.5 %copy-start.6 = (s32[128,2]{0,1:T(2,128)S(1)}, s32[128,2]{0,1:T(2,128)}, u32[]{:S(2)}) copy-start(s32[128,2]{0,1:T(2,128)} %param.6) | copy-start | bytes 3076
  9.6 38.0 %copy-start.8 = (u32[32]{0:T(128)S(1)}, u32[32]{0:T(128)}, u32[]{:S(2)}) copy-start(u32[32]{0:T(128)} %constant.91) | copy-start | bytes 388
  14.4 1.3 copy-start.5
  15.8 28.4 %collective-permute-start.1 = (bf16[512,2048]{1,0:T(8,128)(2,1)S(1)}, bf16[512,2048]{1,0:T(8,128)(2,1)}, u32[]{:S(2)}, u32[]{:S(2)}) collective-permute-start(bf16[512,2048]{1,0:T(8,128)(2,1)S(1)} %maximum_select_fusion), channel_id=1, source_target_pairs={{0,2},{2,4},{4,6},{3,1},{5,3},{7,5},{8,10},{10,12},{12,14},{11,9},... | collective-permute-start | bytes 6291464 | tf_op jit(solution)/shard_map/ppermute | solution.py:72
  44.1 4.7 %collective-permute-start.2 = (bf16[512,2048]{1,0:T(8,128)(2,1)}, bf16[512,2048]{1,0:T(8,128)(2,1)}, u32[]{:S(2)}, u32[]{:S(2)}) collective-permute-start(bf16[512,2048]{1,0:T(8,128)(2,1)} %collective-permute-done.1), channel_id=1, source_target_pairs={{2,4},{4,6},{3,1},{5,3},{10,12},{12,14},{11,9},{13,11},{18,20},{20... | collective-permute-start | bytes 6291464 | tf_op jit(solution)/shard_map/ppermute | solution.py:72
  48.8 18.7 %collective-permute-start.3 = (bf16[512,2048]{1,0:T(8,128)(2,1)}, bf16[512,2048]{1,0:T(8,128)(2,1)}, u32[]{:S(2)}, u32[]{:S(2)}) collective-permute-start(bf16[512,2048]{1,0:T(8,128)(2,1)} %collective-permute-done.2), channel_id=1, source_target_pairs={{4,6},{3,1},{12,14},{11,9},{20,22},{19,17},{28,30},{27,25}} | collective-permute-start | bytes 6291464 | tf_op jit(solution)/shard_map/ppermute | solution.py:72
  67.6 39.7 %collective-permute-start.6 = (bf16[512,2048]{1,0:T(8,128)(2,1)}, bf16[512,2048]{1,0:T(8,128)(2,1)}, u32[]{:S(2)}, u32[]{:S(2)}) collective-permute-start(bf16[512,2048]{1,0:T(8,128)(2,1)} %collective-permute-done.2), channel_id=1, source_target_pairs={{0,1},{1,0},{2,3},{3,2},{4,5},{5,4},{6,7},{7,6},{8,9},{9,8},{10,11... | collective-permute-start | bytes 6291464 | tf_op jit(solution)/shard_map/ppermute | solution.py:80
  98.5 11.7 %collective-permute-start.4 = (bf16[512,2048]{1,0:T(8,128)(2,1)}, bf16[512,2048]{1,0:T(8,128)(2,1)S(1)}, u32[]{:S(2)}, u32[]{:S(2)}) collective-permute-start(bf16[512,2048]{1,0:T(8,128)(2,1)} %collective-permute-done.1), channel_id=1, source_target_pairs={{0,1},{1,0},{2,3},{3,2},{4,5},{5,4},{6,7},{7,6},{8,9},{9,8},{10,11... | collective-permute-start | bytes 6291464 | tf_op jit(solution)/shard_map/ppermute | solution.py:80
  98.6 11.6 %collective-permute-start.5 = (bf16[512,2048]{1,0:T(8,128)(2,1)}, bf16[512,2048]{1,0:T(8,128)(2,1)}, u32[]{:S(2)}, u32[]{:S(2)}) collective-permute-start(bf16[512,2048]{1,0:T(8,128)(2,1)} %collective-permute-done.3), channel_id=1, source_target_pairs={{0,1},{1,0},{2,3},{3,2},{4,5},{5,4},{6,7},{7,6},{8,9},{9,8},{10,11... | collective-permute-start | bytes 6291464 | tf_op jit(solution)/shard_map/ppermute | solution.py:80
  103.5 17.6 %all-to-all-start = ((f32[4,128,512]{2,1,0:T(8,128)}), f32[4,128,512]{2,1,0:T(8,128)S(1)}, u32[]{:S(2)}, u32[]{:S(2)}) async-start(f32[4,128,512]{2,1,0:T(8,128)} %fusion.10), calls=%async_computation | async-start | bytes 2097152 | tf_op jit(solution)/shard_map/all_to_all | solution.py:83
  110.2 3.5 %copy-start.7 = (bf16[1,1,512,2048]{3,2,1,0:T(8,128)(2,1)S(1)}, bf16[1,1,512,2048]{3,2,1,0:T(8,128)(2,1)}, u32[]{:S(2)}) copy-start(bf16[1,1,512,2048]{3,2,1,0:T(8,128)(2,1)} %param.8) | copy-start | bytes 6291460
  121.2 1.0 copy-start.4
  122.2 39.4 %all-to-all-start.1 = ((f32[4,128,1536]{2,1,0:T(8,128)}), f32[4,128,1536]{2,1,0:T(8,128)S(1)}, u32[]{:S(2)}, u32[]{:S(2)}) async-start(f32[4,128,1536]{2,1,0:T(8,128)} %fusion), calls=%async_computation.1 | async-start | bytes 6291456 | tf_op jit(solution)/shard_map/all_to_all | solution.py:93
  163.4 29.3 %copy-start.2 = (f32[256,2048]{0,1:T(8,128)S(1)}, f32[256,2048]{0,1:T(8,128)}, u32[]{:S(2)}) copy-start(f32[256,2048]{0,1:T(8,128)} %copy.47) | copy-start | bytes 6291460
  199.0 3.0 %copy-start.3 = (f32[256,2048]{0,1:T(8,128)S(1)}, f32[256,2048]{0,1:T(8,128)}, u32[]{:S(2)}) copy-start(f32[256,2048]{0,1:T(8,128)} %get-tuple-element.35) | copy-start | bytes 6291460
  203.8 3.0 %copy-start.1 = (bf16[1,1,512,2048]{3,2,1,0:T(8,128)(2,1)S(1)}, bf16[1,1,512,2048]{3,2,1,0:T(8,128)(2,1)}, u32[]{:S(2)}) copy-start(bf16[1,1,512,2048]{3,2,1,0:T(8,128)(2,1)} %param.7) | copy-start | bytes 6291460
Sparse Core Ops, SparseCore 0:
  67.7 124.9 reduce-scatter.1

commit v15 on v12

--- a/solution.py
+++ b/solution.py
@@ -66,11 +66,6 @@
     chip_w = jnp.where(
         me_c == 0, jnp.concatenate([wbf, partner], axis=0), jnp.concatenate([partner, wbf], axis=0)
     )
-    held = []
-    cur = chip_w
-    for t in range(1, n_z):
-        cur = lax.ppermute(cur, DP, flood_pairs(n_z, t))
-        held.append(cur)
     by_class = inputs_flat.reshape(slot_rows, n_z, CORES, rows)
     in_mine = lax.dynamic_index_in_dim(by_class, me_c, axis=2, keepdims=False)
     in_other = lax.dynamic_index_in_dim(by_class, 1 - me_c, axis=2, keepdims=False)
@@ -83,8 +78,16 @@
         in_mine.reshape(slot_rows, n_z * rows), masked, dims, preferred_element_type=jnp.float32
     )
     chip = (g_mine + g_recv.astype(jnp.float32)).astype(jnp.bfloat16)
-    held, chip = lax.optimization_barrier((tuple(held), chip))
-    owned = lax.psum_scatter(chip, "z", scatter_dimension=0, tiled=True)
+    held = []
+    cur = chip_w
+    owned = None
+    for t in range(1, n_z):
+        if t == n_z - 1 or n_z == 2:
+            cur, chip = lax.optimization_barrier((cur, chip))
+            owned = lax.psum_scatter(chip, "z", scatter_dimension=0, tiled=True)
+        cur = lax.ppermute(cur, DP, flood_pairs(n_z, t))
+        held.append(cur)
+    held = lax.optimization_barrier(tuple(held))
     other_held = lax.ppermute(held, "core", SWAP)
     cols = (((1,), (1,)), ((), ()))
     own_rows = lax.dot_general(masked, chip_w, cols, preferred_element_type=jnp.float32)

time: 192 us -> 265 us (1.38); the launches traced: 189 us -> 265 us
  waiting for transfers between devices: 108 us -> 180 us
  matrix products: 16.8 us -> 21 us
    ppermute x3, waiting for transfers between devices: 60 us -> 141 us  [shards(): cur = lax.ppermute(cur, DP, flood_pairs(n_z, t))]
    reduce_scatter x1, waiting for transfers between devices: 8.78 us -> 0.01 us  [shards(): owned = lax.psum_scatter(chip, 'z', scatter_dimension=0, tiled=True)]
    unnamed x18 -> x24, local copies, waits for them, and re-layouts: 7.21 us -> 6.71 us
  transfers between devices with their start and end apart: 11 -> 11, of which waited for: 6 -> 5; matrix products, arithmetic and copies ran while one was open for 17% -> 15% of each run, Pallas kernels for 0% -> 0%
where the time goes in v15:
time: 265 us
  waiting for transfers between devices  180 us (68%)
  matrix products  21 us (8%)
  other arithmetic  20.4 us (8%)
  between operations  15 us (6%)
  starting transfers between devices  11.9 us (4%)
  local copies, waits for them, and re-layouts  9.06 us (3%)
  blocking collectives  7.37 us (3%)
    ppermute x3, waiting for transfers between devices, shards(): cur = lax.ppermute(cur, DP, flood_pairs(n_z, t))  141 us
    all_to_all x1, waiting for transfers between devices, shards(): lax.all_to_all(rest_rows.reshape(n_expert, capacity, width - CORES * rows...  35.7 us
    unnamed x1, blocking collectives  7.37 us
    unnamed x24, local copies, waits for them, and re-layouts  6.71 us
    dot_general x1, matrix products, shards(): lax.dot_general(in_mine.reshape(slot_rows, n_z * rows), masked, dims, pre...  6.61 us
    sub x1, other arithmetic, adamw(): new_weight = weight - learn_rate * (update + decay * weight)  6.42 us
    select_n x2, other arithmetic, shards(): parts.append(jnp.where(me_z + r < n_z, up, down))  5.64 us
  transfers between devices with their start and end apart: 11, of which 5 were waited for; matrix products, arithmetic and copies ran while one was open for 15% of the time, Pallas kernels for 0%

profile of v15, /device:TPU:24, one launch (start us, length us, event | category | flops | bytes accessed | tf_op | source)
XLA Modules:
  0.0 264.9 jit_solution(4511060016238544218)
XLA Ops:
  7.2 1.7 convert_element_type.42
  9.5 0.6 reduce-window.6
  10.6 0.6 dynamic-slice
  12.2 7.4 %all-reduce = s32[8]{0:T(128)S(1)} all-reduce(s32[8]{0:T(128)S(1)} %dynamic-update-slice), channel_id=2, replica_groups=mesh['expert'=4,'z'=4,'core'=2] {'expert'}, use_global_device_ids=true, to_apply=%add | all-reduce | flops 8 | bytes 64
  19.9 2.9 %copy.29 = bf16[1,1,512,2048]{2,3,1,0:T(8,128)(2,1)S(1)} copy(bf16[1,1,512,2048]{3,2,1,0:T(8,128)(2,1)} %param.7) | data formatting | bytes 4194304 | tf_op args[1]
  22.8 1.2 constant_dynamic-slice_fusion.1
  24.0 0.8 copy-done.5
  24.7 4.3 %convolution_convert_fusion = bf16[1024,2048]{1,0:T(8,128)(2,1)} fusion(bf16[512,1024]{0,1:T(8,128)(2,1)S(1)} %bitcast.47, bf16[1,1,512,2048]{3,2,1,0:T(8,128)(2,1)S(1)} %copy-done.5, pred[512]{0:T(512)(128)(4,1)S(1)} %get-tuple-element.28), kind=kOutput, calls=%fused_computation.9 | convolution fusion | flops 2150629376 | bytes 7340544 | tf_op jit(solution)/shard_map/dot_general | solution.py:73
  29.1 2.6 maximum_select_fusion
  31.7 1.3 collective-permute-start.1
  33.0 26.6 %collective-permute-done.1 = bf16[512,2048]{1,0:T(8,128)(2,1)S(1)} collective-permute-done((bf16[512,2048]{1,0:T(8,128)(2,1)S(1)}, bf16[512,2048]{1,0:T(8,128)(2,1)S(1)}, u32[]{:S(2)}, u32[]{:S(2)}) %collective-permute-start.1) | collective-permute-done | bytes 2097184 | tf_op jit(solution)/shard_map/ppermute | solution.py:88
  59.6 1.3 collective-permute-start.2
  60.9 6.6 %add_convert_fusion = bf16[1024,2048]{1,0:T(8,128)(2,1)} fusion(bf16[1024,2048]{1,0:T(8,128)(2,1)} %collective-permute-done.3, bf16[512,1024]{0,1:T(8,128)(2,1)S(1)} %bitcast.46, bf16[1,1,512,2048]{3,2,1,0:T(8,128)(2,1)S(1)} %copy-done.6, pred[512]{0:T(512)(128)(4,1)S(1)} %get-tuple-element.28), kind=kOutput, calls=%fused_computation | convolution fusion | flops 2154823680 | bytes 11534848 | tf_op jit(solution)/shard_map/dot_general | solution.py:77
  67.5 20.1 %collective-permute-done.2 = bf16[512,2048]{1,0:T(8,128)(2,1)} collective-permute-done((bf16[512,2048]{1,0:T(8,128)(2,1)S(1)}, bf16[512,2048]{1,0:T(8,128)(2,1)}, u32[]{:S(2)}, u32[]{:S(2)}) %collective-permute-start.2) | collective-permute-done | bytes 2097184 | tf_op jit(solution)/shard_map/ppermute | solution.py:88
  87.6 1.3 collective-permute-start.4
  88.9 94.3 %collective-permute-done.4 = bf16[512,2048]{1,0:T(8,128)(2,1)} collective-permute-done((bf16[512,2048]{1,0:T(8,128)(2,1)}, bf16[512,2048]{1,0:T(8,128)(2,1)}, u32[]{:S(2)}, u32[]{:S(2)}) %collective-permute-start.4) | collective-permute-done | bytes 2097184 | tf_op jit(solution)/shard_map/ppermute | solution.py:88
  183.3 0.5 collective-permute-start.5
  183.8 4.5 %fusion.13 = f32[4,128,512]{2,1,0:T(8,128)} fusion(bf16[512,2048]{1,0:T(8,128)(2,1)} %copy-done.2, bf16[4,128,2048]{2,1,0:T(8,128)(2,1)} %bitcast.50, pred[4,128]{1,0:T(4,128)(4,1)S(1)} %get-tuple-element.27), kind=kOutput, calls=%fused_computation.21 | convolution fusion | flops 1074790400 | bytes 5243392 | tf_op jit(solution)/shard_map/dot_general | solution.py:93
  188.3 3.5 %all-to-all-start = ((f32[4,128,512]{2,1,0:T(8,128)}), f32[4,128,512]{2,1,0:T(8,128)S(1)}, u32[]{:S(2)}, u32[]{:S(2)}) async-start(f32[4,128,512]{2,1,0:T(8,128)} %fusion.13), calls=%async_computation | async-start | bytes 2097152 | tf_op jit(solution)/shard_map/all_to_all | solution.py:94
  191.9 2.4 select_select_fusion.1
  194.3 3.2 %select_select_fusion.2 = (bf16[512,2048]{1,0:T(8,128)(2,1)S(1)}, bf16[512,2048]{1,0:T(8,128)(2,1)S(1)}) fusion(bf16[512,2048]{1,0:T(8,128)(2,1)} %collective-permute-done.4, bf16[512,2048]{1,0:T(8,128)(2,1)} %collective-permute-done.6, bf16[512,2048]{1,0:T(8,128)(2,1)} %collective-permute-done.5, bf16[512,2048]{1,0:T(8,128)(2,1)S(1)} %collective-permute-done.1, ...), kind=kLoop, calls=%fused_computation.26 | loop fusion | flops 6291456 | bytes 12582915 | tf_op jit(solution)/shard_map/jit(_where)/select_n | solution.py:101
  197.8 5.3 %fusion = f32[4,128,1536]{2,1,0:T(8,128)} fusion(bf16[512,2048]{1,0:T(8,128)(2,1)S(1)} %get-tuple-element.24, bf16[512,2048]{1,0:T(8,128)(2,1)S(1)} %select_select_fusion.1, bf16[512,2048]{1,0:T(8,128)(2,1)S(1)} %get-tuple-element.23, bf16[4,128,2048]{2,1,0:T(8,128)(2,1)S(1)} %bitcast.51, pred[4,128]{1,0:T(4,128)(4,1)S(1)} %get-tuple-element.27), kind=kOutput, calls=%fused_computation.2 | convolution fusion | flops 3241148416 | bytes 11534848 | tf_op jit(solution)/shard_map/dot_general | solution.py:103
  203.0 3.3 %all-to-all-done = f32[4,128,512]{2,1,0:T(8,128)S(1)} async-done(((f32[4,128,512]{2,1,0:T(8,128)}), f32[4,128,512]{2,1,0:T(8,128)S(1)}, u32[]{:S(2)}, u32[]{:S(2)}) %all-to-all-start) | async-done | bytes 1048608 | tf_op jit(solution)/shard_map/all_to_all | solution.py:94
  206.4 1.0 copy-done.1
  207.3 3.9 %all-to-all-start.1 = ((f32[4,128,1536]{2,1,0:T(8,128)}), f32[4,128,1536]{2,1,0:T(8,128)S(1)}, u32[]{:S(2)}, u32[]{:S(2)}) async-start(f32[4,128,1536]{2,1,0:T(8,128)} %fusion), calls=%async_computation.1 | async-start | bytes 6291456 | tf_op jit(solution)/shard_map/all_to_all | solution.py:104
  211.6 35.7 %all-to-all-done.1 = f32[4,128,1536]{2,1,0:T(8,128)S(1)} async-done(((f32[4,128,1536]{2,1,0:T(8,128)}), f32[4,128,1536]{2,1,0:T(8,128)S(1)}, u32[]{:S(2)}, u32[]{:S(2)}) %all-to-all-start.1) | async-done | bytes 3145760 | tf_op jit(solution)/shard_map/all_to_all | solution.py:104
  247.2 1.8 bitcast_reduce_fusion
  249.0 0.3 convolution_convert_fusion.1
  249.3 0.4 reshape.113
  249.7 1.0 fusion.17
  250.7 0.9 copy.31
  251.6 6.4 %multiply_subtract_fusion = (f32[256,2048]{1,0:T(8,128)}, f32[256,2048]{1,0:T(8,128)}, f32[256,2048]{1,0:T(8,128)}) fusion(f32[256,2048]{1,0:T(8,128)S(1)} %copy-done, bf16[256,2048]{1,0:T(8,128)(2,1)} %reduce-scatter.2.cloned.1.call-done, f32[256,2048]{1,0:T(8,128)} %param.10, f32[256,2048]{1,0:T(8,128)} %param.11), kind=kLoop, calls=%fused_computation.23 | loop fusion | flops 8912896 | bytes 13631488 | tf_op jit(solution)/shard_map/sub | solution.py:23
  (46 shorter events, 2.3 us)
Async XLA Ops:
  7.2 3.4 %copy-start.8 = (u32[32]{0:T(128)S(1)}, u32[32]{0:T(128)}, u32[]{:S(2)}) copy-start(u32[32]{0:T(128)} %constant.98) | copy-start | bytes 388
  7.2 1.9 copy-start.4
  7.2 244.4 %reduce-scatter.2.cloned.1.call-start = ((), (), s32[]{:S(2)}) async-start(), calls=%async_computation.3 | async-start | bytes 5242880 | tf_op jit(solution)/shard_map/reduce_scatter | solution.py:87
  9.0 20.1 %collective-permute-start = (bf16[256,2048]{1,0:T(8,128)(2,1)S(1)}, bf16[256,2048]{1,0:T(8,128)(2,1)}, u32[]{:S(2)}, u32[]{:S(2)}) collective-permute-start(bf16[256,2048]{1,0:T(8,128)(2,1)S(1)} %convert_element_type.42), channel_id=1, source_target_pairs={{0,1},{1,0},{2,3},{3,2},{4,5},{5,4},{6,7},{7,6},{8,9},{9,8},{10,11... | collective-permute-start | bytes 3145736 | tf_op jit(solution)/shard_map/ppermute | solution.py:65
  22.7 2.0 copy-start.5
  29.1 31.8 %collective-permute-start.3 = (bf16[1024,2048]{1,0:T(8,128)(2,1)}, bf16[1024,2048]{1,0:T(8,128)(2,1)}, u32[]{:S(2)}, u32[]{:S(2)}) collective-permute-start(bf16[1024,2048]{1,0:T(8,128)(2,1)} %convolution_convert_fusion), channel_id=1, source_target_pairs={{0,1},{1,0},{2,3},{3,2},{4,5},{5,4},{6,7},{7,6},{8,9},{9,8},{10,11... | collective-permute-start | bytes 12582920 | tf_op jit(solution)/shard_map/ppermute | solution.py:76
  29.1 31.8 %copy-start.3 = (bf16[512,4,1,256]{0,3,2,1:T(8,128)(2,1)S(1)}, bf16[512,4,1,256]{0,3,2,1:T(8,128)(2,1)}, u32[]{:S(2)}) copy-start(bf16[512,4,1,256]{0,3,2,1:T(8,128)(2,1)} %get-tuple-element.25) | copy-start | bytes 3145732
  29.1 31.8 %copy-start.6 = (bf16[1,1,512,2048]{3,2,1,0:T(8,128)(2,1)S(1)}, bf16[1,1,512,2048]{3,2,1,0:T(8,128)(2,1)}, u32[]{:S(2)}) copy-start(bf16[1,1,512,2048]{3,2,1,0:T(8,128)(2,1)} %param.8) | copy-start | bytes 6291460
  31.7 27.9 %copy-start.2 = (bf16[512,2048]{1,0:T(8,128)(2,1)}, bf16[512,2048]{1,0:T(8,128)(2,1)S(1)}, u32[]{:S(2)}) copy-start(bf16[512,2048]{1,0:T(8,128)(2,1)S(1)} %maximum_select_fusion) | copy-start | bytes 6291460
  31.7 27.9 %collective-permute-start.1 = (bf16[512,2048]{1,0:T(8,128)(2,1)S(1)}, bf16[512,2048]{1,0:T(8,128)(2,1)S(1)}, u32[]{:S(2)}, u32[]{:S(2)}) collective-permute-start(bf16[512,2048]{1,0:T(8,128)(2,1)S(1)} %maximum_select_fusion), channel_id=1, source_target_pairs={{0,2},{2,4},{4,6},{3,1},{5,3},{7,5},{8,10},{10,12},{12,14},{11,9},... | collective-permute-start | bytes 6291464 | tf_op jit(solution)/shard_map/ppermute | solution.py:88
  59.6 28.0 %collective-permute-start.2 = (bf16[512,2048]{1,0:T(8,128)(2,1)S(1)}, bf16[512,2048]{1,0:T(8,128)(2,1)}, u32[]{:S(2)}, u32[]{:S(2)}) collective-permute-start(bf16[512,2048]{1,0:T(8,128)(2,1)S(1)} %collective-permute-done.1), channel_id=1, source_target_pairs={{2,4},{4,6},{3,1},{5,3},{10,12},{12,14},{11,9},{13,11},{18,20},{20... | collective-permute-start | bytes 6291464 | tf_op jit(solution)/shard_map/ppermute | solution.py:88
  87.6 95.6 %collective-permute-start.4 = (bf16[512,2048]{1,0:T(8,128)(2,1)}, bf16[512,2048]{1,0:T(8,128)(2,1)}, u32[]{:S(2)}, u32[]{:S(2)}) collective-permute-start(bf16[512,2048]{1,0:T(8,128)(2,1)} %collective-permute-done.2), channel_id=1, source_target_pairs={{4,6},{3,1},{12,14},{11,9},{20,22},{19,17},{28,30},{27,25}} | collective-permute-start | bytes 6291464 | tf_op jit(solution)/shard_map/ppermute | solution.py:88
  183.3 8.6 %collective-permute-start.7 = (bf16[512,2048]{1,0:T(8,128)(2,1)}, bf16[512,2048]{1,0:T(8,128)(2,1)}, u32[]{:S(2)}, u32[]{:S(2)}) collective-permute-start(bf16[512,2048]{1,0:T(8,128)(2,1)} %collective-permute-done.2), channel_id=1, source_target_pairs={{0,1},{1,0},{2,3},{3,2},{4,5},{5,4},{6,7},{7,6},{8,9},{9,8},{10,11... | collective-permute-start | bytes 6291464 | tf_op jit(solution)/shard_map/ppermute | solution.py:91
  183.3 11.1 %collective-permute-start.5 = (bf16[512,2048]{1,0:T(8,128)(2,1)S(1)}, bf16[512,2048]{1,0:T(8,128)(2,1)}, u32[]{:S(2)}, u32[]{:S(2)}) collective-permute-start(bf16[512,2048]{1,0:T(8,128)(2,1)S(1)} %collective-permute-done.1), channel_id=1, source_target_pairs={{0,1},{1,0},{2,3},{3,2},{4,5},{5,4},{6,7},{7,6},{8,9},{9,8},{10,11... | collective-permute-start | bytes 6291464 | tf_op jit(solution)/shard_map/ppermute | solution.py:91
  183.8 10.6 %collective-permute-start.6 = (bf16[512,2048]{1,0:T(8,128)(2,1)}, bf16[512,2048]{1,0:T(8,128)(2,1)}, u32[]{:S(2)}, u32[]{:S(2)}) collective-permute-start(bf16[512,2048]{1,0:T(8,128)(2,1)} %collective-permute-done.4), channel_id=1, source_target_pairs={{0,1},{1,0},{2,3},{3,2},{4,5},{5,4},{6,7},{7,6},{8,9},{9,8},{10,11... | collective-permute-start | bytes 6291464 | tf_op jit(solution)/shard_map/ppermute | solution.py:91
  188.3 18.0 %all-to-all-start = ((f32[4,128,512]{2,1,0:T(8,128)}), f32[4,128,512]{2,1,0:T(8,128)S(1)}, u32[]{:S(2)}, u32[]{:S(2)}) async-start(f32[4,128,512]{2,1,0:T(8,128)} %fusion.13), calls=%async_computation | async-start | bytes 2097152 | tf_op jit(solution)/shard_map/all_to_all | solution.py:94
  194.3 3.5 %copy-start.7 = (bf16[1,1,512,2048]{3,2,1,0:T(8,128)(2,1)S(1)}, bf16[1,1,512,2048]{3,2,1,0:T(8,128)(2,1)}, u32[]{:S(2)}) copy-start(bf16[1,1,512,2048]{3,2,1,0:T(8,128)(2,1)} %param.8) | copy-start | bytes 6291460
  206.4 1.0 copy-start.1
  207.3 39.9 %all-to-all-start.1 = ((f32[4,128,1536]{2,1,0:T(8,128)}), f32[4,128,1536]{2,1,0:T(8,128)S(1)}, u32[]{:S(2)}, u32[]{:S(2)}) async-start(f32[4,128,1536]{2,1,0:T(8,128)} %fusion), calls=%async_computation.1 | async-start | bytes 6291456 | tf_op jit(solution)/shard_map/all_to_all | solution.py:104
  249.0 2.6 copy-start
Sparse Core Ops, SparseCore 0:
  89.1 95.2 reduce-scatter.1

commit v16 on v12

--- a/solution.py
+++ b/solution.py
@@ -19,7 +19,7 @@
 def adamw(weight, moment_one, moment_two, grad):
     new_first = beta_one * moment_one + (1.0 - beta_one) * grad
     new_second = beta_two * moment_two + (1.0 - beta_two) * grad * grad
-    update = new_first / bias_one / (jnp.sqrt(new_second / bias_two) + epsilon)
+    update = new_first * (1.0 / bias_one) / (jnp.sqrt(new_second * (1.0 / bias_two)) + epsilon)
     new_weight = weight - learn_rate * (update + decay * weight)
     return (new_weight, new_first, new_second)
 

time: 192 us -> 192 us (level)
  no operation moved by 1% of the time
where the time goes in v16:
time: 192 us; the launch traced here: 189 us
  waiting for transfers between devices  108 us (56%)
  other arithmetic  20.2 us (11%)
  matrix products  16.8 us (9%)
  between operations  15 us (8%)
  starting transfers between devices  13.7 us (7%)
  local copies, waits for them, and re-layouts  8.59 us (4%)
  blocking collectives  7.37 us (4%)
    ppermute x3, waiting for transfers between devices, shards(): cur = lax.ppermute(cur, DP, flood_pairs(n_z, t))  60 us
    all_to_all x1, waiting for transfers between devices, shards(): lax.all_to_all(rest_rows.reshape(n_expert, capacity, width - CORES * rows...  35.5 us
    reduce_scatter x1, waiting for transfers between devices, shards(): owned = lax.psum_scatter(chip, 'z', scatter_dimension=0, tiled=True)  8.78 us
    unnamed x1, blocking collectives  7.37 us
    unnamed x18, local copies, waits for them, and re-layouts  7.21 us
    sub x1, other arithmetic, adamw(): new_weight = weight - learn_rate * (update + decay * weight)  6.42 us
    select_n x2, other arithmetic, shards(): parts.append(jnp.where(me_z + r < n_z, up, down))  5.63 us
    dot_general x1, matrix products, shards(): lax.dot_general(masked, w_rest, cols, preferred_element_type=jnp.float32)  5.25 us
  transfers between devices with their start and end apart: 11, of which 6 were waited for; matrix products, arithmetic and copies ran while one was open for 17% of the time, Pallas kernels for 0%

profile of v16, /device:TPU:24, one launch (start us, length us, event | category | flops | bytes accessed | tf_op | source)
XLA Modules:
  0.0 189.1 jit_solution(14724514678075123512)
XLA Ops:
  7.2 1.7 convert_element_type.42
  9.5 0.6 reduce-window.6
  10.5 0.6 dynamic-slice
  11.8 2.3 %maximum_select_fusion = bf16[512,2048]{1,0:T(8,128)(2,1)} fusion(bf16[256,2048]{1,0:T(8,128)(2,1)S(1)} %collective-permute-done, bf16[256,2048]{1,0:T(8,128)(2,1)S(1)} %convert_element_type.42, pred[]{:T(512)S(6)} %eq.74), kind=kLoop, calls=%fused_computation.17 | loop fusion | flops 9437184 | bytes 4194305 | tf_op jit(solution)/shard_map/jit(_where)/select_n | solution.py:66
  14.1 1.3 collective-permute-start.1
  15.8 7.4 %all-reduce = s32[8]{0:T(128)S(1)} all-reduce(s32[8]{0:T(128)S(1)} %dynamic-update-slice), channel_id=2, replica_groups=mesh['expert'=4,'z'=4,'core'=2] {'expert'}, use_global_device_ids=true, to_apply=%add | all-reduce | flops 8 | bytes 64
  23.3 2.9 %copy.29 = bf16[1,1,512,2048]{2,3,1,0:T(8,128)(2,1)S(1)} copy(bf16[1,1,512,2048]{3,2,1,0:T(8,128)(2,1)} %param.7) | data formatting | bytes 4194304 | tf_op args[1]
  26.6 1.3 copy-done.3
  27.9 2.4 %convolution_convert_fusion = bf16[1024,2048]{1,0:T(8,128)(2,1)S(1)} fusion(bf16[512,1024]{0,1:T(8,128)(2,1)S(1)} %bitcast.47, bf16[1,1,512,2048]{3,2,1,0:T(8,128)(2,1)S(1)} %copy-done.3, pred[512]{0:T(512)(128)(4,1)S(1)} %get-tuple-element.26), kind=kOutput, calls=%fused_computation.9 | convolution fusion | flops 2150629376 | bytes 7340544 | tf_op jit(solution)/shard_map/dot_general | solution.py:78
  30.3 1.4 collective-permute-start.4
  31.7 10.6 %collective-permute-done.1 = bf16[512,2048]{1,0:T(8,128)(2,1)} collective-permute-done((bf16[512,2048]{1,0:T(8,128)(2,1)}, bf16[512,2048]{1,0:T(8,128)(2,1)}, u32[]{:S(2)}, u32[]{:S(2)}) %collective-permute-start.1) | collective-permute-done | bytes 2097184 | tf_op jit(solution)/shard_map/ppermute | solution.py:72
  42.3 1.3 collective-permute-start.2
  43.6 26.9 %collective-permute-done.2 = bf16[512,2048]{1,0:T(8,128)(2,1)} collective-permute-done((bf16[512,2048]{1,0:T(8,128)(2,1)}, bf16[512,2048]{1,0:T(8,128)(2,1)}, u32[]{:S(2)}, u32[]{:S(2)}) %collective-permute-start.2) | collective-permute-done | bytes 2097184 | tf_op jit(solution)/shard_map/ppermute | solution.py:72
  70.6 1.3 collective-permute-start.3
  71.9 4.4 %add_convert_fusion = bf16[1024,2048]{1,0:T(8,128)(2,1)} fusion(bf16[1024,2048]{1,0:T(8,128)(2,1)S(1)} %collective-permute-done.4, bf16[512,1024]{0,1:T(8,128)(2,1)S(1)} %bitcast.46, bf16[1,1,512,2048]{3,2,1,0:T(8,128)(2,1)S(1)} %copy-done.3, pred[512]{0:T(512)(128)(4,1)S(1)} %get-tuple-element.26), kind=kOutput, calls=%fused_computation | convolution fusion | flops 2154823680 | bytes 11534848 | tf_op jit(solution)/shard_map/dot_general | solution.py:82
  76.2 22.5 %collective-permute-done.3 = bf16[512,2048]{1,0:T(8,128)(2,1)S(1)} collective-permute-done((bf16[512,2048]{1,0:T(8,128)(2,1)}, bf16[512,2048]{1,0:T(8,128)(2,1)S(1)}, u32[]{:S(2)}, u32[]{:S(2)}) %collective-permute-start.3) | collective-permute-done | bytes 2097184 | tf_op jit(solution)/shard_map/ppermute | solution.py:72
  98.8 0.5 collective-permute-start.5
  99.4 4.5 %fusion.13 = f32[4,128,512]{2,1,0:T(8,128)} fusion(bf16[512,2048]{1,0:T(8,128)(2,1)} %maximum_select_fusion, bf16[4,128,2048]{2,1,0:T(8,128)(2,1)} %bitcast.50, pred[4,128]{1,0:T(4,128)(4,1)S(1)} %get-tuple-element.25), kind=kOutput, calls=%fused_computation.21 | convolution fusion | flops 1074790400 | bytes 5243392 | tf_op jit(solution)/shard_map/dot_general | solution.py:90
  103.8 3.7 %all-to-all-start = ((f32[4,128,512]{2,1,0:T(8,128)}), f32[4,128,512]{2,1,0:T(8,128)S(1)}, u32[]{:S(2)}, u32[]{:S(2)}) async-start(f32[4,128,512]{2,1,0:T(8,128)} %fusion.13), calls=%async_computation | async-start | bytes 2097152 | tf_op jit(solution)/shard_map/all_to_all | solution.py:91
  107.6 2.4 %select_select_fusion.1 = bf16[512,2048]{1,0:T(8,128)(2,1)S(1)} fusion(bf16[512,2048]{1,0:T(8,128)(2,1)} %collective-permute-done.2, bf16[512,2048]{1,0:T(8,128)(2,1)} %collective-permute-done.7, pred[]{:T(512)S(6)} %lt.56, pred[]{:T(512)S(6)} %eq.74), kind=kLoop, calls=%fused_computation.25 | loop fusion | flops 3145728 | bytes 6291458 | tf_op jit(solution)/shard_map/jit(_where)/select_n | solution.py:98
  110.1 3.2 %select_select_fusion.2 = (bf16[512,2048]{1,0:T(8,128)(2,1)S(1)}, bf16[512,2048]{1,0:T(8,128)(2,1)S(1)}) fusion(bf16[512,2048]{1,0:T(8,128)(2,1)S(1)} %collective-permute-done.3, bf16[512,2048]{1,0:T(8,128)(2,1)} %collective-permute-done.6, bf16[512,2048]{1,0:T(8,128)(2,1)} %collective-permute-done.5, bf16[512,2048]{1,0:T(8,128)(2,1)} %collective-permute-done.1, ...), kind=kLoop, calls=%fused_computation.26 | loop fusion | flops 6291456 | bytes 12582915 | tf_op jit(solution)/shard_map/jit(_where)/select_n | solution.py:98
  113.5 5.3 %fusion = f32[4,128,1536]{2,1,0:T(8,128)} fusion(bf16[512,2048]{1,0:T(8,128)(2,1)S(1)} %get-tuple-element.22, bf16[512,2048]{1,0:T(8,128)(2,1)S(1)} %select_select_fusion.1, bf16[512,2048]{1,0:T(8,128)(2,1)S(1)} %get-tuple-element.21, bf16[4,128,2048]{2,1,0:T(8,128)(2,1)S(1)} %bitcast.51, pred[4,128]{1,0:T(4,128)(4,1)S(1)} %get-tuple-element.25), kind=kOutput, calls=%fused_computation.2 | convolution fusion | flops 3241148416 | bytes 11534848 | tf_op jit(solution)/shard_map/dot_general | solution.py:100
  118.7 3.2 %all-to-all-done = f32[4,128,512]{2,1,0:T(8,128)S(1)} async-done(((f32[4,128,512]{2,1,0:T(8,128)}), f32[4,128,512]{2,1,0:T(8,128)S(1)}, u32[]{:S(2)}, u32[]{:S(2)}) %all-to-all-start) | async-done | bytes 1048608 | tf_op jit(solution)/shard_map/all_to_all | solution.py:91
  121.9 1.0 copy-done.1
  122.9 3.9 %all-to-all-start.1 = ((f32[4,128,1536]{2,1,0:T(8,128)}), f32[4,128,1536]{2,1,0:T(8,128)S(1)}, u32[]{:S(2)}, u32[]{:S(2)}) async-start(f32[4,128,1536]{2,1,0:T(8,128)} %fusion), calls=%async_computation.1 | async-start | bytes 6291456 | tf_op jit(solution)/shard_map/all_to_all | solution.py:101
  127.2 35.5 %all-to-all-done.1 = f32[4,128,1536]{2,1,0:T(8,128)S(1)} async-done(((f32[4,128,1536]{2,1,0:T(8,128)}), f32[4,128,1536]{2,1,0:T(8,128)S(1)}, u32[]{:S(2)}, u32[]{:S(2)}) %all-to-all-start.1) | async-done | bytes 3145760 | tf_op jit(solution)/shard_map/all_to_all | solution.py:101
  162.7 1.8 bitcast_reduce_fusion
  164.8 0.4 reshape.113
  165.2 1.0 fusion.17
  166.2 0.9 copy.31
  167.1 8.8 %reduce-scatter.2.cloned.1.call-done = bf16[256,2048]{1,0:T(8,128)(2,1)} async-done(((bf16[1024,2048]{1,0:T(8,128)(2,1)}), bf16[256,2048]{1,0:T(8,128)(2,1)}) %reduce-scatter.2.cloned.1.call-update) | async-done | bytes 1048592 | tf_op jit(solution)/shard_map/reduce_scatter | solution.py:87
  175.9 6.4 %multiply_subtract_fusion = (f32[256,2048]{1,0:T(8,128)}, f32[256,2048]{1,0:T(8,128)}, f32[256,2048]{1,0:T(8,128)}) fusion(f32[256,2048]{1,0:T(8,128)S(1)} %copy-done, bf16[256,2048]{1,0:T(8,128)(2,1)} %reduce-scatter.2.cloned.1.call-done, f32[256,2048]{1,0:T(8,128)} %param.10, f32[256,2048]{1,0:T(8,128)} %param.11), kind=kLoop, calls=%fused_computation.23 | loop fusion | flops 8912896 | bytes 13631488 | tf_op jit(solution)/shard_map/sub | solution.py:23
  (40 shorter events, 2.9 us)
Async XLA Ops:
  7.2 3.3 %copy-start.5 = (u32[32]{0:T(128)S(1)}, u32[32]{0:T(128)}, u32[]{:S(2)}) copy-start(u32[32]{0:T(128)} %constant.96) | copy-start | bytes 388
  7.2 1.9 copy-start.2
  7.2 168.7 %reduce-scatter.2.cloned.1.call-start = ((), (), s32[]{:S(2)}) async-start(), calls=%async_computation.3 | async-start | bytes 5242880 | tf_op jit(solution)/shard_map/reduce_scatter | solution.py:87
  9.0 2.8 %collective-permute-start = (bf16[256,2048]{1,0:T(8,128)(2,1)S(1)}, bf16[256,2048]{1,0:T(8,128)(2,1)S(1)}, u32[]{:S(2)}, u32[]{:S(2)}) collective-permute-start(bf16[256,2048]{1,0:T(8,128)(2,1)S(1)} %convert_element_type.42), channel_id=1, source_target_pairs={{0,1},{1,0},{2,3},{3,2},{4,5},{5,4},{6,7},{7,6},{8,9},{9,8},{10,11... | collective-permute-start | bytes 3145736 | tf_op jit(solution)/shard_map/ppermute | solution.py:65
  14.1 28.2 %collective-permute-start.1 = (bf16[512,2048]{1,0:T(8,128)(2,1)}, bf16[512,2048]{1,0:T(8,128)(2,1)}, u32[]{:S(2)}, u32[]{:S(2)}) collective-permute-start(bf16[512,2048]{1,0:T(8,128)(2,1)} %maximum_select_fusion), channel_id=1, source_target_pairs={{0,2},{2,4},{4,6},{3,1},{5,3},{7,5},{8,10},{10,12},{12,14},{11,9},... | collective-permute-start | bytes 6291464 | tf_op jit(solution)/shard_map/ppermute | solution.py:72
  26.3 1.6 copy-start.3
  30.3 41.6 %collective-permute-start.4 = (bf16[1024,2048]{1,0:T(8,128)(2,1)S(1)}, bf16[1024,2048]{1,0:T(8,128)(2,1)S(1)}, u32[]{:S(2)}, u32[]{:S(2)}) collective-permute-start(bf16[1024,2048]{1,0:T(8,128)(2,1)S(1)} %convolution_convert_fusion), channel_id=1, source_target_pairs={{0,1},{1,0},{2,3},{3,2},{4,5},{5,4},{6,7},{7,6},{8,9},{9,8},{10,11... | collective-permute-start | bytes 12582920 | tf_op jit(solution)/shard_map/ppermute | solution.py:81
  42.3 28.2 %collective-permute-start.2 = (bf16[512,2048]{1,0:T(8,128)(2,1)}, bf16[512,2048]{1,0:T(8,128)(2,1)}, u32[]{:S(2)}, u32[]{:S(2)}) collective-permute-start(bf16[512,2048]{1,0:T(8,128)(2,1)} %collective-permute-done.1), channel_id=1, source_target_pairs={{2,4},{4,6},{3,1},{5,3},{10,12},{12,14},{11,9},{13,11},{18,20},{20... | collective-permute-start | bytes 6291464 | tf_op jit(solution)/shard_map/ppermute | solution.py:72
  70.6 28.1 %collective-permute-start.3 = (bf16[512,2048]{1,0:T(8,128)(2,1)}, bf16[512,2048]{1,0:T(8,128)(2,1)S(1)}, u32[]{:S(2)}, u32[]{:S(2)}) collective-permute-start(bf16[512,2048]{1,0:T(8,128)(2,1)} %collective-permute-done.2), channel_id=1, source_target_pairs={{4,6},{3,1},{12,14},{11,9},{20,22},{19,17},{28,30},{27,25}} | collective-permute-start | bytes 6291464 | tf_op jit(solution)/shard_map/ppermute | solution.py:72
  98.7 8.9 %collective-permute-start.7 = (bf16[512,2048]{1,0:T(8,128)(2,1)}, bf16[512,2048]{1,0:T(8,128)(2,1)}, u32[]{:S(2)}, u32[]{:S(2)}) collective-permute-start(bf16[512,2048]{1,0:T(8,128)(2,1)} %collective-permute-done.2), channel_id=1, source_target_pairs={{0,1},{1,0},{2,3},{3,2},{4,5},{5,4},{6,7},{7,6},{8,9},{9,8},{10,11... | collective-permute-start | bytes 6291464 | tf_op jit(solution)/shard_map/ppermute | solution.py:88
  98.8 11.2 %collective-permute-start.5 = (bf16[512,2048]{1,0:T(8,128)(2,1)}, bf16[512,2048]{1,0:T(8,128)(2,1)}, u32[]{:S(2)}, u32[]{:S(2)}) collective-permute-start(bf16[512,2048]{1,0:T(8,128)(2,1)} %collective-permute-done.1), channel_id=1, source_target_pairs={{0,1},{1,0},{2,3},{3,2},{4,5},{5,4},{6,7},{7,6},{8,9},{9,8},{10,11... | collective-permute-start | bytes 6291464 | tf_op jit(solution)/shard_map/ppermute | solution.py:88
  99.3 10.8 %collective-permute-start.6 = (bf16[512,2048]{1,0:T(8,128)(2,1)S(1)}, bf16[512,2048]{1,0:T(8,128)(2,1)}, u32[]{:S(2)}, u32[]{:S(2)}) collective-permute-start(bf16[512,2048]{1,0:T(8,128)(2,1)S(1)} %collective-permute-done.3), channel_id=1, source_target_pairs={{0,1},{1,0},{2,3},{3,2},{4,5},{5,4},{6,7},{7,6},{8,9},{9,8},{10,11... | collective-permute-start | bytes 6291464 | tf_op jit(solution)/shard_map/ppermute | solution.py:88
  103.8 18.1 %all-to-all-start = ((f32[4,128,512]{2,1,0:T(8,128)}), f32[4,128,512]{2,1,0:T(8,128)S(1)}, u32[]{:S(2)}, u32[]{:S(2)}) async-start(f32[4,128,512]{2,1,0:T(8,128)} %fusion.13), calls=%async_computation | async-start | bytes 2097152 | tf_op jit(solution)/shard_map/all_to_all | solution.py:91
  110.0 3.5 %copy-start.4 = (bf16[1,1,512,2048]{3,2,1,0:T(8,128)(2,1)S(1)}, bf16[1,1,512,2048]{3,2,1,0:T(8,128)(2,1)}, u32[]{:S(2)}) copy-start(bf16[1,1,512,2048]{3,2,1,0:T(8,128)(2,1)} %param.8) | copy-start | bytes 6291460
  121.9 1.0 copy-start.1
  122.9 39.8 %all-to-all-start.1 = ((f32[4,128,1536]{2,1,0:T(8,128)}), f32[4,128,1536]{2,1,0:T(8,128)S(1)}, u32[]{:S(2)}, u32[]{:S(2)}) async-start(f32[4,128,1536]{2,1,0:T(8,128)} %fusion), calls=%async_computation.1 | async-start | bytes 6291456 | tf_op jit(solution)/shard_map/all_to_all | solution.py:101
  164.5 11.4 %copy-start = (f32[256,2048]{1,0:T(8,128)S(1)}, f32[256,2048]{1,0:T(8,128)}, u32[]{:S(2)}) copy-start(f32[256,2048]{1,0:T(8,128)} %param.9) | copy-start | bytes 6291460
Sparse Core Ops, SparseCore 0:
  98.8 76.9 reduce-scatter.1

commit v17 on v12

--- a/solution.py
+++ b/solution.py
@@ -63,9 +63,7 @@
 
     wbf = weight.astype(jnp.bfloat16)
     partner = lax.ppermute(wbf, "core", SWAP)
-    chip_w = jnp.where(
-        me_c == 0, jnp.concatenate([wbf, partner], axis=0), jnp.concatenate([partner, wbf], axis=0)
-    )
+    chip_w = jnp.concatenate([wbf, partner], axis=0)
     held = []
     cur = chip_w
     for t in range(1, n_z):
@@ -110,7 +108,12 @@
     token_rel = jnp.dot(
         choose, paired.reshape(experts * capacity, width), preferred_element_type=jnp.float32
     ).astype(jnp.bfloat16)
-    token_grad = jnp.roll(token_rel.reshape(tok_count, n_z, CORES * rows), me_z, axis=1)
+    split = token_rel.reshape(tok_count, n_z, CORES, rows)
+    swapped = jnp.concatenate(
+        [(me_c == 1)[None], me_z + jnp.arange(1, n_z, dtype=jnp.int32) < n_z]
+    )
+    split = jnp.where(swapped[None, :, None, None], split[:, :, ::-1], split)
+    token_grad = jnp.roll(split.reshape(tok_count, n_z, CORES * rows), me_z, axis=1)
     token_grad = token_grad.reshape(tok_count, width)
 
     token_grad, owned = lax.optimization_barrier((token_grad, owned))

time: 192 us -> 192 us (level)
  waiting for transfers between devices: 108 us -> 101 us
  local copies, waits for them, and re-layouts: 8.59 us -> 12.9 us
    reduce_scatter x1, waiting for transfers between devices: 8.78 us -> 3.28 us  [shards(): owned = lax.psum_scatter(chip, 'z', scatter_dimension=0, tiled=True)]
    rev x0 -> x1, local copies, waits for them, and re-layouts: none -> 3.99 us  [shards(): split = jnp.where(swapped[None, :, None, None], split[:, :, ::-1], split)]
    unnamed x18 -> x22, local copies, waits for them, and re-layouts: 7.21 us -> 7.21 us
  transfers between devices with their start and end apart: 11 -> 11, of which waited for: 6 -> 6; matrix products, arithmetic and copies ran while one was open for 17% -> 21% of each run, Pallas kernels for 0% -> 0%
where the time goes in v17:
time: 192 us; the launch traced here: 188 us
  waiting for transfers between devices  101 us (53%)
  other arithmetic  22 us (11%)
  matrix products  16.2 us (8%)
  between operations  15 us (8%)
  starting transfers between devices  13.6 us (7%)
  local copies, waits for them, and re-layouts  12.9 us (7%)
  blocking collectives  7.37 us (4%)
    ppermute x3, waiting for transfers between devices, shards(): cur = lax.ppermute(cur, DP, flood_pairs(n_z, t))  60.1 us
    all_to_all x1, waiting for transfers between devices, shards(): lax.all_to_all(rest_rows.reshape(n_expert, capacity, width - CORES * rows...  35.5 us
    unnamed x1, blocking collectives  7.37 us
    unnamed x22, local copies, waits for them, and re-layouts  7.21 us
    sub x1, other arithmetic, adamw(): new_weight = weight - learn_rate * (update + decay * weight)  6.42 us
    select_n x2, other arithmetic, shards(): parts.append(jnp.where(me_z + r < n_z, up, down))  6.25 us
    dot_general x1, matrix products, shards(): lax.dot_general(masked, w_rest, cols, preferred_element_type=jnp.float32)  5.25 us
    dot_general x1, matrix products, shards(): lax.dot_general(in_mine.reshape(slot_rows, n_z * rows), masked, dims, pre...  4.36 us
  transfers between devices with their start and end apart: 11, of which 6 were waited for; matrix products, arithmetic and copies ran while one was open for 21% of the time, Pallas kernels for 0%

profile of v17, /device:TPU:24, one launch (start us, length us, event | category | flops | bytes accessed | tf_op | source)
XLA Modules:
  0.0 188.5 jit_solution(2458614047952317389)
XLA Ops:
  7.2 1.7 convert_element_type.42
  9.5 0.6 reduce-window.6
  10.5 0.6 dynamic-slice
  11.8 1.6 pad_maximum_fusion.1
  13.3 1.3 collective-permute-start.1
  15.1 7.4 %all-reduce = s32[8]{0:T(128)S(1)} all-reduce(s32[8]{0:T(128)S(1)} %dynamic-update-slice), channel_id=2, replica_groups=mesh['expert'=4,'z'=4,'core'=2] {'expert'}, use_global_device_ids=true, to_apply=%add | all-reduce | flops 8 | bytes 64
  22.5 2.9 %copy.29 = bf16[1,1,512,2048]{2,3,1,0:T(8,128)(2,1)S(1)} copy(bf16[1,1,512,2048]{3,2,1,0:T(8,128)(2,1)} %param.7) | data formatting | bytes 4194304 | tf_op args[1]
  25.9 1.3 copy-done.5
  27.1 2.4 %convolution_convert_fusion = bf16[1024,2048]{1,0:T(8,128)(2,1)S(1)} fusion(bf16[512,1024]{0,1:T(8,128)(2,1)S(1)} %bitcast.48, bf16[1,1,512,2048]{3,2,1,0:T(8,128)(2,1)S(1)} %copy-done.5, pred[512]{0:T(512)(128)(4,1)S(1)} %get-tuple-element.26), kind=kOutput, calls=%fused_computation.9 | convolution fusion | flops 2150629376 | bytes 7340544 | tf_op jit(solution)/shard_map/dot_general | solution.py:76
  29.6 1.4 collective-permute-start.4
  31.0 10.6 %collective-permute-done.1 = bf16[512,2048]{1,0:T(8,128)(2,1)} collective-permute-done((bf16[512,2048]{1,0:T(8,128)(2,1)}, bf16[512,2048]{1,0:T(8,128)(2,1)}, u32[]{:S(2)}, u32[]{:S(2)}) %collective-permute-start.1) | collective-permute-done | bytes 2097184 | tf_op jit(solution)/shard_map/ppermute | solution.py:70
  41.6 1.3 collective-permute-start.2
  42.9 26.9 %collective-permute-done.2 = bf16[512,2048]{1,0:T(8,128)(2,1)} collective-permute-done((bf16[512,2048]{1,0:T(8,128)(2,1)}, bf16[512,2048]{1,0:T(8,128)(2,1)}, u32[]{:S(2)}, u32[]{:S(2)}) %collective-permute-start.2) | collective-permute-done | bytes 2097184 | tf_op jit(solution)/shard_map/ppermute | solution.py:70
  69.8 1.3 collective-permute-start.3
  71.1 4.4 %add_convert_fusion = bf16[1024,2048]{1,0:T(8,128)(2,1)} fusion(bf16[1024,2048]{1,0:T(8,128)(2,1)S(1)} %collective-permute-done.4, bf16[512,1024]{0,1:T(8,128)(2,1)S(1)} %bitcast.47, bf16[1,1,512,2048]{3,2,1,0:T(8,128)(2,1)S(1)} %copy-done.5, pred[512]{0:T(512)(128)(4,1)S(1)} %get-tuple-element.26), kind=kOutput, calls=%fused_computation | convolution fusion | flops 2154823680 | bytes 11534848 | tf_op jit(solution)/shard_map/dot_general | solution.py:80
  75.5 22.6 %collective-permute-done.3 = bf16[512,2048]{1,0:T(8,128)(2,1)} collective-permute-done((bf16[512,2048]{1,0:T(8,128)(2,1)}, bf16[512,2048]{1,0:T(8,128)(2,1)}, u32[]{:S(2)}, u32[]{:S(2)}) %collective-permute-start.3) | collective-permute-done | bytes 2097184 | tf_op jit(solution)/shard_map/ppermute | solution.py:70
  98.7 3.9 %fusion.13 = f32[4,128,512]{2,1,0:T(8,128)} fusion(bf16[4,128,2048]{2,1,0:T(8,128)(2,1)} %bitcast.51, pred[4,128]{1,0:T(4,128)(4,1)S(1)} %get-tuple-element.25, bf16[256,2048]{1,0:T(8,128)(2,1)S(1)} %copy-done.3, bf16[256,2048]{1,0:T(8,128)(2,1)S(1)} %convert_element_type.42), kind=kOutput, calls=%fused_computation.21 | convolution fusion | flops 1078984704 | bytes 5243392 | tf_op jit(solution)/shard_map/dot_general | solution.py:88
  102.6 3.7 %all-to-all-start = ((f32[4,128,512]{2,1,0:T(8,128)}), f32[4,128,512]{2,1,0:T(8,128)S(1)}, u32[]{:S(2)}, u32[]{:S(2)}) async-start(f32[4,128,512]{2,1,0:T(8,128)} %fusion.13), calls=%async_computation | async-start | bytes 2097152 | tf_op jit(solution)/shard_map/all_to_all | solution.py:89
  106.3 2.5 %select_select_fusion.1 = bf16[512,2048]{1,0:T(8,128)(2,1)S(1)} fusion(bf16[512,2048]{1,0:T(8,128)(2,1)} %collective-permute-done.2, bf16[512,2048]{1,0:T(8,128)(2,1)} %collective-permute-done.7, pred[]{:T(512)S(6)} %lt.60, pred[]{:T(512)S(6)} %eq.77), kind=kLoop, calls=%fused_computation.25 | loop fusion | flops 3145728 | bytes 6291458 | tf_op jit(solution)/shard_map/jit(_where)/select_n | solution.py:96
  108.8 3.8 %select_select_fusion.2 = (bf16[512,2048]{1,0:T(8,128)(2,1)S(1)}, bf16[512,2048]{1,0:T(8,128)(2,1)S(1)}) fusion(bf16[512,2048]{1,0:T(8,128)(2,1)} %collective-permute-done.3, bf16[512,2048]{1,0:T(8,128)(2,1)} %collective-permute-done.6, bf16[512,2048]{1,0:T(8,128)(2,1)} %collective-permute-done.5, bf16[512,2048]{1,0:T(8,128)(2,1)} %collective-permute-done.1, ...), kind=kLoop, calls=%fused_computation.26 | loop fusion | flops 6291456 | bytes 12582915 | tf_op jit(solution)/shard_map/jit(_where)/select_n | solution.py:96
  112.8 5.3 %fusion = f32[4,128,1536]{2,1,0:T(8,128)} fusion(bf16[512,2048]{1,0:T(8,128)(2,1)S(1)} %get-tuple-element.22, bf16[512,2048]{1,0:T(8,128)(2,1)S(1)} %select_select_fusion.1, bf16[512,2048]{1,0:T(8,128)(2,1)S(1)} %get-tuple-element.21, bf16[4,128,2048]{2,1,0:T(8,128)(2,1)S(1)} %bitcast.52, pred[4,128]{1,0:T(4,128)(4,1)S(1)} %get-tuple-element.25), kind=kOutput, calls=%fused_computation.2 | convolution fusion | flops 3241148416 | bytes 11534848 | tf_op jit(solution)/shard_map/dot_general | solution.py:98
  118.1 2.6 %all-to-all-done = f32[4,128,512]{2,1,0:T(8,128)S(1)} async-done(((f32[4,128,512]{2,1,0:T(8,128)}), f32[4,128,512]{2,1,0:T(8,128)S(1)}, u32[]{:S(2)}, u32[]{:S(2)}) %all-to-all-start) | async-done | bytes 1048608 | tf_op jit(solution)/shard_map/all_to_all | solution.py:89
  120.7 1.0 copy-done.1
  121.6 3.9 %all-to-all-start.1 = ((f32[4,128,1536]{2,1,0:T(8,128)}), f32[4,128,1536]{2,1,0:T(8,128)S(1)}, u32[]{:S(2)}, u32[]{:S(2)}) async-start(f32[4,128,1536]{2,1,0:T(8,128)} %fusion), calls=%async_computation.1 | async-start | bytes 6291456 | tf_op jit(solution)/shard_map/all_to_all | solution.py:99
  126.0 35.5 %all-to-all-done.1 = f32[4,128,1536]{2,1,0:T(8,128)S(1)} async-done(((f32[4,128,1536]{2,1,0:T(8,128)}), f32[4,128,1536]{2,1,0:T(8,128)S(1)}, u32[]{:S(2)}, u32[]{:S(2)}) %all-to-all-start.1) | async-done | bytes 3145760 | tf_op jit(solution)/shard_map/all_to_all | solution.py:99
  161.4 1.8 bitcast_reduce_fusion
  163.9 4.0 %rev.3 = bf16[128,4,2,256]{3,2,1,0:T(2,128)(2,1)} reverse(bf16[128,4,2,256]{3,2,1,0:T(2,128)(2,1)S(1)} %reshape.117), dimensions={2} | reverse | bytes 1048576 | tf_op jit(solution)/shard_map/rev | solution.py:115
  167.9 1.8 broadcast_select_fusion.4
  170.1 1.0 fusion.17
  171.0 0.9 copy.31
  171.9 3.3 %reduce-scatter.2.cloned.1.call-done = bf16[256,2048]{1,0:T(8,128)(2,1)} async-done(((bf16[1024,2048]{1,0:T(8,128)(2,1)}), bf16[256,2048]{1,0:T(8,128)(2,1)}) %reduce-scatter.2.cloned.1.call-update) | async-done | bytes 1048592 | tf_op jit(solution)/shard_map/reduce_scatter | solution.py:85
  175.2 6.4 %multiply_subtract_fusion = (f32[256,2048]{1,0:T(8,128)}, f32[256,2048]{1,0:T(8,128)}, f32[256,2048]{1,0:T(8,128)}) fusion(f32[256,2048]{1,0:T(8,128)S(1)} %copy-done, bf16[256,2048]{1,0:T(8,128)(2,1)} %reduce-scatter.2.cloned.1.call-done, f32[256,2048]{1,0:T(8,128)} %param.10, f32[256,2048]{1,0:T(8,128)} %param.11), kind=kLoop, calls=%fused_computation.23 | loop fusion | flops 8912896 | bytes 13631488 | tf_op jit(solution)/shard_map/sub | solution.py:23
  (49 shorter events, 4.2 us)
Async XLA Ops:
  7.2 3.3 %copy-start.7 = (u32[32]{0:T(128)S(1)}, u32[32]{0:T(128)}, u32[]{:S(2)}) copy-start(u32[32]{0:T(128)} %constant.100) | copy-start | bytes 388
  7.2 1.9 copy-start.4
  7.2 168.0 %reduce-scatter.2.cloned.1.call-start = ((), (), s32[]{:S(2)}) async-start(), calls=%async_computation.3 | async-start | bytes 5242880 | tf_op jit(solution)/shard_map/reduce_scatter | solution.py:85
  9.0 2.8 %collective-permute-start = (bf16[256,2048]{1,0:T(8,128)(2,1)S(1)}, bf16[256,2048]{1,0:T(8,128)(2,1)S(1)}, u32[]{:S(2)}, u32[]{:S(2)}) collective-permute-start(bf16[256,2048]{1,0:T(8,128)(2,1)S(1)} %convert_element_type.42), channel_id=1, source_target_pairs={{0,1},{1,0},{2,3},{3,2},{4,5},{5,4},{6,7},{7,6},{8,9},{9,8},{10,11... | collective-permute-start | bytes 3145736 | tf_op jit(solution)/shard_map/ppermute | solution.py:65
  11.8 2.9 %copy-start.2 = (bf16[256,2048]{1,0:T(8,128)(2,1)}, bf16[256,2048]{1,0:T(8,128)(2,1)S(1)}, u32[]{:S(2)}) copy-start(bf16[256,2048]{1,0:T(8,128)(2,1)S(1)} %collective-permute-done) | copy-start | bytes 3145732
  13.3 28.2 %collective-permute-start.1 = (bf16[512,2048]{1,0:T(8,128)(2,1)}, bf16[512,2048]{1,0:T(8,128)(2,1)}, u32[]{:S(2)}, u32[]{:S(2)}) collective-permute-start(bf16[512,2048]{1,0:T(8,128)(2,1)} %pad_maximum_fusion.1), channel_id=1, source_target_pairs={{0,2},{2,4},{4,6},{3,1},{5,3},{7,5},{8,10},{10,12},{12,14},{11,9},... | collective-permute-start | bytes 6291464 | tf_op jit(solution)/shard_map/ppermute | solution.py:70
  25.5 1.6 copy-start.5
  29.6 41.5 %collective-permute-start.4 = (bf16[1024,2048]{1,0:T(8,128)(2,1)S(1)}, bf16[1024,2048]{1,0:T(8,128)(2,1)S(1)}, u32[]{:S(2)}, u32[]{:S(2)}) collective-permute-start(bf16[1024,2048]{1,0:T(8,128)(2,1)S(1)} %convolution_convert_fusion), channel_id=1, source_target_pairs={{0,1},{1,0},{2,3},{3,2},{4,5},{5,4},{6,7},{7,6},{8,9},{9,8},{10,11... | collective-permute-start | bytes 12582920 | tf_op jit(solution)/shard_map/ppermute | solution.py:79
  41.6 28.2 %collective-permute-start.2 = (bf16[512,2048]{1,0:T(8,128)(2,1)}, bf16[512,2048]{1,0:T(8,128)(2,1)}, u32[]{:S(2)}, u32[]{:S(2)}) collective-permute-start(bf16[512,2048]{1,0:T(8,128)(2,1)} %collective-permute-done.1), channel_id=1, source_target_pairs={{2,4},{4,6},{3,1},{5,3},{10,12},{12,14},{11,9},{13,11},{18,20},{20... | collective-permute-start | bytes 6291464 | tf_op jit(solution)/shard_map/ppermute | solution.py:70
  69.8 28.2 %collective-permute-start.3 = (bf16[512,2048]{1,0:T(8,128)(2,1)}, bf16[512,2048]{1,0:T(8,128)(2,1)}, u32[]{:S(2)}, u32[]{:S(2)}) collective-permute-start(bf16[512,2048]{1,0:T(8,128)(2,1)} %collective-permute-done.2), channel_id=1, source_target_pairs={{4,6},{3,1},{12,14},{11,9},{20,22},{19,17},{28,30},{27,25}} | collective-permute-start | bytes 6291464 | tf_op jit(solution)/shard_map/ppermute | solution.py:70
  75.5 23.3 %copy-start.3 = (bf16[256,2048]{1,0:T(8,128)(2,1)S(1)}, bf16[256,2048]{1,0:T(8,128)(2,1)}, u32[]{:S(2)}) copy-start(bf16[256,2048]{1,0:T(8,128)(2,1)} %copy-done.2) | copy-start | bytes 3145732
  98.1 8.2 %collective-permute-start.7 = (bf16[512,2048]{1,0:T(8,128)(2,1)}, bf16[512,2048]{1,0:T(8,128)(2,1)}, u32[]{:S(2)}, u32[]{:S(2)}) collective-permute-start(bf16[512,2048]{1,0:T(8,128)(2,1)} %collective-permute-done.2), channel_id=1, source_target_pairs={{0,1},{1,0},{2,3},{3,2},{4,5},{5,4},{6,7},{7,6},{8,9},{9,8},{10,11... | collective-permute-start | bytes 6291464 | tf_op jit(solution)/shard_map/ppermute | solution.py:86
  98.2 10.6 %collective-permute-start.5 = (bf16[512,2048]{1,0:T(8,128)(2,1)}, bf16[512,2048]{1,0:T(8,128)(2,1)}, u32[]{:S(2)}, u32[]{:S(2)}) collective-permute-start(bf16[512,2048]{1,0:T(8,128)(2,1)} %collective-permute-done.1), channel_id=1, source_target_pairs={{0,1},{1,0},{2,3},{3,2},{4,5},{5,4},{6,7},{7,6},{8,9},{9,8},{10,11... | collective-permute-start | bytes 6291464 | tf_op jit(solution)/shard_map/ppermute | solution.py:86
  98.6 10.2 %collective-permute-start.6 = (bf16[512,2048]{1,0:T(8,128)(2,1)}, bf16[512,2048]{1,0:T(8,128)(2,1)}, u32[]{:S(2)}, u32[]{:S(2)}) collective-permute-start(bf16[512,2048]{1,0:T(8,128)(2,1)} %collective-permute-done.3), channel_id=1, source_target_pairs={{0,1},{1,0},{2,3},{3,2},{4,5},{5,4},{6,7},{7,6},{8,9},{9,8},{10,11... | collective-permute-start | bytes 6291464 | tf_op jit(solution)/shard_map/ppermute | solution.py:86
  102.6 18.1 %all-to-all-start = ((f32[4,128,512]{2,1,0:T(8,128)}), f32[4,128,512]{2,1,0:T(8,128)S(1)}, u32[]{:S(2)}, u32[]{:S(2)}) async-start(f32[4,128,512]{2,1,0:T(8,128)} %fusion.13), calls=%async_computation | async-start | bytes 2097152 | tf_op jit(solution)/shard_map/all_to_all | solution.py:89
  108.8 4.1 %copy-start.6 = (bf16[1,1,512,2048]{3,2,1,0:T(8,128)(2,1)S(1)}, bf16[1,1,512,2048]{3,2,1,0:T(8,128)(2,1)}, u32[]{:S(2)}) copy-start(bf16[1,1,512,2048]{3,2,1,0:T(8,128)(2,1)} %param.8) | copy-start | bytes 6291460
  120.7 1.0 copy-start.1
  121.6 39.8 %all-to-all-start.1 = ((f32[4,128,1536]{2,1,0:T(8,128)}), f32[4,128,1536]{2,1,0:T(8,128)S(1)}, u32[]{:S(2)}, u32[]{:S(2)}) async-start(f32[4,128,1536]{2,1,0:T(8,128)} %fusion), calls=%async_computation.1 | async-start | bytes 6291456 | tf_op jit(solution)/shard_map/all_to_all | solution.py:99
  167.9 7.3 %copy-start = (f32[256,2048]{1,0:T(8,128)S(1)}, f32[256,2048]{1,0:T(8,128)}, u32[]{:S(2)}) copy-start(f32[256,2048]{1,0:T(8,128)} %param.9) | copy-start | bytes 6291460
Sparse Core Ops, SparseCore 0:
  98.2 76.9 reduce-scatter.1
